TPU v7x, 512 devices: a whole 4x4x16 slice. The times are simulated.
512 devices in a mesh: dp: 16 (over x, y_lo, core), ctx: 32 (over z, y_hi).
Axes of the slice: x: 4, y: 4 (y_hi: 2, y_lo: 2; y = y_hi * 2 + y_lo), z: 16, core: 2. Of those that a mesh axis runs over, the one named last changes fastest.
Arguments:
- query: bfloat16 [512, 2, 64, 4096], P(('dp', 'ctx')), may hold values from -8 to 8
- keys: bfloat16 [512, 2, 64, 512], P(('dp', 'ctx')), may hold values from -8 to 8
- values: bfloat16 [512, 2, 64, 512], P(('dp', 'ctx')), may hold values from -6 to 6
- grad_out: bfloat16 [512, 2, 64, 4096], P(('dp', 'ctx')), may hold values from -6 to 6
- lengths: int32 [512], replicated, may hold values from 1 to 192, 65536 in all
Outputs:
- grad_query: bfloat16 [512, 2, 64, 4096], P(('dp', 'ctx'))
- grad_keys: bfloat16 [512, 2, 64, 512], P(('dp', 'ctx'))
- grad_values: bfloat16 [512, 2, 64, 512], P(('dp', 'ctx'))
Inputs may be any that keep to these rules, and one draw needn't show every extreme that they name: lengths sum to 65536, and the largest is 192.
All inputs are finite; a program needn't handle non-finite values.
Results may differ from a plain program's by a relative error of at most 0.025.
Values may be sent and summed in bfloat16 or wider, within the bound.
No kernel may reach another device: no remote copies, remote signals or barrier semaphores. Data moves between devices by JAX's collectives and lax.ppermute only.
A program may use at most 64 MiB of HBM per device.

v0:
```python
import math

import jax
import jax.numpy as jnp
from jax import lax
from jax.sharding import PartitionSpec as P

HEAD = 128
REACH = 3


def passed_along(value, axis, steps):
    count = lax.axis_size(axis)
    leading, last = (max(0, -steps), min(count, count - steps))
    return lax.ppermute(value, axis, [(source, source + steps) for source in range(leading, last)])


def doc_index(position, doc_ends):
    return jnp.sum((doc_ends[None, :] <= position[:, None]).astype(jnp.int32), axis=1)


def on_device(query, keys, values, grad_out, lengths):
    shards = lax.axis_size(("dp", "ctx"))
    my_index = lax.axis_index(("dp", "ctx"))
    half_rows = query.shape[2]
    local_rows = 2 * half_rows
    head_size = HEAD
    kv_width = keys.shape[3]
    kv_count = kv_width // head_size
    group_size = query.shape[3] // kv_width
    reach = REACH
    window = (reach + 1) * half_rows
    score_scale = 1.0 / math.sqrt(head_size)
    query_halves = query.reshape(2, half_rows, kv_count, group_size, head_size)
    grad_halves = grad_out.reshape(2, half_rows, kv_count, group_size, head_size)
    own_keys = keys.reshape(2, half_rows, kv_count, head_size)
    own_values = values.reshape(2, half_rows, kv_count, head_size)
    doc_ends = jnp.cumsum(lengths)
    block_ids = jnp.stack([my_index, 2 * shards - 1 - my_index])
    query_pos = block_ids[:, None] * half_rows + jnp.arange(half_rows, dtype=jnp.int32)[None, :]
    query_doc = doc_index(query_pos.reshape(-1), doc_ends).reshape(2, half_rows)
    key_pos = (block_ids[:, None] - reach) * half_rows + jnp.arange(window, dtype=jnp.int32)[
        None, :
    ]
    key_doc = doc_index(key_pos.reshape(-1), doc_ends).reshape(2, window)
    allowed = (
        (key_pos[:, None, :] >= 0)
        & (key_pos[:, None, :] <= query_pos[:, :, None])
        & (key_doc[:, None, :] == query_doc[:, :, None])
    )
    is_turn = my_index == shards - 1
    own = jnp.concatenate(
        [keys.reshape(2, half_rows, kv_width), values.reshape(2, half_rows, kv_width)], 2
    )

    def move_up(pair):
        early_in = passed_along(pair[0], ("dp", "ctx"), 1)
        late_in = passed_along(pair[1], ("dp", "ctx"), -1)
        late_in = jnp.where(is_turn, pair[0], late_in)
        return jnp.stack([early_in, late_in])

    def climb(step, carried):
        current, stacked = carried
        current = move_up(current)
        stacked = lax.dynamic_update_index_in_dim(stacked, current, reach - step, 1)
        return (current, stacked)

    windows = jnp.zeros((2, reach + 1, half_rows, 2 * kv_width), jnp.bfloat16)
    windows = windows.at[:, reach].set(own)
    moved, windows = lax.fori_loop(1, reach + 1, climb, (own, windows))
    query_grads = []
    log_totals = []
    deltas = []
    for half_idx in range(2):
        both_win = windows[half_idx].reshape(window, 2 * kv_width)
        key_win = both_win[:, :kv_width].reshape(window, kv_count, head_size)
        value_win = both_win[:, kv_width:].reshape(window, kv_count, head_size)
        visible = allowed[half_idx][None, None]
        scores = (
            jnp.einsum(
                "qghd,kgd->ghqk",
                query_halves[half_idx],
                key_win,
                preferred_element_type=jnp.float32,
            )
            * score_scale
        )
        masked = jnp.where(visible, scores, -1e30)
        row_top = jnp.max(masked, axis=3)
        summed = jnp.sum(jnp.where(visible, jnp.exp(masked - row_top[..., None]), 0.0), axis=3)
        log_total = row_top + jnp.log(summed)
        probs = jnp.where(visible, jnp.exp(scores - log_total[..., None]), 0.0).astype(jnp.bfloat16)
        attn = jnp.einsum(
            "ghqk,kgd->qghd", probs, value_win, preferred_element_type=jnp.float32
        ).astype(jnp.bfloat16)
        delta = jnp.transpose(
            jnp.sum(grad_halves[half_idx].astype(jnp.float32) * attn.astype(jnp.float32), axis=3),
            (1, 2, 0),
        )
        dprob = jnp.einsum(
            "qghd,kgd->ghqk", grad_halves[half_idx], value_win, preferred_element_type=jnp.float32
        )
        dscore = (probs.astype(jnp.float32) * (dprob - delta[..., None]) * score_scale).astype(
            jnp.bfloat16
        )
        query_grads.append(
            jnp.einsum("ghqk,kgd->qghd", dscore, key_win, preferred_element_type=jnp.float32)
        )
        log_totals.append(log_total)
        deltas.append(delta)

    def key_terms(half_idx, pack, step):
        block_query = pack[0][half_idx].astype(jnp.bfloat16)
        block_grad = pack[1][half_idx].astype(jnp.bfloat16)
        far_pos = (block_ids[half_idx] + step) * half_rows + jnp.arange(half_rows, dtype=jnp.int32)
        far_doc = doc_index(far_pos, doc_ends)
        visible = (
            (query_pos[half_idx][None, :] <= far_pos[:, None])
            & (query_doc[half_idx][None, :] == far_doc[:, None])
        )[None, None]
        scores = (
            jnp.einsum(
                "qghd,kgd->ghqk",
                block_query,
                own_keys[half_idx],
                preferred_element_type=jnp.float32,
            )
            * score_scale
        )
        probs = jnp.where(visible, jnp.exp(scores - pack[2][half_idx][..., None]), 0.0).astype(
            jnp.bfloat16
        )
        dprob = jnp.einsum(
            "qghd,kgd->ghqk", block_grad, own_values[half_idx], preferred_element_type=jnp.float32
        )
        dscore = (
            probs.astype(jnp.float32) * (dprob - pack[3][half_idx][..., None]) * score_scale
        ).astype(jnp.bfloat16)
        key_part = jnp.einsum(
            "ghqk,qghd->kgd", dscore, block_query, preferred_element_type=jnp.float32
        ).reshape(half_rows, kv_width)
        value_part = jnp.einsum(
            "ghqk,qghd->kgd", probs, block_grad, preferred_element_type=jnp.float32
        ).reshape(half_rows, kv_width)
        return jnp.concatenate([key_part, value_part], 1)

    def move_query(pack):
        early_in = passed_along((pack[0][0], pack[1][0], pack[2][0], pack[3][0]), ("dp", "ctx"), -1)
        late_in = passed_along((pack[0][1], pack[1][1], pack[2][1], pack[3][1]), ("dp", "ctx"), 1)
        return tuple(
            (
                jnp.stack([jnp.where(is_turn, pack[member][1], early_in[member]), late_in[member]])
                for member in range(4)
            )
        )

    start_pack = (
        query_halves.astype(jnp.float32),
        grad_halves.astype(jnp.float32),
        jnp.stack(log_totals),
        jnp.stack(deltas),
    )
    start_sum = jnp.stack([key_terms(0, start_pack, 0), key_terms(1, start_pack, 0)])

    def sink(step, carried):
        pack, running = carried
        pack = move_query(pack)
        running = running + jnp.stack([key_terms(0, pack, step), key_terms(1, pack, step)])
        return (pack, running)

    final_pack, summed_grads = lax.fori_loop(1, reach + 1, sink, (start_pack, start_sum))
    summed_grads = summed_grads.reshape(local_rows, 2 * kv_width)
    grad_keys = summed_grads[:, :kv_width].astype(jnp.bfloat16).reshape(keys.shape)
    grad_values = summed_grads[:, kv_width:].astype(jnp.bfloat16).reshape(values.shape)
    grad_query = jnp.stack(query_grads).astype(jnp.bfloat16).reshape(query.shape)
    return (grad_query, grad_keys, grad_values)


def solution(mesh):
    in_specs = (
        P(("dp", "ctx"), None, None, None),
        P(("dp", "ctx"), None, None, None),
        P(("dp", "ctx"), None, None, None),
        P(("dp", "ctx"), None, None, None),
        P(),
    )
    out_specs = (
        P(("dp", "ctx"), None, None, None),
        P(("dp", "ctx"), None, None, None),
        P(("dp", "ctx"), None, None, None),
    )
    return jax.shard_map(
        on_device, mesh=mesh, in_specs=in_specs, out_specs=out_specs, check_vma=False
    )
```

profile of v0, /device:TPU:6, one launch (start us, length us, event | category | flops | bytes accessed | tf_op | source)
XLA Modules:
  0.0 371.8 jit_solution(13986890230365805427)
XLA Ops:
  12.5 52.9 %while.39 = (s32[]{:T(128)}, bf16[2,64,1024]{2,1,0:T(8,128)(2,1)S(1)}, bf16[2,4,64,1024]{3,2,0,1:T(8,128)(2,1)S(1)}, pred[]{:T(512)}, s32[]{:T(128)}, /*index=5*/s32[]{:T(128)}, s32[]{:T(128)}, s32[]{:T(128)}) while((s32[]{:T(128)}, bf16[2,64,1024]{2,1,0:T(8,128)(2,1)S(1)}, bf16[2,4,64,1024]{3,2,0,1:T(8,128)(2,1)S(1)}, pred[]{:T(512)}, ...), condition=%wide.region_1.2_spmd, body=%wide.region_0.0_spmd.sunk | while | flops 589830 | bytes 2752728 | solution.py:70
  12.5 13.6 %collective-permute-start = (bf16[64,1024]{1,0:T(8,128)(2,1)S(1)}, bf16[64,1024]{1,0:T(8,128)(2,1)S(1)}, u32[]{:S(2)}, u32[]{:S(2)}) collective-permute-start(bf16[64,1024]{1,0:T(8,128)(2,1)S(1)} %get-tuple-element.644), channel_id=1, source_target_pairs={{1,0},{2,1},{3,2},{4,3},{5,4},{6,5},{7,6},{8,7},{9,8},{10,9},{11,1... | collective-permute-start | bytes 393224 | tf_op jit(solution)/shard_map/while/body/eval_jaxpr/ppermute | solution.py:15
  29.9 8.1 %collective-permute-done.1 = bf16[64,1024]{1,0:T(8,128)(2,1)S(1)} collective-permute-done((bf16[64,1024]{1,0:T(8,128)(2,1)S(1)}, bf16[64,1024]{1,0:T(8,128)(2,1)S(1)}, u32[]{:S(2)}, u32[]{:S(2)}) %collective-permute-start.1) | collective-permute-done | bytes 131104 | tf_op jit(solution)/shard_map/while/body/eval_jaxpr/ppermute | solution.py:15
  40.0 5.4 %collective-permute-start.1 = (bf16[64,1024]{1,0:T(8,128)(2,1)S(1)}, bf16[64,1024]{1,0:T(8,128)(2,1)S(1)}, u32[]{:S(2)}, u32[]{:S(2)}) collective-permute-start(bf16[64,1024]{1,0:T(8,128)(2,1)S(1)} %get-tuple-element.645), channel_id=1, source_target_pairs={{0,1},{1,2},{2,3},{3,4},{4,5},{5,6},{6,7},{7,8},{8,9},{9,10},{10,1... | collective-permute-start | bytes 393224 | tf_op jit(solution)/shard_map/while/body/eval_jaxpr/ppermute | solution.py:15
  46.5 4.9 %collective-permute-done.1 = bf16[64,1024]{1,0:T(8,128)(2,1)S(1)} collective-permute-done((bf16[64,1024]{1,0:T(8,128)(2,1)S(1)}, bf16[64,1024]{1,0:T(8,128)(2,1)S(1)}, u32[]{:S(2)}, u32[]{:S(2)}) %collective-permute-start.1) | collective-permute-done | bytes 131104 | tf_op jit(solution)/shard_map/while/body/eval_jaxpr/ppermute | solution.py:15
  53.4 5.4 %collective-permute-start.1 = (bf16[64,1024]{1,0:T(8,128)(2,1)S(1)}, bf16[64,1024]{1,0:T(8,128)(2,1)S(1)}, u32[]{:S(2)}, u32[]{:S(2)}) collective-permute-start(bf16[64,1024]{1,0:T(8,128)(2,1)S(1)} %get-tuple-element.645), channel_id=1, source_target_pairs={{0,1},{1,2},{2,3},{3,4},{4,5},{5,6},{6,7},{7,8},{8,9},{9,10},{10,1... | collective-permute-start | bytes 393224 | tf_op jit(solution)/shard_map/while/body/eval_jaxpr/ppermute | solution.py:15
  59.8 5.4 %collective-permute-done.1 = bf16[64,1024]{1,0:T(8,128)(2,1)S(1)} collective-permute-done((bf16[64,1024]{1,0:T(8,128)(2,1)S(1)}, bf16[64,1024]{1,0:T(8,128)(2,1)S(1)}, u32[]{:S(2)}, u32[]{:S(2)}) %collective-permute-start.1) | collective-permute-done | bytes 131104 | tf_op jit(solution)/shard_map/while/body/eval_jaxpr/ppermute | solution.py:15
  74.9 3.4 fusion.84
  82.3 3.0 fusion.87
  90.8 3.5 fusion.83
  96.7 2.3 pad_maximum_fusion.5
  100.7 2.1 fusion.88
  105.3 264.7 %while.40 = (s32[]{:T(128)}, bf16[2,64,4,8,128]{4,1,3,2,0:T(8,128)(2,1)S(1)}, bf16[2,64,4,8,128]{4,1,3,2,0:T(8,128)(2,1)S(1)}, f32[2,4,8,64]{3,2,1,0:T(8,128)S(1...) while((s32[]{:T(128)}, ...), condition=%wide.region_17.18_spmd, body=%wide.region_14.17_spmd.sunk | while | flops 272994304 | bytes 48300408 | solution.py:171
  107.2 7.9 %collective-permute-start.9 = (f32[4,8,64]{2,1,0:T(8,128)S(1)}, f32[4,8,64]{2,1,0:T(8,128)S(1)}, u32[]{:S(2)}, u32[]{:S(2)}) collective-permute-start(f32[4,8,64]{2,1,0:T(8,128)S(1)} %get-tuple-element.671), channel_id=1, source_target_pairs={{1,0},{2,1},{3,2},{4,3},{5,4},{6,5},{7,6},{8,7},{9,8},{10,9},{11,1... | collective-permute-start | bytes 24584 | tf_op jit(solution)/shard_map/while/body/eval_jaxpr/ppermute | solution.py:15
  117.0 7.9 %collective-permute-start.7 = (f32[4,8,64]{2,1,0:T(8,128)S(1)}, f32[4,8,64]{2,1,0:T(8,128)S(1)}, u32[]{:S(2)}, u32[]{:S(2)}) collective-permute-start(f32[4,8,64]{2,1,0:T(8,128)S(1)} %get-tuple-element.669), channel_id=1, source_target_pairs={{1,0},{2,1},{3,2},{4,3},{5,4},{6,5},{7,6},{8,7},{9,8},{10,9},{11,1... | collective-permute-start | bytes 24584 | tf_op jit(solution)/shard_map/while/body/eval_jaxpr/ppermute | solution.py:15
  129.4 7.9 %collective-permute-start.5 = (bf16[64,4,8,128]{3,0,2,1:T(8,128)(2,1)}, bf16[64,4,8,128]{3,0,2,1:T(8,128)(2,1)}, u32[]{:S(2)}, u32[]{:S(2)}) collective-permute-start(bf16[64,4,8,128]{3,0,2,1:T(8,128)(2,1)} %get-tuple-element.666), channel_id=1, source_target_pairs={{1,0},{2,1},{3,2},{4,3},{5,4},{6,5},{7,6},{8,7},{9,8},{10,9},{11,1... | collective-permute-start | bytes 1572872 | tf_op jit(solution)/shard_map/while/body/eval_jaxpr/ppermute | solution.py:15
  137.3 1.9 collective-permute-start.3
  140.1 5.4 %collective-permute-start.2 = (bf16[64,4,8,128]{3,0,2,1:T(8,128)(2,1)}, bf16[64,4,8,128]{3,0,2,1:T(8,128)(2,1)S(1)}, u32[]{:S(2)}, u32[]{:S(2)}) collective-permute-start(bf16[64,4,8,128]{3,0,2,1:T(8,128)(2,1)} %get-tuple-element.662), channel_id=1, source_target_pairs={{0,1},{1,2},{2,3},{3,4},{4,5},{5,6},{6,7},{7,8},{8,9},{9,10},{10,1... | collective-permute-start | bytes 1572872 | tf_op jit(solution)/shard_map/while/body/eval_jaxpr/ppermute | solution.py:15
  147.7 17.7 %collective-permute-done.5 = bf16[64,4,8,128]{3,0,2,1:T(8,128)(2,1)} collective-permute-done((bf16[64,4,8,128]{3,0,2,1:T(8,128)(2,1)}, bf16[64,4,8,128]{3,0,2,1:T(8,128)(2,1)}, u32[]{:S(2)}, u32[]{:S(2)}) %collective-permute-start.5) | collective-permute-done | bytes 524320 | tf_op jit(solution)/shard_map/while/body/eval_jaxpr/ppermute | solution.py:15
  167.3 8.4 %collective-permute-done.3 = bf16[64,4,8,128]{3,0,2,1:T(8,128)(2,1)} collective-permute-done((bf16[64,4,8,128]{3,0,2,1:T(8,128)(2,1)}, bf16[64,4,8,128]{3,0,2,1:T(8,128)(2,1)}, u32[]{:S(2)}, u32[]{:S(2)}) %collective-permute-start.3) | collective-permute-done | bytes 524320 | tf_op jit(solution)/shard_map/while/body/eval_jaxpr/ppermute | solution.py:15
  194.0 7.9 %collective-permute-start.9 = (f32[4,8,64]{2,1,0:T(8,128)S(1)}, f32[4,8,64]{2,1,0:T(8,128)S(1)}, u32[]{:S(2)}, u32[]{:S(2)}) collective-permute-start(f32[4,8,64]{2,1,0:T(8,128)S(1)} %get-tuple-element.671), channel_id=1, source_target_pairs={{1,0},{2,1},{3,2},{4,3},{5,4},{6,5},{7,6},{8,7},{9,8},{10,9},{11,1... | collective-permute-start | bytes 24584 | tf_op jit(solution)/shard_map/while/body/eval_jaxpr/ppermute | solution.py:15
  203.8 7.9 %collective-permute-start.7 = (f32[4,8,64]{2,1,0:T(8,128)S(1)}, f32[4,8,64]{2,1,0:T(8,128)S(1)}, u32[]{:S(2)}, u32[]{:S(2)}) collective-permute-start(f32[4,8,64]{2,1,0:T(8,128)S(1)} %get-tuple-element.669), channel_id=1, source_target_pairs={{1,0},{2,1},{3,2},{4,3},{5,4},{6,5},{7,6},{8,7},{9,8},{10,9},{11,1... | collective-permute-start | bytes 24584 | tf_op jit(solution)/shard_map/while/body/eval_jaxpr/ppermute | solution.py:15
  216.2 7.9 %collective-permute-start.5 = (bf16[64,4,8,128]{3,0,2,1:T(8,128)(2,1)}, bf16[64,4,8,128]{3,0,2,1:T(8,128)(2,1)}, u32[]{:S(2)}, u32[]{:S(2)}) collective-permute-start(bf16[64,4,8,128]{3,0,2,1:T(8,128)(2,1)} %get-tuple-element.666), channel_id=1, source_target_pairs={{1,0},{2,1},{3,2},{4,3},{5,4},{6,5},{7,6},{8,7},{9,8},{10,9},{11,1... | collective-permute-start | bytes 1572872 | tf_op jit(solution)/shard_map/while/body/eval_jaxpr/ppermute | solution.py:15
  226.9 5.4 %collective-permute-start.2 = (bf16[64,4,8,128]{3,0,2,1:T(8,128)(2,1)}, bf16[64,4,8,128]{3,0,2,1:T(8,128)(2,1)S(1)}, u32[]{:S(2)}, u32[]{:S(2)}) collective-permute-start(bf16[64,4,8,128]{3,0,2,1:T(8,128)(2,1)} %get-tuple-element.662), channel_id=1, source_target_pairs={{0,1},{1,2},{2,3},{3,4},{4,5},{5,6},{6,7},{7,8},{8,9},{9,10},{10,1... | collective-permute-start | bytes 1572872 | tf_op jit(solution)/shard_map/while/body/eval_jaxpr/ppermute | solution.py:15
  234.4 20.7 %collective-permute-done.5 = bf16[64,4,8,128]{3,0,2,1:T(8,128)(2,1)} collective-permute-done((bf16[64,4,8,128]{3,0,2,1:T(8,128)(2,1)}, bf16[64,4,8,128]{3,0,2,1:T(8,128)(2,1)}, u32[]{:S(2)}, u32[]{:S(2)}) %collective-permute-start.5) | collective-permute-done | bytes 524320 | tf_op jit(solution)/shard_map/while/body/eval_jaxpr/ppermute | solution.py:15
  257.1 7.8 %collective-permute-done.3 = bf16[64,4,8,128]{3,0,2,1:T(8,128)(2,1)} collective-permute-done((bf16[64,4,8,128]{3,0,2,1:T(8,128)(2,1)}, bf16[64,4,8,128]{3,0,2,1:T(8,128)(2,1)}, u32[]{:S(2)}, u32[]{:S(2)}) %collective-permute-start.3) | collective-permute-done | bytes 524320 | tf_op jit(solution)/shard_map/while/body/eval_jaxpr/ppermute | solution.py:15
  283.2 7.9 %collective-permute-start.9 = (f32[4,8,64]{2,1,0:T(8,128)S(1)}, f32[4,8,64]{2,1,0:T(8,128)S(1)}, u32[]{:S(2)}, u32[]{:S(2)}) collective-permute-start(f32[4,8,64]{2,1,0:T(8,128)S(1)} %get-tuple-element.671), channel_id=1, source_target_pairs={{1,0},{2,1},{3,2},{4,3},{5,4},{6,5},{7,6},{8,7},{9,8},{10,9},{11,1... | collective-permute-start | bytes 24584 | tf_op jit(solution)/shard_map/while/body/eval_jaxpr/ppermute | solution.py:15
  293.0 7.9 %collective-permute-start.7 = (f32[4,8,64]{2,1,0:T(8,128)S(1)}, f32[4,8,64]{2,1,0:T(8,128)S(1)}, u32[]{:S(2)}, u32[]{:S(2)}) collective-permute-start(f32[4,8,64]{2,1,0:T(8,128)S(1)} %get-tuple-element.669), channel_id=1, source_target_pairs={{1,0},{2,1},{3,2},{4,3},{5,4},{6,5},{7,6},{8,7},{9,8},{10,9},{11,1... | collective-permute-start | bytes 24584 | tf_op jit(solution)/shard_map/while/body/eval_jaxpr/ppermute | solution.py:15
  305.4 7.9 %collective-permute-start.5 = (bf16[64,4,8,128]{3,0,2,1:T(8,128)(2,1)}, bf16[64,4,8,128]{3,0,2,1:T(8,128)(2,1)}, u32[]{:S(2)}, u32[]{:S(2)}) collective-permute-start(bf16[64,4,8,128]{3,0,2,1:T(8,128)(2,1)} %get-tuple-element.666), channel_id=1, source_target_pairs={{1,0},{2,1},{3,2},{4,3},{5,4},{6,5},{7,6},{8,7},{9,8},{10,9},{11,1... | collective-permute-start | bytes 1572872 | tf_op jit(solution)/shard_map/while/body/eval_jaxpr/ppermute | solution.py:15
  316.1 5.4 %collective-permute-start.2 = (bf16[64,4,8,128]{3,0,2,1:T(8,128)(2,1)}, bf16[64,4,8,128]{3,0,2,1:T(8,128)(2,1)S(1)}, u32[]{:S(2)}, u32[]{:S(2)}) collective-permute-start(bf16[64,4,8,128]{3,0,2,1:T(8,128)(2,1)} %get-tuple-element.662), channel_id=1, source_target_pairs={{0,1},{1,2},{2,3},{3,4},{4,5},{5,6},{6,7},{7,8},{8,9},{9,10},{10,1... | collective-permute-start | bytes 1572872 | tf_op jit(solution)/shard_map/while/body/eval_jaxpr/ppermute | solution.py:15
  323.6 20.6 %collective-permute-done.5 = bf16[64,4,8,128]{3,0,2,1:T(8,128)(2,1)} collective-permute-done((bf16[64,4,8,128]{3,0,2,1:T(8,128)(2,1)}, bf16[64,4,8,128]{3,0,2,1:T(8,128)(2,1)}, u32[]{:S(2)}, u32[]{:S(2)}) %collective-permute-start.5) | collective-permute-done | bytes 524320 | tf_op jit(solution)/shard_map/while/body/eval_jaxpr/ppermute | solution.py:15
  346.2 7.4 %collective-permute-done.3 = bf16[64,4,8,128]{3,0,2,1:T(8,128)(2,1)} collective-permute-done((bf16[64,4,8,128]{3,0,2,1:T(8,128)(2,1)}, bf16[64,4,8,128]{3,0,2,1:T(8,128)(2,1)}, u32[]{:S(2)}, u32[]{:S(2)}) %collective-permute-start.3) | collective-permute-done | bytes 524320 | tf_op jit(solution)/shard_map/while/body/eval_jaxpr/ppermute | solution.py:15
  (367 shorter events, 140.4 us)
Async XLA Ops:
  12.5 17.3 %collective-permute-start = (bf16[64,1024]{1,0:T(8,128)(2,1)S(1)}, bf16[64,1024]{1,0:T(8,128)(2,1)S(1)}, u32[]{:S(2)}, u32[]{:S(2)}) collective-permute-start(bf16[64,1024]{1,0:T(8,128)(2,1)S(1)} %get-tuple-element.644), channel_id=1, source_target_pairs={{1,0},{2,1},{3,2},{4,3},{5,4},{6,5},{7,6},{8,7},{9,8},{10,9},{11,1... | collective-permute-start | bytes 393224 | tf_op jit(solution)/shard_map/while/body/eval_jaxpr/ppermute | solution.py:15
  26.1 11.9 %collective-permute-start.1 = (bf16[64,1024]{1,0:T(8,128)(2,1)S(1)}, bf16[64,1024]{1,0:T(8,128)(2,1)S(1)}, u32[]{:S(2)}, u32[]{:S(2)}) collective-permute-start(bf16[64,1024]{1,0:T(8,128)(2,1)S(1)} %get-tuple-element.645), channel_id=1, source_target_pairs={{0,1},{1,2},{2,3},{3,4},{4,5},{5,6},{6,7},{7,8},{8,9},{9,10},{10,1... | collective-permute-start | bytes 393224 | tf_op jit(solution)/shard_map/while/body/eval_jaxpr/ppermute | solution.py:15
  38.1 8.4 %collective-permute-start = (bf16[64,1024]{1,0:T(8,128)(2,1)S(1)}, bf16[64,1024]{1,0:T(8,128)(2,1)S(1)}, u32[]{:S(2)}, u32[]{:S(2)}) collective-permute-start(bf16[64,1024]{1,0:T(8,128)(2,1)S(1)} %get-tuple-element.644), channel_id=1, source_target_pairs={{1,0},{2,1},{3,2},{4,3},{5,4},{6,5},{7,6},{8,7},{9,8},{10,9},{11,1... | collective-permute-start | bytes 393224 | tf_op jit(solution)/shard_map/while/body/eval_jaxpr/ppermute | solution.py:15
  40.0 11.4 %collective-permute-start.1 = (bf16[64,1024]{1,0:T(8,128)(2,1)S(1)}, bf16[64,1024]{1,0:T(8,128)(2,1)S(1)}, u32[]{:S(2)}, u32[]{:S(2)}) collective-permute-start(bf16[64,1024]{1,0:T(8,128)(2,1)S(1)} %get-tuple-element.645), channel_id=1, source_target_pairs={{0,1},{1,2},{2,3},{3,4},{4,5},{5,6},{6,7},{7,8},{8,9},{9,10},{10,1... | collective-permute-start | bytes 393224 | tf_op jit(solution)/shard_map/while/body/eval_jaxpr/ppermute | solution.py:15
  51.5 8.4 %collective-permute-start = (bf16[64,1024]{1,0:T(8,128)(2,1)S(1)}, bf16[64,1024]{1,0:T(8,128)(2,1)S(1)}, u32[]{:S(2)}, u32[]{:S(2)}) collective-permute-start(bf16[64,1024]{1,0:T(8,128)(2,1)S(1)} %get-tuple-element.644), channel_id=1, source_target_pairs={{1,0},{2,1},{3,2},{4,3},{5,4},{6,5},{7,6},{8,7},{9,8},{10,9},{11,1... | collective-permute-start | bytes 393224 | tf_op jit(solution)/shard_map/while/body/eval_jaxpr/ppermute | solution.py:15
  53.4 11.9 %collective-permute-start.1 = (bf16[64,1024]{1,0:T(8,128)(2,1)S(1)}, bf16[64,1024]{1,0:T(8,128)(2,1)S(1)}, u32[]{:S(2)}, u32[]{:S(2)}) collective-permute-start(bf16[64,1024]{1,0:T(8,128)(2,1)S(1)} %get-tuple-element.645), channel_id=1, source_target_pairs={{0,1},{1,2},{2,3},{3,4},{4,5},{5,6},{6,7},{7,8},{8,9},{9,10},{10,1... | collective-permute-start | bytes 393224 | tf_op jit(solution)/shard_map/while/body/eval_jaxpr/ppermute | solution.py:15
  105.3 40.3 %collective-permute-start.8 = (f32[4,8,64]{2,1,0:T(8,128)S(1)}, f32[4,8,64]{2,1,0:T(8,128)S(1)}, u32[]{:S(2)}, u32[]{:S(2)}) collective-permute-start(f32[4,8,64]{2,1,0:T(8,128)S(1)} %get-tuple-element.670), channel_id=1, source_target_pairs={{0,1},{1,2},{2,3},{3,4},{4,5},{5,6},{6,7},{7,8},{8,9},{9,10},{10,1... | collective-permute-start | bytes 24584 | tf_op jit(solution)/shard_map/while/body/eval_jaxpr/ppermute | solution.py:15
  107.2 22.2 %collective-permute-start.9 = (f32[4,8,64]{2,1,0:T(8,128)S(1)}, f32[4,8,64]{2,1,0:T(8,128)S(1)}, u32[]{:S(2)}, u32[]{:S(2)}) collective-permute-start(f32[4,8,64]{2,1,0:T(8,128)S(1)} %get-tuple-element.671), channel_id=1, source_target_pairs={{1,0},{2,1},{3,2},{4,3},{5,4},{6,5},{7,6},{8,7},{9,8},{10,9},{11,1... | collective-permute-start | bytes 24584 | tf_op jit(solution)/shard_map/while/body/eval_jaxpr/ppermute | solution.py:15
  115.1 25.0 %collective-permute-start.6 = (f32[4,8,64]{2,1,0:T(8,128)S(1)}, f32[4,8,64]{2,1,0:T(8,128)S(1)}, u32[]{:S(2)}, u32[]{:S(2)}) collective-permute-start(f32[4,8,64]{2,1,0:T(8,128)S(1)} %get-tuple-element.668), channel_id=1, source_target_pairs={{0,1},{1,2},{2,3},{3,4},{4,5},{5,6},{6,7},{7,8},{8,9},{9,10},{10,1... | collective-permute-start | bytes 24584 | tf_op jit(solution)/shard_map/while/body/eval_jaxpr/ppermute | solution.py:15
  117.0 20.2 %collective-permute-start.7 = (f32[4,8,64]{2,1,0:T(8,128)S(1)}, f32[4,8,64]{2,1,0:T(8,128)S(1)}, u32[]{:S(2)}, u32[]{:S(2)}) collective-permute-start(f32[4,8,64]{2,1,0:T(8,128)S(1)} %get-tuple-element.669), channel_id=1, source_target_pairs={{1,0},{2,1},{3,2},{4,3},{5,4},{6,5},{7,6},{8,7},{9,8},{10,9},{11,1... | collective-permute-start | bytes 24584 | tf_op jit(solution)/shard_map/while/body/eval_jaxpr/ppermute | solution.py:15
  126.0 53.6 %collective-permute-start.4 = (bf16[64,4,8,128]{3,0,2,1:T(8,128)(2,1)}, bf16[64,4,8,128]{3,0,2,1:T(8,128)(2,1)S(1)}, u32[]{:S(2)}, u32[]{:S(2)}) collective-permute-start(bf16[64,4,8,128]{3,0,2,1:T(8,128)(2,1)} %get-tuple-element.665), channel_id=1, source_target_pairs={{0,1},{1,2},{2,3},{3,4},{4,5},{5,6},{6,7},{7,8},{8,9},{9,10},{10,1... | collective-permute-start | bytes 1572872 | tf_op jit(solution)/shard_map/while/body/eval_jaxpr/ppermute | solution.py:15
  129.4 35.9 %collective-permute-start.5 = (bf16[64,4,8,128]{3,0,2,1:T(8,128)(2,1)}, bf16[64,4,8,128]{3,0,2,1:T(8,128)(2,1)}, u32[]{:S(2)}, u32[]{:S(2)}) collective-permute-start(bf16[64,4,8,128]{3,0,2,1:T(8,128)(2,1)} %get-tuple-element.666), channel_id=1, source_target_pairs={{1,0},{2,1},{3,2},{4,3},{5,4},{6,5},{7,6},{8,7},{9,8},{10,9},{11,1... | collective-permute-start | bytes 1572872 | tf_op jit(solution)/shard_map/while/body/eval_jaxpr/ppermute | solution.py:15
  137.3 38.4 %collective-permute-start.3 = (bf16[64,4,8,128]{3,0,2,1:T(8,128)(2,1)}, bf16[64,4,8,128]{3,0,2,1:T(8,128)(2,1)}, u32[]{:S(2)}, u32[]{:S(2)}) collective-permute-start(bf16[64,4,8,128]{3,0,2,1:T(8,128)(2,1)} %get-tuple-element.663), channel_id=1, source_target_pairs={{1,0},{2,1},{3,2},{4,3},{5,4},{6,5},{7,6},{8,7},{9,8},{10,9},{11,1... | collective-permute-start | bytes 1572872 | tf_op jit(solution)/shard_map/while/body/eval_jaxpr/ppermute | solution.py:15
  140.1 43.6 %collective-permute-start.2 = (bf16[64,4,8,128]{3,0,2,1:T(8,128)(2,1)}, bf16[64,4,8,128]{3,0,2,1:T(8,128)(2,1)S(1)}, u32[]{:S(2)}, u32[]{:S(2)}) collective-permute-start(bf16[64,4,8,128]{3,0,2,1:T(8,128)(2,1)} %get-tuple-element.662), channel_id=1, source_target_pairs={{0,1},{1,2},{2,3},{3,4},{4,5},{5,6},{6,7},{7,8},{8,9},{9,10},{10,1... | collective-permute-start | bytes 1572872 | tf_op jit(solution)/shard_map/while/body/eval_jaxpr/ppermute | solution.py:15
  192.1 40.3 %collective-permute-start.8 = (f32[4,8,64]{2,1,0:T(8,128)S(1)}, f32[4,8,64]{2,1,0:T(8,128)S(1)}, u32[]{:S(2)}, u32[]{:S(2)}) collective-permute-start(f32[4,8,64]{2,1,0:T(8,128)S(1)} %get-tuple-element.670), channel_id=1, source_target_pairs={{0,1},{1,2},{2,3},{3,4},{4,5},{5,6},{6,7},{7,8},{8,9},{9,10},{10,1... | collective-permute-start | bytes 24584 | tf_op jit(solution)/shard_map/while/body/eval_jaxpr/ppermute | solution.py:15
  194.0 22.2 %collective-permute-start.9 = (f32[4,8,64]{2,1,0:T(8,128)S(1)}, f32[4,8,64]{2,1,0:T(8,128)S(1)}, u32[]{:S(2)}, u32[]{:S(2)}) collective-permute-start(f32[4,8,64]{2,1,0:T(8,128)S(1)} %get-tuple-element.671), channel_id=1, source_target_pairs={{1,0},{2,1},{3,2},{4,3},{5,4},{6,5},{7,6},{8,7},{9,8},{10,9},{11,1... | collective-permute-start | bytes 24584 | tf_op jit(solution)/shard_map/while/body/eval_jaxpr/ppermute | solution.py:15
  201.9 25.0 %collective-permute-start.6 = (f32[4,8,64]{2,1,0:T(8,128)S(1)}, f32[4,8,64]{2,1,0:T(8,128)S(1)}, u32[]{:S(2)}, u32[]{:S(2)}) collective-permute-start(f32[4,8,64]{2,1,0:T(8,128)S(1)} %get-tuple-element.668), channel_id=1, source_target_pairs={{0,1},{1,2},{2,3},{3,4},{4,5},{5,6},{6,7},{7,8},{8,9},{9,10},{10,1... | collective-permute-start | bytes 24584 | tf_op jit(solution)/shard_map/while/body/eval_jaxpr/ppermute | solution.py:15
  203.8 20.2 %collective-permute-start.7 = (f32[4,8,64]{2,1,0:T(8,128)S(1)}, f32[4,8,64]{2,1,0:T(8,128)S(1)}, u32[]{:S(2)}, u32[]{:S(2)}) collective-permute-start(f32[4,8,64]{2,1,0:T(8,128)S(1)} %get-tuple-element.669), channel_id=1, source_target_pairs={{1,0},{2,1},{3,2},{4,3},{5,4},{6,5},{7,6},{8,7},{9,8},{10,9},{11,1... | collective-permute-start | bytes 24584 | tf_op jit(solution)/shard_map/while/body/eval_jaxpr/ppermute | solution.py:15
  212.8 56.0 %collective-permute-start.4 = (bf16[64,4,8,128]{3,0,2,1:T(8,128)(2,1)}, bf16[64,4,8,128]{3,0,2,1:T(8,128)(2,1)S(1)}, u32[]{:S(2)}, u32[]{:S(2)}) collective-permute-start(bf16[64,4,8,128]{3,0,2,1:T(8,128)(2,1)} %get-tuple-element.665), channel_id=1, source_target_pairs={{0,1},{1,2},{2,3},{3,4},{4,5},{5,6},{6,7},{7,8},{8,9},{9,10},{10,1... | collective-permute-start | bytes 1572872 | tf_op jit(solution)/shard_map/while/body/eval_jaxpr/ppermute | solution.py:15
  216.2 39.0 %collective-permute-start.5 = (bf16[64,4,8,128]{3,0,2,1:T(8,128)(2,1)}, bf16[64,4,8,128]{3,0,2,1:T(8,128)(2,1)}, u32[]{:S(2)}, u32[]{:S(2)}) collective-permute-start(bf16[64,4,8,128]{3,0,2,1:T(8,128)(2,1)} %get-tuple-element.666), channel_id=1, source_target_pairs={{1,0},{2,1},{3,2},{4,3},{5,4},{6,5},{7,6},{8,7},{9,8},{10,9},{11,1... | collective-permute-start | bytes 1572872 | tf_op jit(solution)/shard_map/while/body/eval_jaxpr/ppermute | solution.py:15
  224.1 40.8 %collective-permute-start.3 = (bf16[64,4,8,128]{3,0,2,1:T(8,128)(2,1)}, bf16[64,4,8,128]{3,0,2,1:T(8,128)(2,1)}, u32[]{:S(2)}, u32[]{:S(2)}) collective-permute-start(bf16[64,4,8,128]{3,0,2,1:T(8,128)(2,1)} %get-tuple-element.663), channel_id=1, source_target_pairs={{1,0},{2,1},{3,2},{4,3},{5,4},{6,5},{7,6},{8,7},{9,8},{10,9},{11,1... | collective-permute-start | bytes 1572872 | tf_op jit(solution)/shard_map/while/body/eval_jaxpr/ppermute | solution.py:15
  226.9 46.0 %collective-permute-start.2 = (bf16[64,4,8,128]{3,0,2,1:T(8,128)(2,1)}, bf16[64,4,8,128]{3,0,2,1:T(8,128)(2,1)S(1)}, u32[]{:S(2)}, u32[]{:S(2)}) collective-permute-start(bf16[64,4,8,128]{3,0,2,1:T(8,128)(2,1)} %get-tuple-element.662), channel_id=1, source_target_pairs={{0,1},{1,2},{2,3},{3,4},{4,5},{5,6},{6,7},{7,8},{8,9},{9,10},{10,1... | collective-permute-start | bytes 1572872 | tf_op jit(solution)/shard_map/while/body/eval_jaxpr/ppermute | solution.py:15
  234.4 32.3 %copy-start.9 = (f32[4,8,64]{1,2,0:T(8,128)S(1)}, f32[4,8,64]{1,2,0:T(8,128)}, u32[]{:S(2)}) copy-start(f32[4,8,64]{1,2,0:T(8,128)} %copy.479) | copy-start | bytes 24580 | tf_op jit(solution)/shard_map/while
  234.4 32.3 %copy-start.15 = (bf16[2,64,4,128]{3,1,2,0:T(8,128)(2,1)S(1)}, bf16[2,64,4,128]{3,1,2,0:T(8,128)(2,1)}, u32[]{:S(2)}) copy-start(bf16[2,64,4,128]{3,1,2,0:T(8,128)(2,1)} %get-tuple-element.749) | copy-start | bytes 393220 | tf_op jit(solution)/shard_map/while
  281.3 40.3 %collective-permute-start.8 = (f32[4,8,64]{2,1,0:T(8,128)S(1)}, f32[4,8,64]{2,1,0:T(8,128)S(1)}, u32[]{:S(2)}, u32[]{:S(2)}) collective-permute-start(f32[4,8,64]{2,1,0:T(8,128)S(1)} %get-tuple-element.670), channel_id=1, source_target_pairs={{0,1},{1,2},{2,3},{3,4},{4,5},{5,6},{6,7},{7,8},{8,9},{9,10},{10,1... | collective-permute-start | bytes 24584 | tf_op jit(solution)/shard_map/while/body/eval_jaxpr/ppermute | solution.py:15
  283.2 22.2 %collective-permute-start.9 = (f32[4,8,64]{2,1,0:T(8,128)S(1)}, f32[4,8,64]{2,1,0:T(8,128)S(1)}, u32[]{:S(2)}, u32[]{:S(2)}) collective-permute-start(f32[4,8,64]{2,1,0:T(8,128)S(1)} %get-tuple-element.671), channel_id=1, source_target_pairs={{1,0},{2,1},{3,2},{4,3},{5,4},{6,5},{7,6},{8,7},{9,8},{10,9},{11,1... | collective-permute-start | bytes 24584 | tf_op jit(solution)/shard_map/while/body/eval_jaxpr/ppermute | solution.py:15
  291.1 25.0 %collective-permute-start.6 = (f32[4,8,64]{2,1,0:T(8,128)S(1)}, f32[4,8,64]{2,1,0:T(8,128)S(1)}, u32[]{:S(2)}, u32[]{:S(2)}) collective-permute-start(f32[4,8,64]{2,1,0:T(8,128)S(1)} %get-tuple-element.668), channel_id=1, source_target_pairs={{0,1},{1,2},{2,3},{3,4},{4,5},{5,6},{6,7},{7,8},{8,9},{9,10},{10,1... | collective-permute-start | bytes 24584 | tf_op jit(solution)/shard_map/while/body/eval_jaxpr/ppermute | solution.py:15
  293.0 20.2 %collective-permute-start.7 = (f32[4,8,64]{2,1,0:T(8,128)S(1)}, f32[4,8,64]{2,1,0:T(8,128)S(1)}, u32[]{:S(2)}, u32[]{:S(2)}) collective-permute-start(f32[4,8,64]{2,1,0:T(8,128)S(1)} %get-tuple-element.669), channel_id=1, source_target_pairs={{1,0},{2,1},{3,2},{4,3},{5,4},{6,5},{7,6},{8,7},{9,8},{10,9},{11,1... | collective-permute-start | bytes 24584 | tf_op jit(solution)/shard_map/while/body/eval_jaxpr/ppermute | solution.py:15
  302.0 55.6 %collective-permute-start.4 = (bf16[64,4,8,128]{3,0,2,1:T(8,128)(2,1)}, bf16[64,4,8,128]{3,0,2,1:T(8,128)(2,1)S(1)}, u32[]{:S(2)}, u32[]{:S(2)}) collective-permute-start(bf16[64,4,8,128]{3,0,2,1:T(8,128)(2,1)} %get-tuple-element.665), channel_id=1, source_target_pairs={{0,1},{1,2},{2,3},{3,4},{4,5},{5,6},{6,7},{7,8},{8,9},{9,10},{10,1... | collective-permute-start | bytes 1572872 | tf_op jit(solution)/shard_map/while/body/eval_jaxpr/ppermute | solution.py:15
  305.4 38.9 %collective-permute-start.5 = (bf16[64,4,8,128]{3,0,2,1:T(8,128)(2,1)}, bf16[64,4,8,128]{3,0,2,1:T(8,128)(2,1)}, u32[]{:S(2)}, u32[]{:S(2)}) collective-permute-start(bf16[64,4,8,128]{3,0,2,1:T(8,128)(2,1)} %get-tuple-element.666), channel_id=1, source_target_pairs={{1,0},{2,1},{3,2},{4,3},{5,4},{6,5},{7,6},{8,7},{9,8},{10,9},{11,1... | collective-permute-start | bytes 1572872 | tf_op jit(solution)/shard_map/while/body/eval_jaxpr/ppermute | solution.py:15
  313.3 40.4 %collective-permute-start.3 = (bf16[64,4,8,128]{3,0,2,1:T(8,128)(2,1)}, bf16[64,4,8,128]{3,0,2,1:T(8,128)(2,1)}, u32[]{:S(2)}, u32[]{:S(2)}) collective-permute-start(bf16[64,4,8,128]{3,0,2,1:T(8,128)(2,1)} %get-tuple-element.663), channel_id=1, source_target_pairs={{1,0},{2,1},{3,2},{4,3},{5,4},{6,5},{7,6},{8,7},{9,8},{10,9},{11,1... | collective-permute-start | bytes 1572872 | tf_op jit(solution)/shard_map/while/body/eval_jaxpr/ppermute | solution.py:15
  316.1 45.6 %collective-permute-start.2 = (bf16[64,4,8,128]{3,0,2,1:T(8,128)(2,1)}, bf16[64,4,8,128]{3,0,2,1:T(8,128)(2,1)S(1)}, u32[]{:S(2)}, u32[]{:S(2)}) collective-permute-start(bf16[64,4,8,128]{3,0,2,1:T(8,128)(2,1)} %get-tuple-element.662), channel_id=1, source_target_pairs={{0,1},{1,2},{2,3},{3,4},{4,5},{5,6},{6,7},{7,8},{8,9},{9,10},{10,1... | collective-permute-start | bytes 1572872 | tf_op jit(solution)/shard_map/while/body/eval_jaxpr/ppermute | solution.py:15
  (60 other events, 386.1 us)
where the time goes:
time: 374 us; the launch traced here: 372 us
  starting transfers between devices  140 us (37%)
  waiting for transfers between devices  105 us (28%)
  matrix products  44.7 us (12%)
  local copies, waits for them, and re-layouts  41.4 us (11%)
  other arithmetic  38.1 us (10%)
    ppermute x30, starting transfers between devices, passed_along(): lax.ppermute(value, axis, [(source, source + steps) for source in range(l...  140 us
    ppermute x30, waiting for transfers between devices, passed_along(): lax.ppermute(value, axis, [(source, source + steps) for source in range(l...  105 us
    dot_general x8, matrix products, key_terms(): jnp.einsum('ghqk,qghd->kgd', dscore, block_query, preferred_element_type=...  10.7 us
    dot_general x8, matrix products, key_terms(): jnp.einsum('qghd,kgd->ghqk', block_query, own_keys[half_idx], preferred_e...  9.71 us
    dot_general x8, matrix products, key_terms(): jnp.einsum('ghqk,qghd->kgd', probs, block_grad, preferred_element_type=jn...  8.43 us
  transfers between devices with their start and end apart: 30, of which 12 were waited for; matrix products, arithmetic and copies ran while one was open for 12% of the time, Pallas kernels for 0%

commit v1 on v0

v1 whole, which is shorter than its diff:
```python
import functools
import math

import jax
import jax.numpy as jnp
from jax import lax
from jax.experimental import pallas as pl
from jax.experimental.pallas import tpu as pltpu
from jax.sharding import PartitionSpec as P

HEAD = 128
REACH = 3
AXIS = ("dp", "ctx")


def shifted(value, steps):
    count = lax.axis_size(AXIS)
    pairs = [(s, s + steps) for s in range(count) if 0 <= s + steps < count]
    return lax.ppermute(value, AXIS, pairs)


def window_kernel(lo_ref, q_ref, do_ref, w0, w1, w2, w3, dq_ref, p0, p1, p2, p3, *, groups, group_size):
    half_rows = q_ref.shape[1]
    window = 4 * half_rows
    kv_width = groups * HEAD
    scale = 1.0 / math.sqrt(HEAD)
    lo = lo_ref[0]
    rows = lax.broadcasted_iota(jnp.int32, (half_rows, window), 0)
    cols = lax.broadcasted_iota(jnp.int32, (half_rows, window), 1)
    visible = (cols >= lo) & (cols <= rows + (window - half_rows))
    bias = jnp.where(visible, 0.0, -1e30).astype(jnp.float32)
    bias = jnp.concatenate([bias] * group_size, axis=0)
    wins = (w0, w1, w2, w3)
    outs = (p0, p1, p2, p3)
    for g in range(groups):
        base = g * group_size * HEAD
        qg = jnp.concatenate(
            [q_ref[0, :, base + h * HEAD:base + (h + 1) * HEAD] for h in range(group_size)], axis=0
        )
        dog = jnp.concatenate(
            [do_ref[0, :, base + h * HEAD:base + (h + 1) * HEAD] for h in range(group_size)], axis=0
        )
        kg = jnp.concatenate([w[0, :, g * HEAD:(g + 1) * HEAD] for w in wins], axis=0)
        vg = jnp.concatenate(
            [w[0, :, kv_width + g * HEAD:kv_width + (g + 1) * HEAD] for w in wins], axis=0
        )
        nt = (((1,), (1,)), ((), ()))
        tn = (((0,), (0,)), ((), ()))
        scores = lax.dot_general(qg, kg, nt, preferred_element_type=jnp.float32) * scale
        masked = scores + bias
        top = jnp.max(masked, axis=1, keepdims=True)
        expd = jnp.exp(masked - top)
        total = jnp.sum(expd, axis=1, keepdims=True)
        probs = (expd * (1.0 / total)).astype(jnp.bfloat16)
        attn = jnp.dot(probs, vg, preferred_element_type=jnp.float32).astype(jnp.bfloat16)
        delta = jnp.sum(dog.astype(jnp.float32) * attn.astype(jnp.float32), axis=1, keepdims=True)
        dprob = lax.dot_general(dog, vg, nt, preferred_element_type=jnp.float32)
        dscore = (probs.astype(jnp.float32) * (dprob - delta) * scale).astype(jnp.bfloat16)
        dq = jnp.dot(dscore, kg, preferred_element_type=jnp.float32).astype(jnp.bfloat16)
        for h in range(group_size):
            dq_ref[0, :, base + h * HEAD:base + (h + 1) * HEAD] = dq[h * half_rows:(h + 1) * half_rows]
        dk = lax.dot_general(dscore, qg, tn, preferred_element_type=jnp.float32)
        dv = lax.dot_general(probs, dog, tn, preferred_element_type=jnp.float32)
        for j in range(4):
            outs[j][0, :, g * HEAD:(g + 1) * HEAD] = dk[j * half_rows:(j + 1) * half_rows]
            outs[j][0, :, kv_width + g * HEAD:kv_width + (g + 1) * HEAD] = dv[
                j * half_rows:(j + 1) * half_rows
            ]


def window_grads(lo, q, do, wins):
    halves, half_rows, width = q.shape
    kv2 = wins[0].shape[2]
    groups = kv2 // (2 * HEAD)
    group_size = width // (groups * HEAD)
    kernel = functools.partial(window_kernel, groups=groups, group_size=group_size)
    q_spec = pl.BlockSpec((1, half_rows, width), lambda h: (h, 0, 0))
    w_spec = pl.BlockSpec((1, half_rows, kv2), lambda h: (h, 0, 0))
    lo_spec = pl.BlockSpec((1, half_rows, 1), lambda h: (h, 0, 0))
    flops = 6 * 2 * halves * groups * group_size * half_rows * 4 * half_rows * HEAD
    return pl.pallas_call(
        kernel,
        grid=(halves,),
        in_specs=[lo_spec, q_spec, q_spec] + [w_spec] * 4,
        out_specs=[q_spec] + [w_spec] * 4,
        out_shape=[jax.ShapeDtypeStruct(q.shape, jnp.bfloat16)]
        + [jax.ShapeDtypeStruct((halves, half_rows, kv2), jnp.float32)] * 4,
        cost_estimate=pl.CostEstimate(
            flops=flops,
            transcendentals=halves * groups * group_size * half_rows * 4 * half_rows,
            bytes_accessed=4 * q.size + 4 * 2 * wins[0].size + 4 * 4 * wins[0].size,
        ),
    )(lo, q, do, *wins)


def on_device(query, keys, values, grad_out, lengths):
    n = lax.axis_size(AXIS)
    me = lax.axis_index(AXIS)
    half_rows = query.shape[2]
    kv_width = keys.shape[3]
    q = query[0]
    do = grad_out[0]
    kv = jnp.concatenate([keys[0], values[0]], axis=2)
    early, late = kv[0], kv[1]
    at_top = me == n - 1
    below_top = me == n - 2

    e1 = shifted(early, 1)
    l1 = shifted(kv, -1)
    e2 = shifted(jnp.stack([early, e1]), 2)
    l2 = shifted(jnp.stack([late, jnp.where(at_top, early, l1[1])]), -2)
    late_slots = [
        jnp.where(at_top, e2[0], jnp.where(below_top, early, l2[1])),
        jnp.where(at_top, e1, jnp.where(below_top, l1[0], l2[0])),
        jnp.where(at_top, early, l1[1]),
        late,
    ]
    early_slots = [e2[1], e2[0], e1, early]
    wins = [jnp.stack([a, b]) for a, b in zip(early_slots, late_slots)]

    doc_ends = jnp.cumsum(lengths)
    block_ids = jnp.stack([me, 2 * n - 1 - me])
    query_pos = block_ids[:, None] * half_rows + jnp.arange(half_rows, dtype=jnp.int32)[None, :]
    ends = doc_ends[None, None, :]
    doc_start = jnp.max(jnp.where(ends <= query_pos[:, :, None], ends, 0), axis=2)
    lo = (doc_start - (block_ids[:, None] - REACH) * half_rows).astype(jnp.int32)[:, :, None]

    dq, p0, p1, p2, p3 = window_grads(lo, q, do, wins)

    zero = jnp.zeros_like(p0[0])
    p1e = p1[0] + jnp.where(at_top, p0[1], zero)
    p2e = p2[0] + jnp.where(at_top, p1[1], zero)
    a_e = shifted(jnp.stack([p1e, p0[0]]), -2)
    a_l = shifted(jnp.stack([p1[1], p0[1]]), 2)
    b_e = shifted(p2e + a_e[1], -1)
    b_l = shifted(jnp.stack([p2[1] + a_l[1], p1[1]]), 1)
    final_early = (
        p3[0]
        + a_e[0]
        + b_e
        + jnp.where(at_top, p2[1] + a_l[1] + b_l[1], zero)
        + jnp.where(below_top, p0[1], zero)
    )
    final_late = p3[1] + a_l[0] + b_l[0]
    final = jnp.stack([final_early, final_late])
    grad_keys = final[:, :, :kv_width].astype(jnp.bfloat16).reshape(keys.shape)
    grad_values = final[:, :, kv_width:].astype(jnp.bfloat16).reshape(values.shape)
    return (dq.reshape(query.shape), grad_keys, grad_values)


def solution(mesh):
    spec = P(AXIS, None, None, None)
    return jax.shard_map(
        on_device,
        mesh=mesh,
        in_specs=(spec, spec, spec, spec, P()),
        out_specs=(spec, spec, spec),
        check_vma=False,
    )
```

time: 374 us -> 114 us (0.30)
  the two profiles are of different devices: /device:TPU:6 before, /device:TPU:9 now
where the time goes in v1:
time: 114 us
  waiting for transfers between devices  62 us (54%)
  starting transfers between devices  33.9 us (30%)
  Pallas kernels  9.63 us (8%)
  other arithmetic  5.85 us (5%)
  local copies, waits for them, and re-layouts  1.72 us (2%)
    ppermute x8, waiting for transfers between devices, shifted(): return lax.ppermute(value, AXIS, pairs)  62 us
    ppermute x8, starting transfers between devices, shifted(): return lax.ppermute(value, AXIS, pairs)  33.9 us
    pallas_call x1, Pallas kernels, window_grads(): pl.pallas_call(kernel, grid=(halves,), in_specs=[lo_spec, q_spec, q_spec]...  9.63 us
  transfers between devices with their start and end apart: 8, of which 8 were waited for; matrix products, arithmetic and copies ran while one was open for 2% of the time, Pallas kernels for 0%

profile of v1, /device:TPU:9, one launch (start us, length us, event | category | flops | bytes accessed | tf_op | source)
XLA Modules:
  0.0 113.9 jit_solution(6135260249444651635)
XLA Ops:
  0.7 1.0 pad_maximum_fusion.3.w3
  1.7 13.4 %collective-permute-start.2 = (bf16[2,64,1024]{2,1,0:T(8,128)(2,1)S(1)}, bf16[2,64,1024]{2,1,0:T(8,128)(2,1)S(1)}, u32[]{:S(2)}, u32[]{:S(2)}) collective-permute-start(bf16[2,64,1024]{2,1,0:T(8,128)(2,1)S(1)} %pad_maximum_fusion.3.w3), channel_id=1, source_target_pairs={{1,0},{2,1},{3,2},{4,3},{5,4},{6,5},{7,6},{8,7},{9,8},{10,9},{11,1... | collective-permute-start | bytes 786440 | tf_op jit(solution)/shard_map/ppermute | solution.py:19
  15.1 0.7 copy-done.7
  15.8 0.3 reduce-window.9
  16.1 0.1 slice.90
  16.2 0.1 slice_reduce_fusion
  16.3 0.1 broadcast_multiply_fusion
  16.5 4.0 %collective-permute-done.2 = bf16[2,64,1024]{2,1,0:T(8,128)(2,1)S(1)} collective-permute-done((bf16[2,64,1024]{2,1,0:T(8,128)(2,1)S(1)}, bf16[2,64,1024]{2,1,0:T(8,128)(2,1)S(1)}, u32[]{:S(2)}, u32[]{:S(2)}) %collective-permute-start.2) | collective-permute-done | bytes 262176 | tf_op jit(solution)/shard_map/ppermute | solution.py:19
  20.6 1.9 %collective-permute-start = (bf16[64,1024]{1,0:T(8,128)(2,1)S(1)}, bf16[64,1024]{1,0:T(8,128)(2,1)S(1)}, u32[]{:S(2)}, u32[]{:S(2)}) collective-permute-start(bf16[64,1024]{1,0:T(8,128)(2,1)S(1)} %bitcast.45), channel_id=1, source_target_pairs={{0,1},{1,2},{2,3},{3,4},{4,5},{5,6},{6,7},{7,8},{8,9},{9,10},{10,1... | collective-permute-start | bytes 393224 | tf_op jit(solution)/shard_map/ppermute | solution.py:19
  22.6 0.2 select_reduce_fusion
  22.8 10.1 %collective-permute-done = bf16[64,1024]{1,0:T(8,128)(2,1)S(1)} collective-permute-done((bf16[64,1024]{1,0:T(8,128)(2,1)S(1)}, bf16[64,1024]{1,0:T(8,128)(2,1)S(1)}, u32[]{:S(2)}, u32[]{:S(2)}) %collective-permute-start) | collective-permute-done | bytes 131104 | tf_op jit(solution)/shard_map/ppermute | solution.py:19
  32.9 0.7 pad_maximum_fusion.4
  33.6 2.0 %collective-permute-start.3 = (bf16[2,64,1024]{2,1,0:T(8,128)(2,1)S(1)}, bf16[2,64,1024]{2,1,0:T(8,128)(2,1)S(1)}, u32[]{:S(2)}, u32[]{:S(2)}) collective-permute-start(bf16[2,64,1024]{2,1,0:T(8,128)(2,1)S(1)} %get-tuple-element.28), channel_id=1, source_target_pairs={{2,0},{3,1},{4,2},{5,3},{6,4},{7,5},{8,6},{9,7},{10,8},{11,9},{12,... | collective-permute-start | bytes 786440 | tf_op jit(solution)/shard_map/ppermute | solution.py:19
  35.6 0.1 add_multiply_fusion
  35.7 0.1 copy.11
  35.8 3.3 %collective-permute-start.1 = (bf16[2,64,1024]{2,1,0:T(8,128)(2,1)S(1)}, bf16[2,64,1024]{2,1,0:T(8,128)(2,1)S(1)}, u32[]{:S(2)}, u32[]{:S(2)}) collective-permute-start(bf16[2,64,1024]{2,1,0:T(8,128)(2,1)S(1)} %get-tuple-element.27), channel_id=1, source_target_pairs={{0,2},{1,3},{2,4},{3,5},{4,6},{5,7},{6,8},{7,9},{8,10},{9,11},{10,... | collective-permute-start | bytes 786440 | tf_op jit(solution)/shard_map/ppermute | solution.py:19
  39.1 0.7 broadcast_subtract_fusion.lo_ref
  39.8 2.2 %collective-permute-done.3 = bf16[2,64,1024]{2,1,0:T(8,128)(2,1)S(1)} collective-permute-done((bf16[2,64,1024]{2,1,0:T(8,128)(2,1)S(1)}, bf16[2,64,1024]{2,1,0:T(8,128)(2,1)S(1)}, u32[]{:S(2)}, u32[]{:S(2)}) %collective-permute-start.3) | collective-permute-done | bytes 262176 | tf_op jit(solution)/shard_map/ppermute | solution.py:19
  42.0 3.9 %collective-permute-done.1 = bf16[2,64,1024]{2,1,0:T(8,128)(2,1)S(1)} collective-permute-done((bf16[2,64,1024]{2,1,0:T(8,128)(2,1)S(1)}, bf16[2,64,1024]{2,1,0:T(8,128)(2,1)S(1)}, u32[]{:S(2)}, u32[]{:S(2)}) %collective-permute-start.1) | collective-permute-done | bytes 262176 | tf_op jit(solution)/shard_map/ppermute | solution.py:19
  46.0 0.9 pad_maximum_fusion.7
  46.8 9.6 %shard_map.76 = (bf16[2,64,4096]{2,1,0:T(8,128)(2,1)}, f32[2,64,1024]{2,1,0:T(8,128)}, f32[2,64,1024]{2,1,0:T(8,128)}, f32[2,64,1024]{2,1,0:T(8,128)}, f32[2,64,1024]{2,1,0:T(8,128)}) custom-call(s32[2,64,1]{2,1,0:T(8,128)} %broadcast_subtract_fusion.lo_ref, bf16[2,64,4096]{2,1,0:T(8,128)(2,1)} %bitcast.53, bf16[2,64,4096]{2,1,0:T(8,128)(2,1)} %bitcast.54, ...), custom_call_target="tpu_custom_call" | custom-call | flops 1610612736 | bytes 5242880 | tf_op jit(solution)/shard_map/pallas_call | solution.py:81
  56.5 1.2 %select_add_fusion = (f32[1,64,1024]{2,1,0:T(8,128)S(1)}, f32[1,64,1024]{2,1,0:T(8,128)S(1)}, f32[1,64,1024]{2,1,0:T(8,128)S(1)}) fusion(f32[2,64,1024]{2,1,0:T(8,128)} %get-tuple-element.10, pred[]{:T(512)S(6)} %eq.6, f32[2,64,1024]{2,1,0:T(8,128)} %get-tuple-element.11), kind=kLoop, calls=%fused_computation.28 | loop fusion | flops 131072 | bytes 1572865 | tf_op jit(solution)/shard_map/add | solution.py:131
  57.7 2.1 %collective-permute-start.4 = (f32[2,64,1024]{2,1,0:T(8,128)S(1)}, f32[2,64,1024]{2,1,0:T(8,128)S(1)}, u32[]{:S(2)}, u32[]{:S(2)}) collective-permute-start(f32[2,64,1024]{2,1,0:T(8,128)S(1)} %pad_maximum_fusion), channel_id=1, source_target_pairs={{2,0},{3,1},{4,2},{5,3},{6,4},{7,5},{8,6},{9,7},{10,8},{11,9},{12,... | collective-permute-start | bytes 1572872 | tf_op jit(solution)/shard_map/ppermute | solution.py:19
  59.8 13.3 %collective-permute-done.4 = f32[2,64,1024]{2,1,0:T(8,128)S(1)} collective-permute-done((f32[2,64,1024]{2,1,0:T(8,128)S(1)}, f32[2,64,1024]{2,1,0:T(8,128)S(1)}, u32[]{:S(2)}, u32[]{:S(2)}) %collective-permute-start.4) | collective-permute-done | bytes 524320 | tf_op jit(solution)/shard_map/ppermute | solution.py:19
  73.2 1.9 %collective-permute-start.6 = (f32[2,64,1024]{2,1,0:T(8,128)S(1)}, f32[2,64,1024]{2,1,0:T(8,128)S(1)}, u32[]{:S(2)}, u32[]{:S(2)}) collective-permute-start(f32[2,64,1024]{2,1,0:T(8,128)S(1)} %pad_maximum_fusion.1), channel_id=1, source_target_pairs={{0,2},{1,3},{2,4},{3,5},{4,6},{5,7},{6,8},{7,9},{8,10},{9,11},{10,... | collective-permute-start | bytes 1572872 | tf_op jit(solution)/shard_map/ppermute | solution.py:19
  75.2 14.8 %collective-permute-done.6 = f32[2,64,1024]{2,1,0:T(8,128)S(1)} collective-permute-done((f32[2,64,1024]{2,1,0:T(8,128)S(1)}, f32[2,64,1024]{2,1,0:T(8,128)S(1)}, u32[]{:S(2)}, u32[]{:S(2)}) %collective-permute-start.6) | collective-permute-done | bytes 524320 | tf_op jit(solution)/shard_map/ppermute | solution.py:19
  90.0 6.0 %collective-permute-start.7 = (f32[2,64,1024]{2,1,0:T(8,128)S(1)}, f32[2,64,1024]{2,1,0:T(8,128)S(1)}, u32[]{:S(2)}, u32[]{:S(2)}) collective-permute-start(f32[2,64,1024]{2,1,0:T(8,128)S(1)} %pad_maximum_fusion.2), channel_id=1, source_target_pairs={{0,1},{1,2},{2,3},{3,4},{4,5},{5,6},{6,7},{7,8},{8,9},{9,10},{10,1... | collective-permute-start | bytes 1572872 | tf_op jit(solution)/shard_map/ppermute | solution.py:19
  96.0 3.3 %collective-permute-start.5 = (f32[64,1024]{1,0:T(8,128)S(1)}, f32[64,1024]{1,0:T(8,128)S(1)}, u32[]{:S(2)}, u32[]{:S(2)}) collective-permute-start(f32[64,1024]{1,0:T(8,128)S(1)} %get-tuple-element.15), channel_id=1, source_target_pairs={{1,0},{2,1},{3,2},{4,3},{5,4},{6,5},{7,6},{8,7},{9,8},{10,9},{11,1... | collective-permute-start | bytes 786440 | tf_op jit(solution)/shard_map/ppermute | solution.py:19
  99.4 11.8 %collective-permute-done.7 = f32[2,64,1024]{2,1,0:T(8,128)S(1)} collective-permute-done((f32[2,64,1024]{2,1,0:T(8,128)S(1)}, f32[2,64,1024]{2,1,0:T(8,128)S(1)}, u32[]{:S(2)}, u32[]{:S(2)}) %collective-permute-start.7) | collective-permute-done | bytes 524320 | tf_op jit(solution)/shard_map/ppermute | solution.py:19
  111.2 1.8 %collective-permute-done.5 = f32[64,1024]{1,0:T(8,128)S(1)} collective-permute-done((f32[64,1024]{1,0:T(8,128)S(1)}, f32[64,1024]{1,0:T(8,128)S(1)}, u32[]{:S(2)}, u32[]{:S(2)}) %collective-permute-start.5) | collective-permute-done | bytes 262176 | tf_op jit(solution)/shard_map/ppermute | solution.py:19
  113.1 0.1 fusion.4
  113.2 0.7 slice_bitcast_fusion
  (28 shorter events, 0.6 us)
Async XLA Ops:
  0.6 19.9 %copy-start.4 = (bf16[1,2,64,512]{3,2,1,0:T(8,128)(2,1)S(1)}, bf16[1,2,64,512]{3,2,1,0:T(8,128)(2,1)}, u32[]{:S(2)}) copy-start(bf16[1,2,64,512]{3,2,1,0:T(8,128)(2,1)} %param.7) | copy-start | bytes 393220
  0.6 19.9 %copy-start.5 = (bf16[1,2,64,512]{3,2,1,0:T(8,128)(2,1)S(1)}, bf16[1,2,64,512]{3,2,1,0:T(8,128)(2,1)}, u32[]{:S(2)}) copy-start(bf16[1,2,64,512]{3,2,1,0:T(8,128)(2,1)} %param.6) | copy-start | bytes 393220
  1.7 18.9 %copy-start.6 = (bf16[2,64,1024]{2,1,0:T(8,128)(2,1)}, bf16[2,64,1024]{2,1,0:T(8,128)(2,1)S(1)}, u32[]{:S(2)}) copy-start(bf16[2,64,1024]{2,1,0:T(8,128)(2,1)S(1)} %pad_maximum_fusion.3.w3) | copy-start | bytes 786436
  1.7 18.8 %collective-permute-start.2 = (bf16[2,64,1024]{2,1,0:T(8,128)(2,1)S(1)}, bf16[2,64,1024]{2,1,0:T(8,128)(2,1)S(1)}, u32[]{:S(2)}, u32[]{:S(2)}) collective-permute-start(bf16[2,64,1024]{2,1,0:T(8,128)(2,1)S(1)} %pad_maximum_fusion.3.w3), channel_id=1, source_target_pairs={{1,0},{2,1},{3,2},{4,3},{5,4},{6,5},{7,6},{8,7},{9,8},{10,9},{11,1... | collective-permute-start | bytes 786440 | tf_op jit(solution)/shard_map/ppermute | solution.py:19
  15.1 0.7 copy-start.7
  20.6 12.3 %collective-permute-start = (bf16[64,1024]{1,0:T(8,128)(2,1)S(1)}, bf16[64,1024]{1,0:T(8,128)(2,1)S(1)}, u32[]{:S(2)}, u32[]{:S(2)}) collective-permute-start(bf16[64,1024]{1,0:T(8,128)(2,1)S(1)} %bitcast.45), channel_id=1, source_target_pairs={{0,1},{1,2},{2,3},{3,4},{4,5},{5,6},{6,7},{7,8},{8,9},{9,10},{10,1... | collective-permute-start | bytes 393224 | tf_op jit(solution)/shard_map/ppermute | solution.py:19
  33.6 8.4 %collective-permute-start.3 = (bf16[2,64,1024]{2,1,0:T(8,128)(2,1)S(1)}, bf16[2,64,1024]{2,1,0:T(8,128)(2,1)S(1)}, u32[]{:S(2)}, u32[]{:S(2)}) collective-permute-start(bf16[2,64,1024]{2,1,0:T(8,128)(2,1)S(1)} %get-tuple-element.28), channel_id=1, source_target_pairs={{2,0},{3,1},{4,2},{5,3},{6,4},{7,5},{8,6},{9,7},{10,8},{11,9},{12,... | collective-permute-start | bytes 786440 | tf_op jit(solution)/shard_map/ppermute | solution.py:19
  35.8 10.1 %collective-permute-start.1 = (bf16[2,64,1024]{2,1,0:T(8,128)(2,1)S(1)}, bf16[2,64,1024]{2,1,0:T(8,128)(2,1)S(1)}, u32[]{:S(2)}, u32[]{:S(2)}) collective-permute-start(bf16[2,64,1024]{2,1,0:T(8,128)(2,1)S(1)} %get-tuple-element.27), channel_id=1, source_target_pairs={{0,2},{1,3},{2,4},{3,5},{4,6},{5,7},{6,8},{7,9},{8,10},{9,11},{10,... | collective-permute-start | bytes 786440 | tf_op jit(solution)/shard_map/ppermute | solution.py:19
  57.6 15.5 %copy-start.1 = (f32[2,64,1024]{2,1,0:T(8,128)S(1)}, f32[2,64,1024]{2,1,0:T(8,128)}, u32[]{:S(2)}) copy-start(f32[2,64,1024]{2,1,0:T(8,128)} %get-tuple-element.12) | copy-start | bytes 1572868
  57.6 15.5 %copy-start.3 = (f32[2,64,1024]{2,1,0:T(8,128)S(1)}, f32[2,64,1024]{2,1,0:T(8,128)}, u32[]{:S(2)}) copy-start(f32[2,64,1024]{2,1,0:T(8,128)} %get-tuple-element.10) | copy-start | bytes 1572868
  57.7 15.4 %collective-permute-start.4 = (f32[2,64,1024]{2,1,0:T(8,128)S(1)}, f32[2,64,1024]{2,1,0:T(8,128)S(1)}, u32[]{:S(2)}, u32[]{:S(2)}) collective-permute-start(f32[2,64,1024]{2,1,0:T(8,128)S(1)} %pad_maximum_fusion), channel_id=1, source_target_pairs={{2,0},{3,1},{4,2},{5,3},{6,4},{7,5},{8,6},{9,7},{10,8},{11,9},{12,... | collective-permute-start | bytes 1572872 | tf_op jit(solution)/shard_map/ppermute | solution.py:19
  73.2 16.7 %collective-permute-start.6 = (f32[2,64,1024]{2,1,0:T(8,128)S(1)}, f32[2,64,1024]{2,1,0:T(8,128)S(1)}, u32[]{:S(2)}, u32[]{:S(2)}) collective-permute-start(f32[2,64,1024]{2,1,0:T(8,128)S(1)} %pad_maximum_fusion.1), channel_id=1, source_target_pairs={{0,2},{1,3},{2,4},{3,5},{4,6},{5,7},{6,8},{7,9},{8,10},{9,11},{10,... | collective-permute-start | bytes 1572872 | tf_op jit(solution)/shard_map/ppermute | solution.py:19
  90.0 21.2 %copy-start.2 = (f32[2,64,1024]{2,1,0:T(8,128)S(1)}, f32[2,64,1024]{2,1,0:T(8,128)}, u32[]{:S(2)}) copy-start(f32[2,64,1024]{2,1,0:T(8,128)} %get-tuple-element.9) | copy-start | bytes 1572868
  90.0 23.0 %copy-start = (f32[2,64,1024]{2,1,0:T(8,128)S(1)}, f32[2,64,1024]{2,1,0:T(8,128)}, u32[]{:S(2)}) copy-start(f32[2,64,1024]{2,1,0:T(8,128)} %get-tuple-element.11) | copy-start | bytes 1572868
  90.0 21.1 %collective-permute-start.7 = (f32[2,64,1024]{2,1,0:T(8,128)S(1)}, f32[2,64,1024]{2,1,0:T(8,128)S(1)}, u32[]{:S(2)}, u32[]{:S(2)}) collective-permute-start(f32[2,64,1024]{2,1,0:T(8,128)S(1)} %pad_maximum_fusion.2), channel_id=1, source_target_pairs={{0,1},{1,2},{2,3},{3,4},{4,5},{5,6},{6,7},{7,8},{8,9},{9,10},{10,1... | collective-permute-start | bytes 1572872 | tf_op jit(solution)/shard_map/ppermute | solution.py:19
  96.0 17.0 %collective-permute-start.5 = (f32[64,1024]{1,0:T(8,128)S(1)}, f32[64,1024]{1,0:T(8,128)S(1)}, u32[]{:S(2)}, u32[]{:S(2)}) collective-permute-start(f32[64,1024]{1,0:T(8,128)S(1)} %get-tuple-element.15), channel_id=1, source_target_pairs={{1,0},{2,1},{3,2},{4,3},{5,4},{6,5},{7,6},{8,7},{9,8},{10,9},{11,1... | collective-permute-start | bytes 786440 | tf_op jit(solution)/shard_map/ppermute | solution.py:19

commit v2 on v1

--- a/solution.py
+++ b/solution.py
@@ -128,12 +128,13 @@
     dq, p0, p1, p2, p3 = window_grads(lo, q, do, wins)
 
     zero = jnp.zeros_like(p0[0])
+    link = jnp.bfloat16
     p1e = p1[0] + jnp.where(at_top, p0[1], zero)
     p2e = p2[0] + jnp.where(at_top, p1[1], zero)
-    a_e = shifted(jnp.stack([p1e, p0[0]]), -2)
-    a_l = shifted(jnp.stack([p1[1], p0[1]]), 2)
-    b_e = shifted(p2e + a_e[1], -1)
-    b_l = shifted(jnp.stack([p2[1] + a_l[1], p1[1]]), 1)
+    a_e = shifted(jnp.stack([p1e, p0[0]]).astype(link), -2).astype(jnp.float32)
+    a_l = shifted(jnp.stack([p1[1], p0[1]]).astype(link), 2).astype(jnp.float32)
+    b_e = shifted((p2e + a_e[1]).astype(link), -1).astype(jnp.float32)
+    b_l = shifted(jnp.stack([p2[1] + a_l[1], p1[1]]).astype(link), 1).astype(jnp.float32)
     final_early = (
         p3[0]
         + a_e[0]

time: 114 us -> 93.6 us (0.82)
  the two profiles are of different devices: /device:TPU:9 before, /device:TPU:6 now
where the time goes in v2:
time: 93.6 us; the launch traced here: 93.2 us
  starting transfers between devices  44.3 us (47%)
  waiting for transfers between devices  29.8 us (32%)
  Pallas kernels  9.63 us (10%)
  other arithmetic  5.81 us (6%)
  local copies, waits for them, and re-layouts  2.77 us (3%)
    ppermute x8, starting transfers between devices, shifted(): return lax.ppermute(value, AXIS, pairs)  44.3 us
    ppermute x8, waiting for transfers between devices, shifted(): return lax.ppermute(value, AXIS, pairs)  29.8 us
    pallas_call x1, Pallas kernels, window_grads(): pl.pallas_call(kernel, grid=(halves,), in_specs=[lo_spec, q_spec, q_spec]...  9.63 us
  transfers between devices with their start and end apart: 8, of which 7 were waited for; matrix products, arithmetic and copies ran while one was open for 2% of the time, Pallas kernels for 0%

profile of v2, /device:TPU:6, one launch (start us, length us, event | category | flops | bytes accessed | tf_op | source)
XLA Modules:
  0.0 93.2 jit_solution(8867870458174259385)
XLA Ops:
  0.7 1.0 %pad_maximum_fusion.w3 = bf16[2,64,1024]{2,1,0:T(8,128)(2,1)S(1)} fusion(bf16[2,64,512]{2,1,0:T(8,128)(2,1)} %bitcast.47, bf16[2,64,512]{2,1,0:T(8,128)(2,1)} %bitcast.49), kind=kLoop, calls=%fused_computation.3 | loop fusion | flops 524288 | bytes 524288 | tf_op jit(solution)/shard_map/concatenate | solution.py:103
  1.7 13.6 %collective-permute-start.2 = (bf16[2,64,1024]{2,1,0:T(8,128)(2,1)S(1)}, bf16[2,64,1024]{2,1,0:T(8,128)(2,1)S(1)}, u32[]{:S(2)}, u32[]{:S(2)}) collective-permute-start(bf16[2,64,1024]{2,1,0:T(8,128)(2,1)S(1)} %pad_maximum_fusion.w3), channel_id=1, source_target_pairs={{1,0},{2,1},{3,2},{4,3},{5,4},{6,5},{7,6},{8,7},{9,8},{10,9},{11,1... | collective-permute-start | bytes 786440 | tf_op jit(solution)/shard_map/ppermute | solution.py:19
  15.3 0.7 copy-done.7
  16.0 0.3 reduce-window.9
  16.4 0.1 slice_reduce_fusion
  16.5 0.1 broadcast_multiply_fusion
  16.6 5.2 %collective-permute-done.2 = bf16[2,64,1024]{2,1,0:T(8,128)(2,1)S(1)} collective-permute-done((bf16[2,64,1024]{2,1,0:T(8,128)(2,1)S(1)}, bf16[2,64,1024]{2,1,0:T(8,128)(2,1)S(1)}, u32[]{:S(2)}, u32[]{:S(2)}) %collective-permute-start.2) | collective-permute-done | bytes 262176 | tf_op jit(solution)/shard_map/ppermute | solution.py:19
  21.9 1.9 %collective-permute-start = (bf16[64,1024]{1,0:T(8,128)(2,1)S(1)}, bf16[64,1024]{1,0:T(8,128)(2,1)S(1)}, u32[]{:S(2)}, u32[]{:S(2)}) collective-permute-start(bf16[64,1024]{1,0:T(8,128)(2,1)S(1)} %bitcast.45), channel_id=1, source_target_pairs={{0,1},{1,2},{2,3},{3,4},{4,5},{5,6},{6,7},{7,8},{8,9},{9,10},{10,1... | collective-permute-start | bytes 393224 | tf_op jit(solution)/shard_map/ppermute | solution.py:19
  23.9 0.2 select_reduce_fusion
  24.1 10.0 %collective-permute-done = bf16[64,1024]{1,0:T(8,128)(2,1)S(1)} collective-permute-done((bf16[64,1024]{1,0:T(8,128)(2,1)S(1)}, bf16[64,1024]{1,0:T(8,128)(2,1)S(1)}, u32[]{:S(2)}, u32[]{:S(2)}) %collective-permute-start) | collective-permute-done | bytes 131104 | tf_op jit(solution)/shard_map/ppermute | solution.py:19
  34.1 0.7 pad_maximum_fusion.1
  34.8 1.9 %collective-permute-start.3 = (bf16[2,64,1024]{2,1,0:T(8,128)(2,1)S(1)}, bf16[2,64,1024]{2,1,0:T(8,128)(2,1)S(1)}, u32[]{:S(2)}, u32[]{:S(2)}) collective-permute-start(bf16[2,64,1024]{2,1,0:T(8,128)(2,1)S(1)} %get-tuple-element.27), channel_id=1, source_target_pairs={{2,0},{3,1},{4,2},{5,3},{6,4},{7,5},{8,6},{9,7},{10,8},{11,9},{12,... | collective-permute-start | bytes 786440 | tf_op jit(solution)/shard_map/ppermute | solution.py:19
  36.7 0.1 add_multiply_fusion
  36.8 0.1 copy.11
  36.9 3.9 %collective-permute-start.1 = (bf16[2,64,1024]{2,1,0:T(8,128)(2,1)S(1)}, bf16[2,64,1024]{2,1,0:T(8,128)(2,1)S(1)}, u32[]{:S(2)}, u32[]{:S(2)}) collective-permute-start(bf16[2,64,1024]{2,1,0:T(8,128)(2,1)S(1)} %get-tuple-element.26), channel_id=1, source_target_pairs={{0,2},{1,3},{2,4},{3,5},{4,6},{5,7},{6,8},{7,9},{8,10},{9,11},{10,... | collective-permute-start | bytes 786440 | tf_op jit(solution)/shard_map/ppermute | solution.py:19
  40.8 0.7 broadcast_subtract_fusion.lo_ref
  41.5 2.6 %collective-permute-done.3 = bf16[2,64,1024]{2,1,0:T(8,128)(2,1)S(1)} collective-permute-done((bf16[2,64,1024]{2,1,0:T(8,128)(2,1)S(1)}, bf16[2,64,1024]{2,1,0:T(8,128)(2,1)S(1)}, u32[]{:S(2)}, u32[]{:S(2)}) %collective-permute-start.3) | collective-permute-done | bytes 262176 | tf_op jit(solution)/shard_map/ppermute | solution.py:19
  44.2 4.8 %collective-permute-done.1 = bf16[2,64,1024]{2,1,0:T(8,128)(2,1)S(1)} collective-permute-done((bf16[2,64,1024]{2,1,0:T(8,128)(2,1)S(1)}, bf16[2,64,1024]{2,1,0:T(8,128)(2,1)S(1)}, u32[]{:S(2)}, u32[]{:S(2)}) %collective-permute-start.1) | collective-permute-done | bytes 262176 | tf_op jit(solution)/shard_map/ppermute | solution.py:19
  49.0 0.9 pad_maximum_fusion.4
  49.8 9.6 %shard_map.76 = (bf16[2,64,4096]{2,1,0:T(8,128)(2,1)}, f32[2,64,1024]{2,1,0:T(8,128)}, f32[2,64,1024]{2,1,0:T(8,128)}, f32[2,64,1024]{2,1,0:T(8,128)}, f32[2,64,1024]{2,1,0:T(8,128)}) custom-call(s32[2,64,1]{2,1,0:T(8,128)} %broadcast_subtract_fusion.lo_ref, bf16[2,64,4096]{2,1,0:T(8,128)(2,1)} %bitcast.53, bf16[2,64,4096]{2,1,0:T(8,128)(2,1)} %bitcast.54, ...), custom_call_target="tpu_custom_call" | custom-call | flops 1610612736 | bytes 5242880 | tf_op jit(solution)/shard_map/pallas_call | solution.py:81
  59.5 1.0 %slice.216 = bf16[1,64,1024]{2,1,0:T(8,128)(2,1)S(1)} slice(f32[2,64,1024]{2,1,0:T(8,128)} %get-tuple-element.10), slice={[1:2], [0:64], [0:1024]} | slice | bytes 262144 | tf_op jit(solution)/shard_map/slice | solution.py:133
  60.5 1.1 %add_convert_fusion = bf16[1,64,1024]{2,1,0:T(8,128)(2,1)S(1)} fusion(f32[2,64,1024]{2,1,0:T(8,128)} %get-tuple-element.10, f32[2,64,1024]{2,1,0:T(8,128)} %get-tuple-element.11, pred[]{:T(512)S(6)} %eq.6), kind=kLoop, calls=%fused_computation.29 | loop fusion | flops 196608 | bytes 655361 | tf_op jit(solution)/shard_map/convert.6
  61.6 1.9 %collective-permute-start.6 = (bf16[2,64,1024]{2,1,0:T(8,128)(2,1)S(1)}, bf16[2,64,1024]{2,1,0:T(8,128)(2,1)S(1)}, u32[]{:S(2)}, u32[]{:S(2)}) collective-permute-start(bf16[2,64,1024]{2,1,0:T(8,128)(2,1)S(1)} %pad_maximum_fusion.7), channel_id=1, source_target_pairs={{0,2},{1,3},{2,4},{3,5},{4,6},{5,7},{6,8},{7,9},{8,10},{9,11},{10,... | collective-permute-start | bytes 786440 | tf_op jit(solution)/shard_map/ppermute | solution.py:19
  63.6 6.7 %collective-permute-start.4 = (bf16[2,64,1024]{2,1,0:T(8,128)(2,1)S(1)}, bf16[2,64,1024]{2,1,0:T(8,128)(2,1)S(1)}, u32[]{:S(2)}, u32[]{:S(2)}) collective-permute-start(bf16[2,64,1024]{2,1,0:T(8,128)(2,1)S(1)} %pad_maximum_fusion.6), channel_id=1, source_target_pairs={{2,0},{3,1},{4,2},{5,3},{6,4},{7,5},{8,6},{9,7},{10,8},{11,9},{12,... | collective-permute-start | bytes 786440 | tf_op jit(solution)/shard_map/ppermute | solution.py:19
  70.3 2.1 %collective-permute-done.6 = bf16[2,64,1024]{2,1,0:T(8,128)(2,1)S(1)} collective-permute-done((bf16[2,64,1024]{2,1,0:T(8,128)(2,1)S(1)}, bf16[2,64,1024]{2,1,0:T(8,128)(2,1)S(1)}, u32[]{:S(2)}, u32[]{:S(2)}) %collective-permute-start.6) | collective-permute-done | bytes 262176 | tf_op jit(solution)/shard_map/ppermute | solution.py:19
  72.4 1.7 %collective-permute-done.4 = bf16[2,64,1024]{2,1,0:T(8,128)(2,1)S(1)} collective-permute-done((bf16[2,64,1024]{2,1,0:T(8,128)(2,1)S(1)}, bf16[2,64,1024]{2,1,0:T(8,128)(2,1)S(1)}, u32[]{:S(2)}, u32[]{:S(2)}) %collective-permute-start.4) | collective-permute-done | bytes 262176 | tf_op jit(solution)/shard_map/ppermute | solution.py:19
  74.2 0.1 fusion.8
  74.3 6.6 %collective-permute-start.7 = (bf16[2,64,1024]{2,1,0:T(8,128)(2,1)S(1)}, bf16[2,64,1024]{2,1,0:T(8,128)(2,1)S(1)}, u32[]{:S(2)}, u32[]{:S(2)}) collective-permute-start(bf16[2,64,1024]{2,1,0:T(8,128)(2,1)S(1)} %pad_maximum_fusion.8), channel_id=1, source_target_pairs={{0,1},{1,2},{2,3},{3,4},{4,5},{5,6},{6,7},{7,8},{8,9},{9,10},{10,1... | collective-permute-start | bytes 786440 | tf_op jit(solution)/shard_map/ppermute | solution.py:19
  81.0 7.7 %collective-permute-start.5 = (bf16[64,1024]{1,0:T(8,128)(2,1)S(1)}, bf16[64,1024]{1,0:T(8,128)(2,1)S(1)}, u32[]{:S(2)}, u32[]{:S(2)}) collective-permute-start(bf16[64,1024]{1,0:T(8,128)(2,1)S(1)} %get-tuple-element.15), channel_id=1, source_target_pairs={{1,0},{2,1},{3,2},{4,3},{5,4},{6,5},{7,6},{8,7},{9,8},{10,9},{11,1... | collective-permute-start | bytes 393224 | tf_op jit(solution)/shard_map/ppermute | solution.py:19
  88.7 3.4 %collective-permute-done.7 = bf16[2,64,1024]{2,1,0:T(8,128)(2,1)S(1)} collective-permute-done((bf16[2,64,1024]{2,1,0:T(8,128)(2,1)S(1)}, bf16[2,64,1024]{2,1,0:T(8,128)(2,1)S(1)}, u32[]{:S(2)}, u32[]{:S(2)}) %collective-permute-start.7) | collective-permute-done | bytes 262176 | tf_op jit(solution)/shard_map/ppermute | solution.py:19
  92.3 0.1 fusion.4
  92.4 0.7 slice_bitcast_fusion
  (32 shorter events, 0.7 us)
Async XLA Ops:
  0.6 21.2 %copy-start.4 = (bf16[1,2,64,512]{3,2,1,0:T(8,128)(2,1)S(1)}, bf16[1,2,64,512]{3,2,1,0:T(8,128)(2,1)}, u32[]{:S(2)}) copy-start(bf16[1,2,64,512]{3,2,1,0:T(8,128)(2,1)} %param.7) | copy-start | bytes 393220
  0.6 21.2 %copy-start.5 = (bf16[1,2,64,512]{3,2,1,0:T(8,128)(2,1)S(1)}, bf16[1,2,64,512]{3,2,1,0:T(8,128)(2,1)}, u32[]{:S(2)}) copy-start(bf16[1,2,64,512]{3,2,1,0:T(8,128)(2,1)} %param.6) | copy-start | bytes 393220
  1.7 20.2 %copy-start.6 = (bf16[2,64,1024]{2,1,0:T(8,128)(2,1)}, bf16[2,64,1024]{2,1,0:T(8,128)(2,1)S(1)}, u32[]{:S(2)}) copy-start(bf16[2,64,1024]{2,1,0:T(8,128)(2,1)S(1)} %pad_maximum_fusion.w3) | copy-start | bytes 786436
  1.7 20.1 %collective-permute-start.2 = (bf16[2,64,1024]{2,1,0:T(8,128)(2,1)S(1)}, bf16[2,64,1024]{2,1,0:T(8,128)(2,1)S(1)}, u32[]{:S(2)}, u32[]{:S(2)}) collective-permute-start(bf16[2,64,1024]{2,1,0:T(8,128)(2,1)S(1)} %pad_maximum_fusion.w3), channel_id=1, source_target_pairs={{1,0},{2,1},{3,2},{4,3},{5,4},{6,5},{7,6},{8,7},{9,8},{10,9},{11,1... | collective-permute-start | bytes 786440 | tf_op jit(solution)/shard_map/ppermute | solution.py:19
  15.3 0.7 copy-start.7
  21.9 12.2 %collective-permute-start = (bf16[64,1024]{1,0:T(8,128)(2,1)S(1)}, bf16[64,1024]{1,0:T(8,128)(2,1)S(1)}, u32[]{:S(2)}, u32[]{:S(2)}) collective-permute-start(bf16[64,1024]{1,0:T(8,128)(2,1)S(1)} %bitcast.45), channel_id=1, source_target_pairs={{0,1},{1,2},{2,3},{3,4},{4,5},{5,6},{6,7},{7,8},{8,9},{9,10},{10,1... | collective-permute-start | bytes 393224 | tf_op jit(solution)/shard_map/ppermute | solution.py:19
  34.8 9.3 %collective-permute-start.3 = (bf16[2,64,1024]{2,1,0:T(8,128)(2,1)S(1)}, bf16[2,64,1024]{2,1,0:T(8,128)(2,1)S(1)}, u32[]{:S(2)}, u32[]{:S(2)}) collective-permute-start(bf16[2,64,1024]{2,1,0:T(8,128)(2,1)S(1)} %get-tuple-element.27), channel_id=1, source_target_pairs={{2,0},{3,1},{4,2},{5,3},{6,4},{7,5},{8,6},{9,7},{10,8},{11,9},{12,... | collective-permute-start | bytes 786440 | tf_op jit(solution)/shard_map/ppermute | solution.py:19
  36.9 12.0 %collective-permute-start.1 = (bf16[2,64,1024]{2,1,0:T(8,128)(2,1)S(1)}, bf16[2,64,1024]{2,1,0:T(8,128)(2,1)S(1)}, u32[]{:S(2)}, u32[]{:S(2)}) collective-permute-start(bf16[2,64,1024]{2,1,0:T(8,128)(2,1)S(1)} %get-tuple-element.26), channel_id=1, source_target_pairs={{0,2},{1,3},{2,4},{3,5},{4,6},{5,7},{6,8},{7,9},{8,10},{9,11},{10,... | collective-permute-start | bytes 786440 | tf_op jit(solution)/shard_map/ppermute | solution.py:19
  59.5 2.1 %copy-start = (f32[2,64,1024]{2,1,0:T(8,128)S(1)}, f32[2,64,1024]{2,1,0:T(8,128)}, u32[]{:S(2)}) copy-start(f32[2,64,1024]{2,1,0:T(8,128)} %get-tuple-element.11) | copy-start | bytes 1572868
  61.6 10.7 %collective-permute-start.6 = (bf16[2,64,1024]{2,1,0:T(8,128)(2,1)S(1)}, bf16[2,64,1024]{2,1,0:T(8,128)(2,1)S(1)}, u32[]{:S(2)}, u32[]{:S(2)}) collective-permute-start(bf16[2,64,1024]{2,1,0:T(8,128)(2,1)S(1)} %pad_maximum_fusion.7), channel_id=1, source_target_pairs={{0,2},{1,3},{2,4},{3,5},{4,6},{5,7},{6,8},{7,9},{8,10},{9,11},{10,... | collective-permute-start | bytes 786440 | tf_op jit(solution)/shard_map/ppermute | solution.py:19
  63.6 10.5 %collective-permute-start.4 = (bf16[2,64,1024]{2,1,0:T(8,128)(2,1)S(1)}, bf16[2,64,1024]{2,1,0:T(8,128)(2,1)S(1)}, u32[]{:S(2)}, u32[]{:S(2)}) collective-permute-start(bf16[2,64,1024]{2,1,0:T(8,128)(2,1)S(1)} %pad_maximum_fusion.6), channel_id=1, source_target_pairs={{2,0},{3,1},{4,2},{5,3},{6,4},{7,5},{8,6},{9,7},{10,8},{11,9},{12,... | collective-permute-start | bytes 786440 | tf_op jit(solution)/shard_map/ppermute | solution.py:19
  72.3 1.8 %copy-start.2 = (f32[2,64,1024]{2,1,0:T(8,128)S(1)}, f32[2,64,1024]{2,1,0:T(8,128)}, u32[]{:S(2)}) copy-start(f32[2,64,1024]{2,1,0:T(8,128)} %get-tuple-element.10) | copy-start | bytes 1572868
  72.4 1.8 %copy-start.1 = (f32[2,64,1024]{2,1,0:T(8,128)S(1)}, f32[2,64,1024]{2,1,0:T(8,128)}, u32[]{:S(2)}) copy-start(f32[2,64,1024]{2,1,0:T(8,128)} %get-tuple-element.12) | copy-start | bytes 1572868
  74.3 17.9 %copy-start.3 = (f32[2,64,1024]{2,1,0:T(8,128)S(1)}, f32[2,64,1024]{2,1,0:T(8,128)}, u32[]{:S(2)}) copy-start(f32[2,64,1024]{2,1,0:T(8,128)} %get-tuple-element.9) | copy-start | bytes 1572868
  74.3 17.8 %collective-permute-start.7 = (bf16[2,64,1024]{2,1,0:T(8,128)(2,1)S(1)}, bf16[2,64,1024]{2,1,0:T(8,128)(2,1)S(1)}, u32[]{:S(2)}, u32[]{:S(2)}) collective-permute-start(bf16[2,64,1024]{2,1,0:T(8,128)(2,1)S(1)} %pad_maximum_fusion.8), channel_id=1, source_target_pairs={{0,1},{1,2},{2,3},{3,4},{4,5},{5,6},{6,7},{7,8},{8,9},{9,10},{10,1... | collective-permute-start | bytes 786440 | tf_op jit(solution)/shard_map/ppermute | solution.py:19
  81.0 11.3 %collective-permute-start.5 = (bf16[64,1024]{1,0:T(8,128)(2,1)S(1)}, bf16[64,1024]{1,0:T(8,128)(2,1)S(1)}, u32[]{:S(2)}, u32[]{:S(2)}) collective-permute-start(bf16[64,1024]{1,0:T(8,128)(2,1)S(1)} %get-tuple-element.15), channel_id=1, source_target_pairs={{1,0},{2,1},{3,2},{4,3},{5,4},{6,5},{7,6},{8,7},{9,8},{10,9},{11,1... | collective-permute-start | bytes 393224 | tf_op jit(solution)/shard_map/ppermute | solution.py:19

commit v3 on v2

--- a/solution.py
+++ b/solution.py
@@ -105,17 +105,16 @@
     at_top = me == n - 1
     below_top = me == n - 2
 
-    e1 = shifted(early, 1)
-    l1 = shifted(kv, -1)
-    e2 = shifted(jnp.stack([early, e1]), 2)
-    l2 = shifted(jnp.stack([late, jnp.where(at_top, early, l1[1])]), -2)
+    e1, e2, e3 = (shifted(early, k) for k in (1, 2, 3))
+    l1, l2 = (shifted(kv, -k) for k in (1, 2))
+    l3 = shifted(late, -3)
     late_slots = [
-        jnp.where(at_top, e2[0], jnp.where(below_top, early, l2[1])),
-        jnp.where(at_top, e1, jnp.where(below_top, l1[0], l2[0])),
+        jnp.where(at_top, e2, jnp.where(below_top, early, jnp.where(me == n - 3, l2[0], l3))),
+        jnp.where(at_top, e1, jnp.where(below_top, l1[0], l2[1])),
         jnp.where(at_top, early, l1[1]),
         late,
     ]
-    early_slots = [e2[1], e2[0], e1, early]
+    early_slots = [e3, e2, e1, early]
     wins = [jnp.stack([a, b]) for a, b in zip(early_slots, late_slots)]
 
     doc_ends = jnp.cumsum(lengths)
@@ -131,18 +130,21 @@
     link = jnp.bfloat16
     p1e = p1[0] + jnp.where(at_top, p0[1], zero)
     p2e = p2[0] + jnp.where(at_top, p1[1], zero)
-    a_e = shifted(jnp.stack([p1e, p0[0]]).astype(link), -2).astype(jnp.float32)
-    a_l = shifted(jnp.stack([p1[1], p0[1]]).astype(link), 2).astype(jnp.float32)
-    b_e = shifted((p2e + a_e[1]).astype(link), -1).astype(jnp.float32)
-    b_l = shifted(jnp.stack([p2[1] + a_l[1], p1[1]]).astype(link), 1).astype(jnp.float32)
+    r_e1 = shifted(p2e.astype(link), -1).astype(jnp.float32)
+    r_e2 = shifted(p1e.astype(link), -2).astype(jnp.float32)
+    r_e3 = shifted(p0[0].astype(link), -3).astype(jnp.float32)
+    r_l1 = shifted(jnp.stack([p2[1], p1[1]]).astype(link), 1).astype(jnp.float32)
+    r_l2 = shifted(jnp.stack([p1[1], p0[1]]).astype(link), 2).astype(jnp.float32)
+    r_l3 = shifted(p0[1].astype(link), 3).astype(jnp.float32)
     final_early = (
         p3[0]
-        + a_e[0]
-        + b_e
-        + jnp.where(at_top, p2[1] + a_l[1] + b_l[1], zero)
+        + r_e1
+        + r_e2
+        + r_e3
+        + jnp.where(at_top, p2[1] + r_l1[1] + r_l2[1], zero)
         + jnp.where(below_top, p0[1], zero)
     )
-    final_late = p3[1] + a_l[0] + b_l[0]
+    final_late = p3[1] + r_l1[0] + r_l2[0] + r_l3
     final = jnp.stack([final_early, final_late])
     grad_keys = final[:, :, :kv_width].astype(jnp.bfloat16).reshape(keys.shape)
     grad_values = final[:, :, kv_width:].astype(jnp.bfloat16).reshape(values.shape)

time: 93.6 us -> 94 us (level)
  waiting for transfers between devices: 29.8 us -> 16.1 us
  starting transfers between devices: 44.3 us -> 57.6 us
  local copies, waits for them, and re-layouts: 2.77 us -> 3.74 us
    ppermute x8 -> x12, waiting for transfers between devices: 29.8 us -> 16.1 us  [shifted(): return lax.ppermute(value, AXIS, pairs)]
    ppermute x8 -> x12, starting transfers between devices: 44.3 us -> 57.6 us  [shifted(): return lax.ppermute(value, AXIS, pairs)]
    another operation x8 -> x5, other arithmetic: 1.58 us -> 0.48 us
    another operation x3 -> x4, other arithmetic: 1.62 us -> 2.37 us  [on_device(): wins = [jnp.stack([a, b]) for a, b in zip(early_slots, late_slots)]]
  transfers between devices with their start and end apart: 8 -> 12, of which waited for: 7 -> 5; matrix products, arithmetic and copies ran while one was open for 2% -> 4% of each run, Pallas kernels for 0% -> 0%
where the time goes in v3:
time: 94 us; the launch traced here: 93.5 us
  starting transfers between devices  57.6 us (61%)
  waiting for transfers between devices  16.1 us (17%)
  Pallas kernels  9.63 us (10%)
  other arithmetic  5.47 us (6%)
  local copies, waits for them, and re-layouts  3.74 us (4%)
  between operations  0.96 us (1%)
    ppermute x12, starting transfers between devices, shifted(): return lax.ppermute(value, AXIS, pairs)  57.6 us
    ppermute x12, waiting for transfers between devices, shifted(): return lax.ppermute(value, AXIS, pairs)  16.1 us
    pallas_call x1, Pallas kernels, window_grads(): pl.pallas_call(kernel, grid=(halves,), in_specs=[lo_spec, q_spec, q_spec]...  9.63 us
    another operation x4, other arithmetic, on_device(): wins = [jnp.stack([a, b]) for a, b in zip(early_slots, late_slots)]  2.37 us
  transfers between devices with their start and end apart: 12, of which 5 were waited for; matrix products, arithmetic and copies ran while one was open for 4% of the time, Pallas kernels for 0%

profile of v3, /device:TPU:6, one launch (start us, length us, event | category | flops | bytes accessed | tf_op | source)
XLA Modules:
  0.0 93.5 jit_solution(10723984043812892643)
XLA Ops:
  0.7 1.0 %pad_maximum_fusion.w3 = bf16[2,64,1024]{2,1,0:T(8,128)(2,1)S(1)} fusion(bf16[2,64,512]{2,1,0:T(8,128)(2,1)} %bitcast.78, bf16[2,64,512]{2,1,0:T(8,128)(2,1)} %bitcast.81), kind=kLoop, calls=%fused_computation.3 | loop fusion | flops 524288 | bytes 524288 | tf_op jit(solution)/shard_map/concatenate | solution.py:103
  1.7 13.6 %collective-permute-start.5 = (bf16[2,64,1024]{2,1,0:T(8,128)(2,1)S(1)}, bf16[2,64,1024]{2,1,0:T(8,128)(2,1)S(1)}, u32[]{:S(2)}, u32[]{:S(2)}) collective-permute-start(bf16[2,64,1024]{2,1,0:T(8,128)(2,1)S(1)} %pad_maximum_fusion.w3), channel_id=1, source_target_pairs={{1,0},{2,1},{3,2},{4,3},{5,4},{6,5},{7,6},{8,7},{9,8},{10,9},{11,1... | collective-permute-start | bytes 786440 | tf_op jit(solution)/shard_map/ppermute | solution.py:19
  15.3 2.9 %collective-permute-start.2 = (bf16[2,64,1024]{2,1,0:T(8,128)(2,1)S(1)}, bf16[2,64,1024]{2,1,0:T(8,128)(2,1)S(1)}, u32[]{:S(2)}, u32[]{:S(2)}) collective-permute-start(bf16[2,64,1024]{2,1,0:T(8,128)(2,1)S(1)} %pad_maximum_fusion.w3), channel_id=1, source_target_pairs={{2,0},{3,1},{4,2},{5,3},{6,4},{7,5},{8,6},{9,7},{10,8},{11,9},{12,... | collective-permute-start | bytes 786440 | tf_op jit(solution)/shard_map/ppermute | solution.py:19
  18.2 0.7 copy-done.7
  18.9 0.3 reduce-window.9
  19.3 0.1 slice_reduce_fusion
  19.7 0.2 select_reduce_fusion
  20.0 1.9 %collective-permute-done.5 = bf16[2,64,1024]{2,1,0:T(8,128)(2,1)S(1)} collective-permute-done((bf16[2,64,1024]{2,1,0:T(8,128)(2,1)S(1)}, bf16[2,64,1024]{2,1,0:T(8,128)(2,1)S(1)}, u32[]{:S(2)}, u32[]{:S(2)}) %collective-permute-start.5) | collective-permute-done | bytes 262176 | tf_op jit(solution)/shard_map/ppermute | solution.py:19
  22.0 1.9 %collective-permute-start.4 = (bf16[64,1024]{1,0:T(8,128)(2,1)S(1)}, bf16[64,1024]{1,0:T(8,128)(2,1)S(1)}, u32[]{:S(2)}, u32[]{:S(2)}) collective-permute-start(bf16[64,1024]{1,0:T(8,128)(2,1)S(1)} %get-tuple-element.22), channel_id=1, source_target_pairs={{0,1},{1,2},{2,3},{3,4},{4,5},{5,6},{6,7},{7,8},{8,9},{9,10},{10,1... | collective-permute-start | bytes 393224 | tf_op jit(solution)/shard_map/ppermute | solution.py:19
  23.9 1.9 %collective-permute-start.1 = (bf16[64,1024]{1,0:T(8,128)(2,1)S(1)}, bf16[64,1024]{1,0:T(8,128)(2,1)S(1)}, u32[]{:S(2)}, u32[]{:S(2)}) collective-permute-start(bf16[64,1024]{1,0:T(8,128)(2,1)S(1)} %get-tuple-element.22), channel_id=1, source_target_pairs={{0,2},{1,3},{2,4},{3,5},{4,6},{5,7},{6,8},{7,9},{8,10},{9,11},{10,... | collective-permute-start | bytes 393224 | tf_op jit(solution)/shard_map/ppermute | solution.py:19
  25.9 9.2 %collective-permute-start.3 = (bf16[64,1024]{1,0:T(8,128)(2,1)S(1)}, bf16[64,1024]{1,0:T(8,128)(2,1)S(1)}, u32[]{:S(2)}, u32[]{:S(2)}) collective-permute-start(bf16[64,1024]{1,0:T(8,128)(2,1)S(1)} %get-tuple-element.23), channel_id=1, source_target_pairs={{3,0},{4,1},{5,2},{6,3},{7,4},{8,5},{9,6},{10,7},{11,8},{12,9},{13... | collective-permute-start | bytes 393224 | tf_op jit(solution)/shard_map/ppermute | solution.py:19
  35.1 0.7 broadcast_subtract_fusion.lo_ref
  35.8 1.9 %collective-permute-start = (bf16[64,1024]{1,0:T(8,128)(2,1)S(1)}, bf16[64,1024]{1,0:T(8,128)(2,1)S(1)}, u32[]{:S(2)}, u32[]{:S(2)}) collective-permute-start(bf16[64,1024]{1,0:T(8,128)(2,1)S(1)} %get-tuple-element.22), channel_id=1, source_target_pairs={{0,3},{1,4},{2,5},{3,6},{4,7},{5,8},{6,9},{7,10},{8,11},{9,12},{10... | collective-permute-start | bytes 393224 | tf_op jit(solution)/shard_map/ppermute | solution.py:19
  37.7 3.5 %collective-permute-done.3 = bf16[64,1024]{1,0:T(8,128)(2,1)S(1)} collective-permute-done((bf16[64,1024]{1,0:T(8,128)(2,1)S(1)}, bf16[64,1024]{1,0:T(8,128)(2,1)S(1)}, u32[]{:S(2)}, u32[]{:S(2)}) %collective-permute-start.3) | collective-permute-done | bytes 131104 | tf_op jit(solution)/shard_map/ppermute | solution.py:19
  41.2 0.1 fusion.18
  41.3 0.8 pad_maximum_fusion.3.w2
  42.1 0.7 pad_maximum_fusion.2.w1
  42.8 6.9 %collective-permute-done = bf16[64,1024]{1,0:T(8,128)(2,1)S(1)} collective-permute-done((bf16[64,1024]{1,0:T(8,128)(2,1)S(1)}, bf16[64,1024]{1,0:T(8,128)(2,1)S(1)}, u32[]{:S(2)}, u32[]{:S(2)}) %collective-permute-start) | collective-permute-done | bytes 131104 | tf_op jit(solution)/shard_map/ppermute | solution.py:19
  49.8 0.7 pad_maximum_fusion.1.w0
  50.5 9.6 %shard_map.76 = (bf16[2,64,4096]{2,1,0:T(8,128)(2,1)}, f32[2,64,1024]{2,1,0:T(8,128)}, f32[2,64,1024]{2,1,0:T(8,128)}, f32[2,64,1024]{2,1,0:T(8,128)}, f32[2,64,1024]{2,1,0:T(8,128)}) custom-call(s32[2,64,1]{2,1,0:T(8,128)} %broadcast_subtract_fusion.lo_ref, bf16[2,64,4096]{2,1,0:T(8,128)(2,1)} %bitcast.90, bf16[2,64,4096]{2,1,0:T(8,128)(2,1)} %bitcast.91, ...), custom_call_target="tpu_custom_call" | custom-call | flops 1610612736 | bytes 5242880 | tf_op jit(solution)/shard_map/pallas_call | solution.py:81
  60.1 1.0 %slice.208 = bf16[1,64,1024]{2,1,0:T(8,128)(2,1)S(1)} slice(f32[2,64,1024]{2,1,0:T(8,128)} %get-tuple-element.11), slice={[1:2], [0:64], [0:1024]} | slice | bytes 262144 | tf_op jit(solution)/shard_map/slice | solution.py:132
  61.2 1.0 %slice.207 = bf16[1,64,1024]{2,1,0:T(8,128)(2,1)S(1)} slice(f32[2,64,1024]{2,1,0:T(8,128)} %get-tuple-element.10), slice={[1:2], [0:64], [0:1024]} | slice | bytes 262144 | tf_op jit(solution)/shard_map/slice | solution.py:144
  62.2 2.1 %collective-permute-start.9 = (bf16[2,64,1024]{2,1,0:T(8,128)(2,1)S(1)}, bf16[2,64,1024]{2,1,0:T(8,128)(2,1)S(1)}, u32[]{:S(2)}, u32[]{:S(2)}) collective-permute-start(bf16[2,64,1024]{2,1,0:T(8,128)(2,1)S(1)} %get-tuple-element.26), channel_id=1, source_target_pairs={{0,1},{1,2},{2,3},{3,4},{4,5},{5,6},{6,7},{7,8},{8,9},{9,10},{10,1... | collective-permute-start | bytes 786440 | tf_op jit(solution)/shard_map/ppermute | solution.py:19
  64.3 2.7 %collective-permute-start.10 = (bf16[2,64,1024]{2,1,0:T(8,128)(2,1)S(1)}, bf16[2,64,1024]{2,1,0:T(8,128)(2,1)S(1)}, u32[]{:S(2)}, u32[]{:S(2)}) collective-permute-start(bf16[2,64,1024]{2,1,0:T(8,128)(2,1)S(1)} %get-tuple-element.27), channel_id=1, source_target_pairs={{0,2},{1,3},{2,4},{3,5},{4,6},{5,7},{6,8},{7,9},{8,10},{9,11},{10,... | collective-permute-start | bytes 786440 | tf_op jit(solution)/shard_map/ppermute | solution.py:19
  67.2 8.2 %collective-permute-start.6 = (bf16[64,1024]{1,0:T(8,128)(2,1)S(1)}, bf16[64,1024]{1,0:T(8,128)(2,1)S(1)}, u32[]{:S(2)}, u32[]{:S(2)}) collective-permute-start(bf16[64,1024]{1,0:T(8,128)(2,1)S(1)} %get-tuple-element.15), channel_id=1, source_target_pairs={{1,0},{2,1},{3,2},{4,3},{5,4},{6,5},{7,6},{8,7},{9,8},{10,9},{11,1... | collective-permute-start | bytes 393224 | tf_op jit(solution)/shard_map/ppermute | solution.py:19
  75.3 2.5 %collective-permute-start.7 = (bf16[64,1024]{1,0:T(8,128)(2,1)S(1)}, bf16[64,1024]{1,0:T(8,128)(2,1)S(1)}, u32[]{:S(2)}, u32[]{:S(2)}) collective-permute-start(bf16[64,1024]{1,0:T(8,128)(2,1)S(1)} %get-tuple-element.16), channel_id=1, source_target_pairs={{2,0},{3,1},{4,2},{5,3},{6,4},{7,5},{8,6},{9,7},{10,8},{11,9},{12,... | collective-permute-start | bytes 393224 | tf_op jit(solution)/shard_map/ppermute | solution.py:19
  77.9 1.9 %collective-permute-start.11 = (bf16[64,1024]{1,0:T(8,128)(2,1)S(1)}, bf16[64,1024]{1,0:T(8,128)(2,1)S(1)}, u32[]{:S(2)}, u32[]{:S(2)}) collective-permute-start(bf16[64,1024]{1,0:T(8,128)(2,1)S(1)} %bitcast.84), channel_id=1, source_target_pairs={{0,3},{1,4},{2,5},{3,6},{4,7},{5,8},{6,9},{7,10},{8,11},{9,12},{10... | collective-permute-start | bytes 393224 | tf_op jit(solution)/shard_map/ppermute | solution.py:19
  79.8 8.8 %collective-permute-start.8 = (bf16[64,1024]{1,0:T(8,128)(2,1)S(1)}, bf16[64,1024]{1,0:T(8,128)(2,1)S(1)}, u32[]{:S(2)}, u32[]{:S(2)}) collective-permute-start(bf16[64,1024]{1,0:T(8,128)(2,1)S(1)} %get-tuple-element.17), channel_id=1, source_target_pairs={{3,0},{4,1},{5,2},{6,3},{7,4},{8,5},{9,6},{10,7},{11,8},{12,9},{13... | collective-permute-start | bytes 393224 | tf_op jit(solution)/shard_map/ppermute | solution.py:19
  88.7 3.3 %collective-permute-done.11 = bf16[64,1024]{1,0:T(8,128)(2,1)S(1)} collective-permute-done((bf16[64,1024]{1,0:T(8,128)(2,1)S(1)}, bf16[64,1024]{1,0:T(8,128)(2,1)S(1)}, u32[]{:S(2)}, u32[]{:S(2)}) %collective-permute-start.11) | collective-permute-done | bytes 131104 | tf_op jit(solution)/shard_map/ppermute | solution.py:19
  92.0 0.5 collective-permute-done.8
  92.5 0.3 fusion.7
  92.8 0.7 slice_bitcast_fusion
  (36 shorter events, 0.9 us)
Async XLA Ops:
  0.6 21.3 %copy-start = (bf16[1,2,64,512]{3,2,1,0:T(8,128)(2,1)S(1)}, bf16[1,2,64,512]{3,2,1,0:T(8,128)(2,1)}, u32[]{:S(2)}) copy-start(bf16[1,2,64,512]{3,2,1,0:T(8,128)(2,1)} %param.7) | copy-start | bytes 393220
  0.6 21.3 %copy-start.1 = (bf16[1,2,64,512]{3,2,1,0:T(8,128)(2,1)S(1)}, bf16[1,2,64,512]{3,2,1,0:T(8,128)(2,1)}, u32[]{:S(2)}) copy-start(bf16[1,2,64,512]{3,2,1,0:T(8,128)(2,1)} %param.6) | copy-start | bytes 393220
  1.7 20.3 %copy-start.6 = (bf16[2,64,1024]{2,1,0:T(8,128)(2,1)}, bf16[2,64,1024]{2,1,0:T(8,128)(2,1)S(1)}, u32[]{:S(2)}) copy-start(bf16[2,64,1024]{2,1,0:T(8,128)(2,1)S(1)} %pad_maximum_fusion.w3) | copy-start | bytes 786436
  1.7 20.2 %collective-permute-start.5 = (bf16[2,64,1024]{2,1,0:T(8,128)(2,1)S(1)}, bf16[2,64,1024]{2,1,0:T(8,128)(2,1)S(1)}, u32[]{:S(2)}, u32[]{:S(2)}) collective-permute-start(bf16[2,64,1024]{2,1,0:T(8,128)(2,1)S(1)} %pad_maximum_fusion.w3), channel_id=1, source_target_pairs={{1,0},{2,1},{3,2},{4,3},{5,4},{6,5},{7,6},{8,7},{9,8},{10,9},{11,1... | collective-permute-start | bytes 786440 | tf_op jit(solution)/shard_map/ppermute | solution.py:19
  15.3 22.4 %collective-permute-start.2 = (bf16[2,64,1024]{2,1,0:T(8,128)(2,1)S(1)}, bf16[2,64,1024]{2,1,0:T(8,128)(2,1)S(1)}, u32[]{:S(2)}, u32[]{:S(2)}) collective-permute-start(bf16[2,64,1024]{2,1,0:T(8,128)(2,1)S(1)} %pad_maximum_fusion.w3), channel_id=1, source_target_pairs={{2,0},{3,1},{4,2},{5,3},{6,4},{7,5},{8,6},{9,7},{10,8},{11,9},{12,... | collective-permute-start | bytes 786440 | tf_op jit(solution)/shard_map/ppermute | solution.py:19
  18.2 0.7 copy-start.7
  22.0 19.2 %collective-permute-start.4 = (bf16[64,1024]{1,0:T(8,128)(2,1)S(1)}, bf16[64,1024]{1,0:T(8,128)(2,1)S(1)}, u32[]{:S(2)}, u32[]{:S(2)}) collective-permute-start(bf16[64,1024]{1,0:T(8,128)(2,1)S(1)} %get-tuple-element.22), channel_id=1, source_target_pairs={{0,1},{1,2},{2,3},{3,4},{4,5},{5,6},{6,7},{7,8},{8,9},{9,10},{10,1... | collective-permute-start | bytes 393224 | tf_op jit(solution)/shard_map/ppermute | solution.py:19
  23.9 17.2 %collective-permute-start.1 = (bf16[64,1024]{1,0:T(8,128)(2,1)S(1)}, bf16[64,1024]{1,0:T(8,128)(2,1)S(1)}, u32[]{:S(2)}, u32[]{:S(2)}) collective-permute-start(bf16[64,1024]{1,0:T(8,128)(2,1)S(1)} %get-tuple-element.22), channel_id=1, source_target_pairs={{0,2},{1,3},{2,4},{3,5},{4,6},{5,7},{6,8},{7,9},{8,10},{9,11},{10,... | collective-permute-start | bytes 393224 | tf_op jit(solution)/shard_map/ppermute | solution.py:19
  25.9 15.3 %collective-permute-start.3 = (bf16[64,1024]{1,0:T(8,128)(2,1)S(1)}, bf16[64,1024]{1,0:T(8,128)(2,1)S(1)}, u32[]{:S(2)}, u32[]{:S(2)}) collective-permute-start(bf16[64,1024]{1,0:T(8,128)(2,1)S(1)} %get-tuple-element.23), channel_id=1, source_target_pairs={{3,0},{4,1},{5,2},{6,3},{7,4},{8,5},{9,6},{10,7},{11,8},{12,9},{13... | collective-permute-start | bytes 393224 | tf_op jit(solution)/shard_map/ppermute | solution.py:19
  35.8 14.0 %collective-permute-start = (bf16[64,1024]{1,0:T(8,128)(2,1)S(1)}, bf16[64,1024]{1,0:T(8,128)(2,1)S(1)}, u32[]{:S(2)}, u32[]{:S(2)}) collective-permute-start(bf16[64,1024]{1,0:T(8,128)(2,1)S(1)} %get-tuple-element.22), channel_id=1, source_target_pairs={{0,3},{1,4},{2,5},{3,6},{4,7},{5,8},{6,9},{7,10},{8,11},{9,12},{10... | collective-permute-start | bytes 393224 | tf_op jit(solution)/shard_map/ppermute | solution.py:19
  60.1 2.0 %copy-start.2 = (f32[2,64,1024]{2,1,0:T(8,128)S(1)}, f32[2,64,1024]{2,1,0:T(8,128)}, u32[]{:S(2)}) copy-start(f32[2,64,1024]{2,1,0:T(8,128)} %get-tuple-element.12) | copy-start | bytes 1572868
  62.1 4.9 %copy-start.4 = (f32[2,64,1024]{2,1,0:T(8,128)S(1)}, f32[2,64,1024]{2,1,0:T(8,128)}, u32[]{:S(2)}) copy-start(f32[2,64,1024]{2,1,0:T(8,128)} %get-tuple-element.10) | copy-start | bytes 1572868
  62.2 4.9 %copy-start.3 = (f32[2,64,1024]{2,1,0:T(8,128)S(1)}, f32[2,64,1024]{2,1,0:T(8,128)}, u32[]{:S(2)}) copy-start(f32[2,64,1024]{2,1,0:T(8,128)} %get-tuple-element.11) | copy-start | bytes 1572868
  62.2 17.6 %collective-permute-start.9 = (bf16[2,64,1024]{2,1,0:T(8,128)(2,1)S(1)}, bf16[2,64,1024]{2,1,0:T(8,128)(2,1)S(1)}, u32[]{:S(2)}, u32[]{:S(2)}) collective-permute-start(bf16[2,64,1024]{2,1,0:T(8,128)(2,1)S(1)} %get-tuple-element.26), channel_id=1, source_target_pairs={{0,1},{1,2},{2,3},{3,4},{4,5},{5,6},{6,7},{7,8},{8,9},{9,10},{10,1... | collective-permute-start | bytes 786440 | tf_op jit(solution)/shard_map/ppermute | solution.py:19
  64.3 24.3 %collective-permute-start.10 = (bf16[2,64,1024]{2,1,0:T(8,128)(2,1)S(1)}, bf16[2,64,1024]{2,1,0:T(8,128)(2,1)S(1)}, u32[]{:S(2)}, u32[]{:S(2)}) collective-permute-start(bf16[2,64,1024]{2,1,0:T(8,128)(2,1)S(1)} %get-tuple-element.27), channel_id=1, source_target_pairs={{0,2},{1,3},{2,4},{3,5},{4,6},{5,7},{6,8},{7,9},{8,10},{9,11},{10,... | collective-permute-start | bytes 786440 | tf_op jit(solution)/shard_map/ppermute | solution.py:19
  67.2 21.5 %collective-permute-start.6 = (bf16[64,1024]{1,0:T(8,128)(2,1)S(1)}, bf16[64,1024]{1,0:T(8,128)(2,1)S(1)}, u32[]{:S(2)}, u32[]{:S(2)}) collective-permute-start(bf16[64,1024]{1,0:T(8,128)(2,1)S(1)} %get-tuple-element.15), channel_id=1, source_target_pairs={{1,0},{2,1},{3,2},{4,3},{5,4},{6,5},{7,6},{8,7},{9,8},{10,9},{11,1... | collective-permute-start | bytes 393224 | tf_op jit(solution)/shard_map/ppermute | solution.py:19
  75.3 13.4 %collective-permute-start.7 = (bf16[64,1024]{1,0:T(8,128)(2,1)S(1)}, bf16[64,1024]{1,0:T(8,128)(2,1)S(1)}, u32[]{:S(2)}, u32[]{:S(2)}) collective-permute-start(bf16[64,1024]{1,0:T(8,128)(2,1)S(1)} %get-tuple-element.16), channel_id=1, source_target_pairs={{2,0},{3,1},{4,2},{5,3},{6,4},{7,5},{8,6},{9,7},{10,8},{11,9},{12,... | collective-permute-start | bytes 393224 | tf_op jit(solution)/shard_map/ppermute | solution.py:19
  77.9 14.1 %collective-permute-start.11 = (bf16[64,1024]{1,0:T(8,128)(2,1)S(1)}, bf16[64,1024]{1,0:T(8,128)(2,1)S(1)}, u32[]{:S(2)}, u32[]{:S(2)}) collective-permute-start(bf16[64,1024]{1,0:T(8,128)(2,1)S(1)} %bitcast.84), channel_id=1, source_target_pairs={{0,3},{1,4},{2,5},{3,6},{4,7},{5,8},{6,9},{7,10},{8,11},{9,12},{10... | collective-permute-start | bytes 393224 | tf_op jit(solution)/shard_map/ppermute | solution.py:19
  79.8 12.7 %collective-permute-start.8 = (bf16[64,1024]{1,0:T(8,128)(2,1)S(1)}, bf16[64,1024]{1,0:T(8,128)(2,1)S(1)}, u32[]{:S(2)}, u32[]{:S(2)}) collective-permute-start(bf16[64,1024]{1,0:T(8,128)(2,1)S(1)} %get-tuple-element.17), channel_id=1, source_target_pairs={{3,0},{4,1},{5,2},{6,3},{7,4},{8,5},{9,6},{10,7},{11,8},{12,9},{13... | collective-permute-start | bytes 393224 | tf_op jit(solution)/shard_map/ppermute | solution.py:19
  88.6 3.9 %copy-start.5 = (f32[2,64,1024]{2,1,0:T(8,128)S(1)}, f32[2,64,1024]{2,1,0:T(8,128)}, u32[]{:S(2)}) copy-start(f32[2,64,1024]{2,1,0:T(8,128)} %get-tuple-element.9) | copy-start | bytes 1572868

commit v4 on v2

--- a/solution.py
+++ b/solution.py
@@ -106,13 +106,14 @@
     below_top = me == n - 2
 
     e1 = shifted(early, 1)
-    l1 = shifted(kv, -1)
+    l1 = shifted(late, -1)
+    turn = lax.ppermute(early, AXIS, [(n - 1, n - 2)])
     e2 = shifted(jnp.stack([early, e1]), 2)
-    l2 = shifted(jnp.stack([late, jnp.where(at_top, early, l1[1])]), -2)
+    l2 = shifted(jnp.stack([late, jnp.where(at_top, early, l1)]), -2)
     late_slots = [
         jnp.where(at_top, e2[0], jnp.where(below_top, early, l2[1])),
-        jnp.where(at_top, e1, jnp.where(below_top, l1[0], l2[0])),
-        jnp.where(at_top, early, l1[1]),
+        jnp.where(at_top, e1, jnp.where(below_top, turn, l2[0])),
+        jnp.where(at_top, early, l1),
         late,
     ]
     early_slots = [e2[1], e2[0], e1, early]
@@ -134,15 +135,16 @@
     a_e = shifted(jnp.stack([p1e, p0[0]]).astype(link), -2).astype(jnp.float32)
     a_l = shifted(jnp.stack([p1[1], p0[1]]).astype(link), 2).astype(jnp.float32)
     b_e = shifted((p2e + a_e[1]).astype(link), -1).astype(jnp.float32)
-    b_l = shifted(jnp.stack([p2[1] + a_l[1], p1[1]]).astype(link), 1).astype(jnp.float32)
+    b_l = shifted((p2[1] + a_l[1]).astype(link), 1).astype(jnp.float32)
+    back = lax.ppermute(p1[1].astype(link), AXIS, [(n - 2, n - 1)]).astype(jnp.float32)
     final_early = (
         p3[0]
         + a_e[0]
         + b_e
-        + jnp.where(at_top, p2[1] + a_l[1] + b_l[1], zero)
+        + jnp.where(at_top, p2[1] + a_l[1] + back, zero)
         + jnp.where(below_top, p0[1], zero)
     )
-    final_late = p3[1] + a_l[0] + b_l[0]
+    final_late = p3[1] + a_l[0] + b_l
     final = jnp.stack([final_early, final_late])
     grad_keys = final[:, :, :kv_width].astype(jnp.bfloat16).reshape(keys.shape)
     grad_values = final[:, :, kv_width:].astype(jnp.bfloat16).reshape(values.shape)

time: 93.6 us -> 95.8 us (1.024)
  other arithmetic: 5.81 us -> 7.01 us
    ppermute x0 -> x2, starting transfers between devices: none -> 1.33 us  [the longest x1 0.67 us: on_device(): lax.ppermute(p1[1].astype(link), AXIS, [(n - 2, n - 1)]).astype(jnp.float32)]
    ppermute x8, starting transfers between devices: 44.3 us -> 43.2 us  [shifted(): return lax.ppermute(value, AXIS, pairs)]
    another operation x3 -> x4, other arithmetic: 1.62 us -> 2.23 us  [on_device(): wins = [jnp.stack([a, b]) for a, b in zip(early_slots, late_slots)]]
  transfers between devices with their start and end apart: 8 -> 10, of which waited for: 7 -> 8; matrix products, arithmetic and copies ran while one was open for 2% -> 4% of each run, Pallas kernels for 0% -> 0%
where the time goes in v4:
time: 95.8 us; the launch traced here: 95.3 us
  starting transfers between devices  44.5 us (46%)
  waiting for transfers between devices  30.5 us (32%)
  Pallas kernels  9.61 us (10%)
  other arithmetic  7.01 us (7%)
  local copies, waits for them, and re-layouts  2.79 us (3%)
    ppermute x8, starting transfers between devices, shifted(): return lax.ppermute(value, AXIS, pairs)  43.2 us
    ppermute x8, waiting for transfers between devices, shifted(): return lax.ppermute(value, AXIS, pairs)  30.5 us
    pallas_call x1, Pallas kernels, window_grads(): pl.pallas_call(kernel, grid=(halves,), in_specs=[lo_spec, q_spec, q_spec]...  9.61 us
    another operation x4, other arithmetic, on_device(): wins = [jnp.stack([a, b]) for a, b in zip(early_slots, late_slots)]  2.23 us
  transfers between devices with their start and end apart: 10, of which 8 were waited for; matrix products, arithmetic and copies ran while one was open for 4% of the time, Pallas kernels for 0%

profile of v4, /device:TPU:6, one launch (start us, length us, event | category | flops | bytes accessed | tf_op | source)
XLA Modules:
  0.0 95.3 jit_solution(7079930317704816358)
XLA Ops:
  0.7 0.9 fusion.12
  1.6 13.6 %collective-permute-start.2 = (bf16[64,1024]{1,0:T(8,128)(2,1)S(1)}, bf16[64,1024]{1,0:T(8,128)(2,1)S(1)}, u32[]{:S(2)}, u32[]{:S(2)}) collective-permute-start(bf16[64,1024]{1,0:T(8,128)(2,1)S(1)} %bitcast.71), channel_id=1, source_target_pairs={{1,0},{2,1},{3,2},{4,3},{5,4},{6,5},{7,6},{8,7},{9,8},{10,9},{11,1... | collective-permute-start | bytes 393224 | tf_op jit(solution)/shard_map/ppermute | solution.py:19
  15.2 0.7 copy-done.6
  15.8 0.3 reduce-window.9
  16.6 2.3 %collective-permute-done.2 = bf16[64,1024]{1,0:T(8,128)(2,1)S(1)} collective-permute-done((bf16[64,1024]{1,0:T(8,128)(2,1)S(1)}, bf16[64,1024]{1,0:T(8,128)(2,1)S(1)}, u32[]{:S(2)}, u32[]{:S(2)}) %collective-permute-start.2) | collective-permute-done | bytes 131104 | tf_op jit(solution)/shard_map/ppermute | solution.py:19
  19.0 1.9 %collective-permute-start = (bf16[64,1024]{1,0:T(8,128)(2,1)S(1)}, bf16[64,1024]{1,0:T(8,128)(2,1)S(1)}, u32[]{:S(2)}, u32[]{:S(2)}) collective-permute-start(bf16[64,1024]{1,0:T(8,128)(2,1)S(1)} %bitcast.69), channel_id=1, source_target_pairs={{0,1},{1,2},{2,3},{3,4},{4,5},{5,6},{6,7},{7,8},{8,9},{9,10},{10,1... | collective-permute-start | bytes 393224 | tf_op jit(solution)/shard_map/ppermute | solution.py:19
  20.9 0.2 select_reduce_fusion
  21.3 0.7 collective-permute-start.4
  21.9 9.2 %collective-permute-done = bf16[64,1024]{1,0:T(8,128)(2,1)S(1)} collective-permute-done((bf16[64,1024]{1,0:T(8,128)(2,1)S(1)}, bf16[64,1024]{1,0:T(8,128)(2,1)S(1)}, u32[]{:S(2)}, u32[]{:S(2)}) %collective-permute-start) | collective-permute-done | bytes 131104 | tf_op jit(solution)/shard_map/ppermute | solution.py:19
  31.1 0.8 pad_maximum_fusion.1
  31.9 1.9 %collective-permute-start.3 = (bf16[2,64,1024]{2,1,0:T(8,128)(2,1)S(1)}, bf16[2,64,1024]{2,1,0:T(8,128)(2,1)S(1)}, u32[]{:S(2)}, u32[]{:S(2)}) collective-permute-start(bf16[2,64,1024]{2,1,0:T(8,128)(2,1)S(1)} %get-tuple-element.28), channel_id=1, source_target_pairs={{2,0},{3,1},{4,2},{5,3},{6,4},{7,5},{8,6},{9,7},{10,8},{11,9},{12,... | collective-permute-start | bytes 786440 | tf_op jit(solution)/shard_map/ppermute | solution.py:19
  33.8 0.7 broadcast_subtract_fusion.lo_ref
  34.5 3.9 %collective-permute-start.1 = (bf16[2,64,1024]{2,1,0:T(8,128)(2,1)S(1)}, bf16[2,64,1024]{2,1,0:T(8,128)(2,1)S(1)}, u32[]{:S(2)}, u32[]{:S(2)}) collective-permute-start(bf16[2,64,1024]{2,1,0:T(8,128)(2,1)S(1)} %get-tuple-element.27), channel_id=1, source_target_pairs={{0,2},{1,3},{2,4},{3,5},{4,6},{5,7},{6,8},{7,9},{8,10},{9,11},{10,... | collective-permute-start | bytes 786440 | tf_op jit(solution)/shard_map/ppermute | solution.py:19
  38.4 0.7 pad_maximum_fusion.w3
  39.2 2.0 %collective-permute-done.3 = bf16[2,64,1024]{2,1,0:T(8,128)(2,1)S(1)} collective-permute-done((bf16[2,64,1024]{2,1,0:T(8,128)(2,1)S(1)}, bf16[2,64,1024]{2,1,0:T(8,128)(2,1)S(1)}, u32[]{:S(2)}, u32[]{:S(2)}) %collective-permute-start.3) | collective-permute-done | bytes 262176 | tf_op jit(solution)/shard_map/ppermute | solution.py:19
  41.2 5.3 %collective-permute-done.1 = bf16[2,64,1024]{2,1,0:T(8,128)(2,1)S(1)} collective-permute-done((bf16[2,64,1024]{2,1,0:T(8,128)(2,1)S(1)}, bf16[2,64,1024]{2,1,0:T(8,128)(2,1)S(1)}, u32[]{:S(2)}, u32[]{:S(2)}) %collective-permute-start.1) | collective-permute-done | bytes 262176 | tf_op jit(solution)/shard_map/ppermute | solution.py:19
  46.5 0.7 pad_maximum_fusion.5.w1
  47.3 0.7 pad_maximum_fusion.4.w0
  48.0 9.6 %shard_map.76 = (bf16[2,64,4096]{2,1,0:T(8,128)(2,1)}, f32[2,64,1024]{2,1,0:T(8,128)}, f32[2,64,1024]{2,1,0:T(8,128)}, f32[2,64,1024]{2,1,0:T(8,128)}, f32[2,64,1024]{2,1,0:T(8,128)}) custom-call(s32[2,64,1]{2,1,0:T(8,128)} %broadcast_subtract_fusion.lo_ref, bf16[2,64,4096]{2,1,0:T(8,128)(2,1)} %bitcast.75, bf16[2,64,4096]{2,1,0:T(8,128)(2,1)} %bitcast.76, ...), custom_call_target="tpu_custom_call" | custom-call | flops 1610612736 | bytes 5242880 | tf_op jit(solution)/shard_map/pallas_call | solution.py:81
  57.6 1.0 %slice.191 = bf16[1,64,1024]{2,1,0:T(8,128)(2,1)S(1)} slice(f32[2,64,1024]{2,1,0:T(8,128)} %get-tuple-element.10), slice={[1:2], [0:64], [0:1024]} | slice | bytes 262144 | tf_op jit(solution)/shard_map/slice | solution.py:134
  58.6 1.1 %add_convert_fusion = bf16[1,64,1024]{2,1,0:T(8,128)(2,1)S(1)} fusion(f32[2,64,1024]{2,1,0:T(8,128)} %get-tuple-element.10, f32[2,64,1024]{2,1,0:T(8,128)} %get-tuple-element.11, pred[]{:T(512)S(6)} %eq.6), kind=kLoop, calls=%fused_computation.28 | loop fusion | flops 196608 | bytes 655361 | tf_op jit(solution)/shard_map/convert.4
  59.8 2.1 %collective-permute-start.7 = (bf16[2,64,1024]{2,1,0:T(8,128)(2,1)S(1)}, bf16[2,64,1024]{2,1,0:T(8,128)(2,1)S(1)}, u32[]{:S(2)}, u32[]{:S(2)}) collective-permute-start(bf16[2,64,1024]{2,1,0:T(8,128)(2,1)S(1)} %pad_maximum_fusion.7), channel_id=1, source_target_pairs={{0,2},{1,3},{2,4},{3,5},{4,6},{5,7},{6,8},{7,9},{8,10},{9,11},{10,... | collective-permute-start | bytes 786440 | tf_op jit(solution)/shard_map/ppermute | solution.py:19
  61.9 6.7 %collective-permute-start.5 = (bf16[2,64,1024]{2,1,0:T(8,128)(2,1)S(1)}, bf16[2,64,1024]{2,1,0:T(8,128)(2,1)S(1)}, u32[]{:S(2)}, u32[]{:S(2)}) collective-permute-start(bf16[2,64,1024]{2,1,0:T(8,128)(2,1)S(1)} %pad_maximum_fusion.6), channel_id=1, source_target_pairs={{2,0},{3,1},{4,2},{5,3},{6,4},{7,5},{8,6},{9,7},{10,8},{11,9},{12,... | collective-permute-start | bytes 786440 | tf_op jit(solution)/shard_map/ppermute | solution.py:19
  68.6 0.7 collective-permute-start.8
  69.3 1.4 %collective-permute-done.7 = bf16[2,64,1024]{2,1,0:T(8,128)(2,1)S(1)} collective-permute-done((bf16[2,64,1024]{2,1,0:T(8,128)(2,1)S(1)}, bf16[2,64,1024]{2,1,0:T(8,128)(2,1)S(1)}, u32[]{:S(2)}, u32[]{:S(2)}) %collective-permute-start.7) | collective-permute-done | bytes 262176 | tf_op jit(solution)/shard_map/ppermute | solution.py:19
  70.7 1.7 %collective-permute-done.5 = bf16[2,64,1024]{2,1,0:T(8,128)(2,1)S(1)} collective-permute-done((bf16[2,64,1024]{2,1,0:T(8,128)(2,1)S(1)}, bf16[2,64,1024]{2,1,0:T(8,128)(2,1)S(1)}, u32[]{:S(2)}, u32[]{:S(2)}) %collective-permute-start.5) | collective-permute-done | bytes 262176 | tf_op jit(solution)/shard_map/ppermute | solution.py:19
  72.6 11.3 %collective-permute-start.6 = (bf16[64,1024]{1,0:T(8,128)(2,1)S(1)}, bf16[64,1024]{1,0:T(8,128)(2,1)S(1)}, u32[]{:S(2)}, u32[]{:S(2)}) collective-permute-start(bf16[64,1024]{1,0:T(8,128)(2,1)S(1)} %get-tuple-element.17), channel_id=1, source_target_pairs={{1,0},{2,1},{3,2},{4,3},{5,4},{6,5},{7,6},{8,7},{9,8},{10,9},{11,1... | collective-permute-start | bytes 393224 | tf_op jit(solution)/shard_map/ppermute | solution.py:19
  83.8 1.9 %collective-permute-start.9 = (bf16[64,1024]{1,0:T(8,128)(2,1)S(1)}, bf16[64,1024]{1,0:T(8,128)(2,1)S(1)}, u32[]{:S(2)}, u32[]{:S(2)}) collective-permute-start(bf16[64,1024]{1,0:T(8,128)(2,1)S(1)} %get-tuple-element.18), channel_id=1, source_target_pairs={{0,1},{1,2},{2,3},{3,4},{4,5},{5,6},{6,7},{7,8},{8,9},{9,10},{10,1... | collective-permute-start | bytes 393224 | tf_op jit(solution)/shard_map/ppermute | solution.py:19
  85.8 0.6 collective-permute-done.6
  86.3 8.0 %collective-permute-done.9 = bf16[64,1024]{1,0:T(8,128)(2,1)S(1)} collective-permute-done((bf16[64,1024]{1,0:T(8,128)(2,1)S(1)}, bf16[64,1024]{1,0:T(8,128)(2,1)S(1)}, u32[]{:S(2)}, u32[]{:S(2)}) %collective-permute-start.9) | collective-permute-done | bytes 131104 | tf_op jit(solution)/shard_map/ppermute | solution.py:19
  94.4 0.2 fusion.9
  94.6 0.7 slice_bitcast_fusion
  (34 shorter events, 1.0 us)
Async XLA Ops:
  0.6 18.3 %copy-start.3 = (bf16[1,2,64,512]{3,2,1,0:T(8,128)(2,1)S(1)}, bf16[1,2,64,512]{3,2,1,0:T(8,128)(2,1)}, u32[]{:S(2)}) copy-start(bf16[1,2,64,512]{3,2,1,0:T(8,128)(2,1)} %param.6) | copy-start | bytes 393220
  0.6 18.3 %copy-start.4 = (bf16[1,2,64,512]{3,2,1,0:T(8,128)(2,1)S(1)}, bf16[1,2,64,512]{3,2,1,0:T(8,128)(2,1)}, u32[]{:S(2)}) copy-start(bf16[1,2,64,512]{3,2,1,0:T(8,128)(2,1)} %param.7) | copy-start | bytes 393220
  1.6 17.3 %collective-permute-start.2 = (bf16[64,1024]{1,0:T(8,128)(2,1)S(1)}, bf16[64,1024]{1,0:T(8,128)(2,1)S(1)}, u32[]{:S(2)}, u32[]{:S(2)}) collective-permute-start(bf16[64,1024]{1,0:T(8,128)(2,1)S(1)} %bitcast.71), channel_id=1, source_target_pairs={{1,0},{2,1},{3,2},{4,3},{5,4},{6,5},{7,6},{8,7},{9,8},{10,9},{11,1... | collective-permute-start | bytes 393224 | tf_op jit(solution)/shard_map/ppermute | solution.py:19
  15.2 0.7 copy-start.6
  19.0 12.2 %collective-permute-start = (bf16[64,1024]{1,0:T(8,128)(2,1)S(1)}, bf16[64,1024]{1,0:T(8,128)(2,1)S(1)}, u32[]{:S(2)}, u32[]{:S(2)}) collective-permute-start(bf16[64,1024]{1,0:T(8,128)(2,1)S(1)} %bitcast.69), channel_id=1, source_target_pairs={{0,1},{1,2},{2,3},{3,4},{4,5},{5,6},{6,7},{7,8},{8,9},{9,10},{10,1... | collective-permute-start | bytes 393224 | tf_op jit(solution)/shard_map/ppermute | solution.py:19
  21.3 17.9 %collective-permute-start.4 = (bf16[64,1024]{1,0:T(8,128)(2,1)S(1)}, bf16[64,1024]{1,0:T(8,128)(2,1)S(1)}, u32[]{:S(2)}, u32[]{:S(2)}) collective-permute-start(bf16[64,1024]{1,0:T(8,128)(2,1)S(1)} %bitcast.70), channel_id=1, source_target_pairs={{511,510}} | collective-permute-start | bytes 393224 | tf_op jit(solution)/shard_map/ppermute | solution.py:110
  31.9 9.3 %collective-permute-start.3 = (bf16[2,64,1024]{2,1,0:T(8,128)(2,1)S(1)}, bf16[2,64,1024]{2,1,0:T(8,128)(2,1)S(1)}, u32[]{:S(2)}, u32[]{:S(2)}) collective-permute-start(bf16[2,64,1024]{2,1,0:T(8,128)(2,1)S(1)} %get-tuple-element.28), channel_id=1, source_target_pairs={{2,0},{3,1},{4,2},{5,3},{6,4},{7,5},{8,6},{9,7},{10,8},{11,9},{12,... | collective-permute-start | bytes 786440 | tf_op jit(solution)/shard_map/ppermute | solution.py:19
  34.5 12.0 %collective-permute-start.1 = (bf16[2,64,1024]{2,1,0:T(8,128)(2,1)S(1)}, bf16[2,64,1024]{2,1,0:T(8,128)(2,1)S(1)}, u32[]{:S(2)}, u32[]{:S(2)}) collective-permute-start(bf16[2,64,1024]{2,1,0:T(8,128)(2,1)S(1)} %get-tuple-element.27), channel_id=1, source_target_pairs={{0,2},{1,3},{2,4},{3,5},{4,6},{5,7},{6,8},{7,9},{8,10},{9,11},{10,... | collective-permute-start | bytes 786440 | tf_op jit(solution)/shard_map/ppermute | solution.py:19
  57.6 2.1 %copy-start = (f32[2,64,1024]{2,1,0:T(8,128)S(1)}, f32[2,64,1024]{2,1,0:T(8,128)}, u32[]{:S(2)}) copy-start(f32[2,64,1024]{2,1,0:T(8,128)} %get-tuple-element.11) | copy-start | bytes 1572868
  59.8 8.8 %copy-start.2 = (f32[2,64,1024]{2,1,0:T(8,128)S(1)}, f32[2,64,1024]{2,1,0:T(8,128)}, u32[]{:S(2)}) copy-start(f32[2,64,1024]{2,1,0:T(8,128)} %get-tuple-element.10) | copy-start | bytes 1572868
  59.8 10.8 %collective-permute-start.7 = (bf16[2,64,1024]{2,1,0:T(8,128)(2,1)S(1)}, bf16[2,64,1024]{2,1,0:T(8,128)(2,1)S(1)}, u32[]{:S(2)}, u32[]{:S(2)}) collective-permute-start(bf16[2,64,1024]{2,1,0:T(8,128)(2,1)S(1)} %pad_maximum_fusion.7), channel_id=1, source_target_pairs={{0,2},{1,3},{2,4},{3,5},{4,6},{5,7},{6,8},{7,9},{8,10},{9,11},{10,... | collective-permute-start | bytes 786440 | tf_op jit(solution)/shard_map/ppermute | solution.py:19
  61.9 10.5 %collective-permute-start.5 = (bf16[2,64,1024]{2,1,0:T(8,128)(2,1)S(1)}, bf16[2,64,1024]{2,1,0:T(8,128)(2,1)S(1)}, u32[]{:S(2)}, u32[]{:S(2)}) collective-permute-start(bf16[2,64,1024]{2,1,0:T(8,128)(2,1)S(1)} %pad_maximum_fusion.6), channel_id=1, source_target_pairs={{2,0},{3,1},{4,2},{5,3},{6,4},{7,5},{8,6},{9,7},{10,8},{11,9},{12,... | collective-permute-start | bytes 786440 | tf_op jit(solution)/shard_map/ppermute | solution.py:19
  68.6 17.2 %collective-permute-start.8 = (bf16[64,1024]{1,0:T(8,128)(2,1)S(1)}, bf16[64,1024]{1,0:T(8,128)(2,1)S(1)}, u32[]{:S(2)}, u32[]{:S(2)}) collective-permute-start(bf16[64,1024]{1,0:T(8,128)(2,1)S(1)} %slice_bitcast_fusion.3), channel_id=1, source_target_pairs={{510,511}} | collective-permute-start | bytes 393224 | tf_op jit(solution)/shard_map/ppermute | solution.py:139
  70.7 1.8 %copy-start.1 = (f32[2,64,1024]{2,1,0:T(8,128)S(1)}, f32[2,64,1024]{2,1,0:T(8,128)}, u32[]{:S(2)}) copy-start(f32[2,64,1024]{2,1,0:T(8,128)} %get-tuple-element.12) | copy-start | bytes 1572868
  72.5 21.9 %copy-start.5 = (f32[2,64,1024]{2,1,0:T(8,128)S(1)}, f32[2,64,1024]{2,1,0:T(8,128)}, u32[]{:S(2)}) copy-start(f32[2,64,1024]{2,1,0:T(8,128)} %get-tuple-element.9) | copy-start | bytes 1572868
  72.6 13.8 %collective-permute-start.6 = (bf16[64,1024]{1,0:T(8,128)(2,1)S(1)}, bf16[64,1024]{1,0:T(8,128)(2,1)S(1)}, u32[]{:S(2)}, u32[]{:S(2)}) collective-permute-start(bf16[64,1024]{1,0:T(8,128)(2,1)S(1)} %get-tuple-element.17), channel_id=1, source_target_pairs={{1,0},{2,1},{3,2},{4,3},{5,4},{6,5},{7,6},{8,7},{9,8},{10,9},{11,1... | collective-permute-start | bytes 393224 | tf_op jit(solution)/shard_map/ppermute | solution.py:19
  83.8 10.5 %collective-permute-start.9 = (bf16[64,1024]{1,0:T(8,128)(2,1)S(1)}, bf16[64,1024]{1,0:T(8,128)(2,1)S(1)}, u32[]{:S(2)}, u32[]{:S(2)}) collective-permute-start(bf16[64,1024]{1,0:T(8,128)(2,1)S(1)} %get-tuple-element.18), channel_id=1, source_target_pairs={{0,1},{1,2},{2,3},{3,4},{4,5},{5,6},{6,7},{7,8},{8,9},{9,10},{10,1... | collective-permute-start | bytes 393224 | tf_op jit(solution)/shard_map/ppermute | solution.py:19

commit v5 on v4

v5 whole, which is shorter than its diff:
```python
import functools
import math

import jax
import jax.numpy as jnp
from jax import lax
from jax.experimental import pallas as pl
from jax.experimental.pallas import tpu as pltpu
from jax.sharding import PartitionSpec as P

HEAD = 128
REACH = 3
AXIS = ("dp", "ctx")


def shifted(value, steps):
    count = lax.axis_size(AXIS)
    pairs = [(s, s + steps) for s in range(count) if 0 <= s + steps < count]
    return lax.ppermute(value, AXIS, pairs)


def window_half(half, slot, lo_ref, q_ref, do_ref, groups, group_size, emit):
    half_rows = q_ref.shape[1]
    window = 4 * half_rows
    kv_width = groups * HEAD
    scale = 1.0 / math.sqrt(HEAD)
    lo = lo_ref[0]
    rows = lax.broadcasted_iota(jnp.int32, (half_rows, window), 0)
    cols = lax.broadcasted_iota(jnp.int32, (half_rows, window), 1)
    visible = (cols >= lo) & (cols <= rows + (window - half_rows))
    bias = jnp.where(visible, 0.0, -1e30).astype(jnp.float32)
    bias = jnp.concatenate([bias] * group_size, axis=0)
    nt = (((1,), (1,)), ((), ()))
    tn = (((0,), (0,)), ((), ()))
    for g in range(groups):
        base = g * group_size * HEAD
        qg = jnp.concatenate(
            [q_ref[0, :, base + h * HEAD:base + (h + 1) * HEAD] for h in range(group_size)], axis=0
        )
        dog = jnp.concatenate(
            [do_ref[0, :, base + h * HEAD:base + (h + 1) * HEAD] for h in range(group_size)], axis=0
        )
        kg = jnp.concatenate([slot(j, g * HEAD) for j in range(4)], axis=0)
        vg = jnp.concatenate([slot(j, kv_width + g * HEAD) for j in range(4)], axis=0)
        scores = lax.dot_general(qg, kg, nt, preferred_element_type=jnp.float32) * scale
        masked = scores + bias
        top = jnp.max(masked, axis=1, keepdims=True)
        expd = jnp.exp(masked - top)
        total = jnp.sum(expd, axis=1, keepdims=True)
        probs = (expd * (1.0 / total)).astype(jnp.bfloat16)
        attn = jnp.dot(probs, vg, preferred_element_type=jnp.float32).astype(jnp.bfloat16)
        delta = jnp.sum(dog.astype(jnp.float32) * attn.astype(jnp.float32), axis=1, keepdims=True)
        dprob = lax.dot_general(dog, vg, nt, preferred_element_type=jnp.float32)
        dscore = (probs.astype(jnp.float32) * (dprob - delta) * scale).astype(jnp.bfloat16)
        dq = jnp.dot(dscore, kg, preferred_element_type=jnp.float32).astype(jnp.bfloat16)
        for h in range(group_size):
            emit("dq", h, base + h * HEAD, dq[h * half_rows:(h + 1) * half_rows])
        dk = lax.dot_general(dscore, qg, tn, preferred_element_type=jnp.float32)
        dv = lax.dot_general(probs, dog, tn, preferred_element_type=jnp.float32)
        for j in range(4):
            emit("part", j, g * HEAD, dk[j * half_rows:(j + 1) * half_rows])
            emit("part", j, kv_width + g * HEAD, dv[j * half_rows:(j + 1) * half_rows])


def window_kernel(
    flags, lo_ref, q_ref, do_ref, kv, e1, e2, l1, l2, turn,
    dq_ref, a_e, a_l, p2_ref, p3_ref, kept, *, groups, group_size
):
    step = pl.program_id(0)
    at_top = flags[0] != 0
    below_top = flags[1] != 0

    def tile(ref, lanes, *lead):
        return ref[lead + (slice(None), pl.ds(lanes, HEAD))]

    def store_dq(h, lanes, value):
        dq_ref[0, :, pl.ds(lanes, HEAD)] = value

    def late_slot(j, lanes):
        if j == 0:
            regular = jnp.where(below_top, tile(kv, lanes, 0), tile(l2, lanes, 1))
            return jnp.where(at_top, tile(e2, lanes, 0), regular)
        if j == 1:
            regular = jnp.where(below_top, tile(turn, lanes), tile(l2, lanes, 0))
            return jnp.where(at_top, tile(e1, lanes), regular)
        if j == 2:
            return jnp.where(at_top, tile(kv, lanes, 0), tile(l1, lanes))
        return tile(kv, lanes, 1)

    def early_slot(j, lanes):
        return (
            tile(e2, lanes, 1), tile(e2, lanes, 0), tile(e1, lanes), tile(kv, lanes, 0)
        )[j]

    def late_emit(kind, j, lanes, value):
        if kind == "dq":
            store_dq(j, lanes, value)
            return
        cols = pl.ds(lanes, HEAD)
        if j < 3:
            kept[j, :, cols] = value
        if j == 0:
            a_l[1, :, cols] = value.astype(a_l.dtype)
        elif j == 1:
            a_l[0, :, cols] = value.astype(a_l.dtype)
        elif j == 2:
            p2_ref[0, :, cols] = value.astype(p2_ref.dtype)
        else:
            p3_ref[0, :, cols] = value

    def early_emit(kind, j, lanes, value):
        if kind == "dq":
            store_dq(j, lanes, value)
            return
        cols = pl.ds(lanes, HEAD)
        zero = jnp.zeros_like(value)
        if j == 0:
            a_e[1, :, cols] = value.astype(a_e.dtype)
        elif j == 1:
            merged = value + jnp.where(at_top, kept[0, :, cols], zero)
            a_e[0, :, cols] = merged.astype(a_e.dtype)
        elif j == 2:
            merged = value + jnp.where(at_top, kept[1, :, cols], zero)
            p2_ref[0, :, cols] = merged.astype(p2_ref.dtype)
        else:
            merged = (
                value
                + jnp.where(at_top, kept[2, :, cols], zero)
                + jnp.where(below_top, kept[0, :, cols], zero)
            )
            p3_ref[0, :, cols] = merged

    @pl.when(step == 0)
    def _():
        window_half(1, late_slot, lo_ref, q_ref, do_ref, groups, group_size, late_emit)

    @pl.when(step == 1)
    def _():
        window_half(0, early_slot, lo_ref, q_ref, do_ref, groups, group_size, early_emit)


def window_grads(flags, lo, q, do, kv, e1, e2, l1, l2, turn):
    halves, half_rows, width = q.shape
    kv2 = kv.shape[2]
    groups = kv2 // (2 * HEAD)
    group_size = width // (groups * HEAD)
    kernel = functools.partial(window_kernel, groups=groups, group_size=group_size)
    q_spec = pl.BlockSpec((1, half_rows, width), lambda s: (1 - s, 0, 0))
    lo_spec = pl.BlockSpec((1, half_rows, 1), lambda s: (1 - s, 0, 0))
    part_spec = pl.BlockSpec((1, half_rows, kv2), lambda s: (1 - s, 0, 0))
    pair_spec = pl.BlockSpec((2, half_rows, kv2), lambda s: (0, 0, 0))
    one_spec = pl.BlockSpec((half_rows, kv2), lambda s: (0, 0))
    flops = 6 * 2 * halves * groups * group_size * half_rows * 4 * half_rows * HEAD
    pair = jax.ShapeDtypeStruct((2, half_rows, kv2), jnp.bfloat16)
    return pl.pallas_call(
        kernel,
        grid=(halves,),
        in_specs=[
            pl.BlockSpec(memory_space=pltpu.SMEM),
            lo_spec,
            q_spec,
            q_spec,
            pair_spec,
            one_spec,
            pair_spec,
            one_spec,
            pair_spec,
            one_spec,
        ],
        out_specs=[q_spec, pair_spec, pair_spec, part_spec, part_spec],
        out_shape=[
            jax.ShapeDtypeStruct(q.shape, jnp.bfloat16),
            pair,
            pair,
            jax.ShapeDtypeStruct((halves, half_rows, kv2), jnp.bfloat16),
            jax.ShapeDtypeStruct((halves, half_rows, kv2), jnp.float32),
        ],
        scratch_shapes=[pltpu.VMEM((3, half_rows, kv2), jnp.float32)],
        cost_estimate=pl.CostEstimate(
            flops=flops,
            transcendentals=halves * groups * group_size * half_rows * 4 * half_rows,
            bytes_accessed=4 * q.size + 10 * kv.size,
        ),
    )(flags, lo, q, do, kv, e1, e2, l1, l2, turn)


def on_device(query, keys, values, grad_out, lengths):
    n = lax.axis_size(AXIS)
    me = lax.axis_index(AXIS)
    half_rows = query.shape[2]
    kv_width = keys.shape[3]
    q = query[0]
    do = grad_out[0]
    kv = jnp.concatenate([keys[0], values[0]], axis=2)
    early, late = kv[0], kv[1]
    at_top = me == n - 1
    below_top = me == n - 2

    e1 = shifted(early, 1)
    l1 = shifted(late, -1)
    turn = lax.ppermute(early, AXIS, [(n - 1, n - 2)])
    e2 = shifted(jnp.stack([early, e1]), 2)
    l2 = shifted(jnp.stack([late, jnp.where(at_top, early, l1)]), -2)

    doc_ends = jnp.cumsum(lengths)
    block_ids = jnp.stack([me, 2 * n - 1 - me])
    query_pos = block_ids[:, None] * half_rows + jnp.arange(half_rows, dtype=jnp.int32)[None, :]
    ends = doc_ends[None, None, :]
    doc_start = jnp.max(jnp.where(ends <= query_pos[:, :, None], ends, 0), axis=2)
    lo = (doc_start - (block_ids[:, None] - REACH) * half_rows).astype(jnp.int32)[:, :, None]
    flags = jnp.stack([at_top, below_top]).astype(jnp.int32)

    dq, a_e, a_l, p2, p3 = window_grads(flags, lo, q, do, kv, e1, e2, l1, l2, turn)

    zero = jnp.zeros_like(p3[0])
    link = jnp.bfloat16
    a_e = shifted(a_e, -2).astype(jnp.float32)
    back = lax.ppermute(a_l[0], AXIS, [(n - 2, n - 1)]).astype(jnp.float32)
    a_l = shifted(a_l, 2).astype(jnp.float32)
    b_e = shifted((p2[0].astype(jnp.float32) + a_e[1]).astype(link), -1).astype(jnp.float32)
    b_l = shifted((p2[1].astype(jnp.float32) + a_l[1]).astype(link), 1).astype(jnp.float32)
    final_early = p3[0] + a_e[0] + b_e + jnp.where(at_top, a_l[1] + back, zero)
    final_late = p3[1] + a_l[0] + b_l
    final = jnp.stack([final_early, final_late])
    grad_keys = final[:, :, :kv_width].astype(jnp.bfloat16).reshape(keys.shape)
    grad_values = final[:, :, kv_width:].astype(jnp.bfloat16).reshape(values.shape)
    return (dq.reshape(query.shape), grad_keys, grad_values)


def solution(mesh):
    spec = P(AXIS, None, None, None)
    return jax.shard_map(
        on_device,
        mesh=mesh,
        in_specs=(spec, spec, spec, spec, P()),
        out_specs=(spec, spec, spec),
        check_vma=False,
    )
```

time: 95.8 us -> 82.2 us (0.86)
  waiting for transfers between devices: 30.5 us -> 20.6 us
  starting transfers between devices: 44.5 us -> 41.3 us
  other arithmetic: 7.01 us -> 4.2 us
  local copies, waits for them, and re-layouts: 2.79 us -> 4.59 us
    ppermute x8, waiting for transfers between devices: 30.5 us -> 20.6 us  [shifted(): return lax.ppermute(value, AXIS, pairs)]
    another operation x11 -> x5, other arithmetic: 3.78 us -> 0.47 us  [the longest x4 2.23 us: on_device(): wins = [jnp.stack([a, b]) for a, b in zip(early_slots, late_slots)]]
    ppermute x8, starting transfers between devices: 43.2 us -> 39.9 us  [shifted(): return lax.ppermute(value, AXIS, pairs)]
    unnamed x14 -> x20, local copies, waits for them, and re-layouts: 0.7 us -> 2.65 us
    slice x3 -> x1, local copies, waits for them, and re-layouts: 1.13 us -> 0.07 us  [the longest x1 1.02 us: on_device(): p2e = p2[0] + jnp.where(at_top, p1[1], zero)]
  transfers between devices with their start and end apart: 10 -> 10, of which waited for: 8 -> 6; matrix products, arithmetic and copies ran while one was open for 4% -> 5% of each run, Pallas kernels for 0% -> 0%
where the time goes in v5:
time: 82.2 us; the launch traced here: 81.8 us
  starting transfers between devices  41.3 us (50%)
  waiting for transfers between devices  20.6 us (25%)
  Pallas kernels  10.1 us (12%)
  local copies, waits for them, and re-layouts  4.59 us (6%)
  other arithmetic  4.2 us (5%)
  between operations  0.87 us (1%)
    ppermute x8, starting transfers between devices, shifted(): return lax.ppermute(value, AXIS, pairs)  39.9 us
    ppermute x8, waiting for transfers between devices, shifted(): return lax.ppermute(value, AXIS, pairs)  20.6 us
    pallas_call x1, Pallas kernels, window_grads(): pl.pallas_call(kernel, grid=(halves,), in_specs=[pl.BlockSpec(memory_spac...  10.1 us
    unnamed x20, local copies, waits for them, and re-layouts  2.65 us
  transfers between devices with their start and end apart: 10, of which 6 were waited for; matrix products, arithmetic and copies ran while one was open for 5% of the time, Pallas kernels for 0%

profile of v5, /device:TPU:6, one launch (start us, length us, event | category | flops | bytes accessed | tf_op | source)
XLA Modules:
  0.0 81.8 jit_solution(5765511284863815529)
XLA Ops:
  0.7 0.9 %fusion.11 = bf16[1,64,1024]{2,1,0:T(8,128)(2,1)S(1)} fusion(bf16[2,64,512]{2,1,0:T(8,128)(2,1)} %bitcast.57, bf16[2,64,512]{2,1,0:T(8,128)(2,1)} %bitcast.54), kind=kLoop, calls=%fused_computation.25 | loop fusion | flops 262144 | bytes 393216 | tf_op jit(solution)/shard_map/concatenate | solution.py:194
  1.6 13.6 %collective-permute-start.2 = (bf16[64,1024]{1,0:T(8,128)(2,1)S(1)}, bf16[64,1024]{1,0:T(8,128)(2,1)S(1)}, u32[]{:S(2)}, u32[]{:S(2)}) collective-permute-start(bf16[64,1024]{1,0:T(8,128)(2,1)S(1)} %bitcast.60), channel_id=1, source_target_pairs={{1,0},{2,1},{3,2},{4,3},{5,4},{6,5},{7,6},{8,7},{9,8},{10,9},{11,1... | collective-permute-start | bytes 393224 | tf_op jit(solution)/shard_map/ppermute | solution.py:19
  15.2 0.7 copy-done.6
  15.8 0.3 reduce-window.9
  16.2 0.1 slice_reduce_fusion
  16.6 0.2 select_reduce_fusion
  16.8 2.1 %collective-permute-done.2.l1 = bf16[64,1024]{1,0:T(8,128)(2,1)S(1)} collective-permute-done((bf16[64,1024]{1,0:T(8,128)(2,1)S(1)}, bf16[64,1024]{1,0:T(8,128)(2,1)S(1)}, u32[]{:S(2)}, u32[]{:S(2)}) %collective-permute-start.2) | collective-permute-done | bytes 131104 | tf_op jit(solution)/shard_map/ppermute | solution.py:19
  19.0 0.6 copy-done.4
  19.6 1.9 %collective-permute-start = (bf16[64,1024]{1,0:T(8,128)(2,1)S(1)}, bf16[64,1024]{1,0:T(8,128)(2,1)S(1)}, u32[]{:S(2)}, u32[]{:S(2)}) collective-permute-start(bf16[64,1024]{1,0:T(8,128)(2,1)S(1)} %bitcast.61), channel_id=1, source_target_pairs={{0,1},{1,2},{2,3},{3,4},{4,5},{5,6},{6,7},{7,8},{8,9},{9,10},{10,1... | collective-permute-start | bytes 393224 | tf_op jit(solution)/shard_map/ppermute | solution.py:19
  21.6 0.1 copy.11
  21.7 8.6 %collective-permute-start.3 = (bf16[2,64,1024]{2,1,0:T(8,128)(2,1)S(1)}, bf16[2,64,1024]{2,1,0:T(8,128)(2,1)S(1)}, u32[]{:S(2)}, u32[]{:S(2)}) collective-permute-start(bf16[2,64,1024]{2,1,0:T(8,128)(2,1)S(1)} %pad_maximum_fusion.2), channel_id=1, source_target_pairs={{2,0},{3,1},{4,2},{5,3},{6,4},{7,5},{8,6},{9,7},{10,8},{11,9},{12,... | collective-permute-start | bytes 786440 | tf_op jit(solution)/shard_map/ppermute | solution.py:19
  30.3 1.4 %collective-permute-done.e1 = bf16[64,1024]{1,0:T(8,128)(2,1)S(1)} collective-permute-done((bf16[64,1024]{1,0:T(8,128)(2,1)S(1)}, bf16[64,1024]{1,0:T(8,128)(2,1)S(1)}, u32[]{:S(2)}, u32[]{:S(2)}) %collective-permute-start) | collective-permute-done | bytes 131104 | tf_op jit(solution)/shard_map/ppermute | solution.py:19
  31.8 0.6 copy-done.5
  32.4 1.9 %collective-permute-start.1 = (bf16[2,64,1024]{2,1,0:T(8,128)(2,1)S(1)}, bf16[2,64,1024]{2,1,0:T(8,128)(2,1)S(1)}, u32[]{:S(2)}, u32[]{:S(2)}) collective-permute-start(bf16[2,64,1024]{2,1,0:T(8,128)(2,1)S(1)} %pad_maximum_fusion.1), channel_id=1, source_target_pairs={{0,2},{1,3},{2,4},{3,5},{4,6},{5,7},{6,8},{7,9},{8,10},{9,11},{10,... | collective-permute-start | bytes 786440 | tf_op jit(solution)/shard_map/ppermute | solution.py:19
  34.3 0.7 broadcast_subtract_fusion.lo_ref
  35.0 0.7 collective-permute-start.4
  35.7 0.6 add_convert_fusion.flags
  36.3 0.7 pad_maximum_fusion.kv
  37.0 7.2 %collective-permute-done.1.e2 = bf16[2,64,1024]{2,1,0:T(8,128)(2,1)S(1)} collective-permute-done((bf16[2,64,1024]{2,1,0:T(8,128)(2,1)S(1)}, bf16[2,64,1024]{2,1,0:T(8,128)(2,1)S(1)}, u32[]{:S(2)}, u32[]{:S(2)}) %collective-permute-start.1) | collective-permute-done | bytes 262176 | tf_op jit(solution)/shard_map/ppermute | solution.py:19
  44.2 0.7 copy-done.8
  45.0 10.1 %shard_map.76 = (bf16[2,64,4096]{2,1,0:T(8,128)(2,1)}, bf16[2,64,1024]{2,1,0:T(8,128)(2,1)}, bf16[2,64,1024]{2,1,0:T(8,128)(2,1)}, bf16[2,64,1024]{2,1,0:T(8,128)(2,1)}, f32[2,64,1024]{2,1,0:T(8,128)}) custom-call(s32[2]{0:T(128)} %add_convert_fusion.flags, s32[2,64,1]{2,1,0:T(8,128)} %broadcast_subtract_fusion.lo_ref, bf16[2,64,4096]{2,1,0:T(8,128)(2,1)} %bitcast.66, ...), custom_call_target="tpu_custom_call" | custom-call | flops 1610612736 | bytes 3407872 | tf_op jit(solution)/shard_map/pallas_call | solution.py:155
  55.1 1.9 %collective-permute-start.5 = (bf16[2,64,1024]{2,1,0:T(8,128)(2,1)}, bf16[2,64,1024]{2,1,0:T(8,128)(2,1)S(1)}, u32[]{:S(2)}, u32[]{:S(2)}) collective-permute-start(bf16[2,64,1024]{2,1,0:T(8,128)(2,1)} %get-tuple-element.10), channel_id=1, source_target_pairs={{2,0},{3,1},{4,2},{5,3},{6,4},{7,5},{8,6},{9,7},{10,8},{11,9},{12,... | collective-permute-start | bytes 786440 | tf_op jit(solution)/shard_map/ppermute | solution.py:19
  57.0 3.9 %collective-permute-start.7 = (bf16[2,64,1024]{2,1,0:T(8,128)(2,1)}, bf16[2,64,1024]{2,1,0:T(8,128)(2,1)S(1)}, u32[]{:S(2)}, u32[]{:S(2)}) collective-permute-start(bf16[2,64,1024]{2,1,0:T(8,128)(2,1)} %get-tuple-element.12), channel_id=1, source_target_pairs={{0,2},{1,3},{2,4},{3,5},{4,6},{5,7},{6,8},{7,9},{8,10},{9,11},{10,... | collective-permute-start | bytes 786440 | tf_op jit(solution)/shard_map/ppermute | solution.py:19
  60.9 0.9 %slice_bitcast_fusion.3 = bf16[64,1024]{1,0:T(8,128)(2,1)S(1)} fusion(bf16[2,64,1024]{2,1,0:T(8,128)(2,1)} %get-tuple-element.12), kind=kLoop, calls=%fused_computation.28 | loop fusion | bytes 262144 | tf_op jit(solution)/shard_map/squeeze | solution.py:218
  61.9 0.8 collective-permute-start.8
  62.7 0.9 %collective-permute-done.5 = bf16[2,64,1024]{2,1,0:T(8,128)(2,1)S(1)} collective-permute-done((bf16[2,64,1024]{2,1,0:T(8,128)(2,1)}, bf16[2,64,1024]{2,1,0:T(8,128)(2,1)S(1)}, u32[]{:S(2)}, u32[]{:S(2)}) %collective-permute-start.5) | collective-permute-done | bytes 262176 | tf_op jit(solution)/shard_map/ppermute | solution.py:19
  63.7 4.4 %collective-permute-start.6 = (bf16[64,1024]{1,0:T(8,128)(2,1)S(1)}, bf16[64,1024]{1,0:T(8,128)(2,1)S(1)}, u32[]{:S(2)}, u32[]{:S(2)}) collective-permute-start(bf16[64,1024]{1,0:T(8,128)(2,1)S(1)} %fusion.9), channel_id=1, source_target_pairs={{1,0},{2,1},{3,2},{4,3},{5,4},{6,5},{7,6},{8,7},{9,8},{10,9},{11,1... | collective-permute-start | bytes 393224 | tf_op jit(solution)/shard_map/ppermute | solution.py:19
  68.1 2.2 %collective-permute-done.7 = bf16[2,64,1024]{2,1,0:T(8,128)(2,1)S(1)} collective-permute-done((bf16[2,64,1024]{2,1,0:T(8,128)(2,1)}, bf16[2,64,1024]{2,1,0:T(8,128)(2,1)S(1)}, u32[]{:S(2)}, u32[]{:S(2)}) %collective-permute-start.7) | collective-permute-done | bytes 262176 | tf_op jit(solution)/shard_map/ppermute | solution.py:19
  70.4 3.7 %collective-permute-start.9 = (bf16[64,1024]{1,0:T(8,128)(2,1)S(1)}, bf16[64,1024]{1,0:T(8,128)(2,1)S(1)}, u32[]{:S(2)}, u32[]{:S(2)}) collective-permute-start(bf16[64,1024]{1,0:T(8,128)(2,1)S(1)} %fusion.8), channel_id=1, source_target_pairs={{0,1},{1,2},{2,3},{3,4},{4,5},{5,6},{6,7},{7,8},{8,9},{9,10},{10,1... | collective-permute-start | bytes 393224 | tf_op jit(solution)/shard_map/ppermute | solution.py:19
  74.0 6.8 %collective-permute-done.9 = bf16[64,1024]{1,0:T(8,128)(2,1)S(1)} collective-permute-done((bf16[64,1024]{1,0:T(8,128)(2,1)S(1)}, bf16[64,1024]{1,0:T(8,128)(2,1)S(1)}, u32[]{:S(2)}, u32[]{:S(2)}) %collective-permute-start.9) | collective-permute-done | bytes 131104 | tf_op jit(solution)/shard_map/ppermute | solution.py:19
  80.9 0.1 fusion.7
  81.0 0.7 slice_bitcast_fusion.1
  (34 shorter events, 0.7 us)
Async XLA Ops:
  0.6 18.3 %copy-start = (bf16[1,2,64,512]{3,2,1,0:T(8,128)(2,1)S(1)}, bf16[1,2,64,512]{3,2,1,0:T(8,128)(2,1)}, u32[]{:S(2)}) copy-start(bf16[1,2,64,512]{3,2,1,0:T(8,128)(2,1)} %param.7) | copy-start | bytes 393220
  0.6 18.3 %copy-start.1 = (bf16[1,2,64,512]{3,2,1,0:T(8,128)(2,1)S(1)}, bf16[1,2,64,512]{3,2,1,0:T(8,128)(2,1)}, u32[]{:S(2)}) copy-start(bf16[1,2,64,512]{3,2,1,0:T(8,128)(2,1)} %param.6) | copy-start | bytes 393220
  1.6 17.3 %collective-permute-start.2 = (bf16[64,1024]{1,0:T(8,128)(2,1)S(1)}, bf16[64,1024]{1,0:T(8,128)(2,1)S(1)}, u32[]{:S(2)}, u32[]{:S(2)}) collective-permute-start(bf16[64,1024]{1,0:T(8,128)(2,1)S(1)} %bitcast.60), channel_id=1, source_target_pairs={{1,0},{2,1},{3,2},{4,3},{5,4},{6,5},{7,6},{8,7},{9,8},{10,9},{11,1... | collective-permute-start | bytes 393224 | tf_op jit(solution)/shard_map/ppermute | solution.py:19
  15.1 0.7 copy-start.6
  18.9 0.7 copy-start.4
  19.6 12.2 %collective-permute-start = (bf16[64,1024]{1,0:T(8,128)(2,1)S(1)}, bf16[64,1024]{1,0:T(8,128)(2,1)S(1)}, u32[]{:S(2)}, u32[]{:S(2)}) collective-permute-start(bf16[64,1024]{1,0:T(8,128)(2,1)S(1)} %bitcast.61), channel_id=1, source_target_pairs={{0,1},{1,2},{2,3},{3,4},{4,5},{5,6},{6,7},{7,8},{8,9},{9,10},{10,1... | collective-permute-start | bytes 393224 | tf_op jit(solution)/shard_map/ppermute | solution.py:19
  21.7 15.3 %collective-permute-start.3 = (bf16[2,64,1024]{2,1,0:T(8,128)(2,1)S(1)}, bf16[2,64,1024]{2,1,0:T(8,128)(2,1)S(1)}, u32[]{:S(2)}, u32[]{:S(2)}) collective-permute-start(bf16[2,64,1024]{2,1,0:T(8,128)(2,1)S(1)} %pad_maximum_fusion.2), channel_id=1, source_target_pairs={{2,0},{3,1},{4,2},{5,3},{6,4},{7,5},{8,6},{9,7},{10,8},{11,9},{12,... | collective-permute-start | bytes 786440 | tf_op jit(solution)/shard_map/ppermute | solution.py:19
  31.7 0.7 copy-start.5
  32.4 11.9 %collective-permute-start.1 = (bf16[2,64,1024]{2,1,0:T(8,128)(2,1)S(1)}, bf16[2,64,1024]{2,1,0:T(8,128)(2,1)S(1)}, u32[]{:S(2)}, u32[]{:S(2)}) collective-permute-start(bf16[2,64,1024]{2,1,0:T(8,128)(2,1)S(1)} %pad_maximum_fusion.1), channel_id=1, source_target_pairs={{0,2},{1,3},{2,4},{3,5},{4,6},{5,7},{6,8},{7,9},{8,10},{9,11},{10,... | collective-permute-start | bytes 786440 | tf_op jit(solution)/shard_map/ppermute | solution.py:19
  35.0 2.0 %collective-permute-start.4 = (bf16[64,1024]{1,0:T(8,128)(2,1)S(1)}, bf16[64,1024]{1,0:T(8,128)(2,1)S(1)}, u32[]{:S(2)}, u32[]{:S(2)}) collective-permute-start(bf16[64,1024]{1,0:T(8,128)(2,1)S(1)} %bitcast.62), channel_id=1, source_target_pairs={{511,510}} | collective-permute-start | bytes 393224 | tf_op jit(solution)/shard_map/ppermute | solution.py:201
  37.0 7.2 %copy-start.9 = (bf16[64,1024]{1,0:T(8,128)(2,1)}, bf16[64,1024]{1,0:T(8,128)(2,1)S(1)}, u32[]{:S(2)}) copy-start(bf16[64,1024]{1,0:T(8,128)(2,1)S(1)} %collective-permute-done.4.turn) | copy-start | bytes 393220
  37.0 7.2 %copy-start.7 = (bf16[2,64,1024]{2,1,0:T(8,128)(2,1)}, bf16[2,64,1024]{2,1,0:T(8,128)(2,1)S(1)}, u32[]{:S(2)}) copy-start(bf16[2,64,1024]{2,1,0:T(8,128)(2,1)S(1)} %collective-permute-done.3.l2) | copy-start | bytes 786436
  44.2 0.7 copy-start.8
  55.1 8.5 %collective-permute-start.5 = (bf16[2,64,1024]{2,1,0:T(8,128)(2,1)}, bf16[2,64,1024]{2,1,0:T(8,128)(2,1)S(1)}, u32[]{:S(2)}, u32[]{:S(2)}) collective-permute-start(bf16[2,64,1024]{2,1,0:T(8,128)(2,1)} %get-tuple-element.10), channel_id=1, source_target_pairs={{2,0},{3,1},{4,2},{5,3},{6,4},{7,5},{8,6},{9,7},{10,8},{11,9},{12,... | collective-permute-start | bytes 786440 | tf_op jit(solution)/shard_map/ppermute | solution.py:19
  57.0 13.3 %collective-permute-start.7 = (bf16[2,64,1024]{2,1,0:T(8,128)(2,1)}, bf16[2,64,1024]{2,1,0:T(8,128)(2,1)S(1)}, u32[]{:S(2)}, u32[]{:S(2)}) collective-permute-start(bf16[2,64,1024]{2,1,0:T(8,128)(2,1)} %get-tuple-element.12), channel_id=1, source_target_pairs={{0,2},{1,3},{2,4},{3,5},{4,6},{5,7},{6,8},{7,9},{8,10},{9,11},{10,... | collective-permute-start | bytes 786440 | tf_op jit(solution)/shard_map/ppermute | solution.py:19
  61.9 1.7 %copy-start.3 = (bf16[2,64,1024]{2,1,0:T(8,128)(2,1)S(1)}, bf16[2,64,1024]{2,1,0:T(8,128)(2,1)}, u32[]{:S(2)}) copy-start(bf16[2,64,1024]{2,1,0:T(8,128)(2,1)} %get-tuple-element.11) | copy-start | bytes 786436
  61.9 12.2 %collective-permute-start.8 = (bf16[64,1024]{1,0:T(8,128)(2,1)S(1)}, bf16[64,1024]{1,0:T(8,128)(2,1)S(1)}, u32[]{:S(2)}, u32[]{:S(2)}) collective-permute-start(bf16[64,1024]{1,0:T(8,128)(2,1)S(1)} %slice_bitcast_fusion.3), channel_id=1, source_target_pairs={{510,511}} | collective-permute-start | bytes 393224 | tf_op jit(solution)/shard_map/ppermute | solution.py:218
  63.6 17.2 %copy-start.2 = (f32[2,64,1024]{2,1,0:T(8,128)S(1)}, f32[2,64,1024]{2,1,0:T(8,128)}, u32[]{:S(2)}) copy-start(f32[2,64,1024]{2,1,0:T(8,128)} %get-tuple-element.9) | copy-start | bytes 1572868
  63.7 10.4 %collective-permute-start.6 = (bf16[64,1024]{1,0:T(8,128)(2,1)S(1)}, bf16[64,1024]{1,0:T(8,128)(2,1)S(1)}, u32[]{:S(2)}, u32[]{:S(2)}) collective-permute-start(bf16[64,1024]{1,0:T(8,128)(2,1)S(1)} %fusion.9), channel_id=1, source_target_pairs={{1,0},{2,1},{3,2},{4,3},{5,4},{6,5},{7,6},{8,7},{9,8},{10,9},{11,1... | collective-permute-start | bytes 393224 | tf_op jit(solution)/shard_map/ppermute | solution.py:19
  70.4 10.5 %collective-permute-start.9 = (bf16[64,1024]{1,0:T(8,128)(2,1)S(1)}, bf16[64,1024]{1,0:T(8,128)(2,1)S(1)}, u32[]{:S(2)}, u32[]{:S(2)}) collective-permute-start(bf16[64,1024]{1,0:T(8,128)(2,1)S(1)} %fusion.8), channel_id=1, source_target_pairs={{0,1},{1,2},{2,3},{3,4},{4,5},{5,6},{6,7},{7,8},{8,9},{9,10},{10,1... | collective-permute-start | bytes 393224 | tf_op jit(solution)/shard_map/ppermute | solution.py:19

commit v6 on v5

--- a/solution.py
+++ b/solution.py
@@ -62,41 +62,29 @@
             emit("part", j, kv_width + g * HEAD, dv[j * half_rows:(j + 1) * half_rows])
 
 
-def window_kernel(
-    flags, lo_ref, q_ref, do_ref, kv, e1, e2, l1, l2, turn,
-    dq_ref, a_e, a_l, p2_ref, p3_ref, kept, *, groups, group_size
+def late_kernel(
+    flags, lo_ref, q_ref, do_ref, kv, l1, l2, turn2, turn3,
+    dq_ref, a_l, p2_ref, p3_ref, kept, *, groups, group_size
 ):
-    step = pl.program_id(0)
     at_top = flags[0] != 0
     below_top = flags[1] != 0
 
-    def tile(ref, lanes, *lead):
-        return ref[lead + (slice(None), pl.ds(lanes, HEAD))]
-
-    def store_dq(h, lanes, value):
-        dq_ref[0, :, pl.ds(lanes, HEAD)] = value
-
-    def late_slot(j, lanes):
+    def slot(j, lanes):
+        cols = pl.ds(lanes, HEAD)
         if j == 0:
-            regular = jnp.where(below_top, tile(kv, lanes, 0), tile(l2, lanes, 1))
-            return jnp.where(at_top, tile(e2, lanes, 0), regular)
+            regular = jnp.where(below_top, kv[0, :, cols], l2[1, :, cols])
+            return jnp.where(at_top, turn3[:, cols], regular)
         if j == 1:
-            regular = jnp.where(below_top, tile(turn, lanes), tile(l2, lanes, 0))
-            return jnp.where(at_top, tile(e1, lanes), regular)
+            return jnp.where(at_top | below_top, turn2[:, cols], l2[0, :, cols])
         if j == 2:
-            return jnp.where(at_top, tile(kv, lanes, 0), tile(l1, lanes))
-        return tile(kv, lanes, 1)
-
-    def early_slot(j, lanes):
-        return (
-            tile(e2, lanes, 1), tile(e2, lanes, 0), tile(e1, lanes), tile(kv, lanes, 0)
-        )[j]
-
-    def late_emit(kind, j, lanes, value):
+            return jnp.where(at_top, kv[0, :, cols], l1[:, cols])
+        return kv[1, :, cols]
+
+    def emit(kind, j, lanes, value):
+        cols = pl.ds(lanes, HEAD)
         if kind == "dq":
-            store_dq(j, lanes, value)
+            dq_ref[0, :, cols] = value
             return
-        cols = pl.ds(lanes, HEAD)
         if j < 3:
             kept[j, :, cols] = value
         if j == 0:
@@ -108,11 +96,26 @@
         else:
             p3_ref[0, :, cols] = value
 
-    def early_emit(kind, j, lanes, value):
+    window_half(1, slot, lo_ref, q_ref, do_ref, groups, group_size, emit)
+
+
+def early_kernel(
+    flags, lo_ref, q_ref, do_ref, kv, e1, e2, kept, dq_in, p2_in, p3_in,
+    dq_ref, a_e, p2_ref, p3_ref, *, groups, group_size
+):
+    del dq_in, p2_in, p3_in
+    at_top = flags[0] != 0
+    below_top = flags[1] != 0
+
+    def slot(j, lanes):
+        cols = pl.ds(lanes, HEAD)
+        return (e2[1, :, cols], e2[0, :, cols], e1[:, cols], kv[0, :, cols])[j]
+
+    def emit(kind, j, lanes, value):
+        cols = pl.ds(lanes, HEAD)
         if kind == "dq":
-            store_dq(j, lanes, value)
+            dq_ref[0, :, cols] = value
             return
-        cols = pl.ds(lanes, HEAD)
         zero = jnp.zeros_like(value)
         if j == 0:
             a_e[1, :, cols] = value.astype(a_e.dtype)
@@ -130,58 +133,64 @@
             )
             p3_ref[0, :, cols] = merged
 
-    @pl.when(step == 0)
-    def _():
-        window_half(1, late_slot, lo_ref, q_ref, do_ref, groups, group_size, late_emit)
-
-    @pl.when(step == 1)
-    def _():
-        window_half(0, early_slot, lo_ref, q_ref, do_ref, groups, group_size, early_emit)
-
-
-def window_grads(flags, lo, q, do, kv, e1, e2, l1, l2, turn):
+    window_half(0, slot, lo_ref, q_ref, do_ref, groups, group_size, emit)
+
+
+def window_grads(flags, lo, q, do, kv, e1, e2, l1, l2, turn2, turn3):
     halves, half_rows, width = q.shape
     kv2 = kv.shape[2]
     groups = kv2 // (2 * HEAD)
     group_size = width // (groups * HEAD)
-    kernel = functools.partial(window_kernel, groups=groups, group_size=group_size)
-    q_spec = pl.BlockSpec((1, half_rows, width), lambda s: (1 - s, 0, 0))
-    lo_spec = pl.BlockSpec((1, half_rows, 1), lambda s: (1 - s, 0, 0))
-    part_spec = pl.BlockSpec((1, half_rows, kv2), lambda s: (1 - s, 0, 0))
+    flops = 6 * 2 * groups * group_size * half_rows * 4 * half_rows * HEAD
+    cost = pl.CostEstimate(
+        flops=flops,
+        transcendentals=groups * group_size * half_rows * 4 * half_rows,
+        bytes_accessed=2 * q.size + 6 * kv.size,
+    )
+
+    def half_specs(half):
+        q_spec = pl.BlockSpec((1, half_rows, width), lambda s: (half, 0, 0))
+        lo_spec = pl.BlockSpec((1, half_rows, 1), lambda s: (half, 0, 0))
+        part_spec = pl.BlockSpec((1, half_rows, kv2), lambda s: (half, 0, 0))
+        return q_spec, lo_spec, part_spec
+
     pair_spec = pl.BlockSpec((2, half_rows, kv2), lambda s: (0, 0, 0))
     one_spec = pl.BlockSpec((half_rows, kv2), lambda s: (0, 0))
-    flops = 6 * 2 * halves * groups * group_size * half_rows * 4 * half_rows * HEAD
+    kept_spec = pl.BlockSpec((3, half_rows, kv2), lambda s: (0, 0, 0))
+    smem = pl.BlockSpec(memory_space=pltpu.SMEM)
+    anywhere = pl.BlockSpec(memory_space=pl.ANY)
     pair = jax.ShapeDtypeStruct((2, half_rows, kv2), jnp.bfloat16)
-    return pl.pallas_call(
-        kernel,
-        grid=(halves,),
+    dq_shape = jax.ShapeDtypeStruct(q.shape, jnp.bfloat16)
+    p2_shape = jax.ShapeDtypeStruct((halves, half_rows, kv2), jnp.bfloat16)
+    p3_shape = jax.ShapeDtypeStruct((halves, half_rows, kv2), jnp.float32)
+
+    q_spec, lo_spec, part_spec = half_specs(1)
+    dq, a_l, p2, p3, kept = pl.pallas_call(
+        functools.partial(late_kernel, groups=groups, group_size=group_size),
+        grid=(1,),
+        in_specs=[smem, lo_spec, q_spec, q_spec, pair_spec, one_spec, pair_spec, one_spec, one_spec],
+        out_specs=[q_spec, pair_spec, part_spec, part_spec, kept_spec],
+        out_shape=[
+            dq_shape, pair, p2_shape, p3_shape,
+            jax.ShapeDtypeStruct((3, half_rows, kv2), jnp.float32),
+        ],
+        cost_estimate=cost,
+    )(flags, lo, q, do, kv, l1, l2, turn2, turn3)
+
+    q_spec, lo_spec, part_spec = half_specs(0)
+    dq, a_e, p2, p3 = pl.pallas_call(
+        functools.partial(early_kernel, groups=groups, group_size=group_size),
+        grid=(1,),
         in_specs=[
-            pl.BlockSpec(memory_space=pltpu.SMEM),
-            lo_spec,
-            q_spec,
-            q_spec,
-            pair_spec,
-            one_spec,
-            pair_spec,
-            one_spec,
-            pair_spec,
-            one_spec,
+            smem, lo_spec, q_spec, q_spec, pair_spec, one_spec, pair_spec, kept_spec,
+            anywhere, anywhere, anywhere,
         ],
-        out_specs=[q_spec, pair_spec, pair_spec, part_spec, part_spec],
-        out_shape=[
-            jax.ShapeDtypeStruct(q.shape, jnp.bfloat16),
-            pair,
-            pair,
-            jax.ShapeDtypeStruct((halves, half_rows, kv2), jnp.bfloat16),
-            jax.ShapeDtypeStruct((halves, half_rows, kv2), jnp.float32),
-        ],
-        scratch_shapes=[pltpu.VMEM((3, half_rows, kv2), jnp.float32)],
-        cost_estimate=pl.CostEstimate(
-            flops=flops,
-            transcendentals=halves * groups * group_size * half_rows * 4 * half_rows,
-            bytes_accessed=4 * q.size + 10 * kv.size,
-        ),
-    )(flags, lo, q, do, kv, e1, e2, l1, l2, turn)
+        out_specs=[q_spec, pair_spec, part_spec, part_spec],
+        out_shape=[dq_shape, pair, p2_shape, p3_shape],
+        input_output_aliases={8: 0, 9: 2, 10: 3},
+        cost_estimate=cost,
+    )(flags, lo, q, do, kv, e1, e2, kept, dq, p2, p3)
+    return dq, a_e, a_l, p2, p3
 
 
 def on_device(query, keys, values, grad_out, lengths):
@@ -198,7 +207,8 @@
 
     e1 = shifted(early, 1)
     l1 = shifted(late, -1)
-    turn = lax.ppermute(early, AXIS, [(n - 1, n - 2)])
+    turn2 = lax.ppermute(early, AXIS, [(n - 1, n - 2), (n - 2, n - 1)])
+    turn3 = lax.ppermute(early, AXIS, [(n - 3, n - 1)])
     e2 = shifted(jnp.stack([early, e1]), 2)
     l2 = shifted(jnp.stack([late, jnp.where(at_top, early, l1)]), -2)
 
@@ -210,7 +220,7 @@
     lo = (doc_start - (block_ids[:, None] - REACH) * half_rows).astype(jnp.int32)[:, :, None]
     flags = jnp.stack([at_top, below_top]).astype(jnp.int32)
 
-    dq, a_e, a_l, p2, p3 = window_grads(flags, lo, q, do, kv, e1, e2, l1, l2, turn)
+    dq, a_e, a_l, p2, p3 = window_grads(flags, lo, q, do, kv, e1, e2, l1, l2, turn2, turn3)
 
     zero = jnp.zeros_like(p3[0])
     link = jnp.bfloat16

time: 82.2 us -> 75.9 us (0.923)
  waiting for transfers between devices: 20.6 us -> 8.07 us
  starting transfers between devices: 41.3 us -> 45.3 us
  Pallas kernels: 10.1 us -> 12.3 us
    ppermute x8, waiting for transfers between devices: 20.6 us -> 8.07 us  [shifted(): return lax.ppermute(value, AXIS, pairs)]
    ppermute x8, starting transfers between devices: 39.9 us -> 43.2 us  [shifted(): return lax.ppermute(value, AXIS, pairs)]
    pallas_call x1 -> x2, Pallas kernels: 10.1 us -> 12.3 us  [the longest x1 6.19 us: window_grads(): pl.pallas_call(functools.partial(late_kernel, groups=groups, group_size=g...]
    squeeze x1, local copies, waits for them, and re-layouts: 0.92 us -> 0.01 us  [on_device(): back = lax.ppermute(a_l[0], AXIS, [(n - 2, n - 1)]).astype(jnp.float32)]
    unnamed x20 -> x24, local copies, waits for them, and re-layouts: 2.65 us -> 3.36 us
  transfers between devices with their start and end apart: 10 -> 11, of which waited for: 6 -> 5; matrix products, arithmetic and copies ran while one was open for 5% -> 4% of each run, Pallas kernels for 0% -> 16%
where the time goes in v6:
time: 75.9 us; the launch traced here: 75.2 us
  starting transfers between devices  45.3 us (60%)
  Pallas kernels  12.3 us (16%)
  waiting for transfers between devices  8.07 us (11%)
  local copies, waits for them, and re-layouts  4.38 us (6%)
  other arithmetic  4.15 us (5%)
  between operations  0.92 us (1%)
    ppermute x8, starting transfers between devices, shifted(): return lax.ppermute(value, AXIS, pairs)  43.2 us
    ppermute x8, waiting for transfers between devices, shifted(): return lax.ppermute(value, AXIS, pairs)  8.07 us
    pallas_call x1, Pallas kernels, window_grads(): pl.pallas_call(functools.partial(late_kernel, groups=groups, group_size=g...  6.19 us
    pallas_call x1, Pallas kernels, window_grads(): pl.pallas_call(functools.partial(early_kernel, groups=groups, group_size=...  6.14 us
    unnamed x24, local copies, waits for them, and re-layouts  3.36 us
    concatenate x2, other arithmetic, on_device(): kv = jnp.concatenate([keys[0], values[0]], axis=2)  1.66 us
  transfers between devices with their start and end apart: 11, of which 5 were waited for; matrix products, arithmetic and copies ran while one was open for 4% of the time, Pallas kernels for 16%

profile of v6, /device:TPU:6, one launch (start us, length us, event | category | flops | bytes accessed | tf_op | source)
XLA Modules:
  0.0 75.2 jit_solution(11529099939278738598)
XLA Ops:
  0.7 0.9 %fusion.11 = bf16[1,64,1024]{2,1,0:T(8,128)(2,1)S(1)} fusion(bf16[2,64,512]{2,1,0:T(8,128)(2,1)} %bitcast.61, bf16[2,64,512]{2,1,0:T(8,128)(2,1)} %bitcast.58), kind=kLoop, calls=%fused_computation.25 | loop fusion | flops 262144 | bytes 393216 | tf_op jit(solution)/shard_map/concatenate | solution.py:203
  1.6 13.6 %collective-permute-start.2 = (bf16[64,1024]{1,0:T(8,128)(2,1)S(1)}, bf16[64,1024]{1,0:T(8,128)(2,1)S(1)}, u32[]{:S(2)}, u32[]{:S(2)}) collective-permute-start(bf16[64,1024]{1,0:T(8,128)(2,1)S(1)} %bitcast.65), channel_id=1, source_target_pairs={{1,0},{2,1},{3,2},{4,3},{5,4},{6,5},{7,6},{8,7},{9,8},{10,9},{11,1... | collective-permute-start | bytes 393224 | tf_op jit(solution)/shard_map/ppermute | solution.py:19
  15.3 0.6 copy-done.11
  15.9 0.3 reduce-window.9
  16.3 0.1 slice_reduce_fusion
  16.5 0.2 select_reduce_fusion
  16.9 2.0 %collective-permute-done.2.l1 = bf16[64,1024]{1,0:T(8,128)(2,1)S(1)} collective-permute-done((bf16[64,1024]{1,0:T(8,128)(2,1)S(1)}, bf16[64,1024]{1,0:T(8,128)(2,1)S(1)}, u32[]{:S(2)}, u32[]{:S(2)}) %collective-permute-start.2) | collective-permute-done | bytes 131104 | tf_op jit(solution)/shard_map/ppermute | solution.py:19
  19.0 0.6 copy-done.4
  19.6 1.9 %collective-permute-start = (bf16[64,1024]{1,0:T(8,128)(2,1)S(1)}, bf16[64,1024]{1,0:T(8,128)(2,1)S(1)}, u32[]{:S(2)}, u32[]{:S(2)}) collective-permute-start(bf16[64,1024]{1,0:T(8,128)(2,1)S(1)} %bitcast.67), channel_id=1, source_target_pairs={{0,1},{1,2},{2,3},{3,4},{4,5},{5,6},{6,7},{7,8},{8,9},{9,10},{10,1... | collective-permute-start | bytes 393224 | tf_op jit(solution)/shard_map/ppermute | solution.py:19
  21.5 0.7 broadcast_subtract_fusion.lo_ref
  22.2 0.7 collective-permute-start.4
  22.8 0.7 collective-permute-start.5
  23.6 8.6 %collective-permute-start.3 = (bf16[2,64,1024]{2,1,0:T(8,128)(2,1)S(1)}, bf16[2,64,1024]{2,1,0:T(8,128)(2,1)S(1)}, u32[]{:S(2)}, u32[]{:S(2)}) collective-permute-start(bf16[2,64,1024]{2,1,0:T(8,128)(2,1)S(1)} %pad_maximum_fusion.2), channel_id=1, source_target_pairs={{2,0},{3,1},{4,2},{5,3},{6,4},{7,5},{8,6},{9,7},{10,8},{11,9},{12,... | collective-permute-start | bytes 786440 | tf_op jit(solution)/shard_map/ppermute | solution.py:19
  32.2 0.6 copy-done.5
  32.8 1.9 %collective-permute-start.1 = (bf16[2,64,1024]{2,1,0:T(8,128)(2,1)S(1)}, bf16[2,64,1024]{2,1,0:T(8,128)(2,1)S(1)}, u32[]{:S(2)}, u32[]{:S(2)}) collective-permute-start(bf16[2,64,1024]{2,1,0:T(8,128)(2,1)S(1)} %pad_maximum_fusion.1), channel_id=1, source_target_pairs={{0,2},{1,3},{2,4},{3,5},{4,6},{5,7},{6,8},{7,9},{8,10},{9,11},{10,... | collective-permute-start | bytes 786440 | tf_op jit(solution)/shard_map/ppermute | solution.py:19
  34.8 0.6 add_convert_fusion.flags
  35.3 0.7 pad_maximum_fusion.kv
  36.1 2.1 %collective-permute-done.3.l2 = bf16[2,64,1024]{2,1,0:T(8,128)(2,1)S(1)} collective-permute-done((bf16[2,64,1024]{2,1,0:T(8,128)(2,1)S(1)}, bf16[2,64,1024]{2,1,0:T(8,128)(2,1)S(1)}, u32[]{:S(2)}, u32[]{:S(2)}) %collective-permute-start.3) | collective-permute-done | bytes 262176 | tf_op jit(solution)/shard_map/ppermute | solution.py:19
  38.1 0.7 copy-done.7
  38.8 6.2 %shard_map.76 = (bf16[2,64,4096]{2,1,0:T(8,128)(2,1)}, bf16[2,64,1024]{2,1,0:T(8,128)(2,1)}, bf16[2,64,1024]{2,1,0:T(8,128)(2,1)}, f32[2,64,1024]{2,1,0:T(8,128)}, f32[3,64,1024]{2,1,0:T(8,128)}) custom-call(s32[2]{0:T(128)} %add_convert_fusion.flags, s32[2,64,1]{2,1,0:T(8,128)} %broadcast_subtract_fusion.lo_ref, bf16[2,64,4096]{2,1,0:T(8,128)(2,1)} %bitcast.54, ...), custom_call_target="tpu_custom_call" | custom-call | flops 805306368 | bytes 1835008 | tf_op jit(solution)/shard_map/pallas_call | solution.py:168
  45.0 1.9 %collective-permute-start.8 = (bf16[2,64,1024]{2,1,0:T(8,128)(2,1)}, bf16[2,64,1024]{2,1,0:T(8,128)(2,1)S(1)}, u32[]{:S(2)}, u32[]{:S(2)}) collective-permute-start(bf16[2,64,1024]{2,1,0:T(8,128)(2,1)} %get-tuple-element.20), channel_id=1, source_target_pairs={{0,2},{1,3},{2,4},{3,5},{4,6},{5,7},{6,8},{7,9},{8,10},{9,11},{10,... | collective-permute-start | bytes 786440 | tf_op jit(solution)/shard_map/ppermute | solution.py:19
  47.0 0.7 copy-done.6
  47.7 6.1 %shard_map.77 = (bf16[2,64,4096]{2,1,0:T(8,128)(2,1)}, bf16[2,64,1024]{2,1,0:T(8,128)(2,1)}, bf16[2,64,1024]{2,1,0:T(8,128)(2,1)}, f32[2,64,1024]{2,1,0:T(8,128)}) custom-call(s32[2]{0:T(128)} %add_convert_fusion.flags, s32[2,64,1]{2,1,0:T(8,128)} %broadcast_subtract_fusion.lo_ref, ...), custom_call_target="tpu_custom_call", output_to_operand_aliasing={{0}: (8, {}), {2}: (9, {}), {3}: (10, {})} | custom-call | flops 805306368 | bytes 1835008 | tf_op jit(solution)/shard_map/pallas_call | solution.py:181
  53.8 6.8 %collective-permute-start.6 = (bf16[2,64,1024]{2,1,0:T(8,128)(2,1)}, bf16[2,64,1024]{2,1,0:T(8,128)(2,1)S(1)}, u32[]{:S(2)}, u32[]{:S(2)}) collective-permute-start(bf16[2,64,1024]{2,1,0:T(8,128)(2,1)} %get-tuple-element.18), channel_id=1, source_target_pairs={{2,0},{3,1},{4,2},{5,3},{6,4},{7,5},{8,6},{9,7},{10,8},{11,9},{12,... | collective-permute-start | bytes 786440 | tf_op jit(solution)/shard_map/ppermute | solution.py:19
  60.7 0.8 %collective-permute-start.9 = (bf16[64,1024]{1,0:T(8,128)(2,1)S(1)}, bf16[64,1024]{1,0:T(8,128)(2,1)S(1)}, u32[]{:S(2)}, u32[]{:S(2)}) collective-permute-start(bf16[64,1024]{1,0:T(8,128)(2,1)S(1)} %slice_bitcast_fusion.3), channel_id=1, source_target_pairs={{510,511}} | collective-permute-start | bytes 393224 | tf_op jit(solution)/shard_map/ppermute | solution.py:228
  61.7 2.1 %collective-permute-start.10 = (bf16[64,1024]{1,0:T(8,128)(2,1)S(1)}, bf16[64,1024]{1,0:T(8,128)(2,1)S(1)}, u32[]{:S(2)}, u32[]{:S(2)}) collective-permute-start(bf16[64,1024]{1,0:T(8,128)(2,1)S(1)} %fusion.8), channel_id=1, source_target_pairs={{0,1},{1,2},{2,3},{3,4},{4,5},{5,6},{6,7},{7,8},{8,9},{9,10},{10,1... | collective-permute-start | bytes 393224 | tf_op jit(solution)/shard_map/ppermute | solution.py:19
  63.7 1.4 %collective-permute-done.6 = bf16[2,64,1024]{2,1,0:T(8,128)(2,1)S(1)} collective-permute-done((bf16[2,64,1024]{2,1,0:T(8,128)(2,1)}, bf16[2,64,1024]{2,1,0:T(8,128)(2,1)S(1)}, u32[]{:S(2)}, u32[]{:S(2)}) %collective-permute-start.6) | collective-permute-done | bytes 262176 | tf_op jit(solution)/shard_map/ppermute | solution.py:19
  65.2 6.5 %collective-permute-start.7 = (bf16[64,1024]{1,0:T(8,128)(2,1)S(1)}, bf16[64,1024]{1,0:T(8,128)(2,1)S(1)}, u32[]{:S(2)}, u32[]{:S(2)}) collective-permute-start(bf16[64,1024]{1,0:T(8,128)(2,1)S(1)} %fusion.9), channel_id=1, source_target_pairs={{1,0},{2,1},{3,2},{4,3},{5,4},{6,5},{7,6},{8,7},{9,8},{10,9},{11,1... | collective-permute-start | bytes 393224 | tf_op jit(solution)/shard_map/ppermute | solution.py:19
  71.7 1.5 %collective-permute-done.10 = bf16[64,1024]{1,0:T(8,128)(2,1)S(1)} collective-permute-done((bf16[64,1024]{1,0:T(8,128)(2,1)S(1)}, bf16[64,1024]{1,0:T(8,128)(2,1)S(1)}, u32[]{:S(2)}, u32[]{:S(2)}) %collective-permute-start.10) | collective-permute-done | bytes 131104 | tf_op jit(solution)/shard_map/ppermute | solution.py:19
  73.2 1.1 %collective-permute-done.7 = bf16[64,1024]{1,0:T(8,128)(2,1)S(1)} collective-permute-done((bf16[64,1024]{1,0:T(8,128)(2,1)S(1)}, bf16[64,1024]{1,0:T(8,128)(2,1)S(1)}, u32[]{:S(2)}, u32[]{:S(2)}) %collective-permute-start.7) | collective-permute-done | bytes 131104 | tf_op jit(solution)/shard_map/ppermute | solution.py:19
  74.3 0.1 fusion.7
  74.5 0.7 slice_bitcast_fusion.1
  (41 shorter events, 0.9 us)
Async XLA Ops:
  0.6 18.3 %copy-start.1 = (bf16[1,2,64,512]{3,2,1,0:T(8,128)(2,1)S(1)}, bf16[1,2,64,512]{3,2,1,0:T(8,128)(2,1)}, u32[]{:S(2)}) copy-start(bf16[1,2,64,512]{3,2,1,0:T(8,128)(2,1)} %param.7) | copy-start | bytes 393220
  0.6 18.3 %copy-start.2 = (bf16[1,2,64,512]{3,2,1,0:T(8,128)(2,1)S(1)}, bf16[1,2,64,512]{3,2,1,0:T(8,128)(2,1)}, u32[]{:S(2)}) copy-start(bf16[1,2,64,512]{3,2,1,0:T(8,128)(2,1)} %param.6) | copy-start | bytes 393220
  1.6 17.3 %collective-permute-start.2 = (bf16[64,1024]{1,0:T(8,128)(2,1)S(1)}, bf16[64,1024]{1,0:T(8,128)(2,1)S(1)}, u32[]{:S(2)}, u32[]{:S(2)}) collective-permute-start(bf16[64,1024]{1,0:T(8,128)(2,1)S(1)} %bitcast.65), channel_id=1, source_target_pairs={{1,0},{2,1},{3,2},{4,3},{5,4},{6,5},{7,6},{8,7},{9,8},{10,9},{11,1... | collective-permute-start | bytes 393224 | tf_op jit(solution)/shard_map/ppermute | solution.py:19
  15.2 0.7 copy-start.11
  18.9 0.7 copy-start.4
  19.6 12.6 %collective-permute-start = (bf16[64,1024]{1,0:T(8,128)(2,1)S(1)}, bf16[64,1024]{1,0:T(8,128)(2,1)S(1)}, u32[]{:S(2)}, u32[]{:S(2)}) collective-permute-start(bf16[64,1024]{1,0:T(8,128)(2,1)S(1)} %bitcast.67), channel_id=1, source_target_pairs={{0,1},{1,2},{2,3},{3,4},{4,5},{5,6},{6,7},{7,8},{8,9},{9,10},{10,1... | collective-permute-start | bytes 393224 | tf_op jit(solution)/shard_map/ppermute | solution.py:19
  22.2 13.9 %collective-permute-start.4 = (bf16[64,1024]{1,0:T(8,128)(2,1)S(1)}, bf16[64,1024]{1,0:T(8,128)(2,1)S(1)}, u32[]{:S(2)}, u32[]{:S(2)}) collective-permute-start(bf16[64,1024]{1,0:T(8,128)(2,1)S(1)} %bitcast.68), channel_id=1, source_target_pairs={{511,510},{510,511}} | collective-permute-start | bytes 393224 | tf_op jit(solution)/shard_map/ppermute | solution.py:210
  22.8 13.2 %collective-permute-start.5 = (bf16[64,1024]{1,0:T(8,128)(2,1)S(1)}, bf16[64,1024]{1,0:T(8,128)(2,1)S(1)}, u32[]{:S(2)}, u32[]{:S(2)}) collective-permute-start(bf16[64,1024]{1,0:T(8,128)(2,1)S(1)} %bitcast.69), channel_id=1, source_target_pairs={{509,511}} | collective-permute-start | bytes 393224 | tf_op jit(solution)/shard_map/ppermute | solution.py:211
  23.6 14.6 %collective-permute-start.3 = (bf16[2,64,1024]{2,1,0:T(8,128)(2,1)S(1)}, bf16[2,64,1024]{2,1,0:T(8,128)(2,1)S(1)}, u32[]{:S(2)}, u32[]{:S(2)}) collective-permute-start(bf16[2,64,1024]{2,1,0:T(8,128)(2,1)S(1)} %pad_maximum_fusion.2), channel_id=1, source_target_pairs={{2,0},{3,1},{4,2},{5,3},{6,4},{7,5},{8,6},{9,7},{10,8},{11,9},{12,... | collective-permute-start | bytes 786440 | tf_op jit(solution)/shard_map/ppermute | solution.py:19
  32.2 0.7 copy-start.5
  32.8 14.1 %collective-permute-start.1 = (bf16[2,64,1024]{2,1,0:T(8,128)(2,1)S(1)}, bf16[2,64,1024]{2,1,0:T(8,128)(2,1)S(1)}, u32[]{:S(2)}, u32[]{:S(2)}) collective-permute-start(bf16[2,64,1024]{2,1,0:T(8,128)(2,1)S(1)} %pad_maximum_fusion.1), channel_id=1, source_target_pairs={{0,2},{1,3},{2,4},{3,5},{4,6},{5,7},{6,8},{7,9},{8,10},{9,11},{10,... | collective-permute-start | bytes 786440 | tf_op jit(solution)/shard_map/ppermute | solution.py:19
  36.0 2.1 %copy-start.8 = (bf16[64,1024]{1,0:T(8,128)(2,1)}, bf16[64,1024]{1,0:T(8,128)(2,1)S(1)}, u32[]{:S(2)}) copy-start(bf16[64,1024]{1,0:T(8,128)(2,1)S(1)} %collective-permute-done.4.turn2) | copy-start | bytes 393220
  36.1 2.1 %copy-start.9 = (bf16[64,1024]{1,0:T(8,128)(2,1)}, bf16[64,1024]{1,0:T(8,128)(2,1)S(1)}, u32[]{:S(2)}) copy-start(bf16[64,1024]{1,0:T(8,128)(2,1)S(1)} %collective-permute-done.5.turn3) | copy-start | bytes 393220
  38.1 0.7 copy-start.7
  45.0 16.5 %collective-permute-start.8 = (bf16[2,64,1024]{2,1,0:T(8,128)(2,1)}, bf16[2,64,1024]{2,1,0:T(8,128)(2,1)S(1)}, u32[]{:S(2)}, u32[]{:S(2)}) collective-permute-start(bf16[2,64,1024]{2,1,0:T(8,128)(2,1)} %get-tuple-element.20), channel_id=1, source_target_pairs={{0,2},{1,3},{2,4},{3,5},{4,6},{5,7},{6,8},{7,9},{8,10},{9,11},{10,... | collective-permute-start | bytes 786440 | tf_op jit(solution)/shard_map/ppermute | solution.py:19
  47.0 0.7 copy-start.6
  47.7 13.0 %copy-start.10 = (bf16[2,64,1024]{2,1,0:T(8,128)(2,1)S(1)}, bf16[2,64,1024]{2,1,0:T(8,128)(2,1)}, u32[]{:S(2)}) copy-start(bf16[2,64,1024]{2,1,0:T(8,128)(2,1)} %get-tuple-element.20) | copy-start | bytes 786436
  53.8 11.3 %collective-permute-start.6 = (bf16[2,64,1024]{2,1,0:T(8,128)(2,1)}, bf16[2,64,1024]{2,1,0:T(8,128)(2,1)S(1)}, u32[]{:S(2)}, u32[]{:S(2)}) collective-permute-start(bf16[2,64,1024]{2,1,0:T(8,128)(2,1)} %get-tuple-element.18), channel_id=1, source_target_pairs={{2,0},{3,1},{4,2},{5,3},{6,4},{7,5},{8,6},{9,7},{10,8},{11,9},{12,... | collective-permute-start | bytes 786440 | tf_op jit(solution)/shard_map/ppermute | solution.py:19
  60.7 1.0 %copy-start.3 = (bf16[2,64,1024]{2,1,0:T(8,128)(2,1)S(1)}, bf16[2,64,1024]{2,1,0:T(8,128)(2,1)}, u32[]{:S(2)}) copy-start(bf16[2,64,1024]{2,1,0:T(8,128)(2,1)} %get-tuple-element.19) | copy-start | bytes 786436
  60.7 11.0 %collective-permute-start.9 = (bf16[64,1024]{1,0:T(8,128)(2,1)S(1)}, bf16[64,1024]{1,0:T(8,128)(2,1)S(1)}, u32[]{:S(2)}, u32[]{:S(2)}) collective-permute-start(bf16[64,1024]{1,0:T(8,128)(2,1)S(1)} %slice_bitcast_fusion.3), channel_id=1, source_target_pairs={{510,511}} | collective-permute-start | bytes 393224 | tf_op jit(solution)/shard_map/ppermute | solution.py:228
  61.7 12.6 %copy-start = (f32[2,64,1024]{2,1,0:T(8,128)S(1)}, f32[2,64,1024]{2,1,0:T(8,128)}, u32[]{:S(2)}) copy-start(f32[2,64,1024]{2,1,0:T(8,128)} %get-tuple-element.17) | copy-start | bytes 1572868
  61.7 11.5 %collective-permute-start.10 = (bf16[64,1024]{1,0:T(8,128)(2,1)S(1)}, bf16[64,1024]{1,0:T(8,128)(2,1)S(1)}, u32[]{:S(2)}, u32[]{:S(2)}) collective-permute-start(bf16[64,1024]{1,0:T(8,128)(2,1)S(1)} %fusion.8), channel_id=1, source_target_pairs={{0,1},{1,2},{2,3},{3,4},{4,5},{5,6},{6,7},{7,8},{8,9},{9,10},{10,1... | collective-permute-start | bytes 393224 | tf_op jit(solution)/shard_map/ppermute | solution.py:19
  65.2 9.1 %collective-permute-start.7 = (bf16[64,1024]{1,0:T(8,128)(2,1)S(1)}, bf16[64,1024]{1,0:T(8,128)(2,1)S(1)}, u32[]{:S(2)}, u32[]{:S(2)}) collective-permute-start(bf16[64,1024]{1,0:T(8,128)(2,1)S(1)} %fusion.9), channel_id=1, source_target_pairs={{1,0},{2,1},{3,2},{4,3},{5,4},{6,5},{7,6},{8,7},{9,8},{10,9},{11,1... | collective-permute-start | bytes 393224 | tf_op jit(solution)/shard_map/ppermute | solution.py:19

commit v7 on v6

--- a/solution.py
+++ b/solution.py
@@ -19,10 +19,9 @@
     return lax.ppermute(value, AXIS, pairs)
 
 
-def window_half(half, slot, lo_ref, q_ref, do_ref, groups, group_size, emit):
+def window_half(slot, lo_ref, q_ref, do_ref, group_size, emit):
     half_rows = q_ref.shape[1]
     window = 4 * half_rows
-    kv_width = groups * HEAD
     scale = 1.0 / math.sqrt(HEAD)
     lo = lo_ref[0]
     rows = lax.broadcasted_iota(jnp.int32, (half_rows, window), 0)
@@ -32,45 +31,45 @@
     bias = jnp.concatenate([bias] * group_size, axis=0)
     nt = (((1,), (1,)), ((), ()))
     tn = (((0,), (0,)), ((), ()))
-    for g in range(groups):
-        base = g * group_size * HEAD
-        qg = jnp.concatenate(
-            [q_ref[0, :, base + h * HEAD:base + (h + 1) * HEAD] for h in range(group_size)], axis=0
-        )
-        dog = jnp.concatenate(
-            [do_ref[0, :, base + h * HEAD:base + (h + 1) * HEAD] for h in range(group_size)], axis=0
-        )
-        kg = jnp.concatenate([slot(j, g * HEAD) for j in range(4)], axis=0)
-        vg = jnp.concatenate([slot(j, kv_width + g * HEAD) for j in range(4)], axis=0)
-        scores = lax.dot_general(qg, kg, nt, preferred_element_type=jnp.float32) * scale
-        masked = scores + bias
-        top = jnp.max(masked, axis=1, keepdims=True)
-        expd = jnp.exp(masked - top)
-        total = jnp.sum(expd, axis=1, keepdims=True)
-        probs = (expd * (1.0 / total)).astype(jnp.bfloat16)
-        attn = jnp.dot(probs, vg, preferred_element_type=jnp.float32).astype(jnp.bfloat16)
-        delta = jnp.sum(dog.astype(jnp.float32) * attn.astype(jnp.float32), axis=1, keepdims=True)
-        dprob = lax.dot_general(dog, vg, nt, preferred_element_type=jnp.float32)
-        dscore = (probs.astype(jnp.float32) * (dprob - delta) * scale).astype(jnp.bfloat16)
-        dq = jnp.dot(dscore, kg, preferred_element_type=jnp.float32).astype(jnp.bfloat16)
-        for h in range(group_size):
-            emit("dq", h, base + h * HEAD, dq[h * half_rows:(h + 1) * half_rows])
-        dk = lax.dot_general(dscore, qg, tn, preferred_element_type=jnp.float32)
-        dv = lax.dot_general(probs, dog, tn, preferred_element_type=jnp.float32)
-        for j in range(4):
-            emit("part", j, g * HEAD, dk[j * half_rows:(j + 1) * half_rows])
-            emit("part", j, kv_width + g * HEAD, dv[j * half_rows:(j + 1) * half_rows])
+    qg = jnp.concatenate([q_ref[0, :, h * HEAD:(h + 1) * HEAD] for h in range(group_size)], axis=0)
+    dog = jnp.concatenate([do_ref[0, :, h * HEAD:(h + 1) * HEAD] for h in range(group_size)], axis=0)
+    kg = jnp.concatenate([slot(j, False) for j in range(4)], axis=0)
+    vg = jnp.concatenate([slot(j, True) for j in range(4)], axis=0)
+    scores = lax.dot_general(qg, kg, nt, preferred_element_type=jnp.float32) * scale
+    masked = scores + bias
+    top = jnp.max(masked, axis=1, keepdims=True)
+    expd = jnp.exp(masked - top)
+    total = jnp.sum(expd, axis=1, keepdims=True)
+    probs = (expd * (1.0 / total)).astype(jnp.bfloat16)
+    attn = jnp.dot(probs, vg, preferred_element_type=jnp.float32).astype(jnp.bfloat16)
+    delta = jnp.sum(dog.astype(jnp.float32) * attn.astype(jnp.float32), axis=1, keepdims=True)
+    dprob = lax.dot_general(dog, vg, nt, preferred_element_type=jnp.float32)
+    dscore = (probs.astype(jnp.float32) * (dprob - delta) * scale).astype(jnp.bfloat16)
+    dq = jnp.dot(dscore, kg, preferred_element_type=jnp.float32).astype(jnp.bfloat16)
+    for h in range(group_size):
+        emit("dq", h, False, dq[h * half_rows:(h + 1) * half_rows])
+    dk = lax.dot_general(dscore, qg, tn, preferred_element_type=jnp.float32)
+    dv = lax.dot_general(probs, dog, tn, preferred_element_type=jnp.float32)
+    for j in range(4):
+        emit("part", j, False, dk[j * half_rows:(j + 1) * half_rows])
+        emit("part", j, True, dv[j * half_rows:(j + 1) * half_rows])
+
+
+def group_cols(is_value):
+    groups = pl.num_programs(0)
+    lanes = pl.program_id(0) * HEAD + (groups * HEAD if is_value else 0)
+    return pl.ds(pl.multiple_of(lanes, HEAD), HEAD)
 
 
 def late_kernel(
     flags, lo_ref, q_ref, do_ref, kv, l1, l2, turn2, turn3,
-    dq_ref, a_l, p2_ref, p3_ref, kept, *, groups, group_size
+    dq_ref, a_l, p2_ref, p3_ref, kept, *, group_size
 ):
     at_top = flags[0] != 0
     below_top = flags[1] != 0
 
-    def slot(j, lanes):
-        cols = pl.ds(lanes, HEAD)
+    def slot(j, is_value):
+        cols = group_cols(is_value)
         if j == 0:
             regular = jnp.where(below_top, kv[0, :, cols], l2[1, :, cols])
             return jnp.where(at_top, turn3[:, cols], regular)
@@ -80,11 +79,11 @@
             return jnp.where(at_top, kv[0, :, cols], l1[:, cols])
         return kv[1, :, cols]
 
-    def emit(kind, j, lanes, value):
-        cols = pl.ds(lanes, HEAD)
+    def emit(kind, j, is_value, value):
         if kind == "dq":
-            dq_ref[0, :, cols] = value
+            dq_ref[0, :, j * HEAD:(j + 1) * HEAD] = value
             return
+        cols = group_cols(is_value)
         if j < 3:
             kept[j, :, cols] = value
         if j == 0:
@@ -96,26 +95,26 @@
         else:
             p3_ref[0, :, cols] = value
 
-    window_half(1, slot, lo_ref, q_ref, do_ref, groups, group_size, emit)
+    window_half(slot, lo_ref, q_ref, do_ref, group_size, emit)
 
 
 def early_kernel(
     flags, lo_ref, q_ref, do_ref, kv, e1, e2, kept, dq_in, p2_in, p3_in,
-    dq_ref, a_e, p2_ref, p3_ref, *, groups, group_size
+    dq_ref, a_e, p2_ref, p3_ref, *, group_size
 ):
     del dq_in, p2_in, p3_in
     at_top = flags[0] != 0
     below_top = flags[1] != 0
 
-    def slot(j, lanes):
-        cols = pl.ds(lanes, HEAD)
+    def slot(j, is_value):
+        cols = group_cols(is_value)
         return (e2[1, :, cols], e2[0, :, cols], e1[:, cols], kv[0, :, cols])[j]
 
-    def emit(kind, j, lanes, value):
-        cols = pl.ds(lanes, HEAD)
+    def emit(kind, j, is_value, value):
         if kind == "dq":
-            dq_ref[0, :, cols] = value
+            dq_ref[0, :, j * HEAD:(j + 1) * HEAD] = value
             return
+        cols = group_cols(is_value)
         zero = jnp.zeros_like(value)
         if j == 0:
             a_e[1, :, cols] = value.astype(a_e.dtype)
@@ -133,7 +132,7 @@
             )
             p3_ref[0, :, cols] = merged
 
-    window_half(0, slot, lo_ref, q_ref, do_ref, groups, group_size, emit)
+    window_half(slot, lo_ref, q_ref, do_ref, group_size, emit)
 
 
 def window_grads(flags, lo, q, do, kv, e1, e2, l1, l2, turn2, turn3):
@@ -149,14 +148,14 @@
     )
 
     def half_specs(half):
-        q_spec = pl.BlockSpec((1, half_rows, width), lambda s: (half, 0, 0))
-        lo_spec = pl.BlockSpec((1, half_rows, 1), lambda s: (half, 0, 0))
-        part_spec = pl.BlockSpec((1, half_rows, kv2), lambda s: (half, 0, 0))
+        q_spec = pl.BlockSpec((1, half_rows, width // groups), lambda g: (half, 0, g))
+        lo_spec = pl.BlockSpec((1, half_rows, 1), lambda g: (half, 0, 0))
+        part_spec = pl.BlockSpec((1, half_rows, kv2), lambda g: (half, 0, 0))
         return q_spec, lo_spec, part_spec
 
-    pair_spec = pl.BlockSpec((2, half_rows, kv2), lambda s: (0, 0, 0))
-    one_spec = pl.BlockSpec((half_rows, kv2), lambda s: (0, 0))
-    kept_spec = pl.BlockSpec((3, half_rows, kv2), lambda s: (0, 0, 0))
+    pair_spec = pl.BlockSpec((2, half_rows, kv2), lambda g: (0, 0, 0))
+    one_spec = pl.BlockSpec((half_rows, kv2), lambda g: (0, 0))
+    kept_spec = pl.BlockSpec((3, half_rows, kv2), lambda g: (0, 0, 0))
     smem = pl.BlockSpec(memory_space=pltpu.SMEM)
     anywhere = pl.BlockSpec(memory_space=pl.ANY)
     pair = jax.ShapeDtypeStruct((2, half_rows, kv2), jnp.bfloat16)
@@ -166,8 +165,8 @@
 
     q_spec, lo_spec, part_spec = half_specs(1)
     dq, a_l, p2, p3, kept = pl.pallas_call(
-        functools.partial(late_kernel, groups=groups, group_size=group_size),
-        grid=(1,),
+        functools.partial(late_kernel, group_size=group_size),
+        grid=(groups,),
         in_specs=[smem, lo_spec, q_spec, q_spec, pair_spec, one_spec, pair_spec, one_spec, one_spec],
         out_specs=[q_spec, pair_spec, part_spec, part_spec, kept_spec],
         out_shape=[
@@ -179,8 +178,8 @@
 
     q_spec, lo_spec, part_spec = half_specs(0)
     dq, a_e, p2, p3 = pl.pallas_call(
-        functools.partial(early_kernel, groups=groups, group_size=group_size),
-        grid=(1,),
+        functools.partial(early_kernel, group_size=group_size),
+        grid=(groups,),
         in_specs=[
             smem, lo_spec, q_spec, q_spec, pair_spec, one_spec, pair_spec, kept_spec,
             anywhere, anywhere, anywhere,

time: 75.9 us -> 77.3 us (1.018)
  Pallas kernels: 12.3 us -> 13.7 us
    pallas_call x2, Pallas kernels: 12.3 us -> 13.7 us  [the longest x1 6.9 us: window_grads(): pl.pallas_call(functools.partial(late_kernel, group_size=group_size), gri...]
  transfers between devices with their start and end apart: 11 -> 11, of which waited for: 5 -> 5; matrix products, arithmetic and copies ran while one was open for 4% -> 4% of each run, Pallas kernels for 16% -> 18%
where the time goes in v7:
time: 77.3 us; the launch traced here: 76.6 us
  starting transfers between devices  45.3 us (59%)
  Pallas kernels  13.7 us (18%)
  waiting for transfers between devices  8.09 us (10%)
  local copies, waits for them, and re-layouts  4.38 us (6%)
  other arithmetic  4.15 us (5%)
  between operations  0.92 us (1%)
    ppermute x8, starting transfers between devices, shifted(): return lax.ppermute(value, AXIS, pairs)  43.2 us
    ppermute x8, waiting for transfers between devices, shifted(): return lax.ppermute(value, AXIS, pairs)  8.08 us
    pallas_call x1, Pallas kernels, window_grads(): pl.pallas_call(functools.partial(late_kernel, group_size=group_size), gri...  6.9 us
    pallas_call x1, Pallas kernels, window_grads(): pl.pallas_call(functools.partial(early_kernel, group_size=group_size), gr...  6.8 us
    unnamed x24, local copies, waits for them, and re-layouts  3.36 us
    concatenate x2, other arithmetic, on_device(): kv = jnp.concatenate([keys[0], values[0]], axis=2)  1.66 us
  transfers between devices with their start and end apart: 11, of which 5 were waited for; matrix products, arithmetic and copies ran while one was open for 4% of the time, Pallas kernels for 18%

profile of v7, /device:TPU:6, one launch (start us, length us, event | category | flops | bytes accessed | tf_op | source)
XLA Modules:
  0.0 76.6 jit_solution(10271207742364698246)
XLA Ops:
  0.7 0.9 %fusion.11 = bf16[1,64,1024]{2,1,0:T(8,128)(2,1)S(1)} fusion(bf16[2,64,512]{2,1,0:T(8,128)(2,1)} %bitcast.61, bf16[2,64,512]{2,1,0:T(8,128)(2,1)} %bitcast.58), kind=kLoop, calls=%fused_computation.25 | loop fusion | flops 262144 | bytes 393216 | tf_op jit(solution)/shard_map/concatenate | solution.py:202
  1.6 13.6 %collective-permute-start.2 = (bf16[64,1024]{1,0:T(8,128)(2,1)S(1)}, bf16[64,1024]{1,0:T(8,128)(2,1)S(1)}, u32[]{:S(2)}, u32[]{:S(2)}) collective-permute-start(bf16[64,1024]{1,0:T(8,128)(2,1)S(1)} %bitcast.65), channel_id=1, source_target_pairs={{1,0},{2,1},{3,2},{4,3},{5,4},{6,5},{7,6},{8,7},{9,8},{10,9},{11,1... | collective-permute-start | bytes 393224 | tf_op jit(solution)/shard_map/ppermute | solution.py:19
  15.3 0.6 copy-done.11
  15.9 0.3 reduce-window.9
  16.3 0.1 slice_reduce_fusion
  16.5 0.2 select_reduce_fusion
  16.9 2.0 %collective-permute-done.2.l1 = bf16[64,1024]{1,0:T(8,128)(2,1)S(1)} collective-permute-done((bf16[64,1024]{1,0:T(8,128)(2,1)S(1)}, bf16[64,1024]{1,0:T(8,128)(2,1)S(1)}, u32[]{:S(2)}, u32[]{:S(2)}) %collective-permute-start.2) | collective-permute-done | bytes 131104 | tf_op jit(solution)/shard_map/ppermute | solution.py:19
  19.0 0.6 copy-done.4
  19.6 1.9 %collective-permute-start = (bf16[64,1024]{1,0:T(8,128)(2,1)S(1)}, bf16[64,1024]{1,0:T(8,128)(2,1)S(1)}, u32[]{:S(2)}, u32[]{:S(2)}) collective-permute-start(bf16[64,1024]{1,0:T(8,128)(2,1)S(1)} %bitcast.67), channel_id=1, source_target_pairs={{0,1},{1,2},{2,3},{3,4},{4,5},{5,6},{6,7},{7,8},{8,9},{9,10},{10,1... | collective-permute-start | bytes 393224 | tf_op jit(solution)/shard_map/ppermute | solution.py:19
  21.5 0.7 broadcast_subtract_fusion.lo_ref
  22.2 0.7 collective-permute-start.4
  22.8 0.7 collective-permute-start.5
  23.6 8.6 %collective-permute-start.3 = (bf16[2,64,1024]{2,1,0:T(8,128)(2,1)S(1)}, bf16[2,64,1024]{2,1,0:T(8,128)(2,1)S(1)}, u32[]{:S(2)}, u32[]{:S(2)}) collective-permute-start(bf16[2,64,1024]{2,1,0:T(8,128)(2,1)S(1)} %pad_maximum_fusion.2), channel_id=1, source_target_pairs={{2,0},{3,1},{4,2},{5,3},{6,4},{7,5},{8,6},{9,7},{10,8},{11,9},{12,... | collective-permute-start | bytes 786440 | tf_op jit(solution)/shard_map/ppermute | solution.py:19
  32.2 0.6 copy-done.5
  32.8 1.9 %collective-permute-start.1 = (bf16[2,64,1024]{2,1,0:T(8,128)(2,1)S(1)}, bf16[2,64,1024]{2,1,0:T(8,128)(2,1)S(1)}, u32[]{:S(2)}, u32[]{:S(2)}) collective-permute-start(bf16[2,64,1024]{2,1,0:T(8,128)(2,1)S(1)} %pad_maximum_fusion.1), channel_id=1, source_target_pairs={{0,2},{1,3},{2,4},{3,5},{4,6},{5,7},{6,8},{7,9},{8,10},{9,11},{10,... | collective-permute-start | bytes 786440 | tf_op jit(solution)/shard_map/ppermute | solution.py:19
  34.8 0.6 add_convert_fusion.flags
  35.3 0.7 pad_maximum_fusion.kv
  36.1 2.1 %collective-permute-done.3.l2 = bf16[2,64,1024]{2,1,0:T(8,128)(2,1)S(1)} collective-permute-done((bf16[2,64,1024]{2,1,0:T(8,128)(2,1)S(1)}, bf16[2,64,1024]{2,1,0:T(8,128)(2,1)S(1)}, u32[]{:S(2)}, u32[]{:S(2)}) %collective-permute-start.3) | collective-permute-done | bytes 262176 | tf_op jit(solution)/shard_map/ppermute | solution.py:19
  38.1 0.7 copy-done.7
  38.8 6.9 %shard_map.76 = (bf16[2,64,4096]{2,1,0:T(8,128)(2,1)}, bf16[2,64,1024]{2,1,0:T(8,128)(2,1)}, bf16[2,64,1024]{2,1,0:T(8,128)(2,1)}, f32[2,64,1024]{2,1,0:T(8,128)}, f32[3,64,1024]{2,1,0:T(8,128)}) custom-call(s32[2]{0:T(128)} %add_convert_fusion.flags, s32[2,64,1]{2,1,0:T(8,128)} %broadcast_subtract_fusion.lo_ref, bf16[2,64,4096]{2,1,0:T(8,128)(2,1)} %bitcast.54, ...), custom_call_target="tpu_custom_call" | custom-call | flops 805306368 | bytes 1835008 | tf_op jit(solution)/shard_map/pallas_call | solution.py:167
  45.7 1.9 %collective-permute-start.8 = (bf16[2,64,1024]{2,1,0:T(8,128)(2,1)}, bf16[2,64,1024]{2,1,0:T(8,128)(2,1)S(1)}, u32[]{:S(2)}, u32[]{:S(2)}) collective-permute-start(bf16[2,64,1024]{2,1,0:T(8,128)(2,1)} %get-tuple-element.20), channel_id=1, source_target_pairs={{0,2},{1,3},{2,4},{3,5},{4,6},{5,7},{6,8},{7,9},{8,10},{9,11},{10,... | collective-permute-start | bytes 786440 | tf_op jit(solution)/shard_map/ppermute | solution.py:19
  47.7 0.7 copy-done.6
  48.4 6.8 %shard_map.77 = (bf16[2,64,4096]{2,1,0:T(8,128)(2,1)}, bf16[2,64,1024]{2,1,0:T(8,128)(2,1)}, bf16[2,64,1024]{2,1,0:T(8,128)(2,1)}, f32[2,64,1024]{2,1,0:T(8,128)}) custom-call(s32[2]{0:T(128)} %add_convert_fusion.flags, s32[2,64,1]{2,1,0:T(8,128)} %broadcast_subtract_fusion.lo_ref, ...), custom_call_target="tpu_custom_call", output_to_operand_aliasing={{0}: (8, {}), {2}: (9, {}), {3}: (10, {})} | custom-call | flops 805306368 | bytes 1835008 | tf_op jit(solution)/shard_map/pallas_call | solution.py:180
  55.2 6.8 %collective-permute-start.6 = (bf16[2,64,1024]{2,1,0:T(8,128)(2,1)}, bf16[2,64,1024]{2,1,0:T(8,128)(2,1)S(1)}, u32[]{:S(2)}, u32[]{:S(2)}) collective-permute-start(bf16[2,64,1024]{2,1,0:T(8,128)(2,1)} %get-tuple-element.18), channel_id=1, source_target_pairs={{2,0},{3,1},{4,2},{5,3},{6,4},{7,5},{8,6},{9,7},{10,8},{11,9},{12,... | collective-permute-start | bytes 786440 | tf_op jit(solution)/shard_map/ppermute | solution.py:19
  62.1 0.8 %collective-permute-start.9 = (bf16[64,1024]{1,0:T(8,128)(2,1)S(1)}, bf16[64,1024]{1,0:T(8,128)(2,1)S(1)}, u32[]{:S(2)}, u32[]{:S(2)}) collective-permute-start(bf16[64,1024]{1,0:T(8,128)(2,1)S(1)} %slice_bitcast_fusion.3), channel_id=1, source_target_pairs={{510,511}} | collective-permute-start | bytes 393224 | tf_op jit(solution)/shard_map/ppermute | solution.py:227
  63.0 2.1 %collective-permute-start.10 = (bf16[64,1024]{1,0:T(8,128)(2,1)S(1)}, bf16[64,1024]{1,0:T(8,128)(2,1)S(1)}, u32[]{:S(2)}, u32[]{:S(2)}) collective-permute-start(bf16[64,1024]{1,0:T(8,128)(2,1)S(1)} %fusion.8), channel_id=1, source_target_pairs={{0,1},{1,2},{2,3},{3,4},{4,5},{5,6},{6,7},{7,8},{8,9},{9,10},{10,1... | collective-permute-start | bytes 393224 | tf_op jit(solution)/shard_map/ppermute | solution.py:19
  65.1 1.4 %collective-permute-done.6 = bf16[2,64,1024]{2,1,0:T(8,128)(2,1)S(1)} collective-permute-done((bf16[2,64,1024]{2,1,0:T(8,128)(2,1)}, bf16[2,64,1024]{2,1,0:T(8,128)(2,1)S(1)}, u32[]{:S(2)}, u32[]{:S(2)}) %collective-permute-start.6) | collective-permute-done | bytes 262176 | tf_op jit(solution)/shard_map/ppermute | solution.py:19
  66.6 6.4 %collective-permute-start.7 = (bf16[64,1024]{1,0:T(8,128)(2,1)S(1)}, bf16[64,1024]{1,0:T(8,128)(2,1)S(1)}, u32[]{:S(2)}, u32[]{:S(2)}) collective-permute-start(bf16[64,1024]{1,0:T(8,128)(2,1)S(1)} %fusion.9), channel_id=1, source_target_pairs={{1,0},{2,1},{3,2},{4,3},{5,4},{6,5},{7,6},{8,7},{9,8},{10,9},{11,1... | collective-permute-start | bytes 393224 | tf_op jit(solution)/shard_map/ppermute | solution.py:19
  73.1 1.5 %collective-permute-done.10 = bf16[64,1024]{1,0:T(8,128)(2,1)S(1)} collective-permute-done((bf16[64,1024]{1,0:T(8,128)(2,1)S(1)}, bf16[64,1024]{1,0:T(8,128)(2,1)S(1)}, u32[]{:S(2)}, u32[]{:S(2)}) %collective-permute-start.10) | collective-permute-done | bytes 131104 | tf_op jit(solution)/shard_map/ppermute | solution.py:19
  74.6 1.1 %collective-permute-done.7 = bf16[64,1024]{1,0:T(8,128)(2,1)S(1)} collective-permute-done((bf16[64,1024]{1,0:T(8,128)(2,1)S(1)}, bf16[64,1024]{1,0:T(8,128)(2,1)S(1)}, u32[]{:S(2)}, u32[]{:S(2)}) %collective-permute-start.7) | collective-permute-done | bytes 131104 | tf_op jit(solution)/shard_map/ppermute | solution.py:19
  75.7 0.1 fusion.7
  75.9 0.7 slice_bitcast_fusion.1
  (41 shorter events, 0.9 us)
Async XLA Ops:
  0.6 18.3 %copy-start.1 = (bf16[1,2,64,512]{3,2,1,0:T(8,128)(2,1)S(1)}, bf16[1,2,64,512]{3,2,1,0:T(8,128)(2,1)}, u32[]{:S(2)}) copy-start(bf16[1,2,64,512]{3,2,1,0:T(8,128)(2,1)} %param.7) | copy-start | bytes 393220
  0.6 18.3 %copy-start.2 = (bf16[1,2,64,512]{3,2,1,0:T(8,128)(2,1)S(1)}, bf16[1,2,64,512]{3,2,1,0:T(8,128)(2,1)}, u32[]{:S(2)}) copy-start(bf16[1,2,64,512]{3,2,1,0:T(8,128)(2,1)} %param.6) | copy-start | bytes 393220
  1.6 17.3 %collective-permute-start.2 = (bf16[64,1024]{1,0:T(8,128)(2,1)S(1)}, bf16[64,1024]{1,0:T(8,128)(2,1)S(1)}, u32[]{:S(2)}, u32[]{:S(2)}) collective-permute-start(bf16[64,1024]{1,0:T(8,128)(2,1)S(1)} %bitcast.65), channel_id=1, source_target_pairs={{1,0},{2,1},{3,2},{4,3},{5,4},{6,5},{7,6},{8,7},{9,8},{10,9},{11,1... | collective-permute-start | bytes 393224 | tf_op jit(solution)/shard_map/ppermute | solution.py:19
  15.2 0.7 copy-start.11
  18.9 0.7 copy-start.4
  19.6 12.6 %collective-permute-start = (bf16[64,1024]{1,0:T(8,128)(2,1)S(1)}, bf16[64,1024]{1,0:T(8,128)(2,1)S(1)}, u32[]{:S(2)}, u32[]{:S(2)}) collective-permute-start(bf16[64,1024]{1,0:T(8,128)(2,1)S(1)} %bitcast.67), channel_id=1, source_target_pairs={{0,1},{1,2},{2,3},{3,4},{4,5},{5,6},{6,7},{7,8},{8,9},{9,10},{10,1... | collective-permute-start | bytes 393224 | tf_op jit(solution)/shard_map/ppermute | solution.py:19
  22.2 13.9 %collective-permute-start.4 = (bf16[64,1024]{1,0:T(8,128)(2,1)S(1)}, bf16[64,1024]{1,0:T(8,128)(2,1)S(1)}, u32[]{:S(2)}, u32[]{:S(2)}) collective-permute-start(bf16[64,1024]{1,0:T(8,128)(2,1)S(1)} %bitcast.68), channel_id=1, source_target_pairs={{511,510},{510,511}} | collective-permute-start | bytes 393224 | tf_op jit(solution)/shard_map/ppermute | solution.py:209
  22.8 13.2 %collective-permute-start.5 = (bf16[64,1024]{1,0:T(8,128)(2,1)S(1)}, bf16[64,1024]{1,0:T(8,128)(2,1)S(1)}, u32[]{:S(2)}, u32[]{:S(2)}) collective-permute-start(bf16[64,1024]{1,0:T(8,128)(2,1)S(1)} %bitcast.69), channel_id=1, source_target_pairs={{509,511}} | collective-permute-start | bytes 393224 | tf_op jit(solution)/shard_map/ppermute | solution.py:210
  23.6 14.6 %collective-permute-start.3 = (bf16[2,64,1024]{2,1,0:T(8,128)(2,1)S(1)}, bf16[2,64,1024]{2,1,0:T(8,128)(2,1)S(1)}, u32[]{:S(2)}, u32[]{:S(2)}) collective-permute-start(bf16[2,64,1024]{2,1,0:T(8,128)(2,1)S(1)} %pad_maximum_fusion.2), channel_id=1, source_target_pairs={{2,0},{3,1},{4,2},{5,3},{6,4},{7,5},{8,6},{9,7},{10,8},{11,9},{12,... | collective-permute-start | bytes 786440 | tf_op jit(solution)/shard_map/ppermute | solution.py:19
  32.2 0.7 copy-start.5
  32.8 14.8 %collective-permute-start.1 = (bf16[2,64,1024]{2,1,0:T(8,128)(2,1)S(1)}, bf16[2,64,1024]{2,1,0:T(8,128)(2,1)S(1)}, u32[]{:S(2)}, u32[]{:S(2)}) collective-permute-start(bf16[2,64,1024]{2,1,0:T(8,128)(2,1)S(1)} %pad_maximum_fusion.1), channel_id=1, source_target_pairs={{0,2},{1,3},{2,4},{3,5},{4,6},{5,7},{6,8},{7,9},{8,10},{9,11},{10,... | collective-permute-start | bytes 786440 | tf_op jit(solution)/shard_map/ppermute | solution.py:19
  36.0 2.1 %copy-start.8 = (bf16[64,1024]{1,0:T(8,128)(2,1)}, bf16[64,1024]{1,0:T(8,128)(2,1)S(1)}, u32[]{:S(2)}) copy-start(bf16[64,1024]{1,0:T(8,128)(2,1)S(1)} %collective-permute-done.4.turn2) | copy-start | bytes 393220
  36.1 2.1 %copy-start.9 = (bf16[64,1024]{1,0:T(8,128)(2,1)}, bf16[64,1024]{1,0:T(8,128)(2,1)S(1)}, u32[]{:S(2)}) copy-start(bf16[64,1024]{1,0:T(8,128)(2,1)S(1)} %collective-permute-done.5.turn3) | copy-start | bytes 393220
  38.1 0.7 copy-start.7
  45.7 17.1 %collective-permute-start.8 = (bf16[2,64,1024]{2,1,0:T(8,128)(2,1)}, bf16[2,64,1024]{2,1,0:T(8,128)(2,1)S(1)}, u32[]{:S(2)}, u32[]{:S(2)}) collective-permute-start(bf16[2,64,1024]{2,1,0:T(8,128)(2,1)} %get-tuple-element.20), channel_id=1, source_target_pairs={{0,2},{1,3},{2,4},{3,5},{4,6},{5,7},{6,8},{7,9},{8,10},{9,11},{10,... | collective-permute-start | bytes 786440 | tf_op jit(solution)/shard_map/ppermute | solution.py:19
  47.7 0.7 copy-start.6
  48.4 13.6 %copy-start.10 = (bf16[2,64,1024]{2,1,0:T(8,128)(2,1)S(1)}, bf16[2,64,1024]{2,1,0:T(8,128)(2,1)}, u32[]{:S(2)}) copy-start(bf16[2,64,1024]{2,1,0:T(8,128)(2,1)} %get-tuple-element.20) | copy-start | bytes 786436
  55.2 11.3 %collective-permute-start.6 = (bf16[2,64,1024]{2,1,0:T(8,128)(2,1)}, bf16[2,64,1024]{2,1,0:T(8,128)(2,1)S(1)}, u32[]{:S(2)}, u32[]{:S(2)}) collective-permute-start(bf16[2,64,1024]{2,1,0:T(8,128)(2,1)} %get-tuple-element.18), channel_id=1, source_target_pairs={{2,0},{3,1},{4,2},{5,3},{6,4},{7,5},{8,6},{9,7},{10,8},{11,9},{12,... | collective-permute-start | bytes 786440 | tf_op jit(solution)/shard_map/ppermute | solution.py:19
  62.1 1.0 %copy-start.3 = (bf16[2,64,1024]{2,1,0:T(8,128)(2,1)S(1)}, bf16[2,64,1024]{2,1,0:T(8,128)(2,1)}, u32[]{:S(2)}) copy-start(bf16[2,64,1024]{2,1,0:T(8,128)(2,1)} %get-tuple-element.19) | copy-start | bytes 786436
  62.1 11.0 %collective-permute-start.9 = (bf16[64,1024]{1,0:T(8,128)(2,1)S(1)}, bf16[64,1024]{1,0:T(8,128)(2,1)S(1)}, u32[]{:S(2)}, u32[]{:S(2)}) collective-permute-start(bf16[64,1024]{1,0:T(8,128)(2,1)S(1)} %slice_bitcast_fusion.3), channel_id=1, source_target_pairs={{510,511}} | collective-permute-start | bytes 393224 | tf_op jit(solution)/shard_map/ppermute | solution.py:227
  63.0 12.6 %copy-start = (f32[2,64,1024]{2,1,0:T(8,128)S(1)}, f32[2,64,1024]{2,1,0:T(8,128)}, u32[]{:S(2)}) copy-start(f32[2,64,1024]{2,1,0:T(8,128)} %get-tuple-element.17) | copy-start | bytes 1572868
  63.0 11.5 %collective-permute-start.10 = (bf16[64,1024]{1,0:T(8,128)(2,1)S(1)}, bf16[64,1024]{1,0:T(8,128)(2,1)S(1)}, u32[]{:S(2)}, u32[]{:S(2)}) collective-permute-start(bf16[64,1024]{1,0:T(8,128)(2,1)S(1)} %fusion.8), channel_id=1, source_target_pairs={{0,1},{1,2},{2,3},{3,4},{4,5},{5,6},{6,7},{7,8},{8,9},{9,10},{10,1... | collective-permute-start | bytes 393224 | tf_op jit(solution)/shard_map/ppermute | solution.py:19
  66.6 9.1 %collective-permute-start.7 = (bf16[64,1024]{1,0:T(8,128)(2,1)S(1)}, bf16[64,1024]{1,0:T(8,128)(2,1)S(1)}, u32[]{:S(2)}, u32[]{:S(2)}) collective-permute-start(bf16[64,1024]{1,0:T(8,128)(2,1)S(1)} %fusion.9), channel_id=1, source_target_pairs={{1,0},{2,1},{3,2},{4,3},{5,4},{6,5},{7,6},{8,7},{9,8},{10,9},{11,1... | collective-permute-start | bytes 393224 | tf_op jit(solution)/shard_map/ppermute | solution.py:19

commit v8 on v6

--- a/solution.py
+++ b/solution.py
@@ -20,7 +20,7 @@
 
 
 def window_half(half, slot, lo_ref, q_ref, do_ref, groups, group_size, emit):
-    half_rows = q_ref.shape[1]
+    half_rows = q_ref.buf.shape[2]
     window = 4 * half_rows
     kv_width = groups * HEAD
     scale = 1.0 / math.sqrt(HEAD)
@@ -34,11 +34,12 @@
     tn = (((0,), (0,)), ((), ()))
     for g in range(groups):
         base = g * group_size * HEAD
+        q_ref.wait(g)
         qg = jnp.concatenate(
-            [q_ref[0, :, base + h * HEAD:base + (h + 1) * HEAD] for h in range(group_size)], axis=0
+            [q_ref.buf[0, g, :, h * HEAD:(h + 1) * HEAD] for h in range(group_size)], axis=0
         )
         dog = jnp.concatenate(
-            [do_ref[0, :, base + h * HEAD:base + (h + 1) * HEAD] for h in range(group_size)], axis=0
+            [q_ref.buf[1, g, :, h * HEAD:(h + 1) * HEAD] for h in range(group_size)], axis=0
         )
         kg = jnp.concatenate([slot(j, g * HEAD) for j in range(4)], axis=0)
         vg = jnp.concatenate([slot(j, kv_width + g * HEAD) for j in range(4)], axis=0)
@@ -62,10 +63,31 @@
             emit("part", j, kv_width + g * HEAD, dv[j * half_rows:(j + 1) * half_rows])
 
 
+class GroupLoader:
+    def __init__(self, half, q_hbm, do_hbm, buf, sems):
+        self.buf = buf
+        self.copies = []
+        width = buf.shape[3]
+        for g in range(buf.shape[1]):
+            pair = []
+            for k, src in enumerate((q_hbm, do_hbm)):
+                copy = pltpu.make_async_copy(
+                    src.at[half, :, pl.ds(g * width, width)], buf.at[k, g], sems.at[k, g]
+                )
+                copy.start()
+                pair.append(copy)
+            self.copies.append(pair)
+
+    def wait(self, g):
+        for copy in self.copies[g]:
+            copy.wait()
+
+
 def late_kernel(
-    flags, lo_ref, q_ref, do_ref, kv, l1, l2, turn2, turn3,
-    dq_ref, a_l, p2_ref, p3_ref, kept, *, groups, group_size
+    flags, lo_ref, q_hbm, do_hbm, kv, l1, l2, turn2, turn3,
+    dq_ref, a_l, p2_ref, p3_ref, kept, buf, sems, *, groups, group_size
 ):
+    q_ref = GroupLoader(1, q_hbm, do_hbm, buf, sems)
     at_top = flags[0] != 0
     below_top = flags[1] != 0
 
@@ -96,13 +118,14 @@
         else:
             p3_ref[0, :, cols] = value
 
-    window_half(1, slot, lo_ref, q_ref, do_ref, groups, group_size, emit)
+    window_half(1, slot, lo_ref, q_ref, None, groups, group_size, emit)
 
 
 def early_kernel(
-    flags, lo_ref, q_ref, do_ref, kv, e1, e2, kept, dq_in, p2_in, p3_in,
-    dq_ref, a_e, p2_ref, p3_ref, *, groups, group_size
+    flags, lo_ref, q_hbm, do_hbm, kv, e1, e2, kept, dq_in, p2_in, p3_in,
+    dq_ref, a_e, p2_ref, p3_ref, buf, sems, *, groups, group_size
 ):
+    q_ref = GroupLoader(0, q_hbm, do_hbm, buf, sems)
     del dq_in, p2_in, p3_in
     at_top = flags[0] != 0
     below_top = flags[1] != 0
@@ -133,7 +156,7 @@
             )
             p3_ref[0, :, cols] = merged
 
-    window_half(0, slot, lo_ref, q_ref, do_ref, groups, group_size, emit)
+    window_half(0, slot, lo_ref, q_ref, None, groups, group_size, emit)
 
 
 def window_grads(flags, lo, q, do, kv, e1, e2, l1, l2, turn2, turn3):
@@ -168,11 +191,15 @@
     dq, a_l, p2, p3, kept = pl.pallas_call(
         functools.partial(late_kernel, groups=groups, group_size=group_size),
         grid=(1,),
-        in_specs=[smem, lo_spec, q_spec, q_spec, pair_spec, one_spec, pair_spec, one_spec, one_spec],
+        in_specs=[smem, lo_spec, anywhere, anywhere, pair_spec, one_spec, pair_spec, one_spec, one_spec],
         out_specs=[q_spec, pair_spec, part_spec, part_spec, kept_spec],
         out_shape=[
             dq_shape, pair, p2_shape, p3_shape,
             jax.ShapeDtypeStruct((3, half_rows, kv2), jnp.float32),
+        ],
+        scratch_shapes=[
+            pltpu.VMEM((2, groups, half_rows, width // groups), jnp.bfloat16),
+            pltpu.SemaphoreType.DMA((2, groups)),
         ],
         cost_estimate=cost,
     )(flags, lo, q, do, kv, l1, l2, turn2, turn3)
@@ -182,12 +209,16 @@
         functools.partial(early_kernel, groups=groups, group_size=group_size),
         grid=(1,),
         in_specs=[
-            smem, lo_spec, q_spec, q_spec, pair_spec, one_spec, pair_spec, kept_spec,
+            smem, lo_spec, anywhere, anywhere, pair_spec, one_spec, pair_spec, kept_spec,
             anywhere, anywhere, anywhere,
         ],
         out_specs=[q_spec, pair_spec, part_spec, part_spec],
         out_shape=[dq_shape, pair, p2_shape, p3_shape],
         input_output_aliases={8: 0, 9: 2, 10: 3},
+        scratch_shapes=[
+            pltpu.VMEM((2, groups, half_rows, width // groups), jnp.bfloat16),
+            pltpu.SemaphoreType.DMA((2, groups)),
+        ],
         cost_estimate=cost,
     )(flags, lo, q, do, kv, e1, e2, kept, dq, p2, p3)
     return dq, a_e, a_l, p2, p3

time: 75.9 us -> 78.8 us (1.038)
  Pallas kernels: 12.3 us -> 15.2 us
    pallas_call x1, Pallas kernels: 6.19 us -> 7.62 us  [window_grads(): pl.pallas_call(functools.partial(late_kernel, groups=groups, group_size=g...]
    pallas_call x1, Pallas kernels: 6.14 us -> 7.57 us  [window_grads(): pl.pallas_call(functools.partial(early_kernel, groups=groups, group_size=...]
  transfers between devices with their start and end apart: 11 -> 11, of which waited for: 5 -> 5; matrix products, arithmetic and copies ran while one was open for 4% -> 4% of each run, Pallas kernels for 16% -> 19%
where the time goes in v8:
time: 78.8 us; the launch traced here: 78.1 us
  starting transfers between devices  45.4 us (58%)
  Pallas kernels  15.2 us (19%)
  waiting for transfers between devices  8.09 us (10%)
  local copies, waits for them, and re-layouts  4.38 us (6%)
  other arithmetic  4.15 us (5%)
  between operations  0.94 us (1%)
    ppermute x8, starting transfers between devices, shifted(): return lax.ppermute(value, AXIS, pairs)  43.2 us
    ppermute x8, waiting for transfers between devices, shifted(): return lax.ppermute(value, AXIS, pairs)  8.08 us
    pallas_call x1, Pallas kernels, window_grads(): pl.pallas_call(functools.partial(late_kernel, groups=groups, group_size=g...  7.62 us
    pallas_call x1, Pallas kernels, window_grads(): pl.pallas_call(functools.partial(early_kernel, groups=groups, group_size=...  7.57 us
    unnamed x24, local copies, waits for them, and re-layouts  3.36 us
    concatenate x2, other arithmetic, on_device(): kv = jnp.concatenate([keys[0], values[0]], axis=2)  1.66 us
  transfers between devices with their start and end apart: 11, of which 5 were waited for; matrix products, arithmetic and copies ran while one was open for 4% of the time, Pallas kernels for 19%

profile of v8, /device:TPU:6, one launch (start us, length us, event | category | flops | bytes accessed | tf_op | source)
XLA Modules:
  0.0 78.1 jit_solution(11652267505635093380)
XLA Ops:
  0.7 0.9 %fusion.11 = bf16[1,64,1024]{2,1,0:T(8,128)(2,1)S(1)} fusion(bf16[2,64,512]{2,1,0:T(8,128)(2,1)} %bitcast.61, bf16[2,64,512]{2,1,0:T(8,128)(2,1)} %bitcast.58), kind=kLoop, calls=%fused_computation.25 | loop fusion | flops 262144 | bytes 393216 | tf_op jit(solution)/shard_map/concatenate | solution.py:234
  1.6 13.6 %collective-permute-start.2 = (bf16[64,1024]{1,0:T(8,128)(2,1)S(1)}, bf16[64,1024]{1,0:T(8,128)(2,1)S(1)}, u32[]{:S(2)}, u32[]{:S(2)}) collective-permute-start(bf16[64,1024]{1,0:T(8,128)(2,1)S(1)} %bitcast.65), channel_id=1, source_target_pairs={{1,0},{2,1},{3,2},{4,3},{5,4},{6,5},{7,6},{8,7},{9,8},{10,9},{11,1... | collective-permute-start | bytes 393224 | tf_op jit(solution)/shard_map/ppermute | solution.py:19
  15.3 0.6 copy-done.11
  15.9 0.3 reduce-window.9
  16.3 0.1 slice_reduce_fusion
  16.5 0.2 select_reduce_fusion
  16.9 2.0 %collective-permute-done.2.l1 = bf16[64,1024]{1,0:T(8,128)(2,1)S(1)} collective-permute-done((bf16[64,1024]{1,0:T(8,128)(2,1)S(1)}, bf16[64,1024]{1,0:T(8,128)(2,1)S(1)}, u32[]{:S(2)}, u32[]{:S(2)}) %collective-permute-start.2) | collective-permute-done | bytes 131104 | tf_op jit(solution)/shard_map/ppermute | solution.py:19
  19.0 0.6 copy-done.4
  19.6 1.9 %collective-permute-start = (bf16[64,1024]{1,0:T(8,128)(2,1)S(1)}, bf16[64,1024]{1,0:T(8,128)(2,1)S(1)}, u32[]{:S(2)}, u32[]{:S(2)}) collective-permute-start(bf16[64,1024]{1,0:T(8,128)(2,1)S(1)} %bitcast.67), channel_id=1, source_target_pairs={{0,1},{1,2},{2,3},{3,4},{4,5},{5,6},{6,7},{7,8},{8,9},{9,10},{10,1... | collective-permute-start | bytes 393224 | tf_op jit(solution)/shard_map/ppermute | solution.py:19
  21.5 0.7 broadcast_subtract_fusion.lo_ref
  22.2 0.7 collective-permute-start.4
  22.8 0.7 collective-permute-start.5
  23.6 8.6 %collective-permute-start.3 = (bf16[2,64,1024]{2,1,0:T(8,128)(2,1)S(1)}, bf16[2,64,1024]{2,1,0:T(8,128)(2,1)S(1)}, u32[]{:S(2)}, u32[]{:S(2)}) collective-permute-start(bf16[2,64,1024]{2,1,0:T(8,128)(2,1)S(1)} %pad_maximum_fusion.2), channel_id=1, source_target_pairs={{2,0},{3,1},{4,2},{5,3},{6,4},{7,5},{8,6},{9,7},{10,8},{11,9},{12,... | collective-permute-start | bytes 786440 | tf_op jit(solution)/shard_map/ppermute | solution.py:19
  32.2 0.6 copy-done.5
  32.8 1.9 %collective-permute-start.1 = (bf16[2,64,1024]{2,1,0:T(8,128)(2,1)S(1)}, bf16[2,64,1024]{2,1,0:T(8,128)(2,1)S(1)}, u32[]{:S(2)}, u32[]{:S(2)}) collective-permute-start(bf16[2,64,1024]{2,1,0:T(8,128)(2,1)S(1)} %pad_maximum_fusion.1), channel_id=1, source_target_pairs={{0,2},{1,3},{2,4},{3,5},{4,6},{5,7},{6,8},{7,9},{8,10},{9,11},{10,... | collective-permute-start | bytes 786440 | tf_op jit(solution)/shard_map/ppermute | solution.py:19
  34.8 0.6 add_convert_fusion.flags
  35.3 0.7 pad_maximum_fusion.kv
  36.1 2.1 %collective-permute-done.3.l2 = bf16[2,64,1024]{2,1,0:T(8,128)(2,1)S(1)} collective-permute-done((bf16[2,64,1024]{2,1,0:T(8,128)(2,1)S(1)}, bf16[2,64,1024]{2,1,0:T(8,128)(2,1)S(1)}, u32[]{:S(2)}, u32[]{:S(2)}) %collective-permute-start.3) | collective-permute-done | bytes 262176 | tf_op jit(solution)/shard_map/ppermute | solution.py:19
  38.1 0.7 copy-done.7
  38.8 7.6 %shard_map.76 = (bf16[2,64,4096]{2,1,0:T(8,128)(2,1)}, bf16[2,64,1024]{2,1,0:T(8,128)(2,1)}, bf16[2,64,1024]{2,1,0:T(8,128)(2,1)}, f32[2,64,1024]{2,1,0:T(8,128)}, f32[3,64,1024]{2,1,0:T(8,128)}) custom-call(s32[2]{0:T(128)} %add_convert_fusion.flags, s32[2,64,1]{2,1,0:T(8,128)} %broadcast_subtract_fusion.lo_ref, bf16[2,64,4096]{2,1,0:T(8,128)(2,1)} %bitcast.54, ...), custom_call_target="tpu_custom_call" | custom-call | flops 805306368 | bytes 1835008 | tf_op jit(solution)/shard_map/pallas_call | solution.py:191
  46.5 1.9 %collective-permute-start.8 = (bf16[2,64,1024]{2,1,0:T(8,128)(2,1)}, bf16[2,64,1024]{2,1,0:T(8,128)(2,1)S(1)}, u32[]{:S(2)}, u32[]{:S(2)}) collective-permute-start(bf16[2,64,1024]{2,1,0:T(8,128)(2,1)} %get-tuple-element.20), channel_id=1, source_target_pairs={{0,2},{1,3},{2,4},{3,5},{4,6},{5,7},{6,8},{7,9},{8,10},{9,11},{10,... | collective-permute-start | bytes 786440 | tf_op jit(solution)/shard_map/ppermute | solution.py:19
  48.4 0.7 copy-done.6
  49.1 7.6 %shard_map.77 = (bf16[2,64,4096]{2,1,0:T(8,128)(2,1)}, bf16[2,64,1024]{2,1,0:T(8,128)(2,1)}, bf16[2,64,1024]{2,1,0:T(8,128)(2,1)}, f32[2,64,1024]{2,1,0:T(8,128)}) custom-call(s32[2]{0:T(128)} %add_convert_fusion.flags, s32[2,64,1]{2,1,0:T(8,128)} %broadcast_subtract_fusion.lo_ref, ...), custom_call_target="tpu_custom_call", output_to_operand_aliasing={{0}: (8, {}), {2}: (9, {}), {3}: (10, {})} | custom-call | flops 805306368 | bytes 1835008 | tf_op jit(solution)/shard_map/pallas_call | solution.py:208
  56.7 6.8 %collective-permute-start.6 = (bf16[2,64,1024]{2,1,0:T(8,128)(2,1)}, bf16[2,64,1024]{2,1,0:T(8,128)(2,1)S(1)}, u32[]{:S(2)}, u32[]{:S(2)}) collective-permute-start(bf16[2,64,1024]{2,1,0:T(8,128)(2,1)} %get-tuple-element.18), channel_id=1, source_target_pairs={{2,0},{3,1},{4,2},{5,3},{6,4},{7,5},{8,6},{9,7},{10,8},{11,9},{12,... | collective-permute-start | bytes 786440 | tf_op jit(solution)/shard_map/ppermute | solution.py:19
  63.6 0.8 %collective-permute-start.9 = (bf16[64,1024]{1,0:T(8,128)(2,1)S(1)}, bf16[64,1024]{1,0:T(8,128)(2,1)S(1)}, u32[]{:S(2)}, u32[]{:S(2)}) collective-permute-start(bf16[64,1024]{1,0:T(8,128)(2,1)S(1)} %slice_bitcast_fusion.3), channel_id=1, source_target_pairs={{510,511}} | collective-permute-start | bytes 393224 | tf_op jit(solution)/shard_map/ppermute | solution.py:259
  64.6 2.1 %collective-permute-start.10 = (bf16[64,1024]{1,0:T(8,128)(2,1)S(1)}, bf16[64,1024]{1,0:T(8,128)(2,1)S(1)}, u32[]{:S(2)}, u32[]{:S(2)}) collective-permute-start(bf16[64,1024]{1,0:T(8,128)(2,1)S(1)} %fusion.8), channel_id=1, source_target_pairs={{0,1},{1,2},{2,3},{3,4},{4,5},{5,6},{6,7},{7,8},{8,9},{9,10},{10,1... | collective-permute-start | bytes 393224 | tf_op jit(solution)/shard_map/ppermute | solution.py:19
  66.6 1.4 %collective-permute-done.6 = bf16[2,64,1024]{2,1,0:T(8,128)(2,1)S(1)} collective-permute-done((bf16[2,64,1024]{2,1,0:T(8,128)(2,1)}, bf16[2,64,1024]{2,1,0:T(8,128)(2,1)S(1)}, u32[]{:S(2)}, u32[]{:S(2)}) %collective-permute-start.6) | collective-permute-done | bytes 262176 | tf_op jit(solution)/shard_map/ppermute | solution.py:19
  68.1 6.4 %collective-permute-start.7 = (bf16[64,1024]{1,0:T(8,128)(2,1)S(1)}, bf16[64,1024]{1,0:T(8,128)(2,1)S(1)}, u32[]{:S(2)}, u32[]{:S(2)}) collective-permute-start(bf16[64,1024]{1,0:T(8,128)(2,1)S(1)} %fusion.9), channel_id=1, source_target_pairs={{1,0},{2,1},{3,2},{4,3},{5,4},{6,5},{7,6},{8,7},{9,8},{10,9},{11,1... | collective-permute-start | bytes 393224 | tf_op jit(solution)/shard_map/ppermute | solution.py:19
  74.6 1.5 %collective-permute-done.10 = bf16[64,1024]{1,0:T(8,128)(2,1)S(1)} collective-permute-done((bf16[64,1024]{1,0:T(8,128)(2,1)S(1)}, bf16[64,1024]{1,0:T(8,128)(2,1)S(1)}, u32[]{:S(2)}, u32[]{:S(2)}) %collective-permute-start.10) | collective-permute-done | bytes 131104 | tf_op jit(solution)/shard_map/ppermute | solution.py:19
  76.1 1.1 %collective-permute-done.7 = bf16[64,1024]{1,0:T(8,128)(2,1)S(1)} collective-permute-done((bf16[64,1024]{1,0:T(8,128)(2,1)S(1)}, bf16[64,1024]{1,0:T(8,128)(2,1)S(1)}, u32[]{:S(2)}, u32[]{:S(2)}) %collective-permute-start.7) | collective-permute-done | bytes 131104 | tf_op jit(solution)/shard_map/ppermute | solution.py:19
  77.2 0.1 fusion.7
  77.4 0.7 slice_bitcast_fusion.1
  (41 shorter events, 0.9 us)
Async XLA Ops:
  0.6 18.3 %copy-start.1 = (bf16[1,2,64,512]{3,2,1,0:T(8,128)(2,1)S(1)}, bf16[1,2,64,512]{3,2,1,0:T(8,128)(2,1)}, u32[]{:S(2)}) copy-start(bf16[1,2,64,512]{3,2,1,0:T(8,128)(2,1)} %param.7) | copy-start | bytes 393220
  0.6 18.3 %copy-start.2 = (bf16[1,2,64,512]{3,2,1,0:T(8,128)(2,1)S(1)}, bf16[1,2,64,512]{3,2,1,0:T(8,128)(2,1)}, u32[]{:S(2)}) copy-start(bf16[1,2,64,512]{3,2,1,0:T(8,128)(2,1)} %param.6) | copy-start | bytes 393220
  1.6 17.3 %collective-permute-start.2 = (bf16[64,1024]{1,0:T(8,128)(2,1)S(1)}, bf16[64,1024]{1,0:T(8,128)(2,1)S(1)}, u32[]{:S(2)}, u32[]{:S(2)}) collective-permute-start(bf16[64,1024]{1,0:T(8,128)(2,1)S(1)} %bitcast.65), channel_id=1, source_target_pairs={{1,0},{2,1},{3,2},{4,3},{5,4},{6,5},{7,6},{8,7},{9,8},{10,9},{11,1... | collective-permute-start | bytes 393224 | tf_op jit(solution)/shard_map/ppermute | solution.py:19
  15.2 0.7 copy-start.11
  18.9 0.7 copy-start.4
  19.6 12.6 %collective-permute-start = (bf16[64,1024]{1,0:T(8,128)(2,1)S(1)}, bf16[64,1024]{1,0:T(8,128)(2,1)S(1)}, u32[]{:S(2)}, u32[]{:S(2)}) collective-permute-start(bf16[64,1024]{1,0:T(8,128)(2,1)S(1)} %bitcast.67), channel_id=1, source_target_pairs={{0,1},{1,2},{2,3},{3,4},{4,5},{5,6},{6,7},{7,8},{8,9},{9,10},{10,1... | collective-permute-start | bytes 393224 | tf_op jit(solution)/shard_map/ppermute | solution.py:19
  22.2 13.9 %collective-permute-start.4 = (bf16[64,1024]{1,0:T(8,128)(2,1)S(1)}, bf16[64,1024]{1,0:T(8,128)(2,1)S(1)}, u32[]{:S(2)}, u32[]{:S(2)}) collective-permute-start(bf16[64,1024]{1,0:T(8,128)(2,1)S(1)} %bitcast.68), channel_id=1, source_target_pairs={{511,510},{510,511}} | collective-permute-start | bytes 393224 | tf_op jit(solution)/shard_map/ppermute | solution.py:241
  22.8 13.2 %collective-permute-start.5 = (bf16[64,1024]{1,0:T(8,128)(2,1)S(1)}, bf16[64,1024]{1,0:T(8,128)(2,1)S(1)}, u32[]{:S(2)}, u32[]{:S(2)}) collective-permute-start(bf16[64,1024]{1,0:T(8,128)(2,1)S(1)} %bitcast.69), channel_id=1, source_target_pairs={{509,511}} | collective-permute-start | bytes 393224 | tf_op jit(solution)/shard_map/ppermute | solution.py:242
  23.6 14.6 %collective-permute-start.3 = (bf16[2,64,1024]{2,1,0:T(8,128)(2,1)S(1)}, bf16[2,64,1024]{2,1,0:T(8,128)(2,1)S(1)}, u32[]{:S(2)}, u32[]{:S(2)}) collective-permute-start(bf16[2,64,1024]{2,1,0:T(8,128)(2,1)S(1)} %pad_maximum_fusion.2), channel_id=1, source_target_pairs={{2,0},{3,1},{4,2},{5,3},{6,4},{7,5},{8,6},{9,7},{10,8},{11,9},{12,... | collective-permute-start | bytes 786440 | tf_op jit(solution)/shard_map/ppermute | solution.py:19
  32.2 0.7 copy-start.5
  32.8 15.6 %collective-permute-start.1 = (bf16[2,64,1024]{2,1,0:T(8,128)(2,1)S(1)}, bf16[2,64,1024]{2,1,0:T(8,128)(2,1)S(1)}, u32[]{:S(2)}, u32[]{:S(2)}) collective-permute-start(bf16[2,64,1024]{2,1,0:T(8,128)(2,1)S(1)} %pad_maximum_fusion.1), channel_id=1, source_target_pairs={{0,2},{1,3},{2,4},{3,5},{4,6},{5,7},{6,8},{7,9},{8,10},{9,11},{10,... | collective-permute-start | bytes 786440 | tf_op jit(solution)/shard_map/ppermute | solution.py:19
  36.0 2.1 %copy-start.8 = (bf16[64,1024]{1,0:T(8,128)(2,1)}, bf16[64,1024]{1,0:T(8,128)(2,1)S(1)}, u32[]{:S(2)}) copy-start(bf16[64,1024]{1,0:T(8,128)(2,1)S(1)} %collective-permute-done.4.turn2) | copy-start | bytes 393220
  36.1 2.1 %copy-start.9 = (bf16[64,1024]{1,0:T(8,128)(2,1)}, bf16[64,1024]{1,0:T(8,128)(2,1)S(1)}, u32[]{:S(2)}) copy-start(bf16[64,1024]{1,0:T(8,128)(2,1)S(1)} %collective-permute-done.5.turn3) | copy-start | bytes 393220
  38.1 0.7 copy-start.7
  46.5 17.9 %collective-permute-start.8 = (bf16[2,64,1024]{2,1,0:T(8,128)(2,1)}, bf16[2,64,1024]{2,1,0:T(8,128)(2,1)S(1)}, u32[]{:S(2)}, u32[]{:S(2)}) collective-permute-start(bf16[2,64,1024]{2,1,0:T(8,128)(2,1)} %get-tuple-element.20), channel_id=1, source_target_pairs={{0,2},{1,3},{2,4},{3,5},{4,6},{5,7},{6,8},{7,9},{8,10},{9,11},{10,... | collective-permute-start | bytes 786440 | tf_op jit(solution)/shard_map/ppermute | solution.py:19
  48.4 0.7 copy-start.6
  49.1 14.4 %copy-start.10 = (bf16[2,64,1024]{2,1,0:T(8,128)(2,1)S(1)}, bf16[2,64,1024]{2,1,0:T(8,128)(2,1)}, u32[]{:S(2)}) copy-start(bf16[2,64,1024]{2,1,0:T(8,128)(2,1)} %get-tuple-element.20) | copy-start | bytes 786436
  56.7 11.3 %collective-permute-start.6 = (bf16[2,64,1024]{2,1,0:T(8,128)(2,1)}, bf16[2,64,1024]{2,1,0:T(8,128)(2,1)S(1)}, u32[]{:S(2)}, u32[]{:S(2)}) collective-permute-start(bf16[2,64,1024]{2,1,0:T(8,128)(2,1)} %get-tuple-element.18), channel_id=1, source_target_pairs={{2,0},{3,1},{4,2},{5,3},{6,4},{7,5},{8,6},{9,7},{10,8},{11,9},{12,... | collective-permute-start | bytes 786440 | tf_op jit(solution)/shard_map/ppermute | solution.py:19
  63.6 1.0 %copy-start.3 = (bf16[2,64,1024]{2,1,0:T(8,128)(2,1)S(1)}, bf16[2,64,1024]{2,1,0:T(8,128)(2,1)}, u32[]{:S(2)}) copy-start(bf16[2,64,1024]{2,1,0:T(8,128)(2,1)} %get-tuple-element.19) | copy-start | bytes 786436
  63.6 11.0 %collective-permute-start.9 = (bf16[64,1024]{1,0:T(8,128)(2,1)S(1)}, bf16[64,1024]{1,0:T(8,128)(2,1)S(1)}, u32[]{:S(2)}, u32[]{:S(2)}) collective-permute-start(bf16[64,1024]{1,0:T(8,128)(2,1)S(1)} %slice_bitcast_fusion.3), channel_id=1, source_target_pairs={{510,511}} | collective-permute-start | bytes 393224 | tf_op jit(solution)/shard_map/ppermute | solution.py:259
  64.6 12.6 %copy-start = (f32[2,64,1024]{2,1,0:T(8,128)S(1)}, f32[2,64,1024]{2,1,0:T(8,128)}, u32[]{:S(2)}) copy-start(f32[2,64,1024]{2,1,0:T(8,128)} %get-tuple-element.17) | copy-start | bytes 1572868
  64.6 11.5 %collective-permute-start.10 = (bf16[64,1024]{1,0:T(8,128)(2,1)S(1)}, bf16[64,1024]{1,0:T(8,128)(2,1)S(1)}, u32[]{:S(2)}, u32[]{:S(2)}) collective-permute-start(bf16[64,1024]{1,0:T(8,128)(2,1)S(1)} %fusion.8), channel_id=1, source_target_pairs={{0,1},{1,2},{2,3},{3,4},{4,5},{5,6},{6,7},{7,8},{8,9},{9,10},{10,1... | collective-permute-start | bytes 393224 | tf_op jit(solution)/shard_map/ppermute | solution.py:19
  68.1 9.1 %collective-permute-start.7 = (bf16[64,1024]{1,0:T(8,128)(2,1)S(1)}, bf16[64,1024]{1,0:T(8,128)(2,1)S(1)}, u32[]{:S(2)}, u32[]{:S(2)}) collective-permute-start(bf16[64,1024]{1,0:T(8,128)(2,1)S(1)} %fusion.9), channel_id=1, source_target_pairs={{1,0},{2,1},{3,2},{4,3},{5,4},{6,5},{7,6},{8,7},{9,8},{10,9},{11,1... | collective-permute-start | bytes 393224 | tf_op jit(solution)/shard_map/ppermute | solution.py:19

commit v9 on v6

--- a/solution.py
+++ b/solution.py
@@ -64,7 +64,7 @@
 
 def late_kernel(
     flags, lo_ref, q_ref, do_ref, kv, l1, l2, turn2, turn3,
-    dq_ref, a_l, p2_ref, p3_ref, kept, *, groups, group_size
+    dq_ref, s0, s1, s2, p3_ref, kept, *, groups, group_size
 ):
     at_top = flags[0] != 0
     below_top = flags[1] != 0
@@ -87,12 +87,7 @@
             return
         if j < 3:
             kept[j, :, cols] = value
-        if j == 0:
-            a_l[1, :, cols] = value.astype(a_l.dtype)
-        elif j == 1:
-            a_l[0, :, cols] = value.astype(a_l.dtype)
-        elif j == 2:
-            p2_ref[0, :, cols] = value.astype(p2_ref.dtype)
+            (s0, s1, s2)[j][:, cols] = value.astype(s0.dtype)
         else:
             p3_ref[0, :, cols] = value
 
@@ -100,10 +95,10 @@
 
 
 def early_kernel(
-    flags, lo_ref, q_ref, do_ref, kv, e1, e2, kept, dq_in, p2_in, p3_in,
-    dq_ref, a_e, p2_ref, p3_ref, *, groups, group_size
+    flags, lo_ref, q_ref, do_ref, kv, e1, e2, kept, dq_in, p3_in,
+    dq_ref, s0, s1, s2, p3_ref, *, groups, group_size
 ):
-    del dq_in, p2_in, p3_in
+    del dq_in, p3_in
     at_top = flags[0] != 0
     below_top = flags[1] != 0
 
@@ -118,13 +113,13 @@
             return
         zero = jnp.zeros_like(value)
         if j == 0:
-            a_e[1, :, cols] = value.astype(a_e.dtype)
+            s0[:, cols] = value.astype(s0.dtype)
         elif j == 1:
             merged = value + jnp.where(at_top, kept[0, :, cols], zero)
-            a_e[0, :, cols] = merged.astype(a_e.dtype)
+            s1[:, cols] = merged.astype(s1.dtype)
         elif j == 2:
             merged = value + jnp.where(at_top, kept[1, :, cols], zero)
-            p2_ref[0, :, cols] = merged.astype(p2_ref.dtype)
+            s2[:, cols] = merged.astype(s2.dtype)
         else:
             merged = (
                 value
@@ -165,32 +160,33 @@
     p3_shape = jax.ShapeDtypeStruct((halves, half_rows, kv2), jnp.float32)
 
     q_spec, lo_spec, part_spec = half_specs(1)
-    dq, a_l, p2, p3, kept = pl.pallas_call(
+    slot_shape = jax.ShapeDtypeStruct((half_rows, kv2), jnp.bfloat16)
+    dq, l0, l1p, l2p, p3, kept = pl.pallas_call(
         functools.partial(late_kernel, groups=groups, group_size=group_size),
         grid=(1,),
         in_specs=[smem, lo_spec, q_spec, q_spec, pair_spec, one_spec, pair_spec, one_spec, one_spec],
-        out_specs=[q_spec, pair_spec, part_spec, part_spec, kept_spec],
+        out_specs=[q_spec, one_spec, one_spec, one_spec, part_spec, kept_spec],
         out_shape=[
-            dq_shape, pair, p2_shape, p3_shape,
+            dq_shape, slot_shape, slot_shape, slot_shape, p3_shape,
             jax.ShapeDtypeStruct((3, half_rows, kv2), jnp.float32),
         ],
         cost_estimate=cost,
     )(flags, lo, q, do, kv, l1, l2, turn2, turn3)
 
     q_spec, lo_spec, part_spec = half_specs(0)
-    dq, a_e, p2, p3 = pl.pallas_call(
+    dq, e0, e1p, e2p, p3 = pl.pallas_call(
         functools.partial(early_kernel, groups=groups, group_size=group_size),
         grid=(1,),
         in_specs=[
             smem, lo_spec, q_spec, q_spec, pair_spec, one_spec, pair_spec, kept_spec,
-            anywhere, anywhere, anywhere,
+            anywhere, anywhere,
         ],
-        out_specs=[q_spec, pair_spec, part_spec, part_spec],
-        out_shape=[dq_shape, pair, p2_shape, p3_shape],
-        input_output_aliases={8: 0, 9: 2, 10: 3},
+        out_specs=[q_spec, one_spec, one_spec, one_spec, part_spec],
+        out_shape=[dq_shape, slot_shape, slot_shape, slot_shape, p3_shape],
+        input_output_aliases={8: 0, 9: 4},
         cost_estimate=cost,
-    )(flags, lo, q, do, kv, e1, e2, kept, dq, p2, p3)
-    return dq, a_e, a_l, p2, p3
+    )(flags, lo, q, do, kv, e1, e2, kept, dq, p3)
+    return dq, (e0, e1p, e2p), (l0, l1p, l2p), p3
 
 
 def on_device(query, keys, values, grad_out, lengths):
@@ -220,17 +216,20 @@
     lo = (doc_start - (block_ids[:, None] - REACH) * half_rows).astype(jnp.int32)[:, :, None]
     flags = jnp.stack([at_top, below_top]).astype(jnp.int32)
 
-    dq, a_e, a_l, p2, p3 = window_grads(flags, lo, q, do, kv, e1, e2, l1, l2, turn2, turn3)
-
+    dq, early_parts, late_parts, p3 = window_grads(
+        flags, lo, q, do, kv, e1, e2, l1, l2, turn2, turn3
+    )
+
+    f32 = jnp.float32
     zero = jnp.zeros_like(p3[0])
-    link = jnp.bfloat16
-    a_e = shifted(a_e, -2).astype(jnp.float32)
-    back = lax.ppermute(a_l[0], AXIS, [(n - 2, n - 1)]).astype(jnp.float32)
-    a_l = shifted(a_l, 2).astype(jnp.float32)
-    b_e = shifted((p2[0].astype(jnp.float32) + a_e[1]).astype(link), -1).astype(jnp.float32)
-    b_l = shifted((p2[1].astype(jnp.float32) + a_l[1]).astype(link), 1).astype(jnp.float32)
-    final_early = p3[0] + a_e[0] + b_e + jnp.where(at_top, a_l[1] + back, zero)
-    final_late = p3[1] + a_l[0] + b_l
+    from_right = [shifted(early_parts[2 - k], -(k + 1)).astype(f32) for k in range(3)]
+    from_left = [shifted(late_parts[2 - k], k + 1).astype(f32) for k in range(3)]
+    back2 = lax.ppermute(late_parts[1], AXIS, [(n - 2, n - 1)]).astype(f32)
+    back3 = lax.ppermute(late_parts[0], AXIS, [(n - 3, n - 1)]).astype(f32)
+    final_early = p3[0] + from_right[0] + from_right[1] + from_right[2] + jnp.where(
+        at_top, back2 + back3, zero
+    )
+    final_late = p3[1] + from_left[0] + from_left[1] + from_left[2]
     final = jnp.stack([final_early, final_late])
     grad_keys = final[:, :, :kv_width].astype(jnp.bfloat16).reshape(keys.shape)
     grad_values = final[:, :, kv_width:].astype(jnp.bfloat16).reshape(values.shape)

time: 75.9 us -> 84.7 us (1.12)
  starting transfers between devices: 45.3 us -> 52.4 us
  waiting for transfers between devices: 8.07 us -> 9.37 us
  other arithmetic: 4.15 us -> 5.09 us
    ppermute x8 -> x10, starting transfers between devices: 43.2 us -> 49.8 us  [shifted(): return lax.ppermute(value, AXIS, pairs)]
    ppermute x8 -> x10, waiting for transfers between devices: 8.07 us -> 9.36 us  [shifted(): return lax.ppermute(value, AXIS, pairs)]
    another operation x1, other arithmetic: 0.14 us -> 1.22 us  [on_device(): final = jnp.stack([final_early, final_late])]
    unnamed x24 -> x18, local copies, waits for them, and re-layouts: 3.36 us -> 2.58 us
  transfers between devices with their start and end apart: 11 -> 14, of which waited for: 5 -> 3; matrix products, arithmetic and copies ran while one was open for 4% -> 4% of each run, Pallas kernels for 16% -> 15%
where the time goes in v9:
time: 84.7 us; the launch traced here: 83.7 us
  starting transfers between devices  52.4 us (62%)
  Pallas kernels  12.3 us (15%)
  waiting for transfers between devices  9.37 us (11%)
  other arithmetic  5.09 us (6%)
  local copies, waits for them, and re-layouts  3.59 us (4%)
  between operations  0.92 us (1%)
    ppermute x10, starting transfers between devices, shifted(): return lax.ppermute(value, AXIS, pairs)  49.8 us
    ppermute x10, waiting for transfers between devices, shifted(): return lax.ppermute(value, AXIS, pairs)  9.36 us
    pallas_call x1, Pallas kernels, window_grads(): pl.pallas_call(functools.partial(late_kernel, groups=groups, group_size=g...  6.19 us
    pallas_call x1, Pallas kernels, window_grads(): pl.pallas_call(functools.partial(early_kernel, groups=groups, group_size=...  6.1 us
    unnamed x18, local copies, waits for them, and re-layouts  2.58 us
  transfers between devices with their start and end apart: 14, of which 3 were waited for; matrix products, arithmetic and copies ran while one was open for 4% of the time, Pallas kernels for 15%

profile of v9, /device:TPU:6, one launch (start us, length us, event | category | flops | bytes accessed | tf_op | source)
XLA Modules:
  0.0 83.7 jit_solution(10173993317172661882)
XLA Ops:
  0.7 0.9 %fusion.8 = bf16[1,64,1024]{2,1,0:T(8,128)(2,1)S(1)} fusion(bf16[2,64,512]{2,1,0:T(8,128)(2,1)} %bitcast.52, bf16[2,64,512]{2,1,0:T(8,128)(2,1)} %bitcast.49), kind=kLoop, calls=%fused_computation.19 | loop fusion | flops 262144 | bytes 393216 | tf_op jit(solution)/shard_map/concatenate | solution.py:199
  1.6 13.6 %collective-permute-start.2 = (bf16[64,1024]{1,0:T(8,128)(2,1)S(1)}, bf16[64,1024]{1,0:T(8,128)(2,1)S(1)}, u32[]{:S(2)}, u32[]{:S(2)}) collective-permute-start(bf16[64,1024]{1,0:T(8,128)(2,1)S(1)} %bitcast.57), channel_id=1, source_target_pairs={{1,0},{2,1},{3,2},{4,3},{5,4},{6,5},{7,6},{8,7},{9,8},{10,9},{11,1... | collective-permute-start | bytes 393224 | tf_op jit(solution)/shard_map/ppermute | solution.py:19
  15.3 0.6 copy-done.8
  15.9 0.3 reduce-window.9
  16.3 0.1 slice_reduce_fusion
  16.5 0.2 select_reduce_fusion
  16.9 2.0 %collective-permute-done.2.l1 = bf16[64,1024]{1,0:T(8,128)(2,1)S(1)} collective-permute-done((bf16[64,1024]{1,0:T(8,128)(2,1)S(1)}, bf16[64,1024]{1,0:T(8,128)(2,1)S(1)}, u32[]{:S(2)}, u32[]{:S(2)}) %collective-permute-start.2) | collective-permute-done | bytes 131104 | tf_op jit(solution)/shard_map/ppermute | solution.py:19
  19.0 0.6 copy-done.2
  19.6 1.9 %collective-permute-start = (bf16[64,1024]{1,0:T(8,128)(2,1)S(1)}, bf16[64,1024]{1,0:T(8,128)(2,1)S(1)}, u32[]{:S(2)}, u32[]{:S(2)}) collective-permute-start(bf16[64,1024]{1,0:T(8,128)(2,1)S(1)} %bitcast.58), channel_id=1, source_target_pairs={{0,1},{1,2},{2,3},{3,4},{4,5},{5,6},{6,7},{7,8},{8,9},{9,10},{10,1... | collective-permute-start | bytes 393224 | tf_op jit(solution)/shard_map/ppermute | solution.py:19
  21.5 0.7 broadcast_subtract_fusion.lo_ref
  22.2 0.7 collective-permute-start.4
  22.9 0.7 collective-permute-start.5
  23.6 8.6 %collective-permute-start.3 = (bf16[2,64,1024]{2,1,0:T(8,128)(2,1)S(1)}, bf16[2,64,1024]{2,1,0:T(8,128)(2,1)S(1)}, u32[]{:S(2)}, u32[]{:S(2)}) collective-permute-start(bf16[2,64,1024]{2,1,0:T(8,128)(2,1)S(1)} %pad_maximum_fusion.2), channel_id=1, source_target_pairs={{2,0},{3,1},{4,2},{5,3},{6,4},{7,5},{8,6},{9,7},{10,8},{11,9},{12,... | collective-permute-start | bytes 786440 | tf_op jit(solution)/shard_map/ppermute | solution.py:19
  32.2 0.6 copy-done.3
  32.8 1.9 %collective-permute-start.1 = (bf16[2,64,1024]{2,1,0:T(8,128)(2,1)S(1)}, bf16[2,64,1024]{2,1,0:T(8,128)(2,1)S(1)}, u32[]{:S(2)}, u32[]{:S(2)}) collective-permute-start(bf16[2,64,1024]{2,1,0:T(8,128)(2,1)S(1)} %pad_maximum_fusion.1), channel_id=1, source_target_pairs={{0,2},{1,3},{2,4},{3,5},{4,6},{5,7},{6,8},{7,9},{8,10},{9,11},{10,... | collective-permute-start | bytes 786440 | tf_op jit(solution)/shard_map/ppermute | solution.py:19
  34.8 0.6 add_convert_fusion.flags
  35.3 0.7 pad_maximum_fusion.kv
  36.1 2.1 %collective-permute-done.3.l2 = bf16[2,64,1024]{2,1,0:T(8,128)(2,1)S(1)} collective-permute-done((bf16[2,64,1024]{2,1,0:T(8,128)(2,1)S(1)}, bf16[2,64,1024]{2,1,0:T(8,128)(2,1)S(1)}, u32[]{:S(2)}, u32[]{:S(2)}) %collective-permute-start.3) | collective-permute-done | bytes 262176 | tf_op jit(solution)/shard_map/ppermute | solution.py:19
  38.1 0.7 copy-done.4
  38.8 6.2 %shard_map.76 = (bf16[2,64,4096]{2,1,0:T(8,128)(2,1)}, bf16[64,1024]{1,0:T(8,128)(2,1)}, bf16[64,1024]{1,0:T(8,128)(2,1)}, bf16[64,1024]{1,0:T(8,128)(2,1)}, f32...) custom-call(s32[2]{0:T(128)} %add_convert_fusion.flags, s32[2,64,1]{2,1,0:T(8,128)} %broadcast_subtract_fusion.lo_ref, ...), custom_call_target="tpu_custom_call" | custom-call | flops 805306368 | bytes 1835008 | tf_op jit(solution)/shard_map/pallas_call | solution.py:164
  45.0 1.9 %collective-permute-start.11 = (bf16[64,1024]{1,0:T(8,128)(2,1)}, bf16[64,1024]{1,0:T(8,128)(2,1)S(1)}, u32[]{:S(2)}, u32[]{:S(2)}) collective-permute-start(bf16[64,1024]{1,0:T(8,128)(2,1)} %get-tuple-element.24), channel_id=1, source_target_pairs={{0,1},{1,2},{2,3},{3,4},{4,5},{5,6},{6,7},{7,8},{8,9},{9,10},{10,1... | collective-permute-start | bytes 393224 | tf_op jit(solution)/shard_map/ppermute | solution.py:19
  46.9 1.9 %collective-permute-start.12 = (bf16[64,1024]{1,0:T(8,128)(2,1)}, bf16[64,1024]{1,0:T(8,128)(2,1)S(1)}, u32[]{:S(2)}, u32[]{:S(2)}) collective-permute-start(bf16[64,1024]{1,0:T(8,128)(2,1)} %get-tuple-element.22), channel_id=1, source_target_pairs={{0,2},{1,3},{2,4},{3,5},{4,6},{5,7},{6,8},{7,9},{8,10},{9,11},{10,... | collective-permute-start | bytes 393224 | tf_op jit(solution)/shard_map/ppermute | solution.py:19
  48.9 0.7 collective-permute-start.9
  49.5 2.1 %collective-permute-start.13 = (bf16[64,1024]{1,0:T(8,128)(2,1)}, bf16[64,1024]{1,0:T(8,128)(2,1)S(1)}, u32[]{:S(2)}, u32[]{:S(2)}) collective-permute-start(bf16[64,1024]{1,0:T(8,128)(2,1)} %get-tuple-element.23), channel_id=1, source_target_pairs={{0,3},{1,4},{2,5},{3,6},{4,7},{5,8},{6,9},{7,10},{8,11},{9,12},{10... | collective-permute-start | bytes 393224 | tf_op jit(solution)/shard_map/ppermute | solution.py:19
  51.6 0.7 collective-permute-start.10
  52.3 6.1 %shard_map.77 = (bf16[2,64,4096]{2,1,0:T(8,128)(2,1)}, bf16[64,1024]{1,0:T(8,128)(2,1)}, bf16[64,1024]{1,0:T(8,128)(2,1)}, bf16[64,1024]{1,0:T(8,128)(2,1)}, f32[2,64,1024]{2,1,0:T(8,128)}) custom-call(s32[2]{0:T(128)} %add_convert_fusion.flags, s32[2,64,1]{2,1,0:T(8,128)} %broadcast_subtract_fusion.lo_ref, ...), custom_call_target="tpu_custom_call", output_to_operand_aliasing={{0}: (8, {}), {4}: (9, {})} | custom-call | flops 805306368 | bytes 1835008 | tf_op jit(solution)/shard_map/pallas_call | solution.py:177
  58.4 7.7 %collective-permute-start.6 = (bf16[64,1024]{1,0:T(8,128)(2,1)}, bf16[64,1024]{1,0:T(8,128)(2,1)S(1)}, u32[]{:S(2)}, u32[]{:S(2)}) collective-permute-start(bf16[64,1024]{1,0:T(8,128)(2,1)} %get-tuple-element.19), channel_id=1, source_target_pairs={{1,0},{2,1},{3,2},{4,3},{5,4},{6,5},{7,6},{8,7},{9,8},{10,9},{11,1... | collective-permute-start | bytes 393224 | tf_op jit(solution)/shard_map/ppermute | solution.py:19
  66.2 4.7 %collective-permute-start.7 = (bf16[64,1024]{1,0:T(8,128)(2,1)}, bf16[64,1024]{1,0:T(8,128)(2,1)S(1)}, u32[]{:S(2)}, u32[]{:S(2)}) collective-permute-start(bf16[64,1024]{1,0:T(8,128)(2,1)} %get-tuple-element.20), channel_id=1, source_target_pairs={{2,0},{3,1},{4,2},{5,3},{6,4},{7,5},{8,6},{9,7},{10,8},{11,9},{12,... | collective-permute-start | bytes 393224 | tf_op jit(solution)/shard_map/ppermute | solution.py:19
  70.9 5.5 %collective-permute-start.8 = (bf16[64,1024]{1,0:T(8,128)(2,1)}, bf16[64,1024]{1,0:T(8,128)(2,1)S(1)}, u32[]{:S(2)}, u32[]{:S(2)}) collective-permute-start(bf16[64,1024]{1,0:T(8,128)(2,1)} %get-tuple-element.21), channel_id=1, source_target_pairs={{3,0},{4,1},{5,2},{6,3},{7,4},{8,5},{9,6},{10,7},{11,8},{12,9},{13... | collective-permute-start | bytes 393224 | tf_op jit(solution)/shard_map/ppermute | solution.py:19
  76.4 5.3 %collective-permute-done.8 = bf16[64,1024]{1,0:T(8,128)(2,1)S(1)} collective-permute-done((bf16[64,1024]{1,0:T(8,128)(2,1)}, bf16[64,1024]{1,0:T(8,128)(2,1)S(1)}, u32[]{:S(2)}, u32[]{:S(2)}) %collective-permute-start.8) | collective-permute-done | bytes 131104 | tf_op jit(solution)/shard_map/ppermute | solution.py:19
  81.7 1.2 %fusion.6 = (bf16[1,64,1024]{2,1,0:T(8,128)(2,1)S(1)}, bf16[1,64,1024]{2,1,0:T(8,128)(2,1)S(1)}) fusion(bf16[64,1024]{1,0:T(8,128)(2,1)S(1)} %collective-permute-done.10, bf16[64,1024]{1,0:T(8,128)(2,1)S(1)} %collective-permute-done.9, bf16[64,1024]{1,0:T(8,128)(2,1)S(1)} %collective-permute-done.8, bf16[64,1024]{1,0:T(8,128)(2,1)S(1)} %collective-permute-done.7, ...), kind=kLoop, calls=%fused_computation.16 | loop fusion | flops 1245184 | bytes 1835009 | tf_op jit(solution)/shard_map/stack | solution.py:233
  83.0 0.7 slice_bitcast_fusion
  (36 shorter events, 0.7 us)
Async XLA Ops:
  0.6 18.3 %copy-start = (bf16[1,2,64,512]{3,2,1,0:T(8,128)(2,1)S(1)}, bf16[1,2,64,512]{3,2,1,0:T(8,128)(2,1)}, u32[]{:S(2)}) copy-start(bf16[1,2,64,512]{3,2,1,0:T(8,128)(2,1)} %param.7) | copy-start | bytes 393220
  0.6 18.3 %copy-start.1 = (bf16[1,2,64,512]{3,2,1,0:T(8,128)(2,1)S(1)}, bf16[1,2,64,512]{3,2,1,0:T(8,128)(2,1)}, u32[]{:S(2)}) copy-start(bf16[1,2,64,512]{3,2,1,0:T(8,128)(2,1)} %param.6) | copy-start | bytes 393220
  1.6 17.3 %collective-permute-start.2 = (bf16[64,1024]{1,0:T(8,128)(2,1)S(1)}, bf16[64,1024]{1,0:T(8,128)(2,1)S(1)}, u32[]{:S(2)}, u32[]{:S(2)}) collective-permute-start(bf16[64,1024]{1,0:T(8,128)(2,1)S(1)} %bitcast.57), channel_id=1, source_target_pairs={{1,0},{2,1},{3,2},{4,3},{5,4},{6,5},{7,6},{8,7},{9,8},{10,9},{11,1... | collective-permute-start | bytes 393224 | tf_op jit(solution)/shard_map/ppermute | solution.py:19
  15.2 0.7 copy-start.8
  18.9 0.7 copy-start.2
  19.6 12.6 %collective-permute-start = (bf16[64,1024]{1,0:T(8,128)(2,1)S(1)}, bf16[64,1024]{1,0:T(8,128)(2,1)S(1)}, u32[]{:S(2)}, u32[]{:S(2)}) collective-permute-start(bf16[64,1024]{1,0:T(8,128)(2,1)S(1)} %bitcast.58), channel_id=1, source_target_pairs={{0,1},{1,2},{2,3},{3,4},{4,5},{5,6},{6,7},{7,8},{8,9},{9,10},{10,1... | collective-permute-start | bytes 393224 | tf_op jit(solution)/shard_map/ppermute | solution.py:19
  22.2 13.9 %collective-permute-start.4 = (bf16[64,1024]{1,0:T(8,128)(2,1)S(1)}, bf16[64,1024]{1,0:T(8,128)(2,1)S(1)}, u32[]{:S(2)}, u32[]{:S(2)}) collective-permute-start(bf16[64,1024]{1,0:T(8,128)(2,1)S(1)} %bitcast.59), channel_id=1, source_target_pairs={{511,510},{510,511}} | collective-permute-start | bytes 393224 | tf_op jit(solution)/shard_map/ppermute | solution.py:206
  22.9 13.2 %collective-permute-start.5 = (bf16[64,1024]{1,0:T(8,128)(2,1)S(1)}, bf16[64,1024]{1,0:T(8,128)(2,1)S(1)}, u32[]{:S(2)}, u32[]{:S(2)}) collective-permute-start(bf16[64,1024]{1,0:T(8,128)(2,1)S(1)} %bitcast.60), channel_id=1, source_target_pairs={{509,511}} | collective-permute-start | bytes 393224 | tf_op jit(solution)/shard_map/ppermute | solution.py:207
  23.6 14.6 %collective-permute-start.3 = (bf16[2,64,1024]{2,1,0:T(8,128)(2,1)S(1)}, bf16[2,64,1024]{2,1,0:T(8,128)(2,1)S(1)}, u32[]{:S(2)}, u32[]{:S(2)}) collective-permute-start(bf16[2,64,1024]{2,1,0:T(8,128)(2,1)S(1)} %pad_maximum_fusion.2), channel_id=1, source_target_pairs={{2,0},{3,1},{4,2},{5,3},{6,4},{7,5},{8,6},{9,7},{10,8},{11,9},{12,... | collective-permute-start | bytes 786440 | tf_op jit(solution)/shard_map/ppermute | solution.py:19
  32.2 0.7 copy-start.3
  32.8 18.8 %collective-permute-start.1 = (bf16[2,64,1024]{2,1,0:T(8,128)(2,1)S(1)}, bf16[2,64,1024]{2,1,0:T(8,128)(2,1)S(1)}, u32[]{:S(2)}, u32[]{:S(2)}) collective-permute-start(bf16[2,64,1024]{2,1,0:T(8,128)(2,1)S(1)} %pad_maximum_fusion.1), channel_id=1, source_target_pairs={{0,2},{1,3},{2,4},{3,5},{4,6},{5,7},{6,8},{7,9},{8,10},{9,11},{10,... | collective-permute-start | bytes 786440 | tf_op jit(solution)/shard_map/ppermute | solution.py:19
  36.1 2.1 %copy-start.6 = (bf16[64,1024]{1,0:T(8,128)(2,1)}, bf16[64,1024]{1,0:T(8,128)(2,1)S(1)}, u32[]{:S(2)}) copy-start(bf16[64,1024]{1,0:T(8,128)(2,1)S(1)} %collective-permute-done.4.turn2) | copy-start | bytes 393220
  36.1 2.1 %copy-start.7 = (bf16[64,1024]{1,0:T(8,128)(2,1)}, bf16[64,1024]{1,0:T(8,128)(2,1)S(1)}, u32[]{:S(2)}) copy-start(bf16[64,1024]{1,0:T(8,128)(2,1)S(1)} %collective-permute-done.5.turn3) | copy-start | bytes 393220
  38.1 0.7 copy-start.4
  45.0 13.4 %collective-permute-start.11 = (bf16[64,1024]{1,0:T(8,128)(2,1)}, bf16[64,1024]{1,0:T(8,128)(2,1)S(1)}, u32[]{:S(2)}, u32[]{:S(2)}) collective-permute-start(bf16[64,1024]{1,0:T(8,128)(2,1)} %get-tuple-element.24), channel_id=1, source_target_pairs={{0,1},{1,2},{2,3},{3,4},{4,5},{5,6},{6,7},{7,8},{8,9},{9,10},{10,1... | collective-permute-start | bytes 393224 | tf_op jit(solution)/shard_map/ppermute | solution.py:19
  46.9 19.2 %collective-permute-start.12 = (bf16[64,1024]{1,0:T(8,128)(2,1)}, bf16[64,1024]{1,0:T(8,128)(2,1)S(1)}, u32[]{:S(2)}, u32[]{:S(2)}) collective-permute-start(bf16[64,1024]{1,0:T(8,128)(2,1)} %get-tuple-element.22), channel_id=1, source_target_pairs={{0,2},{1,3},{2,4},{3,5},{4,6},{5,7},{6,8},{7,9},{8,10},{9,11},{10,... | collective-permute-start | bytes 393224 | tf_op jit(solution)/shard_map/ppermute | solution.py:19
  48.9 22.0 %collective-permute-start.9 = (bf16[64,1024]{1,0:T(8,128)(2,1)}, bf16[64,1024]{1,0:T(8,128)(2,1)S(1)}, u32[]{:S(2)}, u32[]{:S(2)}) collective-permute-start(bf16[64,1024]{1,0:T(8,128)(2,1)} %get-tuple-element.22), channel_id=1, source_target_pairs={{510,511}} | collective-permute-start | bytes 393224 | tf_op jit(solution)/shard_map/ppermute | solution.py:227
  49.5 26.8 %collective-permute-start.13 = (bf16[64,1024]{1,0:T(8,128)(2,1)}, bf16[64,1024]{1,0:T(8,128)(2,1)S(1)}, u32[]{:S(2)}, u32[]{:S(2)}) collective-permute-start(bf16[64,1024]{1,0:T(8,128)(2,1)} %get-tuple-element.23), channel_id=1, source_target_pairs={{0,3},{1,4},{2,5},{3,6},{4,7},{5,8},{6,9},{7,10},{8,11},{9,12},{10... | collective-permute-start | bytes 393224 | tf_op jit(solution)/shard_map/ppermute | solution.py:19
  51.6 0.7 copy-start.5
  51.6 24.8 %collective-permute-start.10 = (bf16[64,1024]{1,0:T(8,128)(2,1)}, bf16[64,1024]{1,0:T(8,128)(2,1)S(1)}, u32[]{:S(2)}, u32[]{:S(2)}) collective-permute-start(bf16[64,1024]{1,0:T(8,128)(2,1)} %get-tuple-element.23), channel_id=1, source_target_pairs={{509,511}} | collective-permute-start | bytes 393224 | tf_op jit(solution)/shard_map/ppermute | solution.py:228
  58.4 18.0 %collective-permute-start.6 = (bf16[64,1024]{1,0:T(8,128)(2,1)}, bf16[64,1024]{1,0:T(8,128)(2,1)S(1)}, u32[]{:S(2)}, u32[]{:S(2)}) collective-permute-start(bf16[64,1024]{1,0:T(8,128)(2,1)} %get-tuple-element.19), channel_id=1, source_target_pairs={{1,0},{2,1},{3,2},{4,3},{5,4},{6,5},{7,6},{8,7},{9,8},{10,9},{11,1... | collective-permute-start | bytes 393224 | tf_op jit(solution)/shard_map/ppermute | solution.py:19
  66.2 10.3 %collective-permute-start.7 = (bf16[64,1024]{1,0:T(8,128)(2,1)}, bf16[64,1024]{1,0:T(8,128)(2,1)S(1)}, u32[]{:S(2)}, u32[]{:S(2)}) collective-permute-start(bf16[64,1024]{1,0:T(8,128)(2,1)} %get-tuple-element.20), channel_id=1, source_target_pairs={{2,0},{3,1},{4,2},{5,3},{6,4},{7,5},{8,6},{9,7},{10,8},{11,9},{12,... | collective-permute-start | bytes 393224 | tf_op jit(solution)/shard_map/ppermute | solution.py:19
  70.9 10.8 %collective-permute-start.8 = (bf16[64,1024]{1,0:T(8,128)(2,1)}, bf16[64,1024]{1,0:T(8,128)(2,1)S(1)}, u32[]{:S(2)}, u32[]{:S(2)}) collective-permute-start(bf16[64,1024]{1,0:T(8,128)(2,1)} %get-tuple-element.21), channel_id=1, source_target_pairs={{3,0},{4,1},{5,2},{6,3},{7,4},{8,5},{9,6},{10,7},{11,8},{12,9},{13... | collective-permute-start | bytes 393224 | tf_op jit(solution)/shard_map/ppermute | solution.py:19

commit v10 on v6

--- a/solution.py
+++ b/solution.py
@@ -64,7 +64,7 @@
 
 def late_kernel(
     flags, lo_ref, q_ref, do_ref, kv, l1, l2, turn2, turn3,
-    dq_ref, a_l, p2_ref, p3_ref, kept, *, groups, group_size
+    dq_ref, a_l, p2_ref, p3_ref, *, groups, group_size
 ):
     at_top = flags[0] != 0
     below_top = flags[1] != 0
@@ -85,14 +85,12 @@
         if kind == "dq":
             dq_ref[0, :, cols] = value
             return
-        if j < 3:
-            kept[j, :, cols] = value
         if j == 0:
             a_l[1, :, cols] = value.astype(a_l.dtype)
         elif j == 1:
             a_l[0, :, cols] = value.astype(a_l.dtype)
         elif j == 2:
-            p2_ref[0, :, cols] = value.astype(p2_ref.dtype)
+            p2_ref[:, cols] = value.astype(p2_ref.dtype)
         else:
             p3_ref[0, :, cols] = value
 
@@ -100,10 +98,10 @@
 
 
 def early_kernel(
-    flags, lo_ref, q_ref, do_ref, kv, e1, e2, kept, dq_in, p2_in, p3_in,
+    flags, lo_ref, q_ref, do_ref, kv, e1, e2, a_l, p2_late, dq_in, p3_in,
     dq_ref, a_e, p2_ref, p3_ref, *, groups, group_size
 ):
-    del dq_in, p2_in, p3_in
+    del dq_in, p3_in
     at_top = flags[0] != 0
     below_top = flags[1] != 0
 
@@ -117,19 +115,20 @@
             dq_ref[0, :, cols] = value
             return
         zero = jnp.zeros_like(value)
+        late0 = a_l[1, :, cols].astype(jnp.float32)
         if j == 0:
             a_e[1, :, cols] = value.astype(a_e.dtype)
         elif j == 1:
-            merged = value + jnp.where(at_top, kept[0, :, cols], zero)
+            merged = value + jnp.where(at_top, late0, zero)
             a_e[0, :, cols] = merged.astype(a_e.dtype)
         elif j == 2:
-            merged = value + jnp.where(at_top, kept[1, :, cols], zero)
-            p2_ref[0, :, cols] = merged.astype(p2_ref.dtype)
+            merged = value + jnp.where(at_top, a_l[0, :, cols].astype(jnp.float32), zero)
+            p2_ref[:, cols] = merged.astype(p2_ref.dtype)
         else:
             merged = (
                 value
-                + jnp.where(at_top, kept[2, :, cols], zero)
-                + jnp.where(below_top, kept[0, :, cols], zero)
+                + jnp.where(at_top, p2_late[:, cols].astype(jnp.float32), zero)
+                + jnp.where(below_top, late0, zero)
             )
             p3_ref[0, :, cols] = merged
 
@@ -156,7 +155,6 @@
 
     pair_spec = pl.BlockSpec((2, half_rows, kv2), lambda s: (0, 0, 0))
     one_spec = pl.BlockSpec((half_rows, kv2), lambda s: (0, 0))
-    kept_spec = pl.BlockSpec((3, half_rows, kv2), lambda s: (0, 0, 0))
     smem = pl.BlockSpec(memory_space=pltpu.SMEM)
     anywhere = pl.BlockSpec(memory_space=pl.ANY)
     pair = jax.ShapeDtypeStruct((2, half_rows, kv2), jnp.bfloat16)
@@ -165,32 +163,30 @@
     p3_shape = jax.ShapeDtypeStruct((halves, half_rows, kv2), jnp.float32)
 
     q_spec, lo_spec, part_spec = half_specs(1)
-    dq, a_l, p2, p3, kept = pl.pallas_call(
+    slot_shape = jax.ShapeDtypeStruct((half_rows, kv2), jnp.bfloat16)
+    dq, a_l, p2_late, p3 = pl.pallas_call(
         functools.partial(late_kernel, groups=groups, group_size=group_size),
         grid=(1,),
         in_specs=[smem, lo_spec, q_spec, q_spec, pair_spec, one_spec, pair_spec, one_spec, one_spec],
-        out_specs=[q_spec, pair_spec, part_spec, part_spec, kept_spec],
-        out_shape=[
-            dq_shape, pair, p2_shape, p3_shape,
-            jax.ShapeDtypeStruct((3, half_rows, kv2), jnp.float32),
-        ],
+        out_specs=[q_spec, pair_spec, one_spec, part_spec],
+        out_shape=[dq_shape, pair, slot_shape, p3_shape],
         cost_estimate=cost,
     )(flags, lo, q, do, kv, l1, l2, turn2, turn3)
 
     q_spec, lo_spec, part_spec = half_specs(0)
-    dq, a_e, p2, p3 = pl.pallas_call(
+    dq, a_e, p2_early, p3 = pl.pallas_call(
         functools.partial(early_kernel, groups=groups, group_size=group_size),
         grid=(1,),
         in_specs=[
-            smem, lo_spec, q_spec, q_spec, pair_spec, one_spec, pair_spec, kept_spec,
-            anywhere, anywhere, anywhere,
+            smem, lo_spec, q_spec, q_spec, pair_spec, one_spec, pair_spec, pair_spec, one_spec,
+            anywhere, anywhere,
         ],
-        out_specs=[q_spec, pair_spec, part_spec, part_spec],
-        out_shape=[dq_shape, pair, p2_shape, p3_shape],
-        input_output_aliases={8: 0, 9: 2, 10: 3},
+        out_specs=[q_spec, pair_spec, one_spec, part_spec],
+        out_shape=[dq_shape, pair, slot_shape, p3_shape],
+        input_output_aliases={9: 0, 10: 3},
         cost_estimate=cost,
-    )(flags, lo, q, do, kv, e1, e2, kept, dq, p2, p3)
-    return dq, a_e, a_l, p2, p3
+    )(flags, lo, q, do, kv, e1, e2, a_l, p2_late, dq, p3)
+    return dq, a_e, a_l, (p2_early, p2_late), p3
 
 
 def on_device(query, keys, values, grad_out, lengths):

time: 75.9 us -> 75.4 us (level)
    unnamed x24 -> x26, local copies, waits for them, and re-layouts: 3.36 us -> 3.3 us
where the time goes in v10:
time: 75.4 us; the launch traced here: 74.7 us
  starting transfers between devices  45.3 us (60%)
  Pallas kernels  11.9 us (16%)
  waiting for transfers between devices  8.09 us (11%)
  local copies, waits for them, and re-layouts  4.33 us (6%)
  other arithmetic  4.17 us (6%)
  between operations  0.94 us (1%)
    ppermute x8, starting transfers between devices, shifted(): return lax.ppermute(value, AXIS, pairs)  43.2 us
    ppermute x8, waiting for transfers between devices, shifted(): return lax.ppermute(value, AXIS, pairs)  8.08 us
    pallas_call x1, Pallas kernels, window_grads(): pl.pallas_call(functools.partial(early_kernel, groups=groups, group_size=...  5.97 us
    pallas_call x1, Pallas kernels, window_grads(): pl.pallas_call(functools.partial(late_kernel, groups=groups, group_size=g...  5.89 us
    unnamed x26, local copies, waits for them, and re-layouts  3.3 us
    concatenate x2, other arithmetic, on_device(): kv = jnp.concatenate([keys[0], values[0]], axis=2)  1.65 us
  transfers between devices with their start and end apart: 11, of which 5 were waited for; matrix products, arithmetic and copies ran while one was open for 4% of the time, Pallas kernels for 16%

profile of v10, /device:TPU:6, one launch (start us, length us, event | category | flops | bytes accessed | tf_op | source)
XLA Modules:
  0.0 74.7 jit_solution(17076892828139736011)
XLA Ops:
  0.7 0.9 %fusion.10 = bf16[1,64,1024]{2,1,0:T(8,128)(2,1)S(1)} fusion(bf16[2,64,512]{2,1,0:T(8,128)(2,1)} %bitcast.62, bf16[2,64,512]{2,1,0:T(8,128)(2,1)} %bitcast.59), kind=kLoop, calls=%fused_computation.24 | loop fusion | flops 262144 | bytes 393216 | tf_op jit(solution)/shard_map/concatenate | solution.py:199
  1.6 13.6 %collective-permute-start.2 = (bf16[64,1024]{1,0:T(8,128)(2,1)S(1)}, bf16[64,1024]{1,0:T(8,128)(2,1)S(1)}, u32[]{:S(2)}, u32[]{:S(2)}) collective-permute-start(bf16[64,1024]{1,0:T(8,128)(2,1)S(1)} %bitcast.66), channel_id=1, source_target_pairs={{1,0},{2,1},{3,2},{4,3},{5,4},{6,5},{7,6},{8,7},{9,8},{10,9},{11,1... | collective-permute-start | bytes 393224 | tf_op jit(solution)/shard_map/ppermute | solution.py:19
  15.3 0.6 copy-done.12
  15.9 0.3 reduce-window.9
  16.3 0.1 slice_reduce_fusion
  16.5 0.2 select_reduce_fusion
  16.9 2.0 %collective-permute-done.2.l1 = bf16[64,1024]{1,0:T(8,128)(2,1)S(1)} collective-permute-done((bf16[64,1024]{1,0:T(8,128)(2,1)S(1)}, bf16[64,1024]{1,0:T(8,128)(2,1)S(1)}, u32[]{:S(2)}, u32[]{:S(2)}) %collective-permute-start.2) | collective-permute-done | bytes 131104 | tf_op jit(solution)/shard_map/ppermute | solution.py:19
  19.0 0.6 copy-done.4
  19.6 1.9 %collective-permute-start = (bf16[64,1024]{1,0:T(8,128)(2,1)S(1)}, bf16[64,1024]{1,0:T(8,128)(2,1)S(1)}, u32[]{:S(2)}, u32[]{:S(2)}) collective-permute-start(bf16[64,1024]{1,0:T(8,128)(2,1)S(1)} %bitcast.68), channel_id=1, source_target_pairs={{0,1},{1,2},{2,3},{3,4},{4,5},{5,6},{6,7},{7,8},{8,9},{9,10},{10,1... | collective-permute-start | bytes 393224 | tf_op jit(solution)/shard_map/ppermute | solution.py:19
  21.5 0.7 broadcast_subtract_fusion.lo_ref
  22.2 0.7 collective-permute-start.4
  22.8 0.7 collective-permute-start.5
  23.6 8.6 %collective-permute-start.3 = (bf16[2,64,1024]{2,1,0:T(8,128)(2,1)S(1)}, bf16[2,64,1024]{2,1,0:T(8,128)(2,1)S(1)}, u32[]{:S(2)}, u32[]{:S(2)}) collective-permute-start(bf16[2,64,1024]{2,1,0:T(8,128)(2,1)S(1)} %pad_maximum_fusion.2), channel_id=1, source_target_pairs={{2,0},{3,1},{4,2},{5,3},{6,4},{7,5},{8,6},{9,7},{10,8},{11,9},{12,... | collective-permute-start | bytes 786440 | tf_op jit(solution)/shard_map/ppermute | solution.py:19
  32.2 0.6 copy-done.5
  32.8 1.9 %collective-permute-start.1 = (bf16[2,64,1024]{2,1,0:T(8,128)(2,1)S(1)}, bf16[2,64,1024]{2,1,0:T(8,128)(2,1)S(1)}, u32[]{:S(2)}, u32[]{:S(2)}) collective-permute-start(bf16[2,64,1024]{2,1,0:T(8,128)(2,1)S(1)} %pad_maximum_fusion.1), channel_id=1, source_target_pairs={{0,2},{1,3},{2,4},{3,5},{4,6},{5,7},{6,8},{7,9},{8,10},{9,11},{10,... | collective-permute-start | bytes 786440 | tf_op jit(solution)/shard_map/ppermute | solution.py:19
  34.8 0.6 add_convert_fusion.1.flags
  35.3 0.7 pad_maximum_fusion.kv
  36.1 2.0 %collective-permute-done.3.l2 = bf16[2,64,1024]{2,1,0:T(8,128)(2,1)S(1)} collective-permute-done((bf16[2,64,1024]{2,1,0:T(8,128)(2,1)S(1)}, bf16[2,64,1024]{2,1,0:T(8,128)(2,1)S(1)}, u32[]{:S(2)}, u32[]{:S(2)}) %collective-permute-start.3) | collective-permute-done | bytes 262176 | tf_op jit(solution)/shard_map/ppermute | solution.py:19
  38.1 0.7 copy-done.8
  38.8 5.9 %shard_map.76 = (bf16[2,64,4096]{2,1,0:T(8,128)(2,1)}, bf16[2,64,1024]{2,1,0:T(8,128)(2,1)}, bf16[64,1024]{1,0:T(8,128)(2,1)}, f32[2,64,1024]{2,1,0:T(8,128)}) custom-call(s32[2]{0:T(128)} %add_convert_fusion.1.flags, s32[2,64,1]{2,1,0:T(8,128)} %broadcast_subtract_fusion.lo_ref, bf16[2,64,4096]{2,1,0:T(8,128)(2,1)} %bitcast.55, ...), custom_call_target="tpu_custom_call" | custom-call | flops 805306368 | bytes 1835008 | tf_op jit(solution)/shard_map/pallas_call | solution.py:167
  44.7 1.9 %collective-permute-start.8 = (bf16[2,64,1024]{2,1,0:T(8,128)(2,1)}, bf16[2,64,1024]{2,1,0:T(8,128)(2,1)S(1)}, u32[]{:S(2)}, u32[]{:S(2)}) collective-permute-start(bf16[2,64,1024]{2,1,0:T(8,128)(2,1)} %get-tuple-element.11.a_l), channel_id=1, source_target_pairs={{0,2},{1,3},{2,4},{3,5},{4,6},{5,7},{6,8},{7,9},{8,10},{9,11},{10,... | collective-permute-start | bytes 786440 | tf_op jit(solution)/shard_map/ppermute | solution.py:19
  46.7 0.7 copy-done.7
  47.4 6.0 %shard_map.77 = (bf16[2,64,4096]{2,1,0:T(8,128)(2,1)}, bf16[2,64,1024]{2,1,0:T(8,128)(2,1)}, bf16[64,1024]{1,0:T(8,128)(2,1)}, f32[2,64,1024]{2,1,0:T(8,128)}) custom-call(s32[2]{0:T(128)} %add_convert_fusion.1.flags, s32[2,64,1]{2,1,0:T(8,128)} %broadcast_subtract_fusion.lo_ref, ...), custom_call_target="tpu_custom_call", output_to_operand_aliasing={{0}: (9, {}), {3}: (10, {})} | custom-call | flops 805306368 | bytes 1835008 | tf_op jit(solution)/shard_map/pallas_call | solution.py:177
  53.3 6.8 %collective-permute-start.6 = (bf16[2,64,1024]{2,1,0:T(8,128)(2,1)}, bf16[2,64,1024]{2,1,0:T(8,128)(2,1)S(1)}, u32[]{:S(2)}, u32[]{:S(2)}) collective-permute-start(bf16[2,64,1024]{2,1,0:T(8,128)(2,1)} %get-tuple-element.17), channel_id=1, source_target_pairs={{2,0},{3,1},{4,2},{5,3},{6,4},{7,5},{8,6},{9,7},{10,8},{11,9},{12,... | collective-permute-start | bytes 786440 | tf_op jit(solution)/shard_map/ppermute | solution.py:19
  60.2 0.8 %collective-permute-start.9 = (bf16[64,1024]{1,0:T(8,128)(2,1)S(1)}, bf16[64,1024]{1,0:T(8,128)(2,1)S(1)}, u32[]{:S(2)}, u32[]{:S(2)}) collective-permute-start(bf16[64,1024]{1,0:T(8,128)(2,1)S(1)} %slice_bitcast_fusion.4), channel_id=1, source_target_pairs={{510,511}} | collective-permute-start | bytes 393224 | tf_op jit(solution)/shard_map/ppermute | solution.py:224
  61.1 2.1 %collective-permute-start.10 = (bf16[64,1024]{1,0:T(8,128)(2,1)S(1)}, bf16[64,1024]{1,0:T(8,128)(2,1)S(1)}, u32[]{:S(2)}, u32[]{:S(2)}) collective-permute-start(bf16[64,1024]{1,0:T(8,128)(2,1)S(1)} %add_convert_fusion), channel_id=1, source_target_pairs={{0,1},{1,2},{2,3},{3,4},{4,5},{5,6},{6,7},{7,8},{8,9},{9,10},{10,1... | collective-permute-start | bytes 393224 | tf_op jit(solution)/shard_map/ppermute | solution.py:19
  63.2 1.5 %collective-permute-done.6 = bf16[2,64,1024]{2,1,0:T(8,128)(2,1)S(1)} collective-permute-done((bf16[2,64,1024]{2,1,0:T(8,128)(2,1)}, bf16[2,64,1024]{2,1,0:T(8,128)(2,1)S(1)}, u32[]{:S(2)}, u32[]{:S(2)}) %collective-permute-start.6) | collective-permute-done | bytes 262176 | tf_op jit(solution)/shard_map/ppermute | solution.py:19
  64.8 6.4 %collective-permute-start.7 = (bf16[64,1024]{1,0:T(8,128)(2,1)S(1)}, bf16[64,1024]{1,0:T(8,128)(2,1)S(1)}, u32[]{:S(2)}, u32[]{:S(2)}) collective-permute-start(bf16[64,1024]{1,0:T(8,128)(2,1)S(1)} %fusion.4), channel_id=1, source_target_pairs={{1,0},{2,1},{3,2},{4,3},{5,4},{6,5},{7,6},{8,7},{9,8},{10,9},{11,1... | collective-permute-start | bytes 393224 | tf_op jit(solution)/shard_map/ppermute | solution.py:19
  71.2 1.4 %collective-permute-done.10 = bf16[64,1024]{1,0:T(8,128)(2,1)S(1)} collective-permute-done((bf16[64,1024]{1,0:T(8,128)(2,1)S(1)}, bf16[64,1024]{1,0:T(8,128)(2,1)S(1)}, u32[]{:S(2)}, u32[]{:S(2)}) %collective-permute-start.10) | collective-permute-done | bytes 131104 | tf_op jit(solution)/shard_map/ppermute | solution.py:19
  72.6 1.1 %collective-permute-done.7 = bf16[64,1024]{1,0:T(8,128)(2,1)S(1)} collective-permute-done((bf16[64,1024]{1,0:T(8,128)(2,1)S(1)}, bf16[64,1024]{1,0:T(8,128)(2,1)S(1)}, u32[]{:S(2)}, u32[]{:S(2)}) %collective-permute-start.7) | collective-permute-done | bytes 131104 | tf_op jit(solution)/shard_map/ppermute | solution.py:19
  73.8 0.1 fusion.8
  74.0 0.7 slice_bitcast_fusion.2
  (43 shorter events, 0.9 us)
Async XLA Ops:
  0.6 18.3 %copy-start.1 = (bf16[1,2,64,512]{3,2,1,0:T(8,128)(2,1)S(1)}, bf16[1,2,64,512]{3,2,1,0:T(8,128)(2,1)}, u32[]{:S(2)}) copy-start(bf16[1,2,64,512]{3,2,1,0:T(8,128)(2,1)} %param.7) | copy-start | bytes 393220
  0.6 18.3 %copy-start.2 = (bf16[1,2,64,512]{3,2,1,0:T(8,128)(2,1)S(1)}, bf16[1,2,64,512]{3,2,1,0:T(8,128)(2,1)}, u32[]{:S(2)}) copy-start(bf16[1,2,64,512]{3,2,1,0:T(8,128)(2,1)} %param.6) | copy-start | bytes 393220
  1.6 17.3 %collective-permute-start.2 = (bf16[64,1024]{1,0:T(8,128)(2,1)S(1)}, bf16[64,1024]{1,0:T(8,128)(2,1)S(1)}, u32[]{:S(2)}, u32[]{:S(2)}) collective-permute-start(bf16[64,1024]{1,0:T(8,128)(2,1)S(1)} %bitcast.66), channel_id=1, source_target_pairs={{1,0},{2,1},{3,2},{4,3},{5,4},{6,5},{7,6},{8,7},{9,8},{10,9},{11,1... | collective-permute-start | bytes 393224 | tf_op jit(solution)/shard_map/ppermute | solution.py:19
  15.2 0.7 copy-start.12
  18.9 0.7 copy-start.4
  19.6 12.6 %collective-permute-start = (bf16[64,1024]{1,0:T(8,128)(2,1)S(1)}, bf16[64,1024]{1,0:T(8,128)(2,1)S(1)}, u32[]{:S(2)}, u32[]{:S(2)}) collective-permute-start(bf16[64,1024]{1,0:T(8,128)(2,1)S(1)} %bitcast.68), channel_id=1, source_target_pairs={{0,1},{1,2},{2,3},{3,4},{4,5},{5,6},{6,7},{7,8},{8,9},{9,10},{10,1... | collective-permute-start | bytes 393224 | tf_op jit(solution)/shard_map/ppermute | solution.py:19
  22.2 13.9 %collective-permute-start.4 = (bf16[64,1024]{1,0:T(8,128)(2,1)S(1)}, bf16[64,1024]{1,0:T(8,128)(2,1)S(1)}, u32[]{:S(2)}, u32[]{:S(2)}) collective-permute-start(bf16[64,1024]{1,0:T(8,128)(2,1)S(1)} %bitcast.69), channel_id=1, source_target_pairs={{511,510},{510,511}} | collective-permute-start | bytes 393224 | tf_op jit(solution)/shard_map/ppermute | solution.py:206
  22.8 13.2 %collective-permute-start.5 = (bf16[64,1024]{1,0:T(8,128)(2,1)S(1)}, bf16[64,1024]{1,0:T(8,128)(2,1)S(1)}, u32[]{:S(2)}, u32[]{:S(2)}) collective-permute-start(bf16[64,1024]{1,0:T(8,128)(2,1)S(1)} %bitcast.70), channel_id=1, source_target_pairs={{509,511}} | collective-permute-start | bytes 393224 | tf_op jit(solution)/shard_map/ppermute | solution.py:207
  23.6 14.6 %collective-permute-start.3 = (bf16[2,64,1024]{2,1,0:T(8,128)(2,1)S(1)}, bf16[2,64,1024]{2,1,0:T(8,128)(2,1)S(1)}, u32[]{:S(2)}, u32[]{:S(2)}) collective-permute-start(bf16[2,64,1024]{2,1,0:T(8,128)(2,1)S(1)} %pad_maximum_fusion.2), channel_id=1, source_target_pairs={{2,0},{3,1},{4,2},{5,3},{6,4},{7,5},{8,6},{9,7},{10,8},{11,9},{12,... | collective-permute-start | bytes 786440 | tf_op jit(solution)/shard_map/ppermute | solution.py:19
  32.2 0.7 copy-start.5
  32.8 13.8 %collective-permute-start.1 = (bf16[2,64,1024]{2,1,0:T(8,128)(2,1)S(1)}, bf16[2,64,1024]{2,1,0:T(8,128)(2,1)S(1)}, u32[]{:S(2)}, u32[]{:S(2)}) collective-permute-start(bf16[2,64,1024]{2,1,0:T(8,128)(2,1)S(1)} %pad_maximum_fusion.1), channel_id=1, source_target_pairs={{0,2},{1,3},{2,4},{3,5},{4,6},{5,7},{6,8},{7,9},{8,10},{9,11},{10,... | collective-permute-start | bytes 786440 | tf_op jit(solution)/shard_map/ppermute | solution.py:19
  36.1 2.1 %copy-start.9 = (bf16[64,1024]{1,0:T(8,128)(2,1)}, bf16[64,1024]{1,0:T(8,128)(2,1)S(1)}, u32[]{:S(2)}) copy-start(bf16[64,1024]{1,0:T(8,128)(2,1)S(1)} %collective-permute-done.4.turn2) | copy-start | bytes 393220
  36.1 2.1 %copy-start.10 = (bf16[64,1024]{1,0:T(8,128)(2,1)}, bf16[64,1024]{1,0:T(8,128)(2,1)S(1)}, u32[]{:S(2)}) copy-start(bf16[64,1024]{1,0:T(8,128)(2,1)S(1)} %collective-permute-done.5.turn3) | copy-start | bytes 393220
  38.1 0.7 copy-start.8
  44.7 16.3 %collective-permute-start.8 = (bf16[2,64,1024]{2,1,0:T(8,128)(2,1)}, bf16[2,64,1024]{2,1,0:T(8,128)(2,1)S(1)}, u32[]{:S(2)}, u32[]{:S(2)}) collective-permute-start(bf16[2,64,1024]{2,1,0:T(8,128)(2,1)} %get-tuple-element.11.a_l), channel_id=1, source_target_pairs={{0,2},{1,3},{2,4},{3,5},{4,6},{5,7},{6,8},{7,9},{8,10},{9,11},{10,... | collective-permute-start | bytes 786440 | tf_op jit(solution)/shard_map/ppermute | solution.py:19
  46.7 0.7 copy-start.7
  47.4 12.8 %copy-start.3 = (bf16[2,64,1024]{2,1,0:T(8,128)(2,1)S(1)}, bf16[2,64,1024]{2,1,0:T(8,128)(2,1)}, u32[]{:S(2)}) copy-start(bf16[2,64,1024]{2,1,0:T(8,128)(2,1)} %get-tuple-element.11.a_l) | copy-start | bytes 786436
  53.3 11.3 %collective-permute-start.6 = (bf16[2,64,1024]{2,1,0:T(8,128)(2,1)}, bf16[2,64,1024]{2,1,0:T(8,128)(2,1)S(1)}, u32[]{:S(2)}, u32[]{:S(2)}) collective-permute-start(bf16[2,64,1024]{2,1,0:T(8,128)(2,1)} %get-tuple-element.17), channel_id=1, source_target_pairs={{2,0},{3,1},{4,2},{5,3},{6,4},{7,5},{8,6},{9,7},{10,8},{11,9},{12,... | collective-permute-start | bytes 786440 | tf_op jit(solution)/shard_map/ppermute | solution.py:19
  60.2 0.9 %copy-start.6 = (bf16[64,1024]{1,0:T(8,128)(2,1)S(1)}, bf16[64,1024]{1,0:T(8,128)(2,1)}, u32[]{:S(2)}) copy-start(bf16[64,1024]{1,0:T(8,128)(2,1)} %get-tuple-element.12.p2_late) | copy-start | bytes 393220
  60.2 11.0 %collective-permute-start.9 = (bf16[64,1024]{1,0:T(8,128)(2,1)S(1)}, bf16[64,1024]{1,0:T(8,128)(2,1)S(1)}, u32[]{:S(2)}, u32[]{:S(2)}) collective-permute-start(bf16[64,1024]{1,0:T(8,128)(2,1)S(1)} %slice_bitcast_fusion.4), channel_id=1, source_target_pairs={{510,511}} | collective-permute-start | bytes 393224 | tf_op jit(solution)/shard_map/ppermute | solution.py:224
  61.1 3.6 %copy-start.11 = (bf16[64,1024]{1,0:T(8,128)(2,1)S(1)}, bf16[64,1024]{1,0:T(8,128)(2,1)}, u32[]{:S(2)}) copy-start(bf16[64,1024]{1,0:T(8,128)(2,1)} %get-tuple-element.18) | copy-start | bytes 393220
  61.1 12.6 %copy-start = (f32[2,64,1024]{2,1,0:T(8,128)S(1)}, f32[2,64,1024]{2,1,0:T(8,128)}, u32[]{:S(2)}) copy-start(f32[2,64,1024]{2,1,0:T(8,128)} %get-tuple-element.16) | copy-start | bytes 1572868
  61.1 11.5 %collective-permute-start.10 = (bf16[64,1024]{1,0:T(8,128)(2,1)S(1)}, bf16[64,1024]{1,0:T(8,128)(2,1)S(1)}, u32[]{:S(2)}, u32[]{:S(2)}) collective-permute-start(bf16[64,1024]{1,0:T(8,128)(2,1)S(1)} %add_convert_fusion), channel_id=1, source_target_pairs={{0,1},{1,2},{2,3},{3,4},{4,5},{5,6},{6,7},{7,8},{8,9},{9,10},{10,1... | collective-permute-start | bytes 393224 | tf_op jit(solution)/shard_map/ppermute | solution.py:19
  64.8 9.0 %collective-permute-start.7 = (bf16[64,1024]{1,0:T(8,128)(2,1)S(1)}, bf16[64,1024]{1,0:T(8,128)(2,1)S(1)}, u32[]{:S(2)}, u32[]{:S(2)}) collective-permute-start(bf16[64,1024]{1,0:T(8,128)(2,1)S(1)} %fusion.4), channel_id=1, source_target_pairs={{1,0},{2,1},{3,2},{4,3},{5,4},{6,5},{7,6},{8,7},{9,8},{10,9},{11,1... | collective-permute-start | bytes 393224 | tf_op jit(solution)/shard_map/ppermute | solution.py:19

commit v11 on v10

--- a/solution.py
+++ b/solution.py
@@ -135,7 +135,7 @@
     window_half(0, slot, lo_ref, q_ref, do_ref, groups, group_size, emit)
 
 
-def window_grads(flags, lo, q, do, kv, e1, e2, l1, l2, turn2, turn3):
+def window_grads(flags, lo, q, do, kv, e1, e2, l1, l2, turn2, turn3, between):
     halves, half_rows, width = q.shape
     kv2 = kv.shape[2]
     groups = kv2 // (2 * HEAD)
@@ -174,6 +174,7 @@
     )(flags, lo, q, do, kv, l1, l2, turn2, turn3)
 
     q_spec, lo_spec, part_spec = half_specs(0)
+    q, extra = lax.optimization_barrier((q, between(a_l, p2_late)))
     dq, a_e, p2_early, p3 = pl.pallas_call(
         functools.partial(early_kernel, groups=groups, group_size=group_size),
         grid=(1,),
@@ -186,7 +187,7 @@
         input_output_aliases={9: 0, 10: 3},
         cost_estimate=cost,
     )(flags, lo, q, do, kv, e1, e2, a_l, p2_late, dq, p3)
-    return dq, a_e, a_l, (p2_early, p2_late), p3
+    return dq, a_e, extra, p2_early, p3
 
 
 def on_device(query, keys, values, grad_out, lengths):
@@ -216,15 +217,22 @@
     lo = (doc_start - (block_ids[:, None] - REACH) * half_rows).astype(jnp.int32)[:, :, None]
     flags = jnp.stack([at_top, below_top]).astype(jnp.int32)
 
-    dq, a_e, a_l, p2, p3 = window_grads(flags, lo, q, do, kv, e1, e2, l1, l2, turn2, turn3)
+    link = jnp.bfloat16
+    f32 = jnp.float32
+
+    def late_return(a_l, p2_late):
+        back = lax.ppermute(a_l[0], AXIS, [(n - 2, n - 1)]).astype(f32)
+        a_l = shifted(a_l, 2).astype(f32)
+        b_l = shifted((p2_late.astype(f32) + a_l[1]).astype(link), 1).astype(f32)
+        return a_l, b_l, back
+
+    dq, a_e, (a_l, b_l, back), p2_early, p3 = window_grads(
+        flags, lo, q, do, kv, e1, e2, l1, l2, turn2, turn3, late_return
+    )
 
     zero = jnp.zeros_like(p3[0])
-    link = jnp.bfloat16
-    a_e = shifted(a_e, -2).astype(jnp.float32)
-    back = lax.ppermute(a_l[0], AXIS, [(n - 2, n - 1)]).astype(jnp.float32)
-    a_l = shifted(a_l, 2).astype(jnp.float32)
-    b_e = shifted((p2[0].astype(jnp.float32) + a_e[1]).astype(link), -1).astype(jnp.float32)
-    b_l = shifted((p2[1].astype(jnp.float32) + a_l[1]).astype(link), 1).astype(jnp.float32)
+    a_e = shifted(a_e, -2).astype(f32)
+    b_e = shifted((p2_early.astype(f32) + a_e[1]).astype(link), -1).astype(f32)
     final_early = p3[0] + a_e[0] + b_e + jnp.where(at_top, a_l[1] + back, zero)
     final_late = p3[1] + a_l[0] + b_l
     final = jnp.stack([final_early, final_late])

time: 75.4 us -> 92 us (1.22)
  waiting for transfers between devices: 8.09 us -> 32.8 us
  starting transfers between devices: 45.3 us -> 37.3 us
    ppermute x8, waiting for transfers between devices: 8.08 us -> 32.8 us  [shifted(): return lax.ppermute(value, AXIS, pairs)]
    ppermute x8, starting transfers between devices: 43.2 us -> 35.2 us  [shifted(): return lax.ppermute(value, AXIS, pairs)]
  transfers between devices with their start and end apart: 11 -> 11, of which waited for: 5 -> 5; matrix products, arithmetic and copies ran while one was open for 4% -> 4% of each run, Pallas kernels for 16% -> 6%
where the time goes in v11:
time: 92 us; the launch traced here: 91.5 us
  starting transfers between devices  37.3 us (41%)
  waiting for transfers between devices  32.8 us (36%)
  Pallas kernels  11.8 us (13%)
  local copies, waits for them, and re-layouts  4.36 us (5%)
  other arithmetic  4.22 us (5%)
  between operations  0.96 us (1%)
    ppermute x8, starting transfers between devices, shifted(): return lax.ppermute(value, AXIS, pairs)  35.2 us
    ppermute x8, waiting for transfers between devices, shifted(): return lax.ppermute(value, AXIS, pairs)  32.8 us
    pallas_call x1, Pallas kernels, window_grads(): pl.pallas_call(functools.partial(early_kernel, groups=groups, group_size=...  5.93 us
    pallas_call x1, Pallas kernels, window_grads(): pl.pallas_call(functools.partial(late_kernel, groups=groups, group_size=g...  5.89 us
    unnamed x26, local copies, waits for them, and re-layouts  3.33 us
  transfers between devices with their start and end apart: 11, of which 5 were waited for; matrix products, arithmetic and copies ran while one was open for 4% of the time, Pallas kernels for 6%

profile of v11, /device:TPU:6, one launch (start us, length us, event | category | flops | bytes accessed | tf_op | source)
XLA Modules:
  0.0 91.5 jit_solution(940270723300068364)
XLA Ops:
  0.7 0.9 %fusion.10 = bf16[1,64,1024]{2,1,0:T(8,128)(2,1)S(1)} fusion(bf16[2,64,512]{2,1,0:T(8,128)(2,1)} %bitcast.66, bf16[2,64,512]{2,1,0:T(8,128)(2,1)} %bitcast.63), kind=kLoop, calls=%fused_computation.24 | loop fusion | flops 262144 | bytes 393216 | tf_op jit(solution)/shard_map/concatenate | solution.py:200
  1.6 13.6 %collective-permute-start = (bf16[64,1024]{1,0:T(8,128)(2,1)S(1)}, bf16[64,1024]{1,0:T(8,128)(2,1)S(1)}, u32[]{:S(2)}, u32[]{:S(2)}) collective-permute-start(bf16[64,1024]{1,0:T(8,128)(2,1)S(1)} %bitcast.71), channel_id=1, source_target_pairs={{1,0},{2,1},{3,2},{4,3},{5,4},{6,5},{7,6},{8,7},{9,8},{10,9},{11,1... | collective-permute-start | bytes 393224 | tf_op jit(solution)/shard_map/ppermute | solution.py:19
  15.3 0.6 copy-done.12
  15.9 0.3 reduce-window.9
  16.3 0.1 slice_reduce_fusion
  16.5 0.2 select_reduce_fusion
  16.9 2.0 %collective-permute-done.l1 = bf16[64,1024]{1,0:T(8,128)(2,1)S(1)} collective-permute-done((bf16[64,1024]{1,0:T(8,128)(2,1)S(1)}, bf16[64,1024]{1,0:T(8,128)(2,1)S(1)}, u32[]{:S(2)}, u32[]{:S(2)}) %collective-permute-start) | collective-permute-done | bytes 131104 | tf_op jit(solution)/shard_map/ppermute | solution.py:19
  19.0 0.6 copy-done.4
  19.6 2.5 %collective-permute-start.1 = (bf16[2,64,1024]{2,1,0:T(8,128)(2,1)S(1)}, bf16[2,64,1024]{2,1,0:T(8,128)(2,1)S(1)}, u32[]{:S(2)}, u32[]{:S(2)}) collective-permute-start(bf16[2,64,1024]{2,1,0:T(8,128)(2,1)S(1)} %pad_maximum_fusion.1), channel_id=1, source_target_pairs={{2,0},{3,1},{4,2},{5,3},{6,4},{7,5},{8,6},{9,7},{10,8},{11,9},{12,... | collective-permute-start | bytes 786440 | tf_op jit(solution)/shard_map/ppermute | solution.py:19
  22.2 0.7 broadcast_subtract_fusion.lo_ref
  22.9 0.7 collective-permute-start.3
  23.5 0.7 collective-permute-start.2
  24.2 0.7 pad_maximum_fusion.kv
  24.9 8.8 %collective-permute-start.7 = (bf16[64,1024]{1,0:T(8,128)(2,1)S(1)}, bf16[64,1024]{1,0:T(8,128)(2,1)S(1)}, u32[]{:S(2)}, u32[]{:S(2)}) collective-permute-start(bf16[64,1024]{1,0:T(8,128)(2,1)S(1)} %bitcast.74), channel_id=1, source_target_pairs={{0,1},{1,2},{2,3},{3,4},{4,5},{5,6},{6,7},{7,8},{8,9},{9,10},{10,1... | collective-permute-start | bytes 393224 | tf_op jit(solution)/shard_map/ppermute | solution.py:19
  33.8 0.6 add_convert_fusion.flags
  34.4 0.6 copy-done.9
  35.2 5.9 %shard_map.76 = (bf16[2,64,4096]{2,1,0:T(8,128)(2,1)}, bf16[2,64,1024]{2,1,0:T(8,128)(2,1)}, bf16[64,1024]{1,0:T(8,128)(2,1)}, f32[2,64,1024]{2,1,0:T(8,128)}) custom-call(s32[2]{0:T(128)} %add_convert_fusion.flags, s32[2,64,1]{2,1,0:T(8,128)} %broadcast_subtract_fusion.lo_ref, bf16[2,64,4096]{2,1,0:T(8,128)(2,1)} %bitcast.59, ...), custom_call_target="tpu_custom_call" | custom-call | flops 805306368 | bytes 1835008 | tf_op jit(solution)/shard_map/pallas_call | solution.py:167
  41.1 1.9 %collective-permute-start.4 = (bf16[2,64,1024]{2,1,0:T(8,128)(2,1)}, bf16[2,64,1024]{2,1,0:T(8,128)(2,1)S(1)}, u32[]{:S(2)}, u32[]{:S(2)}) collective-permute-start(bf16[2,64,1024]{2,1,0:T(8,128)(2,1)} %get-tuple-element.15.a_l), channel_id=1, source_target_pairs={{0,2},{1,3},{2,4},{3,5},{4,6},{5,7},{6,8},{7,9},{8,10},{9,11},{10,... | collective-permute-start | bytes 786440 | tf_op jit(solution)/shard_map/ppermute | solution.py:19
  43.0 0.6 copy-done.5
  43.6 1.9 %collective-permute-start.8 = (bf16[2,64,1024]{2,1,0:T(8,128)(2,1)S(1)}, bf16[2,64,1024]{2,1,0:T(8,128)(2,1)S(1)}, u32[]{:S(2)}, u32[]{:S(2)}) collective-permute-start(bf16[2,64,1024]{2,1,0:T(8,128)(2,1)S(1)} %pad_maximum_fusion.2), channel_id=1, source_target_pairs={{0,2},{1,3},{2,4},{3,5},{4,6},{5,7},{6,8},{7,9},{8,10},{9,11},{10,... | collective-permute-start | bytes 786440 | tf_op jit(solution)/shard_map/ppermute | solution.py:19
  45.6 0.8 collective-permute-start.6
  46.4 8.4 %collective-permute-done.4 = bf16[2,64,1024]{2,1,0:T(8,128)(2,1)S(1)} collective-permute-done((bf16[2,64,1024]{2,1,0:T(8,128)(2,1)}, bf16[2,64,1024]{2,1,0:T(8,128)(2,1)S(1)}, u32[]{:S(2)}, u32[]{:S(2)}) %collective-permute-start.4) | collective-permute-done | bytes 262176 | tf_op jit(solution)/shard_map/ppermute | solution.py:19
  54.9 2.1 %collective-permute-start.5 = (bf16[64,1024]{1,0:T(8,128)(2,1)S(1)}, bf16[64,1024]{1,0:T(8,128)(2,1)S(1)}, u32[]{:S(2)}, u32[]{:S(2)}) collective-permute-start(bf16[64,1024]{1,0:T(8,128)(2,1)S(1)} %fusion.7), channel_id=1, source_target_pairs={{0,1},{1,2},{2,3},{3,4},{4,5},{5,6},{6,7},{7,8},{8,9},{9,10},{10,1... | collective-permute-start | bytes 393224 | tf_op jit(solution)/shard_map/ppermute | solution.py:19
  57.1 8.3 %collective-permute-done.5 = bf16[64,1024]{1,0:T(8,128)(2,1)S(1)} collective-permute-done((bf16[64,1024]{1,0:T(8,128)(2,1)S(1)}, bf16[64,1024]{1,0:T(8,128)(2,1)S(1)}, u32[]{:S(2)}, u32[]{:S(2)}) %collective-permute-start.5) | collective-permute-done | bytes 131104 | tf_op jit(solution)/shard_map/ppermute | solution.py:19
  65.5 0.7 copy-done.7
  66.2 5.9 %shard_map.77 = (bf16[2,64,4096]{2,1,0:T(8,128)(2,1)}, bf16[2,64,1024]{2,1,0:T(8,128)(2,1)}, bf16[64,1024]{1,0:T(8,128)(2,1)}, f32[2,64,1024]{2,1,0:T(8,128)}) custom-call(s32[2]{0:T(128)} %add_convert_fusion.flags, s32[2,64,1]{2,1,0:T(8,128)} %broadcast_subtract_fusion.lo_ref, ...), custom_call_target="tpu_custom_call", output_to_operand_aliasing={{0}: (9, {}), {3}: (10, {})} | custom-call | flops 805306368 | bytes 1835008 | tf_op jit(solution)/shard_map/pallas_call | solution.py:178
  72.1 2.1 %collective-permute-start.9 = (bf16[2,64,1024]{2,1,0:T(8,128)(2,1)}, bf16[2,64,1024]{2,1,0:T(8,128)(2,1)S(1)}, u32[]{:S(2)}, u32[]{:S(2)}) collective-permute-start(bf16[2,64,1024]{2,1,0:T(8,128)(2,1)} %get-tuple-element.22), channel_id=1, source_target_pairs={{2,0},{3,1},{4,2},{5,3},{6,4},{7,5},{8,6},{9,7},{10,8},{11,9},{12,... | collective-permute-start | bytes 786440 | tf_op jit(solution)/shard_map/ppermute | solution.py:19
  74.2 8.0 %collective-permute-done.9 = bf16[2,64,1024]{2,1,0:T(8,128)(2,1)S(1)} collective-permute-done((bf16[2,64,1024]{2,1,0:T(8,128)(2,1)}, bf16[2,64,1024]{2,1,0:T(8,128)(2,1)S(1)}, u32[]{:S(2)}, u32[]{:S(2)}) %collective-permute-start.9) | collective-permute-done | bytes 262176 | tf_op jit(solution)/shard_map/ppermute | solution.py:19
  82.2 2.2 %collective-permute-start.10 = (bf16[64,1024]{1,0:T(8,128)(2,1)S(1)}, bf16[64,1024]{1,0:T(8,128)(2,1)S(1)}, u32[]{:S(2)}, u32[]{:S(2)}) collective-permute-start(bf16[64,1024]{1,0:T(8,128)(2,1)S(1)} %fusion.1), channel_id=1, source_target_pairs={{1,0},{2,1},{3,2},{4,3},{5,4},{6,5},{7,6},{8,7},{9,8},{10,9},{11,1... | collective-permute-start | bytes 393224 | tf_op jit(solution)/shard_map/ppermute | solution.py:19
  84.5 6.1 %collective-permute-done.10 = bf16[64,1024]{1,0:T(8,128)(2,1)S(1)} collective-permute-done((bf16[64,1024]{1,0:T(8,128)(2,1)S(1)}, bf16[64,1024]{1,0:T(8,128)(2,1)S(1)}, u32[]{:S(2)}, u32[]{:S(2)}) %collective-permute-start.10) | collective-permute-done | bytes 131104 | tf_op jit(solution)/shard_map/ppermute | solution.py:19
  90.6 0.2 fusion.5
  90.8 0.7 slice_bitcast_fusion.2
  (45 shorter events, 1.0 us)
Async XLA Ops:
  0.6 18.3 %copy-start.1 = (bf16[1,2,64,512]{3,2,1,0:T(8,128)(2,1)S(1)}, bf16[1,2,64,512]{3,2,1,0:T(8,128)(2,1)}, u32[]{:S(2)}) copy-start(bf16[1,2,64,512]{3,2,1,0:T(8,128)(2,1)} %param.7) | copy-start | bytes 393220
  0.6 18.3 %copy-start.2 = (bf16[1,2,64,512]{3,2,1,0:T(8,128)(2,1)S(1)}, bf16[1,2,64,512]{3,2,1,0:T(8,128)(2,1)}, u32[]{:S(2)}) copy-start(bf16[1,2,64,512]{3,2,1,0:T(8,128)(2,1)} %param.6) | copy-start | bytes 393220
  1.6 17.3 %collective-permute-start = (bf16[64,1024]{1,0:T(8,128)(2,1)S(1)}, bf16[64,1024]{1,0:T(8,128)(2,1)S(1)}, u32[]{:S(2)}, u32[]{:S(2)}) collective-permute-start(bf16[64,1024]{1,0:T(8,128)(2,1)S(1)} %bitcast.71), channel_id=1, source_target_pairs={{1,0},{2,1},{3,2},{4,3},{5,4},{6,5},{7,6},{8,7},{9,8},{10,9},{11,1... | collective-permute-start | bytes 393224 | tf_op jit(solution)/shard_map/ppermute | solution.py:19
  15.2 0.7 copy-start.12
  18.9 0.7 copy-start.4
  19.6 14.8 %collective-permute-start.1 = (bf16[2,64,1024]{2,1,0:T(8,128)(2,1)S(1)}, bf16[2,64,1024]{2,1,0:T(8,128)(2,1)S(1)}, u32[]{:S(2)}, u32[]{:S(2)}) collective-permute-start(bf16[2,64,1024]{2,1,0:T(8,128)(2,1)S(1)} %pad_maximum_fusion.1), channel_id=1, source_target_pairs={{2,0},{3,1},{4,2},{5,3},{6,4},{7,5},{8,6},{9,7},{10,8},{11,9},{12,... | collective-permute-start | bytes 786440 | tf_op jit(solution)/shard_map/ppermute | solution.py:19
  22.9 11.5 %collective-permute-start.3 = (bf16[64,1024]{1,0:T(8,128)(2,1)S(1)}, bf16[64,1024]{1,0:T(8,128)(2,1)S(1)}, u32[]{:S(2)}, u32[]{:S(2)}) collective-permute-start(bf16[64,1024]{1,0:T(8,128)(2,1)S(1)} %bitcast.72), channel_id=1, source_target_pairs={{509,511}} | collective-permute-start | bytes 393224 | tf_op jit(solution)/shard_map/ppermute | solution.py:208
  23.5 10.9 %collective-permute-start.2 = (bf16[64,1024]{1,0:T(8,128)(2,1)S(1)}, bf16[64,1024]{1,0:T(8,128)(2,1)S(1)}, u32[]{:S(2)}, u32[]{:S(2)}) collective-permute-start(bf16[64,1024]{1,0:T(8,128)(2,1)S(1)} %bitcast.73), channel_id=1, source_target_pairs={{511,510},{510,511}} | collective-permute-start | bytes 393224 | tf_op jit(solution)/shard_map/ppermute | solution.py:207
  24.9 18.1 %collective-permute-start.7 = (bf16[64,1024]{1,0:T(8,128)(2,1)S(1)}, bf16[64,1024]{1,0:T(8,128)(2,1)S(1)}, u32[]{:S(2)}, u32[]{:S(2)}) collective-permute-start(bf16[64,1024]{1,0:T(8,128)(2,1)S(1)} %bitcast.74), channel_id=1, source_target_pairs={{0,1},{1,2},{2,3},{3,4},{4,5},{5,6},{6,7},{7,8},{8,9},{9,10},{10,1... | collective-permute-start | bytes 393224 | tf_op jit(solution)/shard_map/ppermute | solution.py:19
  34.4 0.7 copy-start.9
  34.4 0.7 copy-start.10
  34.4 0.8 copy-start.8
  41.1 13.8 %collective-permute-start.4 = (bf16[2,64,1024]{2,1,0:T(8,128)(2,1)}, bf16[2,64,1024]{2,1,0:T(8,128)(2,1)S(1)}, u32[]{:S(2)}, u32[]{:S(2)}) collective-permute-start(bf16[2,64,1024]{2,1,0:T(8,128)(2,1)} %get-tuple-element.15.a_l), channel_id=1, source_target_pairs={{0,2},{1,3},{2,4},{3,5},{4,6},{5,7},{6,8},{7,9},{8,10},{9,11},{10,... | collective-permute-start | bytes 786440 | tf_op jit(solution)/shard_map/ppermute | solution.py:19
  43.0 0.7 copy-start.5
  43.0 2.6 %copy-start.3 = (bf16[2,64,1024]{2,1,0:T(8,128)(2,1)S(1)}, bf16[2,64,1024]{2,1,0:T(8,128)(2,1)}, u32[]{:S(2)}) copy-start(bf16[2,64,1024]{2,1,0:T(8,128)(2,1)} %get-tuple-element.15.a_l) | copy-start | bytes 786436
  43.6 21.8 %collective-permute-start.8 = (bf16[2,64,1024]{2,1,0:T(8,128)(2,1)S(1)}, bf16[2,64,1024]{2,1,0:T(8,128)(2,1)S(1)}, u32[]{:S(2)}, u32[]{:S(2)}) collective-permute-start(bf16[2,64,1024]{2,1,0:T(8,128)(2,1)S(1)} %pad_maximum_fusion.2), channel_id=1, source_target_pairs={{0,2},{1,3},{2,4},{3,5},{4,6},{5,7},{6,8},{7,9},{8,10},{9,11},{10,... | collective-permute-start | bytes 786440 | tf_op jit(solution)/shard_map/ppermute | solution.py:19
  45.6 9.3 %copy-start.6 = (bf16[64,1024]{1,0:T(8,128)(2,1)S(1)}, bf16[64,1024]{1,0:T(8,128)(2,1)}, u32[]{:S(2)}) copy-start(bf16[64,1024]{1,0:T(8,128)(2,1)} %get-tuple-element.16.p2_late) | copy-start | bytes 393220
  45.6 11.5 %collective-permute-start.6 = (bf16[64,1024]{1,0:T(8,128)(2,1)S(1)}, bf16[64,1024]{1,0:T(8,128)(2,1)S(1)}, u32[]{:S(2)}, u32[]{:S(2)}) collective-permute-start(bf16[64,1024]{1,0:T(8,128)(2,1)S(1)} %slice_bitcast_fusion.4), channel_id=1, source_target_pairs={{510,511}} | collective-permute-start | bytes 393224 | tf_op jit(solution)/shard_map/ppermute | solution.py:224
  54.9 10.5 %collective-permute-start.5 = (bf16[64,1024]{1,0:T(8,128)(2,1)S(1)}, bf16[64,1024]{1,0:T(8,128)(2,1)S(1)}, u32[]{:S(2)}, u32[]{:S(2)}) collective-permute-start(bf16[64,1024]{1,0:T(8,128)(2,1)S(1)} %fusion.7), channel_id=1, source_target_pairs={{0,1},{1,2},{2,3},{3,4},{4,5},{5,6},{6,7},{7,8},{8,9},{9,10},{10,1... | collective-permute-start | bytes 393224 | tf_op jit(solution)/shard_map/ppermute | solution.py:19
  65.5 0.7 copy-start.7
  72.1 10.1 %copy-start.11 = (bf16[64,1024]{1,0:T(8,128)(2,1)S(1)}, bf16[64,1024]{1,0:T(8,128)(2,1)}, u32[]{:S(2)}) copy-start(bf16[64,1024]{1,0:T(8,128)(2,1)} %get-tuple-element.23) | copy-start | bytes 393220
  72.1 18.5 %copy-start = (f32[2,64,1024]{2,1,0:T(8,128)S(1)}, f32[2,64,1024]{2,1,0:T(8,128)}, u32[]{:S(2)}) copy-start(f32[2,64,1024]{2,1,0:T(8,128)} %get-tuple-element.21) | copy-start | bytes 1572868
  72.1 10.0 %collective-permute-start.9 = (bf16[2,64,1024]{2,1,0:T(8,128)(2,1)}, bf16[2,64,1024]{2,1,0:T(8,128)(2,1)S(1)}, u32[]{:S(2)}, u32[]{:S(2)}) collective-permute-start(bf16[2,64,1024]{2,1,0:T(8,128)(2,1)} %get-tuple-element.22), channel_id=1, source_target_pairs={{2,0},{3,1},{4,2},{5,3},{6,4},{7,5},{8,6},{9,7},{10,8},{11,9},{12,... | collective-permute-start | bytes 786440 | tf_op jit(solution)/shard_map/ppermute | solution.py:19
  82.2 8.4 %collective-permute-start.10 = (bf16[64,1024]{1,0:T(8,128)(2,1)S(1)}, bf16[64,1024]{1,0:T(8,128)(2,1)S(1)}, u32[]{:S(2)}, u32[]{:S(2)}) collective-permute-start(bf16[64,1024]{1,0:T(8,128)(2,1)S(1)} %fusion.1), channel_id=1, source_target_pairs={{1,0},{2,1},{3,2},{4,3},{5,4},{6,5},{7,6},{8,7},{9,8},{10,9},{11,1... | collective-permute-start | bytes 393224 | tf_op jit(solution)/shard_map/ppermute | solution.py:19

commit v12 on v10

--- a/solution.py
+++ b/solution.py
@@ -62,12 +62,26 @@
             emit("part", j, kv_width + g * HEAD, dv[j * half_rows:(j + 1) * half_rows])
 
 
+class OwnBlocks:
+    def __init__(self, keys, values):
+        self.keys = keys
+        self.values = values
+
+    def __getitem__(self, index):
+        half, rows, cols = index
+        width = self.keys.shape[2]
+        if cols.start >= width:
+            return self.values[half, rows, pl.ds(cols.start - width, cols.size)]
+        return self.keys[half, rows, cols]
+
+
 def late_kernel(
-    flags, lo_ref, q_ref, do_ref, kv, l1, l2, turn2, turn3,
+    flags, lo_ref, q_ref, do_ref, keys, values, l1, l2, turn2, turn3,
     dq_ref, a_l, p2_ref, p3_ref, *, groups, group_size
 ):
     at_top = flags[0] != 0
     below_top = flags[1] != 0
+    kv = OwnBlocks(keys, values)
 
     def slot(j, lanes):
         cols = pl.ds(lanes, HEAD)
@@ -98,12 +112,13 @@
 
 
 def early_kernel(
-    flags, lo_ref, q_ref, do_ref, kv, e1, e2, a_l, p2_late, dq_in, p3_in,
+    flags, lo_ref, q_ref, do_ref, keys, values, e1, e2, a_l, p2_late, dq_in, p3_in,
     dq_ref, a_e, p2_ref, p3_ref, *, groups, group_size
 ):
     del dq_in, p3_in
     at_top = flags[0] != 0
     below_top = flags[1] != 0
+    kv = OwnBlocks(keys, values)
 
     def slot(j, lanes):
         cols = pl.ds(lanes, HEAD)
@@ -135,16 +150,16 @@
     window_half(0, slot, lo_ref, q_ref, do_ref, groups, group_size, emit)
 
 
-def window_grads(flags, lo, q, do, kv, e1, e2, l1, l2, turn2, turn3):
+def window_grads(flags, lo, q, do, keys, values, e1, e2, l1, l2, turn2, turn3):
     halves, half_rows, width = q.shape
-    kv2 = kv.shape[2]
+    kv2 = 2 * keys.shape[2]
     groups = kv2 // (2 * HEAD)
     group_size = width // (groups * HEAD)
     flops = 6 * 2 * groups * group_size * half_rows * 4 * half_rows * HEAD
     cost = pl.CostEstimate(
         flops=flops,
         transcendentals=groups * group_size * half_rows * 4 * half_rows,
-        bytes_accessed=2 * q.size + 6 * kv.size,
+        bytes_accessed=2 * q.size + 12 * keys.size,
     )
 
     def half_specs(half):
@@ -154,6 +169,7 @@
         return q_spec, lo_spec, part_spec
 
     pair_spec = pl.BlockSpec((2, half_rows, kv2), lambda s: (0, 0, 0))
+    own_spec = pl.BlockSpec((2, half_rows, kv2 // 2), lambda s: (0, 0, 0))
     one_spec = pl.BlockSpec((half_rows, kv2), lambda s: (0, 0))
     smem = pl.BlockSpec(memory_space=pltpu.SMEM)
     anywhere = pl.BlockSpec(memory_space=pl.ANY)
@@ -167,25 +183,25 @@
     dq, a_l, p2_late, p3 = pl.pallas_call(
         functools.partial(late_kernel, groups=groups, group_size=group_size),
         grid=(1,),
-        in_specs=[smem, lo_spec, q_spec, q_spec, pair_spec, one_spec, pair_spec, one_spec, one_spec],
+        in_specs=[smem, lo_spec, q_spec, q_spec, own_spec, own_spec, one_spec, pair_spec, one_spec, one_spec],
         out_specs=[q_spec, pair_spec, one_spec, part_spec],
         out_shape=[dq_shape, pair, slot_shape, p3_shape],
         cost_estimate=cost,
-    )(flags, lo, q, do, kv, l1, l2, turn2, turn3)
+    )(flags, lo, q, do, keys, values, l1, l2, turn2, turn3)
 
     q_spec, lo_spec, part_spec = half_specs(0)
     dq, a_e, p2_early, p3 = pl.pallas_call(
         functools.partial(early_kernel, groups=groups, group_size=group_size),
         grid=(1,),
         in_specs=[
-            smem, lo_spec, q_spec, q_spec, pair_spec, one_spec, pair_spec, pair_spec, one_spec,
+            smem, lo_spec, q_spec, q_spec, own_spec, own_spec, one_spec, pair_spec, pair_spec, one_spec,
             anywhere, anywhere,
         ],
         out_specs=[q_spec, pair_spec, one_spec, part_spec],
         out_shape=[dq_shape, pair, slot_shape, p3_shape],
-        input_output_aliases={9: 0, 10: 3},
+        input_output_aliases={10: 0, 11: 3},
         cost_estimate=cost,
-    )(flags, lo, q, do, kv, e1, e2, a_l, p2_late, dq, p3)
+    )(flags, lo, q, do, keys, values, e1, e2, a_l, p2_late, dq, p3)
     return dq, a_e, a_l, (p2_early, p2_late), p3
 
 
@@ -216,7 +232,7 @@
     lo = (doc_start - (block_ids[:, None] - REACH) * half_rows).astype(jnp.int32)[:, :, None]
     flags = jnp.stack([at_top, below_top]).astype(jnp.int32)
 
-    dq, a_e, a_l, p2, p3 = window_grads(flags, lo, q, do, kv, e1, e2, l1, l2, turn2, turn3)
+    dq, a_e, a_l, p2, p3 = window_grads(flags, lo, q, do, keys[0], values[0], e1, e2, l1, l2, turn2, turn3)
 
     zero = jnp.zeros_like(p3[0])
     link = jnp.bfloat16

time: 75.4 us -> 74.9 us (level)
    concatenate x2 -> x1, other arithmetic: 1.65 us -> 0.92 us  [on_device(): kv = jnp.concatenate([keys[0], values[0]], axis=2)]
  transfers between devices with their start and end apart: 11 -> 11, of which waited for: 5 -> 6; matrix products, arithmetic and copies ran while one was open for 4% -> 4% of each run, Pallas kernels for 16% -> 16%
where the time goes in v12:
time: 74.9 us; the launch traced here: 74.2 us
  starting transfers between devices  45.3 us (60%)
  Pallas kernels  11.9 us (16%)
  waiting for transfers between devices  8.25 us (11%)
  local copies, waits for them, and re-layouts  4.43 us (6%)
  other arithmetic  3.45 us (5%)
  between operations  0.92 us (1%)
    ppermute x8, starting transfers between devices, shifted(): return lax.ppermute(value, AXIS, pairs)  43.2 us
    ppermute x8, waiting for transfers between devices, shifted(): return lax.ppermute(value, AXIS, pairs)  8.24 us
    pallas_call x1, Pallas kernels, window_grads(): pl.pallas_call(functools.partial(early_kernel, groups=groups, group_size=...  5.99 us
    pallas_call x1, Pallas kernels, window_grads(): pl.pallas_call(functools.partial(late_kernel, groups=groups, group_size=g...  5.88 us
    unnamed x26, local copies, waits for them, and re-layouts  3.41 us
  transfers between devices with their start and end apart: 11, of which 6 were waited for; matrix products, arithmetic and copies ran while one was open for 4% of the time, Pallas kernels for 16%

profile of v12, /device:TPU:6, one launch (start us, length us, event | category | flops | bytes accessed | tf_op | source)
XLA Modules:
  0.0 74.2 jit_solution(14157973467748398854)
XLA Ops:
  0.7 0.9 %pad_maximum_fusion.2 = bf16[1,64,1024]{2,1,0:T(8,128)(2,1)S(1)} fusion(bf16[2,64,512]{2,1,0:T(8,128)(2,1)} %bitcast.63, bf16[2,64,512]{2,1,0:T(8,128)(2,1)} %bitcast.59), kind=kLoop, calls=%fused_computation.23 | loop fusion | flops 262144 | bytes 393216 | tf_op jit(solution)/shard_map/concatenate | solution.py:215
  1.6 13.6 %collective-permute-start.2 = (bf16[64,1024]{1,0:T(8,128)(2,1)S(1)}, bf16[64,1024]{1,0:T(8,128)(2,1)S(1)}, u32[]{:S(2)}, u32[]{:S(2)}) collective-permute-start(bf16[64,1024]{1,0:T(8,128)(2,1)S(1)} %bitcast.69), channel_id=1, source_target_pairs={{1,0},{2,1},{3,2},{4,3},{5,4},{6,5},{7,6},{8,7},{9,8},{10,9},{11,1... | collective-permute-start | bytes 393224 | tf_op jit(solution)/shard_map/ppermute | solution.py:19
  15.2 0.7 copy-done.12
  15.8 0.3 reduce-window.9
  16.3 0.1 slice_reduce_fusion
  16.6 0.2 select_reduce_fusion
  16.8 2.1 %collective-permute-done.2.l1 = bf16[64,1024]{1,0:T(8,128)(2,1)S(1)} collective-permute-done((bf16[64,1024]{1,0:T(8,128)(2,1)S(1)}, bf16[64,1024]{1,0:T(8,128)(2,1)S(1)}, u32[]{:S(2)}, u32[]{:S(2)}) %collective-permute-start.2) | collective-permute-done | bytes 131104 | tf_op jit(solution)/shard_map/ppermute | solution.py:19
  19.0 0.6 copy-done.4
  19.6 1.9 %collective-permute-start = (bf16[64,1024]{1,0:T(8,128)(2,1)S(1)}, bf16[64,1024]{1,0:T(8,128)(2,1)S(1)}, u32[]{:S(2)}, u32[]{:S(2)}) collective-permute-start(bf16[64,1024]{1,0:T(8,128)(2,1)S(1)} %bitcast.70), channel_id=1, source_target_pairs={{0,1},{1,2},{2,3},{3,4},{4,5},{5,6},{6,7},{7,8},{8,9},{9,10},{10,1... | collective-permute-start | bytes 393224 | tf_op jit(solution)/shard_map/ppermute | solution.py:19
  21.6 0.1 copy.12
  21.7 0.7 collective-permute-start.4
  22.4 0.7 collective-permute-start.5
  23.1 8.6 %collective-permute-start.3 = (bf16[2,64,1024]{2,1,0:T(8,128)(2,1)S(1)}, bf16[2,64,1024]{2,1,0:T(8,128)(2,1)S(1)}, u32[]{:S(2)}, u32[]{:S(2)}) collective-permute-start(bf16[2,64,1024]{2,1,0:T(8,128)(2,1)S(1)} %pad_maximum_fusion.1), channel_id=1, source_target_pairs={{2,0},{3,1},{4,2},{5,3},{6,4},{7,5},{8,6},{9,7},{10,8},{11,9},{12,... | collective-permute-start | bytes 786440 | tf_op jit(solution)/shard_map/ppermute | solution.py:19
  31.8 0.6 copy-done.5
  32.4 1.9 %collective-permute-start.1 = (bf16[2,64,1024]{2,1,0:T(8,128)(2,1)S(1)}, bf16[2,64,1024]{2,1,0:T(8,128)(2,1)S(1)}, u32[]{:S(2)}, u32[]{:S(2)}) collective-permute-start(bf16[2,64,1024]{2,1,0:T(8,128)(2,1)S(1)} %pad_maximum_fusion), channel_id=1, source_target_pairs={{0,2},{1,3},{2,4},{3,5},{4,6},{5,7},{6,8},{7,9},{8,10},{9,11},{10,... | collective-permute-start | bytes 786440 | tf_op jit(solution)/shard_map/ppermute | solution.py:19
  34.3 0.7 broadcast_subtract_fusion.lo_ref
  35.0 0.6 add_convert_fusion.1.flags
  35.6 2.0 %collective-permute-done.3.l2 = bf16[2,64,1024]{2,1,0:T(8,128)(2,1)S(1)} collective-permute-done((bf16[2,64,1024]{2,1,0:T(8,128)(2,1)S(1)}, bf16[2,64,1024]{2,1,0:T(8,128)(2,1)S(1)}, u32[]{:S(2)}, u32[]{:S(2)}) %collective-permute-start.3) | collective-permute-done | bytes 262176 | tf_op jit(solution)/shard_map/ppermute | solution.py:19
  37.6 0.7 copy-done.8
  38.4 5.9 %shard_map.76 = (bf16[2,64,4096]{2,1,0:T(8,128)(2,1)}, bf16[2,64,1024]{2,1,0:T(8,128)(2,1)}, bf16[64,1024]{1,0:T(8,128)(2,1)}, f32[2,64,1024]{2,1,0:T(8,128)}) custom-call(s32[2]{0:T(128)} %add_convert_fusion.1.flags, s32[2,64,1]{2,1,0:T(8,128)} %broadcast_subtract_fusion.lo_ref, bf16[2,64,4096]{2,1,0:T(8,128)(2,1)} %bitcast.55, ...), custom_call_target="tpu_custom_call" | custom-call | flops 805306368 | bytes 1835008 | tf_op jit(solution)/shard_map/pallas_call | solution.py:183
  44.2 1.9 %collective-permute-start.8 = (bf16[2,64,1024]{2,1,0:T(8,128)(2,1)}, bf16[2,64,1024]{2,1,0:T(8,128)(2,1)S(1)}, u32[]{:S(2)}, u32[]{:S(2)}) collective-permute-start(bf16[2,64,1024]{2,1,0:T(8,128)(2,1)} %get-tuple-element.11.a_l), channel_id=1, source_target_pairs={{0,2},{1,3},{2,4},{3,5},{4,6},{5,7},{6,8},{7,9},{8,10},{9,11},{10,... | collective-permute-start | bytes 786440 | tf_op jit(solution)/shard_map/ppermute | solution.py:19
  46.2 0.7 copy-done.7
  46.9 6.0 %shard_map.77 = (bf16[2,64,4096]{2,1,0:T(8,128)(2,1)}, bf16[2,64,1024]{2,1,0:T(8,128)(2,1)}, bf16[64,1024]{1,0:T(8,128)(2,1)}, f32[2,64,1024]{2,1,0:T(8,128)}) custom-call(s32[2]{0:T(128)} %add_convert_fusion.1.flags, s32[2,64,1]{2,1,0:T(8,128)} %broadcast_subtract_fusion.lo_ref, ...), custom_call_target="tpu_custom_call", output_to_operand_aliasing={{0}: (10, {}), {3}: (11, {})} | custom-call | flops 805306368 | bytes 1835008 | tf_op jit(solution)/shard_map/pallas_call | solution.py:193
  52.9 6.8 %collective-permute-start.6 = (bf16[2,64,1024]{2,1,0:T(8,128)(2,1)}, bf16[2,64,1024]{2,1,0:T(8,128)(2,1)S(1)}, u32[]{:S(2)}, u32[]{:S(2)}) collective-permute-start(bf16[2,64,1024]{2,1,0:T(8,128)(2,1)} %get-tuple-element.17), channel_id=1, source_target_pairs={{2,0},{3,1},{4,2},{5,3},{6,4},{7,5},{8,6},{9,7},{10,8},{11,9},{12,... | collective-permute-start | bytes 786440 | tf_op jit(solution)/shard_map/ppermute | solution.py:19
  59.7 0.8 %collective-permute-start.9 = (bf16[64,1024]{1,0:T(8,128)(2,1)S(1)}, bf16[64,1024]{1,0:T(8,128)(2,1)S(1)}, u32[]{:S(2)}, u32[]{:S(2)}) collective-permute-start(bf16[64,1024]{1,0:T(8,128)(2,1)S(1)} %slice_bitcast_fusion.4), channel_id=1, source_target_pairs={{510,511}} | collective-permute-start | bytes 393224 | tf_op jit(solution)/shard_map/ppermute | solution.py:240
  60.7 2.1 %collective-permute-start.10 = (bf16[64,1024]{1,0:T(8,128)(2,1)S(1)}, bf16[64,1024]{1,0:T(8,128)(2,1)S(1)}, u32[]{:S(2)}, u32[]{:S(2)}) collective-permute-start(bf16[64,1024]{1,0:T(8,128)(2,1)S(1)} %add_convert_fusion), channel_id=1, source_target_pairs={{0,1},{1,2},{2,3},{3,4},{4,5},{5,6},{6,7},{7,8},{8,9},{9,10},{10,1... | collective-permute-start | bytes 393224 | tf_op jit(solution)/shard_map/ppermute | solution.py:19
  62.7 1.5 %collective-permute-done.6 = bf16[2,64,1024]{2,1,0:T(8,128)(2,1)S(1)} collective-permute-done((bf16[2,64,1024]{2,1,0:T(8,128)(2,1)}, bf16[2,64,1024]{2,1,0:T(8,128)(2,1)S(1)}, u32[]{:S(2)}, u32[]{:S(2)}) %collective-permute-start.6) | collective-permute-done | bytes 262176 | tf_op jit(solution)/shard_map/ppermute | solution.py:19
  64.3 6.4 %collective-permute-start.7 = (bf16[64,1024]{1,0:T(8,128)(2,1)S(1)}, bf16[64,1024]{1,0:T(8,128)(2,1)S(1)}, u32[]{:S(2)}, u32[]{:S(2)}) collective-permute-start(bf16[64,1024]{1,0:T(8,128)(2,1)S(1)} %fusion.4), channel_id=1, source_target_pairs={{1,0},{2,1},{3,2},{4,3},{5,4},{6,5},{7,6},{8,7},{9,8},{10,9},{11,1... | collective-permute-start | bytes 393224 | tf_op jit(solution)/shard_map/ppermute | solution.py:19
  70.7 1.4 %collective-permute-done.10 = bf16[64,1024]{1,0:T(8,128)(2,1)S(1)} collective-permute-done((bf16[64,1024]{1,0:T(8,128)(2,1)S(1)}, bf16[64,1024]{1,0:T(8,128)(2,1)S(1)}, u32[]{:S(2)}, u32[]{:S(2)}) %collective-permute-start.10) | collective-permute-done | bytes 131104 | tf_op jit(solution)/shard_map/ppermute | solution.py:19
  72.2 1.1 %collective-permute-done.7 = bf16[64,1024]{1,0:T(8,128)(2,1)S(1)} collective-permute-done((bf16[64,1024]{1,0:T(8,128)(2,1)S(1)}, bf16[64,1024]{1,0:T(8,128)(2,1)S(1)}, u32[]{:S(2)}, u32[]{:S(2)}) %collective-permute-start.7) | collective-permute-done | bytes 131104 | tf_op jit(solution)/shard_map/ppermute | solution.py:19
  73.3 0.1 fusion.8
  73.5 0.7 slice_bitcast_fusion.2
  (42 shorter events, 0.8 us)
Async XLA Ops:
  0.6 18.3 %copy-start.1 = (bf16[1,2,64,512]{3,2,1,0:T(8,128)(2,1)S(1)}, bf16[1,2,64,512]{3,2,1,0:T(8,128)(2,1)}, u32[]{:S(2)}) copy-start(bf16[1,2,64,512]{3,2,1,0:T(8,128)(2,1)} %param.6) | copy-start | bytes 393220
  0.6 18.3 %copy-start.2 = (bf16[1,2,64,512]{3,2,1,0:T(8,128)(2,1)S(1)}, bf16[1,2,64,512]{3,2,1,0:T(8,128)(2,1)}, u32[]{:S(2)}) copy-start(bf16[1,2,64,512]{3,2,1,0:T(8,128)(2,1)} %param.7) | copy-start | bytes 393220
  1.6 17.3 %collective-permute-start.2 = (bf16[64,1024]{1,0:T(8,128)(2,1)S(1)}, bf16[64,1024]{1,0:T(8,128)(2,1)S(1)}, u32[]{:S(2)}, u32[]{:S(2)}) collective-permute-start(bf16[64,1024]{1,0:T(8,128)(2,1)S(1)} %bitcast.69), channel_id=1, source_target_pairs={{1,0},{2,1},{3,2},{4,3},{5,4},{6,5},{7,6},{8,7},{9,8},{10,9},{11,1... | collective-permute-start | bytes 393224 | tf_op jit(solution)/shard_map/ppermute | solution.py:19
  15.2 0.7 copy-start.12
  18.9 0.7 copy-start.4
  19.6 12.2 %collective-permute-start = (bf16[64,1024]{1,0:T(8,128)(2,1)S(1)}, bf16[64,1024]{1,0:T(8,128)(2,1)S(1)}, u32[]{:S(2)}, u32[]{:S(2)}) collective-permute-start(bf16[64,1024]{1,0:T(8,128)(2,1)S(1)} %bitcast.70), channel_id=1, source_target_pairs={{0,1},{1,2},{2,3},{3,4},{4,5},{5,6},{6,7},{7,8},{8,9},{9,10},{10,1... | collective-permute-start | bytes 393224 | tf_op jit(solution)/shard_map/ppermute | solution.py:19
  21.7 13.9 %collective-permute-start.4 = (bf16[64,1024]{1,0:T(8,128)(2,1)S(1)}, bf16[64,1024]{1,0:T(8,128)(2,1)S(1)}, u32[]{:S(2)}, u32[]{:S(2)}) collective-permute-start(bf16[64,1024]{1,0:T(8,128)(2,1)S(1)} %bitcast.71), channel_id=1, source_target_pairs={{511,510},{510,511}} | collective-permute-start | bytes 393224 | tf_op jit(solution)/shard_map/ppermute | solution.py:222
  22.4 13.2 %collective-permute-start.5 = (bf16[64,1024]{1,0:T(8,128)(2,1)S(1)}, bf16[64,1024]{1,0:T(8,128)(2,1)S(1)}, u32[]{:S(2)}, u32[]{:S(2)}) collective-permute-start(bf16[64,1024]{1,0:T(8,128)(2,1)S(1)} %bitcast.72), channel_id=1, source_target_pairs={{509,511}} | collective-permute-start | bytes 393224 | tf_op jit(solution)/shard_map/ppermute | solution.py:223
  23.1 14.6 %collective-permute-start.3 = (bf16[2,64,1024]{2,1,0:T(8,128)(2,1)S(1)}, bf16[2,64,1024]{2,1,0:T(8,128)(2,1)S(1)}, u32[]{:S(2)}, u32[]{:S(2)}) collective-permute-start(bf16[2,64,1024]{2,1,0:T(8,128)(2,1)S(1)} %pad_maximum_fusion.1), channel_id=1, source_target_pairs={{2,0},{3,1},{4,2},{5,3},{6,4},{7,5},{8,6},{9,7},{10,8},{11,9},{12,... | collective-permute-start | bytes 786440 | tf_op jit(solution)/shard_map/ppermute | solution.py:19
  31.7 0.7 copy-start.5
  32.4 13.8 %collective-permute-start.1 = (bf16[2,64,1024]{2,1,0:T(8,128)(2,1)S(1)}, bf16[2,64,1024]{2,1,0:T(8,128)(2,1)S(1)}, u32[]{:S(2)}, u32[]{:S(2)}) collective-permute-start(bf16[2,64,1024]{2,1,0:T(8,128)(2,1)S(1)} %pad_maximum_fusion), channel_id=1, source_target_pairs={{0,2},{1,3},{2,4},{3,5},{4,6},{5,7},{6,8},{7,9},{8,10},{9,11},{10,... | collective-permute-start | bytes 786440 | tf_op jit(solution)/shard_map/ppermute | solution.py:19
  35.6 2.0 %copy-start.9 = (bf16[64,1024]{1,0:T(8,128)(2,1)}, bf16[64,1024]{1,0:T(8,128)(2,1)S(1)}, u32[]{:S(2)}) copy-start(bf16[64,1024]{1,0:T(8,128)(2,1)S(1)} %collective-permute-done.4.turn2) | copy-start | bytes 393220
  35.6 2.0 %copy-start.10 = (bf16[64,1024]{1,0:T(8,128)(2,1)}, bf16[64,1024]{1,0:T(8,128)(2,1)S(1)}, u32[]{:S(2)}) copy-start(bf16[64,1024]{1,0:T(8,128)(2,1)S(1)} %collective-permute-done.5.turn3) | copy-start | bytes 393220
  37.6 0.7 copy-start.8
  44.2 16.3 %collective-permute-start.8 = (bf16[2,64,1024]{2,1,0:T(8,128)(2,1)}, bf16[2,64,1024]{2,1,0:T(8,128)(2,1)S(1)}, u32[]{:S(2)}, u32[]{:S(2)}) collective-permute-start(bf16[2,64,1024]{2,1,0:T(8,128)(2,1)} %get-tuple-element.11.a_l), channel_id=1, source_target_pairs={{0,2},{1,3},{2,4},{3,5},{4,6},{5,7},{6,8},{7,9},{8,10},{9,11},{10,... | collective-permute-start | bytes 786440 | tf_op jit(solution)/shard_map/ppermute | solution.py:19
  46.2 0.7 copy-start.7
  46.9 12.8 %copy-start.3 = (bf16[2,64,1024]{2,1,0:T(8,128)(2,1)S(1)}, bf16[2,64,1024]{2,1,0:T(8,128)(2,1)}, u32[]{:S(2)}) copy-start(bf16[2,64,1024]{2,1,0:T(8,128)(2,1)} %get-tuple-element.11.a_l) | copy-start | bytes 786436
  52.9 11.3 %collective-permute-start.6 = (bf16[2,64,1024]{2,1,0:T(8,128)(2,1)}, bf16[2,64,1024]{2,1,0:T(8,128)(2,1)S(1)}, u32[]{:S(2)}, u32[]{:S(2)}) collective-permute-start(bf16[2,64,1024]{2,1,0:T(8,128)(2,1)} %get-tuple-element.17), channel_id=1, source_target_pairs={{2,0},{3,1},{4,2},{5,3},{6,4},{7,5},{8,6},{9,7},{10,8},{11,9},{12,... | collective-permute-start | bytes 786440 | tf_op jit(solution)/shard_map/ppermute | solution.py:19
  59.7 0.9 %copy-start.6 = (bf16[64,1024]{1,0:T(8,128)(2,1)S(1)}, bf16[64,1024]{1,0:T(8,128)(2,1)}, u32[]{:S(2)}) copy-start(bf16[64,1024]{1,0:T(8,128)(2,1)} %get-tuple-element.12.p2_late) | copy-start | bytes 393220
  59.7 11.0 %collective-permute-start.9 = (bf16[64,1024]{1,0:T(8,128)(2,1)S(1)}, bf16[64,1024]{1,0:T(8,128)(2,1)S(1)}, u32[]{:S(2)}, u32[]{:S(2)}) collective-permute-start(bf16[64,1024]{1,0:T(8,128)(2,1)S(1)} %slice_bitcast_fusion.4), channel_id=1, source_target_pairs={{510,511}} | collective-permute-start | bytes 393224 | tf_op jit(solution)/shard_map/ppermute | solution.py:240
  60.7 3.6 %copy-start.11 = (bf16[64,1024]{1,0:T(8,128)(2,1)S(1)}, bf16[64,1024]{1,0:T(8,128)(2,1)}, u32[]{:S(2)}) copy-start(bf16[64,1024]{1,0:T(8,128)(2,1)} %get-tuple-element.18) | copy-start | bytes 393220
  60.7 12.6 %copy-start = (f32[2,64,1024]{2,1,0:T(8,128)S(1)}, f32[2,64,1024]{2,1,0:T(8,128)}, u32[]{:S(2)}) copy-start(f32[2,64,1024]{2,1,0:T(8,128)} %get-tuple-element.16) | copy-start | bytes 1572868
  60.7 11.5 %collective-permute-start.10 = (bf16[64,1024]{1,0:T(8,128)(2,1)S(1)}, bf16[64,1024]{1,0:T(8,128)(2,1)S(1)}, u32[]{:S(2)}, u32[]{:S(2)}) collective-permute-start(bf16[64,1024]{1,0:T(8,128)(2,1)S(1)} %add_convert_fusion), channel_id=1, source_target_pairs={{0,1},{1,2},{2,3},{3,4},{4,5},{5,6},{6,7},{7,8},{8,9},{9,10},{10,1... | collective-permute-start | bytes 393224 | tf_op jit(solution)/shard_map/ppermute | solution.py:19
  64.3 9.0 %collective-permute-start.7 = (bf16[64,1024]{1,0:T(8,128)(2,1)S(1)}, bf16[64,1024]{1,0:T(8,128)(2,1)S(1)}, u32[]{:S(2)}, u32[]{:S(2)}) collective-permute-start(bf16[64,1024]{1,0:T(8,128)(2,1)S(1)} %fusion.4), channel_id=1, source_target_pairs={{1,0},{2,1},{3,2},{4,3},{5,4},{6,5},{7,6},{8,7},{9,8},{10,9},{11,1... | collective-permute-start | bytes 393224 | tf_op jit(solution)/shard_map/ppermute | solution.py:19

commit v13 on v12

--- a/solution.py
+++ b/solution.py
@@ -24,7 +24,11 @@
     window = 4 * half_rows
     kv_width = groups * HEAD
     scale = 1.0 / math.sqrt(HEAD)
-    lo = lo_ref[0]
+    block = lo_ref.block(half)
+    ends = lo_ref.ends[...]
+    query_pos = block * half_rows + lax.broadcasted_iota(jnp.int32, (half_rows, ends.shape[1]), 0)
+    doc_start = jnp.max(jnp.where(ends <= query_pos, ends, 0), axis=1, keepdims=True)
+    lo = doc_start - (block - REACH) * half_rows
     rows = lax.broadcasted_iota(jnp.int32, (half_rows, window), 0)
     cols = lax.broadcasted_iota(jnp.int32, (half_rows, window), 1)
     visible = (cols >= lo) & (cols <= rows + (window - half_rows))
@@ -62,6 +66,15 @@
             emit("part", j, kv_width + g * HEAD, dv[j * half_rows:(j + 1) * half_rows])
 
 
+class DocBounds:
+    def __init__(self, flags, ends):
+        self.flags = flags
+        self.ends = ends
+
+    def block(self, half):
+        return self.flags[2 + half]
+
+
 class OwnBlocks:
     def __init__(self, keys, values):
         self.keys = keys
@@ -76,9 +89,10 @@
 
 
 def late_kernel(
-    flags, lo_ref, q_ref, do_ref, keys, values, l1, l2, turn2, turn3,
+    flags, ends_ref, q_ref, do_ref, keys, values, l1, l2, turn2, turn3,
     dq_ref, a_l, p2_ref, p3_ref, *, groups, group_size
 ):
+    lo_ref = DocBounds(flags, ends_ref)
     at_top = flags[0] != 0
     below_top = flags[1] != 0
     kv = OwnBlocks(keys, values)
@@ -112,9 +126,10 @@
 
 
 def early_kernel(
-    flags, lo_ref, q_ref, do_ref, keys, values, e1, e2, a_l, p2_late, dq_in, p3_in,
+    flags, ends_ref, q_ref, do_ref, keys, values, e1, e2, a_l, p2_late, dq_in, p3_in,
     dq_ref, a_e, p2_ref, p3_ref, *, groups, group_size
 ):
+    lo_ref = DocBounds(flags, ends_ref)
     del dq_in, p3_in
     at_top = flags[0] != 0
     below_top = flags[1] != 0
@@ -164,7 +179,7 @@
 
     def half_specs(half):
         q_spec = pl.BlockSpec((1, half_rows, width), lambda s: (half, 0, 0))
-        lo_spec = pl.BlockSpec((1, half_rows, 1), lambda s: (half, 0, 0))
+        lo_spec = pl.BlockSpec(lo.shape, lambda s: (0, 0))
         part_spec = pl.BlockSpec((1, half_rows, kv2), lambda s: (half, 0, 0))
         return q_spec, lo_spec, part_spec
 
@@ -224,13 +239,8 @@
     e2 = shifted(jnp.stack([early, e1]), 2)
     l2 = shifted(jnp.stack([late, jnp.where(at_top, early, l1)]), -2)
 
-    doc_ends = jnp.cumsum(lengths)
-    block_ids = jnp.stack([me, 2 * n - 1 - me])
-    query_pos = block_ids[:, None] * half_rows + jnp.arange(half_rows, dtype=jnp.int32)[None, :]
-    ends = doc_ends[None, None, :]
-    doc_start = jnp.max(jnp.where(ends <= query_pos[:, :, None], ends, 0), axis=2)
-    lo = (doc_start - (block_ids[:, None] - REACH) * half_rows).astype(jnp.int32)[:, :, None]
-    flags = jnp.stack([at_top, below_top]).astype(jnp.int32)
+    lo = jnp.cumsum(lengths).astype(jnp.int32)[None, :]
+    flags = jnp.stack([at_top, below_top, me, 2 * n - 1 - me]).astype(jnp.int32)
 
     dq, a_e, a_l, p2, p3 = window_grads(flags, lo, q, do, keys[0], values[0], e1, e2, l1, l2, turn2, turn3)
 

time: 74.9 us -> 74.8 us (level)
    another operation x4 -> x5, other arithmetic: 0.44 us -> 1.65 us
  transfers between devices with their start and end apart: 11 -> 11, of which waited for: 6 -> 6; matrix products, arithmetic and copies ran while one was open for 4% -> 3% of each run, Pallas kernels for 16% -> 16%
where the time goes in v13:
time: 74.8 us; the launch traced here: 74.1 us
  starting transfers between devices  45.3 us (61%)
  Pallas kernels  11.9 us (16%)
  waiting for transfers between devices  8.82 us (12%)
  local copies, waits for them, and re-layouts  4.3 us (6%)
  other arithmetic  2.95 us (4%)
  between operations  0.91 us (1%)
    ppermute x8, starting transfers between devices, shifted(): return lax.ppermute(value, AXIS, pairs)  43.1 us
    ppermute x8, waiting for transfers between devices, shifted(): return lax.ppermute(value, AXIS, pairs)  8.81 us
    pallas_call x1, Pallas kernels, window_grads(): pl.pallas_call(functools.partial(early_kernel, groups=groups, group_size=...  6 us
    pallas_call x1, Pallas kernels, window_grads(): pl.pallas_call(functools.partial(late_kernel, groups=groups, group_size=g...  5.9 us
    unnamed x26, local copies, waits for them, and re-layouts  3.38 us
  transfers between devices with their start and end apart: 11, of which 6 were waited for; matrix products, arithmetic and copies ran while one was open for 3% of the time, Pallas kernels for 16%

profile of v13, /device:TPU:6, one launch (start us, length us, event | category | flops | bytes accessed | tf_op | source)
XLA Modules:
  0.0 74.1 jit_solution(814454378146316132)
XLA Ops:
  0.7 0.9 %pad_maximum_fusion.2 = bf16[1,64,1024]{2,1,0:T(8,128)(2,1)S(1)} fusion(bf16[2,64,512]{2,1,0:T(8,128)(2,1)} %bitcast.61, bf16[2,64,512]{2,1,0:T(8,128)(2,1)} %bitcast.57), kind=kLoop, calls=%fused_computation.22 | loop fusion | flops 262144 | bytes 393216 | tf_op jit(solution)/shard_map/concatenate | solution.py:230
  1.6 13.6 %collective-permute-start.2 = (bf16[64,1024]{1,0:T(8,128)(2,1)S(1)}, bf16[64,1024]{1,0:T(8,128)(2,1)S(1)}, u32[]{:S(2)}, u32[]{:S(2)}) collective-permute-start(bf16[64,1024]{1,0:T(8,128)(2,1)S(1)} %bitcast.67), channel_id=1, source_target_pairs={{1,0},{2,1},{3,2},{4,3},{5,4},{6,5},{7,6},{8,7},{9,8},{10,9},{11,1... | collective-permute-start | bytes 393224 | tf_op jit(solution)/shard_map/ppermute | solution.py:19
  15.2 0.7 copy-done.12
  15.8 0.3 reduce-window.9
  16.1 0.1 slice.43
  16.3 2.7 %collective-permute-done.2.l1 = bf16[64,1024]{1,0:T(8,128)(2,1)S(1)} collective-permute-done((bf16[64,1024]{1,0:T(8,128)(2,1)S(1)}, bf16[64,1024]{1,0:T(8,128)(2,1)S(1)}, u32[]{:S(2)}, u32[]{:S(2)}) %collective-permute-start.2) | collective-permute-done | bytes 131104 | tf_op jit(solution)/shard_map/ppermute | solution.py:19
  19.0 0.6 copy-done.4
  19.6 1.9 %collective-permute-start = (bf16[64,1024]{1,0:T(8,128)(2,1)S(1)}, bf16[64,1024]{1,0:T(8,128)(2,1)S(1)}, u32[]{:S(2)}, u32[]{:S(2)}) collective-permute-start(bf16[64,1024]{1,0:T(8,128)(2,1)S(1)} %bitcast.68), channel_id=1, source_target_pairs={{0,1},{1,2},{2,3},{3,4},{4,5},{5,6},{6,7},{7,8},{8,9},{9,10},{10,1... | collective-permute-start | bytes 393224 | tf_op jit(solution)/shard_map/ppermute | solution.py:19
  21.5 0.1 slice_reduce_fusion
  21.6 0.7 collective-permute-start.4
  22.3 0.7 collective-permute-start.5
  23.0 8.6 %collective-permute-start.3 = (bf16[2,64,1024]{2,1,0:T(8,128)(2,1)S(1)}, bf16[2,64,1024]{2,1,0:T(8,128)(2,1)S(1)}, u32[]{:S(2)}, u32[]{:S(2)}) collective-permute-start(bf16[2,64,1024]{2,1,0:T(8,128)(2,1)S(1)} %pad_maximum_fusion.1), channel_id=1, source_target_pairs={{2,0},{3,1},{4,2},{5,3},{6,4},{7,5},{8,6},{9,7},{10,8},{11,9},{12,... | collective-permute-start | bytes 786440 | tf_op jit(solution)/shard_map/ppermute | solution.py:19
  31.6 0.1 collective-permute-done.e1
  31.8 0.6 copy-done.5
  32.4 1.9 %collective-permute-start.1 = (bf16[2,64,1024]{2,1,0:T(8,128)(2,1)S(1)}, bf16[2,64,1024]{2,1,0:T(8,128)(2,1)S(1)}, u32[]{:S(2)}, u32[]{:S(2)}) collective-permute-start(bf16[2,64,1024]{2,1,0:T(8,128)(2,1)S(1)} %pad_maximum_fusion), channel_id=1, source_target_pairs={{0,2},{1,3},{2,4},{3,5},{4,6},{5,7},{6,8},{7,9},{8,10},{9,11},{10,... | collective-permute-start | bytes 786440 | tf_op jit(solution)/shard_map/ppermute | solution.py:19
  34.3 0.6 broadcast_add_fusion
  34.9 0.7 pad_add_fusion.flags
  35.6 1.9 %collective-permute-done.3.l2 = bf16[2,64,1024]{2,1,0:T(8,128)(2,1)S(1)} collective-permute-done((bf16[2,64,1024]{2,1,0:T(8,128)(2,1)S(1)}, bf16[2,64,1024]{2,1,0:T(8,128)(2,1)S(1)}, u32[]{:S(2)}, u32[]{:S(2)}) %collective-permute-start.3) | collective-permute-done | bytes 262176 | tf_op jit(solution)/shard_map/ppermute | solution.py:19
  37.6 0.7 copy-done.8
  38.2 5.9 %shard_map.76 = (bf16[2,64,4096]{2,1,0:T(8,128)(2,1)}, bf16[2,64,1024]{2,1,0:T(8,128)(2,1)}, bf16[64,1024]{1,0:T(8,128)(2,1)}, f32[2,64,1024]{2,1,0:T(8,128)}) custom-call(s32[4]{0:T(128)} %pad_add_fusion.flags, s32[1,512]{1,0:T(1,128)} %bitcast.71, bf16[2,64,4096]{2,1,0:T(8,128)(2,1)} %bitcast.53, bf16[2,64,4096]{2,1,0:T(8,128)(2,1)} %bitcast.55, ...), custom_call_target="tpu_custom_call" | custom-call | flops 805306368 | bytes 1835008 | tf_op jit(solution)/shard_map/pallas_call | solution.py:198
  44.1 1.9 %collective-permute-start.8 = (bf16[2,64,1024]{2,1,0:T(8,128)(2,1)}, bf16[2,64,1024]{2,1,0:T(8,128)(2,1)S(1)}, u32[]{:S(2)}, u32[]{:S(2)}) collective-permute-start(bf16[2,64,1024]{2,1,0:T(8,128)(2,1)} %get-tuple-element.11.a_l), channel_id=1, source_target_pairs={{0,2},{1,3},{2,4},{3,5},{4,6},{5,7},{6,8},{7,9},{8,10},{9,11},{10,... | collective-permute-start | bytes 786440 | tf_op jit(solution)/shard_map/ppermute | solution.py:19
  46.1 0.7 copy-done.7
  46.8 6.0 %shard_map.77 = (bf16[2,64,4096]{2,1,0:T(8,128)(2,1)}, bf16[2,64,1024]{2,1,0:T(8,128)(2,1)}, bf16[64,1024]{1,0:T(8,128)(2,1)}, f32[2,64,1024]{2,1,0:T(8,128)}) custom-call(s32[4]{0:T(128)} %pad_add_fusion.flags, s32[1,512]{1,0:T(1,128)} %bitcast.72, bf16[2,64,4096]{2,1,0:T(8,128)(2,1)} %bitcast.54, ...), custom_call_target="tpu_custom_call", output_to_operand_aliasing={{0}: (10, {}), {3}: (11, {})} | custom-call | flops 805306368 | bytes 1835008 | tf_op jit(solution)/shard_map/pallas_call | solution.py:208
  52.8 6.8 %collective-permute-start.6 = (bf16[2,64,1024]{2,1,0:T(8,128)(2,1)}, bf16[2,64,1024]{2,1,0:T(8,128)(2,1)S(1)}, u32[]{:S(2)}, u32[]{:S(2)}) collective-permute-start(bf16[2,64,1024]{2,1,0:T(8,128)(2,1)} %get-tuple-element.17), channel_id=1, source_target_pairs={{2,0},{3,1},{4,2},{5,3},{6,4},{7,5},{8,6},{9,7},{10,8},{11,9},{12,... | collective-permute-start | bytes 786440 | tf_op jit(solution)/shard_map/ppermute | solution.py:19
  59.6 0.8 %collective-permute-start.9 = (bf16[64,1024]{1,0:T(8,128)(2,1)S(1)}, bf16[64,1024]{1,0:T(8,128)(2,1)S(1)}, u32[]{:S(2)}, u32[]{:S(2)}) collective-permute-start(bf16[64,1024]{1,0:T(8,128)(2,1)S(1)} %slice_bitcast_fusion.4), channel_id=1, source_target_pairs={{510,511}} | collective-permute-start | bytes 393224 | tf_op jit(solution)/shard_map/ppermute | solution.py:250
  60.6 2.1 %collective-permute-start.10 = (bf16[64,1024]{1,0:T(8,128)(2,1)S(1)}, bf16[64,1024]{1,0:T(8,128)(2,1)S(1)}, u32[]{:S(2)}, u32[]{:S(2)}) collective-permute-start(bf16[64,1024]{1,0:T(8,128)(2,1)S(1)} %add_convert_fusion), channel_id=1, source_target_pairs={{0,1},{1,2},{2,3},{3,4},{4,5},{5,6},{6,7},{7,8},{8,9},{9,10},{10,1... | collective-permute-start | bytes 393224 | tf_op jit(solution)/shard_map/ppermute | solution.py:19
  62.7 1.5 %collective-permute-done.6 = bf16[2,64,1024]{2,1,0:T(8,128)(2,1)S(1)} collective-permute-done((bf16[2,64,1024]{2,1,0:T(8,128)(2,1)}, bf16[2,64,1024]{2,1,0:T(8,128)(2,1)S(1)}, u32[]{:S(2)}, u32[]{:S(2)}) %collective-permute-start.6) | collective-permute-done | bytes 262176 | tf_op jit(solution)/shard_map/ppermute | solution.py:19
  64.2 6.4 %collective-permute-start.7 = (bf16[64,1024]{1,0:T(8,128)(2,1)S(1)}, bf16[64,1024]{1,0:T(8,128)(2,1)S(1)}, u32[]{:S(2)}, u32[]{:S(2)}) collective-permute-start(bf16[64,1024]{1,0:T(8,128)(2,1)S(1)} %fusion.4), channel_id=1, source_target_pairs={{1,0},{2,1},{3,2},{4,3},{5,4},{6,5},{7,6},{8,7},{9,8},{10,9},{11,1... | collective-permute-start | bytes 393224 | tf_op jit(solution)/shard_map/ppermute | solution.py:19
  70.6 1.4 %collective-permute-done.10 = bf16[64,1024]{1,0:T(8,128)(2,1)S(1)} collective-permute-done((bf16[64,1024]{1,0:T(8,128)(2,1)S(1)}, bf16[64,1024]{1,0:T(8,128)(2,1)S(1)}, u32[]{:S(2)}, u32[]{:S(2)}) %collective-permute-start.10) | collective-permute-done | bytes 131104 | tf_op jit(solution)/shard_map/ppermute | solution.py:19
  72.1 1.2 %collective-permute-done.7 = bf16[64,1024]{1,0:T(8,128)(2,1)S(1)} collective-permute-done((bf16[64,1024]{1,0:T(8,128)(2,1)S(1)}, bf16[64,1024]{1,0:T(8,128)(2,1)S(1)}, u32[]{:S(2)}, u32[]{:S(2)}) %collective-permute-start.7) | collective-permute-done | bytes 131104 | tf_op jit(solution)/shard_map/ppermute | solution.py:19
  73.2 0.1 fusion.8
  73.4 0.7 slice_bitcast_fusion.2
  (36 shorter events, 0.4 us)
Async XLA Ops:
  0.6 18.3 %copy-start.1 = (bf16[1,2,64,512]{3,2,1,0:T(8,128)(2,1)S(1)}, bf16[1,2,64,512]{3,2,1,0:T(8,128)(2,1)}, u32[]{:S(2)}) copy-start(bf16[1,2,64,512]{3,2,1,0:T(8,128)(2,1)} %param.6) | copy-start | bytes 393220
  0.6 18.3 %copy-start.2 = (bf16[1,2,64,512]{3,2,1,0:T(8,128)(2,1)S(1)}, bf16[1,2,64,512]{3,2,1,0:T(8,128)(2,1)}, u32[]{:S(2)}) copy-start(bf16[1,2,64,512]{3,2,1,0:T(8,128)(2,1)} %param.7) | copy-start | bytes 393220
  1.6 17.3 %collective-permute-start.2 = (bf16[64,1024]{1,0:T(8,128)(2,1)S(1)}, bf16[64,1024]{1,0:T(8,128)(2,1)S(1)}, u32[]{:S(2)}, u32[]{:S(2)}) collective-permute-start(bf16[64,1024]{1,0:T(8,128)(2,1)S(1)} %bitcast.67), channel_id=1, source_target_pairs={{1,0},{2,1},{3,2},{4,3},{5,4},{6,5},{7,6},{8,7},{9,8},{10,9},{11,1... | collective-permute-start | bytes 393224 | tf_op jit(solution)/shard_map/ppermute | solution.py:19
  15.2 0.7 copy-start.12
  18.9 0.7 copy-start.4
  19.6 12.2 %collective-permute-start = (bf16[64,1024]{1,0:T(8,128)(2,1)S(1)}, bf16[64,1024]{1,0:T(8,128)(2,1)S(1)}, u32[]{:S(2)}, u32[]{:S(2)}) collective-permute-start(bf16[64,1024]{1,0:T(8,128)(2,1)S(1)} %bitcast.68), channel_id=1, source_target_pairs={{0,1},{1,2},{2,3},{3,4},{4,5},{5,6},{6,7},{7,8},{8,9},{9,10},{10,1... | collective-permute-start | bytes 393224 | tf_op jit(solution)/shard_map/ppermute | solution.py:19
  21.6 14.0 %collective-permute-start.4 = (bf16[64,1024]{1,0:T(8,128)(2,1)S(1)}, bf16[64,1024]{1,0:T(8,128)(2,1)S(1)}, u32[]{:S(2)}, u32[]{:S(2)}) collective-permute-start(bf16[64,1024]{1,0:T(8,128)(2,1)S(1)} %bitcast.69), channel_id=1, source_target_pairs={{511,510},{510,511}} | collective-permute-start | bytes 393224 | tf_op jit(solution)/shard_map/ppermute | solution.py:237
  22.3 13.3 %collective-permute-start.5 = (bf16[64,1024]{1,0:T(8,128)(2,1)S(1)}, bf16[64,1024]{1,0:T(8,128)(2,1)S(1)}, u32[]{:S(2)}, u32[]{:S(2)}) collective-permute-start(bf16[64,1024]{1,0:T(8,128)(2,1)S(1)} %bitcast.70), channel_id=1, source_target_pairs={{509,511}} | collective-permute-start | bytes 393224 | tf_op jit(solution)/shard_map/ppermute | solution.py:238
  23.0 14.6 %collective-permute-start.3 = (bf16[2,64,1024]{2,1,0:T(8,128)(2,1)S(1)}, bf16[2,64,1024]{2,1,0:T(8,128)(2,1)S(1)}, u32[]{:S(2)}, u32[]{:S(2)}) collective-permute-start(bf16[2,64,1024]{2,1,0:T(8,128)(2,1)S(1)} %pad_maximum_fusion.1), channel_id=1, source_target_pairs={{2,0},{3,1},{4,2},{5,3},{6,4},{7,5},{8,6},{9,7},{10,8},{11,9},{12,... | collective-permute-start | bytes 786440 | tf_op jit(solution)/shard_map/ppermute | solution.py:19
  31.7 0.7 copy-start.5
  32.4 13.7 %collective-permute-start.1 = (bf16[2,64,1024]{2,1,0:T(8,128)(2,1)S(1)}, bf16[2,64,1024]{2,1,0:T(8,128)(2,1)S(1)}, u32[]{:S(2)}, u32[]{:S(2)}) collective-permute-start(bf16[2,64,1024]{2,1,0:T(8,128)(2,1)S(1)} %pad_maximum_fusion), channel_id=1, source_target_pairs={{0,2},{1,3},{2,4},{3,5},{4,6},{5,7},{6,8},{7,9},{8,10},{9,11},{10,... | collective-permute-start | bytes 786440 | tf_op jit(solution)/shard_map/ppermute | solution.py:19
  35.6 2.0 %copy-start.9 = (bf16[64,1024]{1,0:T(8,128)(2,1)}, bf16[64,1024]{1,0:T(8,128)(2,1)S(1)}, u32[]{:S(2)}) copy-start(bf16[64,1024]{1,0:T(8,128)(2,1)S(1)} %collective-permute-done.4.turn2) | copy-start | bytes 393220
  35.6 2.0 %copy-start.10 = (bf16[64,1024]{1,0:T(8,128)(2,1)}, bf16[64,1024]{1,0:T(8,128)(2,1)S(1)}, u32[]{:S(2)}) copy-start(bf16[64,1024]{1,0:T(8,128)(2,1)S(1)} %collective-permute-done.5.turn3) | copy-start | bytes 393220
  37.6 0.7 copy-start.8
  44.1 16.3 %collective-permute-start.8 = (bf16[2,64,1024]{2,1,0:T(8,128)(2,1)}, bf16[2,64,1024]{2,1,0:T(8,128)(2,1)S(1)}, u32[]{:S(2)}, u32[]{:S(2)}) collective-permute-start(bf16[2,64,1024]{2,1,0:T(8,128)(2,1)} %get-tuple-element.11.a_l), channel_id=1, source_target_pairs={{0,2},{1,3},{2,4},{3,5},{4,6},{5,7},{6,8},{7,9},{8,10},{9,11},{10,... | collective-permute-start | bytes 786440 | tf_op jit(solution)/shard_map/ppermute | solution.py:19
  46.1 0.7 copy-start.7
  46.8 12.8 %copy-start.3 = (bf16[2,64,1024]{2,1,0:T(8,128)(2,1)S(1)}, bf16[2,64,1024]{2,1,0:T(8,128)(2,1)}, u32[]{:S(2)}) copy-start(bf16[2,64,1024]{2,1,0:T(8,128)(2,1)} %get-tuple-element.11.a_l) | copy-start | bytes 786436
  52.8 11.3 %collective-permute-start.6 = (bf16[2,64,1024]{2,1,0:T(8,128)(2,1)}, bf16[2,64,1024]{2,1,0:T(8,128)(2,1)S(1)}, u32[]{:S(2)}, u32[]{:S(2)}) collective-permute-start(bf16[2,64,1024]{2,1,0:T(8,128)(2,1)} %get-tuple-element.17), channel_id=1, source_target_pairs={{2,0},{3,1},{4,2},{5,3},{6,4},{7,5},{8,6},{9,7},{10,8},{11,9},{12,... | collective-permute-start | bytes 786440 | tf_op jit(solution)/shard_map/ppermute | solution.py:19
  59.6 0.9 %copy-start.6 = (bf16[64,1024]{1,0:T(8,128)(2,1)S(1)}, bf16[64,1024]{1,0:T(8,128)(2,1)}, u32[]{:S(2)}) copy-start(bf16[64,1024]{1,0:T(8,128)(2,1)} %get-tuple-element.12.p2_late) | copy-start | bytes 393220
  59.6 11.0 %collective-permute-start.9 = (bf16[64,1024]{1,0:T(8,128)(2,1)S(1)}, bf16[64,1024]{1,0:T(8,128)(2,1)S(1)}, u32[]{:S(2)}, u32[]{:S(2)}) collective-permute-start(bf16[64,1024]{1,0:T(8,128)(2,1)S(1)} %slice_bitcast_fusion.4), channel_id=1, source_target_pairs={{510,511}} | collective-permute-start | bytes 393224 | tf_op jit(solution)/shard_map/ppermute | solution.py:250
  60.6 3.6 %copy-start.11 = (bf16[64,1024]{1,0:T(8,128)(2,1)S(1)}, bf16[64,1024]{1,0:T(8,128)(2,1)}, u32[]{:S(2)}) copy-start(bf16[64,1024]{1,0:T(8,128)(2,1)} %get-tuple-element.18) | copy-start | bytes 393220
  60.6 12.7 %copy-start = (f32[2,64,1024]{2,1,0:T(8,128)S(1)}, f32[2,64,1024]{2,1,0:T(8,128)}, u32[]{:S(2)}) copy-start(f32[2,64,1024]{2,1,0:T(8,128)} %get-tuple-element.16) | copy-start | bytes 1572868
  60.6 11.5 %collective-permute-start.10 = (bf16[64,1024]{1,0:T(8,128)(2,1)S(1)}, bf16[64,1024]{1,0:T(8,128)(2,1)S(1)}, u32[]{:S(2)}, u32[]{:S(2)}) collective-permute-start(bf16[64,1024]{1,0:T(8,128)(2,1)S(1)} %add_convert_fusion), channel_id=1, source_target_pairs={{0,1},{1,2},{2,3},{3,4},{4,5},{5,6},{6,7},{7,8},{8,9},{9,10},{10,1... | collective-permute-start | bytes 393224 | tf_op jit(solution)/shard_map/ppermute | solution.py:19
  64.2 9.0 %collective-permute-start.7 = (bf16[64,1024]{1,0:T(8,128)(2,1)S(1)}, bf16[64,1024]{1,0:T(8,128)(2,1)S(1)}, u32[]{:S(2)}, u32[]{:S(2)}) collective-permute-start(bf16[64,1024]{1,0:T(8,128)(2,1)S(1)} %fusion.4), channel_id=1, source_target_pairs={{1,0},{2,1},{3,2},{4,3},{5,4},{6,5},{7,6},{8,7},{9,8},{10,9},{11,1... | collective-permute-start | bytes 393224 | tf_op jit(solution)/shard_map/ppermute | solution.py:19

commit v14 on v13

--- a/solution.py
+++ b/solution.py
@@ -232,8 +232,17 @@
     at_top = me == n - 1
     below_top = me == n - 2
 
-    e1 = shifted(early, 1)
-    l1 = shifted(late, -1)
+    even = me % 2 == 0
+    first = lax.ppermute(
+        jnp.where(even, early, late), AXIS,
+        [(s, s ^ 1) for s in range(n)],
+    )
+    second = lax.ppermute(
+        jnp.where(even, late, early), AXIS,
+        [(s, s + 1 if s % 2 else s - 1) for s in range(1, n - 1)],
+    )
+    e1 = jnp.where(even, second, first)
+    l1 = jnp.where(even, first, second)
     turn2 = lax.ppermute(early, AXIS, [(n - 1, n - 2), (n - 2, n - 1)])
     turn3 = lax.ppermute(early, AXIS, [(n - 3, n - 1)])
     e2 = shifted(jnp.stack([early, e1]), 2)

time: 74.8 us -> 82.9 us (1.11)
  waiting for transfers between devices: 8.82 us -> 19.9 us
  starting transfers between devices: 45.3 us -> 43.1 us
  local copies, waits for them, and re-layouts: 4.3 us -> 2.98 us
    ppermute x8 -> x6, starting transfers between devices: 43.1 us -> 25.4 us  [shifted(): return lax.ppermute(value, AXIS, pairs)]
    ppermute x0 -> x2, starting transfers between devices: none -> 15.5 us  [the longest x1 13.6 us: on_device(): lax.ppermute(jnp.where(even, late, early), AXIS, [(s, s + 1 if s % 2 else...]
    ppermute x8 -> x6, waiting for transfers between devices: 8.81 us -> 14.4 us  [shifted(): return lax.ppermute(value, AXIS, pairs)]
    ppermute x0 -> x2, waiting for transfers between devices: none -> 5.54 us  [the longest x1 5.54 us: on_device(): lax.ppermute(jnp.where(even, early, late), AXIS, [(s, s ^ 1) for s in ran...]
    unnamed x26 -> x20, local copies, waits for them, and re-layouts: 3.38 us -> 2.06 us
    select_n x0 -> x2, other arithmetic: none -> 0.99 us  [the longest x1 0.97 us: on_device(): jnp.where(even, early, late)]
    concatenate x1 -> x0, other arithmetic: 0.92 us -> none  [on_device(): kv = jnp.concatenate([keys[0], values[0]], axis=2)]
  transfers between devices with their start and end apart: 11 -> 11, of which waited for: 6 -> 5; matrix products, arithmetic and copies ran while one was open for 3% -> 3% of each run, Pallas kernels for 16% -> 7%
where the time goes in v14:
time: 82.9 us; the launch traced here: 82.4 us
  starting transfers between devices  43.1 us (52%)
  waiting for transfers between devices  19.9 us (24%)
  Pallas kernels  11.9 us (14%)
  other arithmetic  3.64 us (4%)
  local copies, waits for them, and re-layouts  2.98 us (4%)
  between operations  0.91 us (1%)
    ppermute x6, starting transfers between devices, shifted(): return lax.ppermute(value, AXIS, pairs)  25.4 us
    ppermute x6, waiting for transfers between devices, shifted(): return lax.ppermute(value, AXIS, pairs)  14.4 us
    ppermute x1, starting transfers between devices, on_device(): lax.ppermute(jnp.where(even, late, early), AXIS, [(s, s + 1 if s % 2 else...  13.6 us
    pallas_call x1, Pallas kernels, window_grads(): pl.pallas_call(functools.partial(early_kernel, groups=groups, group_size=...  6 us
    pallas_call x1, Pallas kernels, window_grads(): pl.pallas_call(functools.partial(late_kernel, groups=groups, group_size=g...  5.9 us
    ppermute x1, waiting for transfers between devices, on_device(): lax.ppermute(jnp.where(even, early, late), AXIS, [(s, s ^ 1) for s in ran...  5.54 us
    unnamed x20, local copies, waits for them, and re-layouts  2.06 us
    ppermute x1, starting transfers between devices, on_device(): lax.ppermute(jnp.where(even, early, late), AXIS, [(s, s ^ 1) for s in ran...  1.92 us
  transfers between devices with their start and end apart: 11, of which 5 were waited for; matrix products, arithmetic and copies ran while one was open for 3% of the time, Pallas kernels for 7%

profile of v14, /device:TPU:6, one launch (start us, length us, event | category | flops | bytes accessed | tf_op | source)
XLA Modules:
  0.0 82.4 jit_solution(6199553977459964360)
XLA Ops:
  0.6 1.0 %bitcast_select_fusion = (bf16[64,1024]{1,0:T(8,128)(2,1)S(1)}, bf16[1,64,1024]{2,1,0:T(8,128)(2,1)S(1)}, bf16[1,64,1024]{2,1,0:T(8,128)(2,1)S(1)}) fusion(pred[]{:T(512)S(6)} %eq.13, bf16[2,64,512]{2,1,0:T(8,128)(2,1)} %bitcast.66, bf16[2,64,512]{2,1,0:T(8,128)(2,1)} %bitcast.63), kind=kLoop, calls=%fused_computation.23 | loop fusion | flops 589824 | bytes 655361 | tf_op jit(solution)/shard_map/jit(_where)/select_n | solution.py:237
  1.7 13.6 %collective-permute-start = (bf16[64,1024]{1,0:T(8,128)(2,1)S(1)}, bf16[64,1024]{1,0:T(8,128)(2,1)S(1)}, u32[]{:S(2)}, u32[]{:S(2)}) collective-permute-start(bf16[64,1024]{1,0:T(8,128)(2,1)S(1)} %bitcast_select_fusion.1), channel_id=1, source_target_pairs={{1,2},{2,1},{3,4},{4,3},{5,6},{6,5},{7,8},{8,7},{9,10},{10,9},{11,... | collective-permute-start | bytes 393224 | tf_op jit(solution)/shard_map/ppermute | solution.py:240
  15.2 1.9 %collective-permute-start.1 = (bf16[64,1024]{1,0:T(8,128)(2,1)S(1)}, bf16[64,1024]{1,0:T(8,128)(2,1)S(1)}, u32[]{:S(2)}, u32[]{:S(2)}) collective-permute-start(bf16[64,1024]{1,0:T(8,128)(2,1)S(1)} %get-tuple-element.21), channel_id=1, source_target_pairs={{0,1},{1,0},{2,3},{3,2},{4,5},{5,4},{6,7},{7,6},{8,9},{9,8},{10,11... | collective-permute-start | bytes 393224 | tf_op jit(solution)/shard_map/ppermute | solution.py:236
  17.1 0.0 copy-start.9
  17.2 0.7 collective-permute-start.4
  17.8 0.7 collective-permute-start.5
  18.5 0.3 reduce-window.9
  18.8 0.1 slice.43
  18.9 0.1 slice_reduce_fusion
  19.1 5.5 %collective-permute-done.1 = bf16[64,1024]{1,0:T(8,128)(2,1)S(1)} collective-permute-done((bf16[64,1024]{1,0:T(8,128)(2,1)S(1)}, bf16[64,1024]{1,0:T(8,128)(2,1)S(1)}, u32[]{:S(2)}, u32[]{:S(2)}) %collective-permute-start.1) | collective-permute-done | bytes 131104 | tf_op jit(solution)/shard_map/ppermute | solution.py:236
  24.6 0.7 select_bitcast_fusion
  25.3 0.6 copy-done.1
  26.0 1.9 %collective-permute-start.2 = (bf16[2,64,1024]{2,1,0:T(8,128)(2,1)S(1)}, bf16[2,64,1024]{2,1,0:T(8,128)(2,1)S(1)}, u32[]{:S(2)}, u32[]{:S(2)}) collective-permute-start(bf16[2,64,1024]{2,1,0:T(8,128)(2,1)S(1)} %pad_maximum_fusion), channel_id=1, source_target_pairs={{0,2},{1,3},{2,4},{3,5},{4,6},{5,7},{6,8},{7,9},{8,10},{9,11},{10,... | collective-permute-start | bytes 786440 | tf_op jit(solution)/shard_map/ppermute | solution.py:19
  27.9 6.7 %collective-permute-start.3 = (bf16[2,64,1024]{2,1,0:T(8,128)(2,1)S(1)}, bf16[2,64,1024]{2,1,0:T(8,128)(2,1)S(1)}, u32[]{:S(2)}, u32[]{:S(2)}) collective-permute-start(bf16[2,64,1024]{2,1,0:T(8,128)(2,1)S(1)} %pad_maximum_fusion.1), channel_id=1, source_target_pairs={{2,0},{3,1},{4,2},{5,3},{6,4},{7,5},{8,6},{9,7},{10,8},{11,9},{12,... | collective-permute-start | bytes 786440 | tf_op jit(solution)/shard_map/ppermute | solution.py:19
  34.6 0.6 broadcast_add_fusion
  35.2 0.6 pad_add_fusion.flags
  35.8 2.7 %collective-permute-done.3.l2 = bf16[2,64,1024]{2,1,0:T(8,128)(2,1)S(1)} collective-permute-done((bf16[2,64,1024]{2,1,0:T(8,128)(2,1)S(1)}, bf16[2,64,1024]{2,1,0:T(8,128)(2,1)S(1)}, u32[]{:S(2)}, u32[]{:S(2)}) %collective-permute-start.3) | collective-permute-done | bytes 262176 | tf_op jit(solution)/shard_map/ppermute | solution.py:19
  38.6 0.7 copy-done.5
  39.3 5.9 %shard_map.76 = (bf16[2,64,4096]{2,1,0:T(8,128)(2,1)}, bf16[2,64,1024]{2,1,0:T(8,128)(2,1)}, bf16[64,1024]{1,0:T(8,128)(2,1)}, f32[2,64,1024]{2,1,0:T(8,128)}) custom-call(s32[4]{0:T(128)} %pad_add_fusion.flags, s32[1,512]{1,0:T(1,128)} %bitcast.71, bf16[2,64,4096]{2,1,0:T(8,128)(2,1)} %bitcast.57, bf16[2,64,4096]{2,1,0:T(8,128)(2,1)} %bitcast.59, ...), custom_call_target="tpu_custom_call" | custom-call | flops 805306368 | bytes 1835008 | tf_op jit(solution)/shard_map/pallas_call | solution.py:198
  45.2 0.7 copy-done.4
  45.9 6.0 %shard_map.77 = (bf16[2,64,4096]{2,1,0:T(8,128)(2,1)}, bf16[2,64,1024]{2,1,0:T(8,128)(2,1)}, bf16[64,1024]{1,0:T(8,128)(2,1)}, f32[2,64,1024]{2,1,0:T(8,128)}) custom-call(s32[4]{0:T(128)} %pad_add_fusion.flags, s32[1,512]{1,0:T(1,128)} %bitcast.72, bf16[2,64,4096]{2,1,0:T(8,128)(2,1)} %bitcast.58, ...), custom_call_target="tpu_custom_call", output_to_operand_aliasing={{0}: (10, {}), {3}: (11, {})} | custom-call | flops 805306368 | bytes 1835008 | tf_op jit(solution)/shard_map/pallas_call | solution.py:208
  51.9 6.8 %collective-permute-start.6 = (bf16[2,64,1024]{2,1,0:T(8,128)(2,1)}, bf16[2,64,1024]{2,1,0:T(8,128)(2,1)S(1)}, u32[]{:S(2)}, u32[]{:S(2)}) collective-permute-start(bf16[2,64,1024]{2,1,0:T(8,128)(2,1)} %get-tuple-element.17), channel_id=1, source_target_pairs={{2,0},{3,1},{4,2},{5,3},{6,4},{7,5},{8,6},{9,7},{10,8},{11,9},{12,... | collective-permute-start | bytes 786440 | tf_op jit(solution)/shard_map/ppermute | solution.py:19
  58.7 1.9 %collective-permute-start.8 = (bf16[2,64,1024]{2,1,0:T(8,128)(2,1)S(1)}, bf16[2,64,1024]{2,1,0:T(8,128)(2,1)S(1)}, u32[]{:S(2)}, u32[]{:S(2)}) collective-permute-start(bf16[2,64,1024]{2,1,0:T(8,128)(2,1)S(1)} %copy-done.2), channel_id=1, source_target_pairs={{0,2},{1,3},{2,4},{3,5},{4,6},{5,7},{6,8},{7,9},{8,10},{9,11},{10,... | collective-permute-start | bytes 786440 | tf_op jit(solution)/shard_map/ppermute | solution.py:19
  60.7 0.0 copy-start.8
  60.7 0.8 collective-permute-start.9
  61.5 1.4 %collective-permute-done.6 = bf16[2,64,1024]{2,1,0:T(8,128)(2,1)S(1)} collective-permute-done((bf16[2,64,1024]{2,1,0:T(8,128)(2,1)}, bf16[2,64,1024]{2,1,0:T(8,128)(2,1)S(1)}, u32[]{:S(2)}, u32[]{:S(2)}) %collective-permute-start.6) | collective-permute-done | bytes 262176 | tf_op jit(solution)/shard_map/ppermute | solution.py:19
  63.0 5.9 %collective-permute-start.7 = (bf16[64,1024]{1,0:T(8,128)(2,1)S(1)}, bf16[64,1024]{1,0:T(8,128)(2,1)S(1)}, u32[]{:S(2)}, u32[]{:S(2)}) collective-permute-start(bf16[64,1024]{1,0:T(8,128)(2,1)S(1)} %fusion.4), channel_id=1, source_target_pairs={{1,0},{2,1},{3,2},{4,3},{5,4},{6,5},{7,6},{8,7},{9,8},{10,9},{11,1... | collective-permute-start | bytes 393224 | tf_op jit(solution)/shard_map/ppermute | solution.py:19
  68.9 2.0 %collective-permute-done.8 = bf16[2,64,1024]{2,1,0:T(8,128)(2,1)S(1)} collective-permute-done((bf16[2,64,1024]{2,1,0:T(8,128)(2,1)S(1)}, bf16[2,64,1024]{2,1,0:T(8,128)(2,1)S(1)}, u32[]{:S(2)}, u32[]{:S(2)}) %collective-permute-start.8) | collective-permute-done | bytes 262176 | tf_op jit(solution)/shard_map/ppermute | solution.py:19
  71.0 2.3 %collective-permute-start.10 = (bf16[64,1024]{1,0:T(8,128)(2,1)S(1)}, bf16[64,1024]{1,0:T(8,128)(2,1)S(1)}, u32[]{:S(2)}, u32[]{:S(2)}) collective-permute-start(bf16[64,1024]{1,0:T(8,128)(2,1)S(1)} %add_convert_fusion), channel_id=1, source_target_pairs={{0,1},{1,2},{2,3},{3,4},{4,5},{5,6},{6,7},{7,8},{8,9},{9,10},{10,1... | collective-permute-start | bytes 393224 | tf_op jit(solution)/shard_map/ppermute | solution.py:19
  73.3 8.2 %collective-permute-done.10 = bf16[64,1024]{1,0:T(8,128)(2,1)S(1)} collective-permute-done((bf16[64,1024]{1,0:T(8,128)(2,1)S(1)}, bf16[64,1024]{1,0:T(8,128)(2,1)S(1)}, u32[]{:S(2)}, u32[]{:S(2)}) %collective-permute-start.10) | collective-permute-done | bytes 131104 | tf_op jit(solution)/shard_map/ppermute | solution.py:19
  81.5 0.1 fusion.8
  81.7 0.7 slice_bitcast_fusion.2
  (31 shorter events, 0.3 us)
Async XLA Ops:
  1.7 17.4 %collective-permute-start = (bf16[64,1024]{1,0:T(8,128)(2,1)S(1)}, bf16[64,1024]{1,0:T(8,128)(2,1)S(1)}, u32[]{:S(2)}, u32[]{:S(2)}) collective-permute-start(bf16[64,1024]{1,0:T(8,128)(2,1)S(1)} %bitcast_select_fusion.1), channel_id=1, source_target_pairs={{1,2},{2,1},{3,4},{4,3},{5,6},{6,5},{7,8},{8,7},{9,10},{10,9},{11,... | collective-permute-start | bytes 393224 | tf_op jit(solution)/shard_map/ppermute | solution.py:240
  15.2 9.4 %collective-permute-start.1 = (bf16[64,1024]{1,0:T(8,128)(2,1)S(1)}, bf16[64,1024]{1,0:T(8,128)(2,1)S(1)}, u32[]{:S(2)}, u32[]{:S(2)}) collective-permute-start(bf16[64,1024]{1,0:T(8,128)(2,1)S(1)} %get-tuple-element.21), channel_id=1, source_target_pairs={{0,1},{1,0},{2,3},{3,2},{4,5},{5,4},{6,7},{7,6},{8,9},{9,8},{10,11... | collective-permute-start | bytes 393224 | tf_op jit(solution)/shard_map/ppermute | solution.py:236
  17.1 1.4 %copy-start.9 = (s32[512]{0:T(512)S(1)}, s32[512]{0:T(512)}, u32[]{:S(2)}) copy-start(s32[512]{0:T(512)} %param.9) | copy-start | bytes 6148
  17.2 18.7 %collective-permute-start.4 = (bf16[64,1024]{1,0:T(8,128)(2,1)S(1)}, bf16[64,1024]{1,0:T(8,128)(2,1)S(1)}, u32[]{:S(2)}, u32[]{:S(2)}) collective-permute-start(bf16[64,1024]{1,0:T(8,128)(2,1)S(1)} %bitcast.61), channel_id=1, source_target_pairs={{511,510},{510,511}} | collective-permute-start | bytes 393224 | tf_op jit(solution)/shard_map/ppermute | solution.py:246
  17.8 18.0 %collective-permute-start.5 = (bf16[64,1024]{1,0:T(8,128)(2,1)S(1)}, bf16[64,1024]{1,0:T(8,128)(2,1)S(1)}, u32[]{:S(2)}, u32[]{:S(2)}) collective-permute-start(bf16[64,1024]{1,0:T(8,128)(2,1)S(1)} %bitcast.62), channel_id=1, source_target_pairs={{509,511}} | collective-permute-start | bytes 393224 | tf_op jit(solution)/shard_map/ppermute | solution.py:247
  25.3 0.7 copy-start.1
  26.0 19.2 %collective-permute-start.2 = (bf16[2,64,1024]{2,1,0:T(8,128)(2,1)S(1)}, bf16[2,64,1024]{2,1,0:T(8,128)(2,1)S(1)}, u32[]{:S(2)}, u32[]{:S(2)}) collective-permute-start(bf16[2,64,1024]{2,1,0:T(8,128)(2,1)S(1)} %pad_maximum_fusion), channel_id=1, source_target_pairs={{0,2},{1,3},{2,4},{3,5},{4,6},{5,7},{6,8},{7,9},{8,10},{9,11},{10,... | collective-permute-start | bytes 786440 | tf_op jit(solution)/shard_map/ppermute | solution.py:19
  27.9 10.7 %collective-permute-start.3 = (bf16[2,64,1024]{2,1,0:T(8,128)(2,1)S(1)}, bf16[2,64,1024]{2,1,0:T(8,128)(2,1)S(1)}, u32[]{:S(2)}, u32[]{:S(2)}) collective-permute-start(bf16[2,64,1024]{2,1,0:T(8,128)(2,1)S(1)} %pad_maximum_fusion.1), channel_id=1, source_target_pairs={{2,0},{3,1},{4,2},{5,3},{6,4},{7,5},{8,6},{9,7},{10,8},{11,9},{12,... | collective-permute-start | bytes 786440 | tf_op jit(solution)/shard_map/ppermute | solution.py:19
  35.8 2.7 %copy-start.6 = (bf16[64,1024]{1,0:T(8,128)(2,1)}, bf16[64,1024]{1,0:T(8,128)(2,1)S(1)}, u32[]{:S(2)}) copy-start(bf16[64,1024]{1,0:T(8,128)(2,1)S(1)} %collective-permute-done.4.turn2) | copy-start | bytes 393220
  35.8 2.7 %copy-start.7 = (bf16[64,1024]{1,0:T(8,128)(2,1)}, bf16[64,1024]{1,0:T(8,128)(2,1)S(1)}, u32[]{:S(2)}) copy-start(bf16[64,1024]{1,0:T(8,128)(2,1)S(1)} %collective-permute-done.5.turn3) | copy-start | bytes 393220
  38.6 0.7 copy-start.5
  45.2 0.7 copy-start.4
  45.9 12.8 %copy-start.2 = (bf16[2,64,1024]{2,1,0:T(8,128)(2,1)S(1)}, bf16[2,64,1024]{2,1,0:T(8,128)(2,1)}, u32[]{:S(2)}) copy-start(bf16[2,64,1024]{2,1,0:T(8,128)(2,1)} %get-tuple-element.11.a_l) | copy-start | bytes 786436
  51.9 11.0 %collective-permute-start.6 = (bf16[2,64,1024]{2,1,0:T(8,128)(2,1)}, bf16[2,64,1024]{2,1,0:T(8,128)(2,1)S(1)}, u32[]{:S(2)}, u32[]{:S(2)}) collective-permute-start(bf16[2,64,1024]{2,1,0:T(8,128)(2,1)} %get-tuple-element.17), channel_id=1, source_target_pairs={{2,0},{3,1},{4,2},{5,3},{6,4},{7,5},{8,6},{9,7},{10,8},{11,9},{12,... | collective-permute-start | bytes 786440 | tf_op jit(solution)/shard_map/ppermute | solution.py:19
  58.7 12.2 %collective-permute-start.8 = (bf16[2,64,1024]{2,1,0:T(8,128)(2,1)S(1)}, bf16[2,64,1024]{2,1,0:T(8,128)(2,1)S(1)}, u32[]{:S(2)}, u32[]{:S(2)}) collective-permute-start(bf16[2,64,1024]{2,1,0:T(8,128)(2,1)S(1)} %copy-done.2), channel_id=1, source_target_pairs={{0,2},{1,3},{2,4},{3,5},{4,6},{5,7},{6,8},{7,9},{8,10},{9,11},{10,... | collective-permute-start | bytes 786440 | tf_op jit(solution)/shard_map/ppermute | solution.py:19
  60.7 2.3 %copy-start.8 = (bf16[64,1024]{1,0:T(8,128)(2,1)S(1)}, bf16[64,1024]{1,0:T(8,128)(2,1)}, u32[]{:S(2)}) copy-start(bf16[64,1024]{1,0:T(8,128)(2,1)} %get-tuple-element.18) | copy-start | bytes 393220
  60.7 12.6 %collective-permute-start.9 = (bf16[64,1024]{1,0:T(8,128)(2,1)S(1)}, bf16[64,1024]{1,0:T(8,128)(2,1)S(1)}, u32[]{:S(2)}, u32[]{:S(2)}) collective-permute-start(bf16[64,1024]{1,0:T(8,128)(2,1)S(1)} %slice_bitcast_fusion.4), channel_id=1, source_target_pairs={{510,511}} | collective-permute-start | bytes 393224 | tf_op jit(solution)/shard_map/ppermute | solution.py:259
  63.0 8.0 %copy-start.3 = (bf16[64,1024]{1,0:T(8,128)(2,1)S(1)}, bf16[64,1024]{1,0:T(8,128)(2,1)}, u32[]{:S(2)}) copy-start(bf16[64,1024]{1,0:T(8,128)(2,1)} %get-tuple-element.12.p2_late) | copy-start | bytes 393220
  63.0 18.5 %copy-start = (f32[2,64,1024]{2,1,0:T(8,128)S(1)}, f32[2,64,1024]{2,1,0:T(8,128)}, u32[]{:S(2)}) copy-start(f32[2,64,1024]{2,1,0:T(8,128)} %get-tuple-element.16) | copy-start | bytes 1572868
  63.0 10.3 %collective-permute-start.7 = (bf16[64,1024]{1,0:T(8,128)(2,1)S(1)}, bf16[64,1024]{1,0:T(8,128)(2,1)S(1)}, u32[]{:S(2)}, u32[]{:S(2)}) collective-permute-start(bf16[64,1024]{1,0:T(8,128)(2,1)S(1)} %fusion.4), channel_id=1, source_target_pairs={{1,0},{2,1},{3,2},{4,3},{5,4},{6,5},{7,6},{8,7},{9,8},{10,9},{11,1... | collective-permute-start | bytes 393224 | tf_op jit(solution)/shard_map/ppermute | solution.py:19
  71.0 10.5 %collective-permute-start.10 = (bf16[64,1024]{1,0:T(8,128)(2,1)S(1)}, bf16[64,1024]{1,0:T(8,128)(2,1)S(1)}, u32[]{:S(2)}, u32[]{:S(2)}) collective-permute-start(bf16[64,1024]{1,0:T(8,128)(2,1)S(1)} %add_convert_fusion), channel_id=1, source_target_pairs={{0,1},{1,2},{2,3},{3,4},{4,5},{5,6},{6,7},{7,8},{8,9},{9,10},{10,1... | collective-permute-start | bytes 393224 | tf_op jit(solution)/shard_map/ppermute | solution.py:19

commit v15 on v13

--- a/solution.py
+++ b/solution.py
@@ -35,7 +35,6 @@
     bias = jnp.where(visible, 0.0, -1e30).astype(jnp.float32)
     bias = jnp.concatenate([bias] * group_size, axis=0)
     nt = (((1,), (1,)), ((), ()))
-    tn = (((0,), (0,)), ((), ()))
     for g in range(groups):
         base = g * group_size * HEAD
         qg = jnp.concatenate(
@@ -59,8 +58,8 @@
         dq = jnp.dot(dscore, kg, preferred_element_type=jnp.float32).astype(jnp.bfloat16)
         for h in range(group_size):
             emit("dq", h, base + h * HEAD, dq[h * half_rows:(h + 1) * half_rows])
-        dk = lax.dot_general(dscore, qg, tn, preferred_element_type=jnp.float32)
-        dv = lax.dot_general(probs, dog, tn, preferred_element_type=jnp.float32)
+        dk = jnp.dot(qg.T, dscore, preferred_element_type=jnp.float32).T
+        dv = jnp.dot(dog.T, probs, preferred_element_type=jnp.float32).T
         for j in range(4):
             emit("part", j, g * HEAD, dk[j * half_rows:(j + 1) * half_rows])
             emit("part", j, kv_width + g * HEAD, dv[j * half_rows:(j + 1) * half_rows])

time: 74.8 us -> 74.4 us (level)
  transfers between devices with their start and end apart: 11 -> 11, of which waited for: 6 -> 6; matrix products, arithmetic and copies ran while one was open for 3% -> 3% of each run, Pallas kernels for 16% -> 15%
where the time goes in v15:
time: 74.4 us; the launch traced here: 73.7 us
  starting transfers between devices  45.3 us (61%)
  Pallas kernels  11.4 us (15%)
  waiting for transfers between devices  8.8 us (12%)
  local copies, waits for them, and re-layouts  4.3 us (6%)
  other arithmetic  2.95 us (4%)
  between operations  0.91 us (1%)
    ppermute x8, starting transfers between devices, shifted(): return lax.ppermute(value, AXIS, pairs)  43.2 us
    ppermute x8, waiting for transfers between devices, shifted(): return lax.ppermute(value, AXIS, pairs)  8.79 us
    pallas_call x1, Pallas kernels, window_grads(): pl.pallas_call(functools.partial(early_kernel, groups=groups, group_size=...  5.76 us
    pallas_call x1, Pallas kernels, window_grads(): pl.pallas_call(functools.partial(late_kernel, groups=groups, group_size=g...  5.65 us
    unnamed x26, local copies, waits for them, and re-layouts  3.38 us
  transfers between devices with their start and end apart: 11, of which 6 were waited for; matrix products, arithmetic and copies ran while one was open for 3% of the time, Pallas kernels for 15%

profile of v15, /device:TPU:6, one launch (start us, length us, event | category | flops | bytes accessed | tf_op | source)
XLA Modules:
  0.0 73.7 jit_solution(7306175129505069738)
XLA Ops:
  0.7 0.9 %pad_maximum_fusion.2 = bf16[1,64,1024]{2,1,0:T(8,128)(2,1)S(1)} fusion(bf16[2,64,512]{2,1,0:T(8,128)(2,1)} %bitcast.61, bf16[2,64,512]{2,1,0:T(8,128)(2,1)} %bitcast.57), kind=kLoop, calls=%fused_computation.22 | loop fusion | flops 262144 | bytes 393216 | tf_op jit(solution)/shard_map/concatenate | solution.py:229
  1.6 13.6 %collective-permute-start.2 = (bf16[64,1024]{1,0:T(8,128)(2,1)S(1)}, bf16[64,1024]{1,0:T(8,128)(2,1)S(1)}, u32[]{:S(2)}, u32[]{:S(2)}) collective-permute-start(bf16[64,1024]{1,0:T(8,128)(2,1)S(1)} %bitcast.67), channel_id=1, source_target_pairs={{1,0},{2,1},{3,2},{4,3},{5,4},{6,5},{7,6},{8,7},{9,8},{10,9},{11,1... | collective-permute-start | bytes 393224 | tf_op jit(solution)/shard_map/ppermute | solution.py:19
  15.2 0.7 copy-done.12
  15.8 0.3 reduce-window.9
  16.1 0.1 slice.43
  16.3 2.7 %collective-permute-done.2.l1 = bf16[64,1024]{1,0:T(8,128)(2,1)S(1)} collective-permute-done((bf16[64,1024]{1,0:T(8,128)(2,1)S(1)}, bf16[64,1024]{1,0:T(8,128)(2,1)S(1)}, u32[]{:S(2)}, u32[]{:S(2)}) %collective-permute-start.2) | collective-permute-done | bytes 131104 | tf_op jit(solution)/shard_map/ppermute | solution.py:19
  19.0 0.6 copy-done.4
  19.6 1.9 %collective-permute-start = (bf16[64,1024]{1,0:T(8,128)(2,1)S(1)}, bf16[64,1024]{1,0:T(8,128)(2,1)S(1)}, u32[]{:S(2)}, u32[]{:S(2)}) collective-permute-start(bf16[64,1024]{1,0:T(8,128)(2,1)S(1)} %bitcast.68), channel_id=1, source_target_pairs={{0,1},{1,2},{2,3},{3,4},{4,5},{5,6},{6,7},{7,8},{8,9},{9,10},{10,1... | collective-permute-start | bytes 393224 | tf_op jit(solution)/shard_map/ppermute | solution.py:19
  21.5 0.1 slice_reduce_fusion
  21.6 0.7 collective-permute-start.4
  22.3 0.7 collective-permute-start.5
  23.0 8.6 %collective-permute-start.3 = (bf16[2,64,1024]{2,1,0:T(8,128)(2,1)S(1)}, bf16[2,64,1024]{2,1,0:T(8,128)(2,1)S(1)}, u32[]{:S(2)}, u32[]{:S(2)}) collective-permute-start(bf16[2,64,1024]{2,1,0:T(8,128)(2,1)S(1)} %pad_maximum_fusion.1), channel_id=1, source_target_pairs={{2,0},{3,1},{4,2},{5,3},{6,4},{7,5},{8,6},{9,7},{10,8},{11,9},{12,... | collective-permute-start | bytes 786440 | tf_op jit(solution)/shard_map/ppermute | solution.py:19
  31.6 0.1 collective-permute-done.e1
  31.8 0.6 copy-done.5
  32.4 1.9 %collective-permute-start.1 = (bf16[2,64,1024]{2,1,0:T(8,128)(2,1)S(1)}, bf16[2,64,1024]{2,1,0:T(8,128)(2,1)S(1)}, u32[]{:S(2)}, u32[]{:S(2)}) collective-permute-start(bf16[2,64,1024]{2,1,0:T(8,128)(2,1)S(1)} %pad_maximum_fusion), channel_id=1, source_target_pairs={{0,2},{1,3},{2,4},{3,5},{4,6},{5,7},{6,8},{7,9},{8,10},{9,11},{10,... | collective-permute-start | bytes 786440 | tf_op jit(solution)/shard_map/ppermute | solution.py:19
  34.3 0.6 broadcast_add_fusion
  34.9 0.7 pad_add_fusion.flags
  35.6 1.9 %collective-permute-done.3.l2 = bf16[2,64,1024]{2,1,0:T(8,128)(2,1)S(1)} collective-permute-done((bf16[2,64,1024]{2,1,0:T(8,128)(2,1)S(1)}, bf16[2,64,1024]{2,1,0:T(8,128)(2,1)S(1)}, u32[]{:S(2)}, u32[]{:S(2)}) %collective-permute-start.3) | collective-permute-done | bytes 262176 | tf_op jit(solution)/shard_map/ppermute | solution.py:19
  37.6 0.7 copy-done.8
  38.2 5.7 %shard_map.76 = (bf16[2,64,4096]{2,1,0:T(8,128)(2,1)}, bf16[2,64,1024]{2,1,0:T(8,128)(2,1)}, bf16[64,1024]{1,0:T(8,128)(2,1)}, f32[2,64,1024]{2,1,0:T(8,128)}) custom-call(s32[4]{0:T(128)} %pad_add_fusion.flags, s32[1,512]{1,0:T(1,128)} %bitcast.71, bf16[2,64,4096]{2,1,0:T(8,128)(2,1)} %bitcast.53, bf16[2,64,4096]{2,1,0:T(8,128)(2,1)} %bitcast.55, ...), custom_call_target="tpu_custom_call" | custom-call | flops 805306368 | bytes 1835008 | tf_op jit(solution)/shard_map/pallas_call | solution.py:197
  43.9 1.9 %collective-permute-start.8 = (bf16[2,64,1024]{2,1,0:T(8,128)(2,1)}, bf16[2,64,1024]{2,1,0:T(8,128)(2,1)S(1)}, u32[]{:S(2)}, u32[]{:S(2)}) collective-permute-start(bf16[2,64,1024]{2,1,0:T(8,128)(2,1)} %get-tuple-element.11.a_l), channel_id=1, source_target_pairs={{0,2},{1,3},{2,4},{3,5},{4,6},{5,7},{6,8},{7,9},{8,10},{9,11},{10,... | collective-permute-start | bytes 786440 | tf_op jit(solution)/shard_map/ppermute | solution.py:19
  45.8 0.7 copy-done.7
  46.6 5.8 %shard_map.77 = (bf16[2,64,4096]{2,1,0:T(8,128)(2,1)}, bf16[2,64,1024]{2,1,0:T(8,128)(2,1)}, bf16[64,1024]{1,0:T(8,128)(2,1)}, f32[2,64,1024]{2,1,0:T(8,128)}) custom-call(s32[4]{0:T(128)} %pad_add_fusion.flags, s32[1,512]{1,0:T(1,128)} %bitcast.72, bf16[2,64,4096]{2,1,0:T(8,128)(2,1)} %bitcast.54, ...), custom_call_target="tpu_custom_call", output_to_operand_aliasing={{0}: (10, {}), {3}: (11, {})} | custom-call | flops 805306368 | bytes 1835008 | tf_op jit(solution)/shard_map/pallas_call | solution.py:207
  52.3 6.8 %collective-permute-start.6 = (bf16[2,64,1024]{2,1,0:T(8,128)(2,1)}, bf16[2,64,1024]{2,1,0:T(8,128)(2,1)S(1)}, u32[]{:S(2)}, u32[]{:S(2)}) collective-permute-start(bf16[2,64,1024]{2,1,0:T(8,128)(2,1)} %get-tuple-element.17), channel_id=1, source_target_pairs={{2,0},{3,1},{4,2},{5,3},{6,4},{7,5},{8,6},{9,7},{10,8},{11,9},{12,... | collective-permute-start | bytes 786440 | tf_op jit(solution)/shard_map/ppermute | solution.py:19
  59.2 0.8 %collective-permute-start.9 = (bf16[64,1024]{1,0:T(8,128)(2,1)S(1)}, bf16[64,1024]{1,0:T(8,128)(2,1)S(1)}, u32[]{:S(2)}, u32[]{:S(2)}) collective-permute-start(bf16[64,1024]{1,0:T(8,128)(2,1)S(1)} %slice_bitcast_fusion.4), channel_id=1, source_target_pairs={{510,511}} | collective-permute-start | bytes 393224 | tf_op jit(solution)/shard_map/ppermute | solution.py:249
  60.1 2.1 %collective-permute-start.10 = (bf16[64,1024]{1,0:T(8,128)(2,1)S(1)}, bf16[64,1024]{1,0:T(8,128)(2,1)S(1)}, u32[]{:S(2)}, u32[]{:S(2)}) collective-permute-start(bf16[64,1024]{1,0:T(8,128)(2,1)S(1)} %add_convert_fusion), channel_id=1, source_target_pairs={{0,1},{1,2},{2,3},{3,4},{4,5},{5,6},{6,7},{7,8},{8,9},{9,10},{10,1... | collective-permute-start | bytes 393224 | tf_op jit(solution)/shard_map/ppermute | solution.py:19
  62.2 1.5 %collective-permute-done.6 = bf16[2,64,1024]{2,1,0:T(8,128)(2,1)S(1)} collective-permute-done((bf16[2,64,1024]{2,1,0:T(8,128)(2,1)}, bf16[2,64,1024]{2,1,0:T(8,128)(2,1)S(1)}, u32[]{:S(2)}, u32[]{:S(2)}) %collective-permute-start.6) | collective-permute-done | bytes 262176 | tf_op jit(solution)/shard_map/ppermute | solution.py:19
  63.7 6.4 %collective-permute-start.7 = (bf16[64,1024]{1,0:T(8,128)(2,1)S(1)}, bf16[64,1024]{1,0:T(8,128)(2,1)S(1)}, u32[]{:S(2)}, u32[]{:S(2)}) collective-permute-start(bf16[64,1024]{1,0:T(8,128)(2,1)S(1)} %fusion.4), channel_id=1, source_target_pairs={{1,0},{2,1},{3,2},{4,3},{5,4},{6,5},{7,6},{8,7},{9,8},{10,9},{11,1... | collective-permute-start | bytes 393224 | tf_op jit(solution)/shard_map/ppermute | solution.py:19
  70.2 1.4 %collective-permute-done.10 = bf16[64,1024]{1,0:T(8,128)(2,1)S(1)} collective-permute-done((bf16[64,1024]{1,0:T(8,128)(2,1)S(1)}, bf16[64,1024]{1,0:T(8,128)(2,1)S(1)}, u32[]{:S(2)}, u32[]{:S(2)}) %collective-permute-start.10) | collective-permute-done | bytes 131104 | tf_op jit(solution)/shard_map/ppermute | solution.py:19
  71.6 1.2 %collective-permute-done.7 = bf16[64,1024]{1,0:T(8,128)(2,1)S(1)} collective-permute-done((bf16[64,1024]{1,0:T(8,128)(2,1)S(1)}, bf16[64,1024]{1,0:T(8,128)(2,1)S(1)}, u32[]{:S(2)}, u32[]{:S(2)}) %collective-permute-start.7) | collective-permute-done | bytes 131104 | tf_op jit(solution)/shard_map/ppermute | solution.py:19
  72.8 0.1 fusion.8
  72.9 0.7 slice_bitcast_fusion.2
  (36 shorter events, 0.4 us)
Async XLA Ops:
  0.6 18.3 %copy-start.1 = (bf16[1,2,64,512]{3,2,1,0:T(8,128)(2,1)S(1)}, bf16[1,2,64,512]{3,2,1,0:T(8,128)(2,1)}, u32[]{:S(2)}) copy-start(bf16[1,2,64,512]{3,2,1,0:T(8,128)(2,1)} %param.6) | copy-start | bytes 393220
  0.6 18.3 %copy-start.2 = (bf16[1,2,64,512]{3,2,1,0:T(8,128)(2,1)S(1)}, bf16[1,2,64,512]{3,2,1,0:T(8,128)(2,1)}, u32[]{:S(2)}) copy-start(bf16[1,2,64,512]{3,2,1,0:T(8,128)(2,1)} %param.7) | copy-start | bytes 393220
  1.6 17.3 %collective-permute-start.2 = (bf16[64,1024]{1,0:T(8,128)(2,1)S(1)}, bf16[64,1024]{1,0:T(8,128)(2,1)S(1)}, u32[]{:S(2)}, u32[]{:S(2)}) collective-permute-start(bf16[64,1024]{1,0:T(8,128)(2,1)S(1)} %bitcast.67), channel_id=1, source_target_pairs={{1,0},{2,1},{3,2},{4,3},{5,4},{6,5},{7,6},{8,7},{9,8},{10,9},{11,1... | collective-permute-start | bytes 393224 | tf_op jit(solution)/shard_map/ppermute | solution.py:19
  15.2 0.7 copy-start.12
  18.9 0.7 copy-start.4
  19.6 12.2 %collective-permute-start = (bf16[64,1024]{1,0:T(8,128)(2,1)S(1)}, bf16[64,1024]{1,0:T(8,128)(2,1)S(1)}, u32[]{:S(2)}, u32[]{:S(2)}) collective-permute-start(bf16[64,1024]{1,0:T(8,128)(2,1)S(1)} %bitcast.68), channel_id=1, source_target_pairs={{0,1},{1,2},{2,3},{3,4},{4,5},{5,6},{6,7},{7,8},{8,9},{9,10},{10,1... | collective-permute-start | bytes 393224 | tf_op jit(solution)/shard_map/ppermute | solution.py:19
  21.6 14.0 %collective-permute-start.4 = (bf16[64,1024]{1,0:T(8,128)(2,1)S(1)}, bf16[64,1024]{1,0:T(8,128)(2,1)S(1)}, u32[]{:S(2)}, u32[]{:S(2)}) collective-permute-start(bf16[64,1024]{1,0:T(8,128)(2,1)S(1)} %bitcast.69), channel_id=1, source_target_pairs={{511,510},{510,511}} | collective-permute-start | bytes 393224 | tf_op jit(solution)/shard_map/ppermute | solution.py:236
  22.3 13.3 %collective-permute-start.5 = (bf16[64,1024]{1,0:T(8,128)(2,1)S(1)}, bf16[64,1024]{1,0:T(8,128)(2,1)S(1)}, u32[]{:S(2)}, u32[]{:S(2)}) collective-permute-start(bf16[64,1024]{1,0:T(8,128)(2,1)S(1)} %bitcast.70), channel_id=1, source_target_pairs={{509,511}} | collective-permute-start | bytes 393224 | tf_op jit(solution)/shard_map/ppermute | solution.py:237
  23.0 14.6 %collective-permute-start.3 = (bf16[2,64,1024]{2,1,0:T(8,128)(2,1)S(1)}, bf16[2,64,1024]{2,1,0:T(8,128)(2,1)S(1)}, u32[]{:S(2)}, u32[]{:S(2)}) collective-permute-start(bf16[2,64,1024]{2,1,0:T(8,128)(2,1)S(1)} %pad_maximum_fusion.1), channel_id=1, source_target_pairs={{2,0},{3,1},{4,2},{5,3},{6,4},{7,5},{8,6},{9,7},{10,8},{11,9},{12,... | collective-permute-start | bytes 786440 | tf_op jit(solution)/shard_map/ppermute | solution.py:19
  31.7 0.7 copy-start.5
  32.4 13.4 %collective-permute-start.1 = (bf16[2,64,1024]{2,1,0:T(8,128)(2,1)S(1)}, bf16[2,64,1024]{2,1,0:T(8,128)(2,1)S(1)}, u32[]{:S(2)}, u32[]{:S(2)}) collective-permute-start(bf16[2,64,1024]{2,1,0:T(8,128)(2,1)S(1)} %pad_maximum_fusion), channel_id=1, source_target_pairs={{0,2},{1,3},{2,4},{3,5},{4,6},{5,7},{6,8},{7,9},{8,10},{9,11},{10,... | collective-permute-start | bytes 786440 | tf_op jit(solution)/shard_map/ppermute | solution.py:19
  35.6 2.0 %copy-start.9 = (bf16[64,1024]{1,0:T(8,128)(2,1)}, bf16[64,1024]{1,0:T(8,128)(2,1)S(1)}, u32[]{:S(2)}) copy-start(bf16[64,1024]{1,0:T(8,128)(2,1)S(1)} %collective-permute-done.4.turn2) | copy-start | bytes 393220
  35.6 2.0 %copy-start.10 = (bf16[64,1024]{1,0:T(8,128)(2,1)}, bf16[64,1024]{1,0:T(8,128)(2,1)S(1)}, u32[]{:S(2)}) copy-start(bf16[64,1024]{1,0:T(8,128)(2,1)S(1)} %collective-permute-done.5.turn3) | copy-start | bytes 393220
  37.6 0.7 copy-start.8
  43.9 16.1 %collective-permute-start.8 = (bf16[2,64,1024]{2,1,0:T(8,128)(2,1)}, bf16[2,64,1024]{2,1,0:T(8,128)(2,1)S(1)}, u32[]{:S(2)}, u32[]{:S(2)}) collective-permute-start(bf16[2,64,1024]{2,1,0:T(8,128)(2,1)} %get-tuple-element.11.a_l), channel_id=1, source_target_pairs={{0,2},{1,3},{2,4},{3,5},{4,6},{5,7},{6,8},{7,9},{8,10},{9,11},{10,... | collective-permute-start | bytes 786440 | tf_op jit(solution)/shard_map/ppermute | solution.py:19
  45.8 0.7 copy-start.7
  46.6 12.6 %copy-start.3 = (bf16[2,64,1024]{2,1,0:T(8,128)(2,1)S(1)}, bf16[2,64,1024]{2,1,0:T(8,128)(2,1)}, u32[]{:S(2)}) copy-start(bf16[2,64,1024]{2,1,0:T(8,128)(2,1)} %get-tuple-element.11.a_l) | copy-start | bytes 786436
  52.3 11.3 %collective-permute-start.6 = (bf16[2,64,1024]{2,1,0:T(8,128)(2,1)}, bf16[2,64,1024]{2,1,0:T(8,128)(2,1)S(1)}, u32[]{:S(2)}, u32[]{:S(2)}) collective-permute-start(bf16[2,64,1024]{2,1,0:T(8,128)(2,1)} %get-tuple-element.17), channel_id=1, source_target_pairs={{2,0},{3,1},{4,2},{5,3},{6,4},{7,5},{8,6},{9,7},{10,8},{11,9},{12,... | collective-permute-start | bytes 786440 | tf_op jit(solution)/shard_map/ppermute | solution.py:19
  59.2 0.9 %copy-start.6 = (bf16[64,1024]{1,0:T(8,128)(2,1)S(1)}, bf16[64,1024]{1,0:T(8,128)(2,1)}, u32[]{:S(2)}) copy-start(bf16[64,1024]{1,0:T(8,128)(2,1)} %get-tuple-element.12.p2_late) | copy-start | bytes 393220
  59.2 11.0 %collective-permute-start.9 = (bf16[64,1024]{1,0:T(8,128)(2,1)S(1)}, bf16[64,1024]{1,0:T(8,128)(2,1)S(1)}, u32[]{:S(2)}, u32[]{:S(2)}) collective-permute-start(bf16[64,1024]{1,0:T(8,128)(2,1)S(1)} %slice_bitcast_fusion.4), channel_id=1, source_target_pairs={{510,511}} | collective-permute-start | bytes 393224 | tf_op jit(solution)/shard_map/ppermute | solution.py:249
  60.1 3.6 %copy-start.11 = (bf16[64,1024]{1,0:T(8,128)(2,1)S(1)}, bf16[64,1024]{1,0:T(8,128)(2,1)}, u32[]{:S(2)}) copy-start(bf16[64,1024]{1,0:T(8,128)(2,1)} %get-tuple-element.18) | copy-start | bytes 393220
  60.1 12.6 %copy-start = (f32[2,64,1024]{2,1,0:T(8,128)S(1)}, f32[2,64,1024]{2,1,0:T(8,128)}, u32[]{:S(2)}) copy-start(f32[2,64,1024]{2,1,0:T(8,128)} %get-tuple-element.16) | copy-start | bytes 1572868
  60.1 11.5 %collective-permute-start.10 = (bf16[64,1024]{1,0:T(8,128)(2,1)S(1)}, bf16[64,1024]{1,0:T(8,128)(2,1)S(1)}, u32[]{:S(2)}, u32[]{:S(2)}) collective-permute-start(bf16[64,1024]{1,0:T(8,128)(2,1)S(1)} %add_convert_fusion), channel_id=1, source_target_pairs={{0,1},{1,2},{2,3},{3,4},{4,5},{5,6},{6,7},{7,8},{8,9},{9,10},{10,1... | collective-permute-start | bytes 393224 | tf_op jit(solution)/shard_map/ppermute | solution.py:19
  63.7 9.0 %collective-permute-start.7 = (bf16[64,1024]{1,0:T(8,128)(2,1)S(1)}, bf16[64,1024]{1,0:T(8,128)(2,1)S(1)}, u32[]{:S(2)}, u32[]{:S(2)}) collective-permute-start(bf16[64,1024]{1,0:T(8,128)(2,1)S(1)} %fusion.4), channel_id=1, source_target_pairs={{1,0},{2,1},{3,2},{4,3},{5,4},{6,5},{7,6},{8,7},{9,8},{10,9},{11,1... | collective-permute-start | bytes 393224 | tf_op jit(solution)/shard_map/ppermute | solution.py:19
